TPU v7x, 512 devices: a whole 4x4x16 slice. The times are simulated.
512 devices in a mesh: row: 16 (over z), col: 32 (over y, x, core).
Axes of the slice: x: 4, y: 4, z: 16, core: 2. Of those that a mesh axis runs over, the one named last changes fastest.
Arguments:
- node_feats: bfloat16 [262144, 512], P(('row', 'col')), may hold values from -8 to 8
- source_feats: bfloat16 [4096, 512], P('col'), may hold values from -6 to 6
- nbr_blocks: int32 [2048, 8], P(('row', 'col')), may hold values from 0 to 31
- nbr_count: int32 [2048], P(('row', 'col')), may hold values from 1 to 8
- adj_tiles: bfloat16 [2048, 8, 128, 128], P(('row', 'col')), may hold values from -0.1875 to 0.1875
- pos_index: int32 [262144], P(('row', 'col')), may hold values from 0 to 511
- noise_block_rows: int32 [16], replicated, may hold values from 0 to 15
- w_self: bfloat16 [512, 512], replicated, may hold values from -0.25 to 0.25
- w_neigh: bfloat16 [512, 512], replicated, may hold values from -0.25 to 0.25
Outputs:
- grad_self: float32 [512, 512], replicated
- neighbour_weight_gradient: float32 [512, 512], replicated
- loss: float32 [], replicated
All inputs are finite; a program needn't handle non-finite values.
Results may differ from a plain program's by a relative error of at most 0.002.
Values may be sent and summed in bfloat16 or wider, within the bound.
No kernel may reach another device: no remote copies, remote signals or barrier semaphores. Data moves between devices by JAX's collectives and lax.ppermute only.
A program may use at most 64 MiB of HBM per device.

v0:
```python
import jax
import jax.numpy as jnp
from jax import lax
from jax.sharding import PartitionSpec as P

BLOCK = 128
NOISE = 128


softness_divisor = 0.2


def embed(pre):
    return pre * lax.rsqrt(jnp.sum(pre * pre, axis=-1, keepdims=True) + 1e-06)


def body(
    node_feats,
    source_feats,
    nbr_blocks,
    nbr_count,
    adj_tiles,
    pos_index,
    noise_block_rows,
    w_self,
    w_neigh,
):
    rows = node_feats.shape[0]
    width = node_feats.shape[1]
    slots = adj_tiles.shape[1]
    highest = lax.Precision.HIGHEST
    nodes = rows * lax.axis_size("row") * lax.axis_size("col")
    scale_factor = 1.0 / softness_divisor
    valid = jnp.arange(slots, dtype=jnp.int32)[None, :] < nbr_count[:, None]
    tiles = adj_tiles * valid[:, :, None, None].astype(jnp.bfloat16)
    piece = lax.all_gather(source_feats, "col", axis=0, tiled=True)
    count = piece.shape[0] // BLOCK
    blocks = piece.reshape(count, BLOCK, width)
    indicator_matrix = (
        nbr_blocks[:, :, None] == jnp.arange(count, dtype=jnp.int32)[None, None, :]
    ).astype(jnp.bfloat16)
    selected = jnp.einsum(
        "bkc,cjd->bkjd", indicator_matrix, blocks, preferred_element_type=jnp.float32
    ).astype(jnp.bfloat16)
    summed = jnp.einsum("bkij,bkjd->bid", tiles, selected, preferred_element_type=jnp.float32)
    agg = summed.reshape(rows, width).astype(jnp.bfloat16)
    pre = jnp.dot(node_feats, w_self, preferred_element_type=jnp.float32) + jnp.dot(
        agg, w_neigh, preferred_element_type=jnp.float32
    )
    emb32, pull = jax.vjp(embed, pre)
    zeta_bf = emb32.astype(jnp.bfloat16)
    candidates = lax.all_gather(zeta_bf[:NOISE], "row", axis=0, tiled=True)
    my_row = lax.axis_index("row")
    my_noise = noise_block_rows[my_row]
    noise_emb = lax.dynamic_slice_in_dim(candidates, my_noise * NOISE, NOISE, 0).astype(jnp.float32)
    zeta = zeta_bf.astype(jnp.float32)
    pairing = (pos_index[:, None] == jnp.arange(rows, dtype=jnp.int32)[None, :]).astype(jnp.float32)
    partner = jnp.dot(pairing, zeta, precision=highest)
    s_pos = jnp.sum(zeta * partner, axis=-1) * scale_factor
    s_neg = jnp.dot(zeta, noise_emb.T, precision=highest) * scale_factor
    loss_part = (jnp.sum(jax.nn.softplus(-s_pos)) + jnp.sum(jax.nn.softplus(s_neg)) / NOISE) / nodes
    grad_pos = -jax.nn.sigmoid(-s_pos) / nodes
    grad_neg = jax.nn.sigmoid(s_neg) / (NOISE * nodes)
    anchor = scale_factor * (
        grad_pos[:, None] * partner + jnp.dot(grad_neg, noise_emb, precision=highest)
    )
    partner_grad = jnp.dot(pairing.T, scale_factor * grad_pos[:, None] * zeta, precision=highest)
    dnoise = scale_factor * jnp.dot(grad_neg.T, zeta, precision=highest)
    groups = lax.axis_size("row")
    collected = lax.all_gather(dnoise.astype(jnp.bfloat16), "row", axis=0, tiled=True)
    owned = (noise_block_rows == my_row).astype(jnp.float32)
    returned = jnp.dot(
        owned[None, :],
        collected.astype(jnp.float32).reshape(groups, NOISE * width),
        precision=highest,
    )
    returned = returned.reshape(NOISE, width)
    dzeta = anchor + partner_grad
    dzeta = dzeta.at[:NOISE].add(returned)
    gpre = pull(dzeta)[0].astype(jnp.bfloat16)
    part_self = jnp.dot(node_feats.T, gpre, preferred_element_type=jnp.float32)
    neighbour_partial = jnp.dot(agg.T, gpre, preferred_element_type=jnp.float32)
    grad_self, neighbour_weight_gradient, loss = lax.psum(
        (part_self, neighbour_partial, loss_part), ("row", "col")
    )
    return (grad_self, neighbour_weight_gradient, loss)


def solution(mesh):
    in_specs = (
        P(("row", "col"), None),
        P("col", None),
        P(("row", "col"), None),
        P(("row", "col")),
        P(("row", "col"), None, None, None),
        P(("row", "col")),
        P(),
        P(),
        P(),
    )
    out_specs = (P(), P(), P())
    return jax.shard_map(body, mesh=mesh, in_specs=in_specs, out_specs=out_specs, check_vma=False)
```

profile of v0, /device:TPU:1, one launch (start us, length us, event | category | flops | bytes accessed | tf_op | source)
XLA Modules:
  0.0 734.0 jit_solution(15400814606287364603)
XLA Ops:
  7.2 0.7 all-gather.4.cloned.1.call-update
  8.0 0.7 fusion.26
  8.7 1.5 fusion.36
  10.2 68.1 %all-gather.4.cloned.1.call-done = bf16[4096,512]{1,0:T(8,128)(2,1)} async-done(((bf16[128,512]{1,0:T(8,128)(2,1)}), bf16[4096,512]{1,0:T(8,128)(2,1)}) %all-gather.4.cloned.1.call-update) | async-done | bytes 4194320 | tf_op jit(solution)/shard_map/all_gather | solution.py:36
  78.3 5.6 fusion.1
  83.9 2.6 fusion.8
  86.5 0.5 multiply_reduce_fusion.1
  87.0 0.2 copy-done.1
  87.3 0.1 multiply_convert_fusion
  87.4 0.7 slice.24
  88.2 0.6 dynamic_slice.6
  89.4 66.7 %all-gather.6.cloned.1.call-done = bf16[2048,512]{0,1:T(8,128)(2,1)} async-done(((bf16[128,512]{0,1:T(8,128)(2,1)}), bf16[2048,512]{0,1:T(8,128)(2,1)}) %all-gather.6.cloned.1.call-update) | async-done | bytes 2097168 | tf_op jit(solution)/shard_map/all_gather | solution.py:52
  156.1 1.9 fusion.18
  158.0 1.4 fusion.9
  159.4 0.2 all-reduce.3.cloned.1.call-start
  159.7 0.6 fusion.10
  160.3 0.6 fusion.25
  160.9 1.6 fusion.7
  162.5 1.2 convolution_add_fusion.1
  163.7 66.2 %all-gather.8.cloned.1.call-done = bf16[2048,512]{1,0:T(8,128)(2,1)} async-done(((bf16[128,512]{1,0:T(8,128)(2,1)}), bf16[2048,512]{1,0:T(8,128)(2,1)}) %all-gather.8.cloned.1.call-update) | async-done | bytes 2097168 | tf_op jit(solution)/shard_map/all_gather | solution.py:70
  229.9 3.2 reshape.99
  233.1 2.0 fusion.3
  235.1 0.1 copy.18
  235.3 0.1 fusion.19
  235.4 0.3 multiply_reduce_fusion
  235.7 0.3 fusion.11
  235.9 2.5 fusion.37
  238.4 1.4 convolution_bitcast_fusion
  241.1 110.9 %psum.23 = f32[]{:T(128)} all-reduce(f32[]{:T(128)S(6)} %div.45), channel_id=1, replica_groups=mesh['row'=16,'col'=32] {'row','col'}, use_global_device_ids=true, to_apply=%region_7.8 | all-reduce | flops 1 | bytes 8 | tf_op jit(solution)/shard_map/psum | solution.py:83
  351.9 370.7 %all-reduce.3.cloned.1.call-done = (f32[512,512]{0,1:T(8,128)}, f32[512,512]{1,0:T(8,128)}) async-done(((f32[512,512]{0,1:T(8,128)}, f32[512,512]{1,0:T(8,128)}), (f32[512,512]{0,1:T(8,128)}, f32[512,512]{1,0:T(8,128)})) %all-reduce.3.cloned.1.call-update) | async-done | bytes 2097168 | tf_op jit(solution)/shard_map/psum | solution.py:83
  722.6 2.5 copy.12
  725.2 2.3 copy.35
  (19 shorter events, 0.2 us)
Async XLA Ops:
  7.2 1.5 copy-start
  7.2 71.1 %all-gather.4.cloned.1.call-start = ((), (), s32[]{:S(2)}) async-start(), calls=%async_computation | async-start | bytes 4325376 | tf_op jit(solution)/shard_map/all_gather | solution.py:36
  7.9 148.2 %all-gather.6.cloned.1.call-start = ((), (), s32[]{:S(2)}) async-start(), calls=%async_computation.1 | async-start | bytes 2228224 | tf_op jit(solution)/shard_map/all_gather | solution.py:52
  78.3 5.6 copy-start.5
  83.8 2.7 copy-start.2
  86.5 0.8 copy-start.1
  86.5 1.7 copy-start.4
  86.5 73.1 %copy-start.3 = (s32[512]{0:T(512)S(1)}, s32[512]{0:T(512)}, u32[]{:S(2)}) copy-start(s32[512]{0:T(512)} %param.16) | copy-start | bytes 6148
  88.1 141.8 %all-gather.8.cloned.1.call-start = ((), (), s32[]{:S(2)}) async-start(), calls=%async_computation.2 | async-start | bytes 2228224 | tf_op jit(solution)/shard_map/all_gather | solution.py:70
  159.4 563.2 %all-reduce.3.cloned.1.call-start = ((), (), s32[]{:S(2)}) async-start(), calls=%async_computation.3 | async-start | bytes 4194304 | tf_op jit(solution)/shard_map/psum | solution.py:83
Sparse Core Ops, SparseCore 0:
  11.1 67.0 all-gather.3
  88.2 67.8 all-gather.5
  159.5 70.3 all-gather.7
  240.0 482.5 all-reduce.2
where the time goes:
time: 734 us
  waiting for transfers between devices  572 us (78%)
  blocking collectives  111 us (15%)
  matrix products  22.8 us (3%)
  between operations  15.8 us (2%)
  local copies, waits for them, and re-layouts  9.65 us (1%)
    psum x1, waiting for transfers between devices, body(): lax.psum((part_self, neighbour_partial, loss_part), ('row', 'col'))  371 us
    psum x1, blocking collectives, body(): lax.psum((part_self, neighbour_partial, loss_part), ('row', 'col'))  111 us
    all_gather x1, waiting for transfers between devices, body(): piece = lax.all_gather(source_feats, 'col', axis=0, tiled=True)  68.1 us
    all_gather x1, waiting for transfers between devices, body(): candidates = lax.all_gather(zeta_bf[:NOISE], 'row', axis=0, tiled=True)  66.7 us
    all_gather x1, waiting for transfers between devices, body(): lax.all_gather(dnoise.astype(jnp.bfloat16), 'row', axis=0, tiled=True)  66.2 us
  transfers between devices with their start and end apart: 4, of which 4 were waited for; matrix products, arithmetic and copies ran while one was open for 1% of the time, Pallas kernels for 0%

commit v1 on v0

--- a/solution.py
+++ b/solution.py
@@ -8,6 +8,38 @@
 
 
 softness_divisor = 0.2
+
+
+def xor_pairs(size, mask):
+    return [(i, i ^ mask) for i in range(size)]
+
+
+REDUCE_STEPS = (("col", 1), ("col", 2), ("col", 4), ("col", 8), ("col", 16), ("row", 1), ("row", 2), ("row", 4), ("row", 8))
+
+
+def tree_allreduce(buf, extra):
+    taken = []
+    for axis, mask in REDUCE_STEPS:
+        size = lax.axis_size(axis)
+        if mask >= size:
+            continue
+        bit = (lax.axis_index(axis) // mask) % 2
+        half = buf.shape[0] // 2
+        keep = lax.dynamic_slice_in_dim(buf, bit * half, half, 0)
+        send = lax.dynamic_slice_in_dim(buf, (1 - bit) * half, half, 0)
+        got, got_extra = lax.ppermute((send, extra), axis, xor_pairs(size, mask))
+        buf = keep + got
+        extra = extra + got_extra
+        taken.append((axis, mask, bit))
+    for axis, mask, bit in reversed(taken):
+        size = lax.axis_size(axis)
+        got = lax.ppermute(buf, axis, xor_pairs(size, mask))
+        rows = buf.shape[0]
+        out = jnp.zeros((2 * rows,) + buf.shape[1:], buf.dtype)
+        out = lax.dynamic_update_slice_in_dim(out, buf, bit * rows, 0)
+        out = lax.dynamic_update_slice_in_dim(out, got, (1 - bit) * rows, 0)
+        buf = out
+    return buf, extra
 
 
 def embed(pre):
@@ -80,10 +112,11 @@
     gpre = pull(dzeta)[0].astype(jnp.bfloat16)
     part_self = jnp.dot(node_feats.T, gpre, preferred_element_type=jnp.float32)
     neighbour_partial = jnp.dot(agg.T, gpre, preferred_element_type=jnp.float32)
-    grad_self, neighbour_weight_gradient, loss = lax.psum(
-        (part_self, neighbour_partial, loss_part), ("row", "col")
-    )
-    return (grad_self, neighbour_weight_gradient, loss)
+    stacked = jnp.concatenate([part_self, neighbour_partial], axis=0)
+    total, loss_tile = tree_allreduce(stacked, jnp.broadcast_to(loss_part, (8, 128)))
+    grad_self = total[:width]
+    neighbour_weight_gradient = total[width:]
+    return (grad_self, neighbour_weight_gradient, loss_tile[0, 0])
 
 
 def solution(mesh):

time: 734 us -> 482 us (0.66); the launches traced: 734 us -> 473 us
  waiting for transfers between devices: 572 us -> 282 us
  starting transfers between devices: 0.34 us -> 138 us
  blocking collectives: 111 us -> 0 us
    psum x1 -> x0, waiting for transfers between devices: 371 us -> none  [body(): lax.psum((part_self, neighbour_partial, loss_part), ('row', 'col'))]
    ppermute x0 -> x27, starting transfers between devices: none -> 138 us  [the longest x18 83.5 us: tree_allreduce(): got, got_extra = lax.ppermute((send, extra), axis, xor_pairs(size, mask))]
    psum x1 -> x0, blocking collectives: 111 us -> none  [body(): lax.psum((part_self, neighbour_partial, loss_part), ('row', 'col'))]
    ppermute x0 -> x27, waiting for transfers between devices: none -> 80.4 us  [the longest x18 53.3 us: tree_allreduce(): got, got_extra = lax.ppermute((send, extra), axis, xor_pairs(size, mask))]
  transfers between devices with their start and end apart: 4 -> 30, of which waited for: 4 -> 29; matrix products, arithmetic and copies ran while one was open for 1% -> 2% of each run, Pallas kernels for 0% -> 0%
where the time goes in v1:
time: 482 us; the launch traced here: 473 us
  waiting for transfers between devices  282 us (59%)
  starting transfers between devices  138 us (29%)
  matrix products  19.9 us (4%)
  between operations  16.7 us (3%)
  local copies, waits for them, and re-layouts  9.08 us (2%)
  other arithmetic  6.42 us (1%)
    ppermute x18, starting transfers between devices, tree_allreduce(): got, got_extra = lax.ppermute((send, extra), axis, xor_pairs(size, mask))  83.5 us
    all_gather x1, waiting for transfers between devices, body(): piece = lax.all_gather(source_feats, 'col', axis=0, tiled=True)  68.1 us
    all_gather x1, waiting for transfers between devices, body(): candidates = lax.all_gather(zeta_bf[:NOISE], 'row', axis=0, tiled=True)  66.6 us
    all_gather x1, waiting for transfers between devices, body(): lax.all_gather(dnoise.astype(jnp.bfloat16), 'row', axis=0, tiled=True)  66.4 us
    ppermute x9, starting transfers between devices, tree_allreduce(): got = lax.ppermute(buf, axis, xor_pairs(size, mask))  54.6 us
    ppermute x18, waiting for transfers between devices, tree_allreduce(): got, got_extra = lax.ppermute((send, extra), axis, xor_pairs(size, mask))  53.3 us
    ppermute x9, waiting for transfers between devices, tree_allreduce(): got = lax.ppermute(buf, axis, xor_pairs(size, mask))  27.1 us
  transfers between devices with their start and end apart: 30, of which 29 were waited for; matrix products, arithmetic and copies ran while one was open for 2% of the time, Pallas kernels for 0%

profile of v1, /device:TPU:1, one launch (start us, length us, event | category | flops | bytes accessed | tf_op | source)
XLA Modules:
  0.0 472.6 jit_solution(14031274713754208656)
XLA Ops:
  10.2 68.1 %all-gather.4.cloned.1.call-done = bf16[4096,512]{1,0:T(8,128)(2,1)} async-done(((bf16[128,512]{1,0:T(8,128)(2,1)}), bf16[4096,512]{1,0:T(8,128)(2,1)}) %all-gather.4.cloned.1.call-update) | async-done | bytes 4194320 | tf_op jit(solution)/shard_map/all_gather | solution.py:68
  78.3 5.5 %fusion.1 = bf16[4,8,128,512]{3,1,2,0:T(8,128)(2,1)S(1)} fusion(bf16[32,128,512,1]{2,1,0,3:T(8,128)(2,1)} %bitcast.40, s32[4,8]{1,0:T(4,128)S(1)} %copy-done.5), kind=kOutput, calls=%fused_computation.2 | convolution fusion | flops 134218752 | bytes 8388736 | tf_op jit(solution)/shard_map/bkc,cjd->bkjd/dot_general | solution.py:74
  89.5 66.6 %all-gather.6.cloned.1.call-done = bf16[2048,512]{0,1:T(8,128)(2,1)} async-done(((bf16[128,512]{0,1:T(8,128)(2,1)}), bf16[2048,512]{0,1:T(8,128)(2,1)}) %all-gather.6.cloned.1.call-update) | async-done | bytes 2097168 | tf_op jit(solution)/shard_map/all_gather | solution.py:84
  163.4 66.4 %all-gather.8.cloned.1.call-done = bf16[2048,512]{1,0:T(8,128)(2,1)} async-done(((bf16[128,512]{1,0:T(8,128)(2,1)}), bf16[2048,512]{1,0:T(8,128)(2,1)}) %all-gather.8.cloned.1.call-update) | async-done | bytes 2097168 | tf_op jit(solution)/shard_map/all_gather | solution.py:102
  238.6 11.6 %collective-permute-start = (f32[512,512]{1,0:T(8,128)}, f32[512,512]{1,0:T(8,128)}, u32[]{:S(2)}, u32[]{:S(2)}) collective-permute-start(f32[512,512]{1,0:T(8,128)} %fusion.12), channel_id=1, source_target_pairs={{0,1},{1,0},{2,3},{3,2},{4,5},{5,4},{6,7},{7,6},{8,9},{9,8},{10,11... | collective-permute-start | bytes 3145736 | tf_op jit(solution)/shard_map/ppermute | solution.py:30
  258.7 11.9 %collective-permute-done.1 = f32[256,512]{1,0:T(8,128)S(1)} collective-permute-done((f32[256,512]{1,0:T(8,128)S(1)}, f32[256,512]{1,0:T(8,128)S(1)}, u32[]{:S(2)}, u32[]{:S(2)}) %collective-permute-start.1) | collective-permute-done | bytes 524320 | tf_op jit(solution)/shard_map/ppermute | solution.py:30
  271.7 4.6 collective-permute-start.2
  276.4 5.3 %collective-permute-done.2 = f32[128,512]{1,0:T(8,128)S(1)} collective-permute-done((f32[128,512]{1,0:T(8,128)S(1)}, f32[128,512]{1,0:T(8,128)S(1)}, u32[]{:S(2)}, u32[]{:S(2)}) %collective-permute-start.2) | collective-permute-done | bytes 262176 | tf_op jit(solution)/shard_map/ppermute | solution.py:30
  287.5 4.6 collective-permute-start.4
  294.1 3.3 collective-permute-start.5
  304.1 4.8 %collective-permute-start.7 = (f32[4,512]{1,0:T(4,128)S(1)}, f32[4,512]{1,0:T(4,128)S(1)}, u32[]{:S(2)}, u32[]{:S(2)}) collective-permute-start(f32[4,512]{1,0:T(4,128)S(1)} %constant_dynamic-slice_fusion.2), channel_id=1, source_target_pairs={{0,128},{32,160},{64,192},{96,224},{128,0},{160,32},{192,64},{224,... | collective-permute-start | bytes 24584 | tf_op jit(solution)/shard_map/ppermute | solution.py:30
  309.0 3.5 collective-permute-done.7
  312.5 8.3 %collective-permute-start.8 = (f32[2,512]{1,0:T(2,128)S(1)}, f32[2,512]{1,0:T(2,128)S(1)}, u32[]{:S(2)}, u32[]{:S(2)}) collective-permute-start(f32[2,512]{1,0:T(2,128)S(1)} %constant_dynamic-slice_fusion), channel_id=1, source_target_pairs={{0,256},{32,288},{64,320},{96,352},{128,384},{160,416},{192,448},{... | collective-permute-start | bytes 12296 | tf_op jit(solution)/shard_map/ppermute | solution.py:30
  320.7 4.8 %collective-permute-done.8 = f32[2,512]{1,0:T(2,128)S(1)} collective-permute-done((f32[2,512]{1,0:T(2,128)S(1)}, f32[2,512]{1,0:T(2,128)S(1)}, u32[]{:S(2)}, u32[]{:S(2)}) %collective-permute-start.8) | collective-permute-done | bytes 4128 | tf_op jit(solution)/shard_map/ppermute | solution.py:30
  325.5 8.3 %collective-permute-start.9 = (f32[2,512]{1,0:T(2,128)S(1)}, f32[2,512]{1,0:T(2,128)S(1)}, u32[]{:S(2)}, u32[]{:S(2)}) collective-permute-start(f32[2,512]{1,0:T(2,128)S(1)} %get-tuple-element.16), channel_id=1, source_target_pairs={{0,256},{32,288},{64,320},{96,352},{128,384},{160,416},{192,448},{... | collective-permute-start | bytes 12296 | tf_op jit(solution)/shard_map/ppermute | solution.py:36
  333.8 4.8 %collective-permute-done.9 = f32[2,512]{1,0:T(2,128)S(1)} collective-permute-done((f32[2,512]{1,0:T(2,128)S(1)}, f32[2,512]{1,0:T(2,128)S(1)}, u32[]{:S(2)}, u32[]{:S(2)}) %collective-permute-start.9) | collective-permute-done | bytes 4128 | tf_op jit(solution)/shard_map/ppermute | solution.py:36
  338.6 4.8 %collective-permute-start.10 = (f32[4,512]{1,0:T(4,128)S(1)}, f32[4,512]{1,0:T(4,128)S(1)}, u32[]{:S(2)}, u32[]{:S(2)}) collective-permute-start(f32[4,512]{1,0:T(4,128)S(1)} %constant_dynamic-update-slice_fusion.16), channel_id=1, source_target_pairs={{0,128},{32,160},{64,192},{96,224},{128,0},{160,32},{192,64},{224,... | collective-permute-start | bytes 24584 | tf_op jit(solution)/shard_map/ppermute | solution.py:36
  343.4 3.8 collective-permute-done.10
  352.6 3.3 collective-permute-start.12
  357.5 4.6 collective-permute-start.13
  364.0 3.4 collective-permute-start.14
  370.1 4.6 collective-permute-start.15
  374.9 3.9 collective-permute-done.15
  382.0 6.6 %collective-permute-done.16 = f32[256,512]{1,0:T(8,128)S(1)} collective-permute-done((f32[256,512]{1,0:T(8,128)S(1)}, f32[256,512]{1,0:T(8,128)S(1)}, u32[]{:S(2)}, u32[]{:S(2)}) %collective-permute-start.16) | collective-permute-done | bytes 524320 | tf_op jit(solution)/shard_map/ppermute | solution.py:36
  388.7 19.2 %collective-permute-start.17 = (f32[512,512]{1,0:T(8,128)S(1)}, f32[512,512]{1,0:T(8,128)S(1)}, u32[]{:S(2)}, u32[]{:S(2)}) collective-permute-start(f32[512,512]{1,0:T(8,128)S(1)} %constant_dynamic-update-slice_fusion.2), channel_id=1, source_target_pairs={{0,1},{1,0},{2,3},{3,2},{4,5},{5,4},{6,7},{7,6},{8,9},{9,8},{10,11... | collective-permute-start | bytes 3145736 | tf_op jit(solution)/shard_map/ppermute | solution.py:36
  416.6 4.6 collective-permute-start.20
  426.8 4.6 collective-permute-start.22
  432.7 3.3 collective-permute-start.23
  442.3 4.8 %collective-permute-start.25 = (f32[8,128]{1,0:T(8,128)S(1)}, f32[8,128]{1,0:T(8,128)S(1)}, u32[]{:S(2)}, u32[]{:S(2)}) collective-permute-start(f32[8,128]{1,0:T(8,128)S(1)} %add.277), channel_id=1, source_target_pairs={{0,128},{32,160},{64,192},{96,224},{128,0},{160,32},{192,64},{224,... | collective-permute-start | bytes 12296 | tf_op jit(solution)/shard_map/ppermute | solution.py:30
  447.1 3.5 collective-permute-done.25
  450.5 8.4 %collective-permute-start.26 = (f32[8,128]{1,0:T(8,128)S(1)}, f32[8,128]{1,0:T(8,128)S(1)}, u32[]{:S(2)}, u32[]{:S(2)}) collective-permute-start(f32[8,128]{1,0:T(8,128)S(1)} %add.278), channel_id=1, source_target_pairs={{0,256},{32,288},{64,320},{96,352},{128,384},{160,416},{192,448},{... | collective-permute-start | bytes 12296 | tf_op jit(solution)/shard_map/ppermute | solution.py:30
  458.9 4.7 collective-permute-done.26
  (129 shorter events, 85.5 us)
Async XLA Ops:
  7.2 71.1 %copy-start.5 = (s32[4,8]{1,0:T(4,128)S(1)}, s32[4,8]{1,0:T(4,128)}, u32[]{:S(2)}) copy-start(s32[4,8]{1,0:T(4,128)} %param.13) | copy-start | bytes 388
  7.2 71.1 %all-gather.4.cloned.1.call-start = ((), (), s32[]{:S(2)}) async-start(), calls=%async_computation | async-start | bytes 4325376 | tf_op jit(solution)/shard_map/all_gather | solution.py:68
  7.9 148.1 %all-gather.6.cloned.1.call-start = ((), (), s32[]{:S(2)}) async-start(), calls=%async_computation.1 | async-start | bytes 2228224 | tf_op jit(solution)/shard_map/all_gather | solution.py:84
  87.3 72.1 %copy-start.6 = (s32[512]{0:T(512)S(1)}, s32[512]{0:T(512)}, u32[]{:S(2)}) copy-start(s32[512]{0:T(512)} %param.16) | copy-start | bytes 6148
  88.0 141.8 %all-gather.8.cloned.1.call-start = ((), (), s32[]{:S(2)}) async-start(), calls=%async_computation.2 | async-start | bytes 2228224 | tf_op jit(solution)/shard_map/all_gather | solution.py:102
  238.6 14.2 %collective-permute-start = (f32[512,512]{1,0:T(8,128)}, f32[512,512]{1,0:T(8,128)}, u32[]{:S(2)}, u32[]{:S(2)}) collective-permute-start(f32[512,512]{1,0:T(8,128)} %fusion.12), channel_id=1, source_target_pairs={{0,1},{1,0},{2,3},{3,2},{4,5},{5,4},{6,7},{7,6},{8,9},{9,8},{10,11... | collective-permute-start | bytes 3145736 | tf_op jit(solution)/shard_map/ppermute | solution.py:30
  255.5 15.0 %collective-permute-start.1 = (f32[256,512]{1,0:T(8,128)S(1)}, f32[256,512]{1,0:T(8,128)S(1)}, u32[]{:S(2)}, u32[]{:S(2)}) collective-permute-start(f32[256,512]{1,0:T(8,128)S(1)} %constant_dynamic-slice_fusion.9), channel_id=1, source_target_pairs={{0,2},{1,3},{2,0},{3,1},{4,6},{5,7},{6,4},{7,5},{8,10},{9,11},{10,... | collective-permute-start | bytes 1572872 | tf_op jit(solution)/shard_map/ppermute | solution.py:30
  271.7 10.0 %collective-permute-start.2 = (f32[128,512]{1,0:T(8,128)S(1)}, f32[128,512]{1,0:T(8,128)S(1)}, u32[]{:S(2)}, u32[]{:S(2)}) collective-permute-start(f32[128,512]{1,0:T(8,128)S(1)} %constant_dynamic-slice_fusion.8), channel_id=1, source_target_pairs={{0,4},{1,5},{2,6},{3,7},{4,0},{5,1},{6,2},{7,3},{8,12},{9,13},{10,... | collective-permute-start | bytes 786440 | tf_op jit(solution)/shard_map/ppermute | solution.py:30
  281.8 5.7 %collective-permute-start.3 = (f32[64,512]{1,0:T(8,128)S(1)}, f32[64,512]{1,0:T(8,128)S(1)}, u32[]{:S(2)}, u32[]{:S(2)}) collective-permute-start(f32[64,512]{1,0:T(8,128)S(1)} %constant_dynamic-slice_fusion.7), channel_id=1, source_target_pairs={{0,8},{1,9},{2,10},{3,11},{4,12},{5,13},{6,14},{7,15},{8,0},{9,1},... | collective-permute-start | bytes 393224 | tf_op jit(solution)/shard_map/ppermute | solution.py:30
  287.5 6.5 %collective-permute-start.4 = (f32[32,512]{1,0:T(8,128)S(1)}, f32[32,512]{1,0:T(8,128)S(1)}, u32[]{:S(2)}, u32[]{:S(2)}) collective-permute-start(f32[32,512]{1,0:T(8,128)S(1)} %constant_dynamic-slice_fusion.6), channel_id=1, source_target_pairs={{0,16},{1,17},{2,18},{3,19},{4,20},{5,21},{6,22},{7,23},{8,24},{9,... | collective-permute-start | bytes 196616 | tf_op jit(solution)/shard_map/ppermute | solution.py:30
  294.1 4.7 collective-permute-start.5
  298.7 5.4 %collective-permute-start.6 = (f32[8,512]{1,0:T(8,128)S(1)}, f32[8,512]{1,0:T(8,128)S(1)}, u32[]{:S(2)}, u32[]{:S(2)}) collective-permute-start(f32[8,512]{1,0:T(8,128)S(1)} %constant_dynamic-slice_fusion.4), channel_id=1, source_target_pairs={{0,64},{32,96},{64,0},{96,32},{128,192},{160,224},{192,128},{224,1... | collective-permute-start | bytes 49160 | tf_op jit(solution)/shard_map/ppermute | solution.py:30
  304.1 8.3 %collective-permute-start.7 = (f32[4,512]{1,0:T(4,128)S(1)}, f32[4,512]{1,0:T(4,128)S(1)}, u32[]{:S(2)}, u32[]{:S(2)}) collective-permute-start(f32[4,512]{1,0:T(4,128)S(1)} %constant_dynamic-slice_fusion.2), channel_id=1, source_target_pairs={{0,128},{32,160},{64,192},{96,224},{128,0},{160,32},{192,64},{224,... | collective-permute-start | bytes 24584 | tf_op jit(solution)/shard_map/ppermute | solution.py:30
  312.5 13.1 %collective-permute-start.8 = (f32[2,512]{1,0:T(2,128)S(1)}, f32[2,512]{1,0:T(2,128)S(1)}, u32[]{:S(2)}, u32[]{:S(2)}) collective-permute-start(f32[2,512]{1,0:T(2,128)S(1)} %constant_dynamic-slice_fusion), channel_id=1, source_target_pairs={{0,256},{32,288},{64,320},{96,352},{128,384},{160,416},{192,448},{... | collective-permute-start | bytes 12296 | tf_op jit(solution)/shard_map/ppermute | solution.py:30
  325.5 13.1 %collective-permute-start.9 = (f32[2,512]{1,0:T(2,128)S(1)}, f32[2,512]{1,0:T(2,128)S(1)}, u32[]{:S(2)}, u32[]{:S(2)}) collective-permute-start(f32[2,512]{1,0:T(2,128)S(1)} %get-tuple-element.16), channel_id=1, source_target_pairs={{0,256},{32,288},{64,320},{96,352},{128,384},{160,416},{192,448},{... | collective-permute-start | bytes 12296 | tf_op jit(solution)/shard_map/ppermute | solution.py:36
  338.6 8.6 %collective-permute-start.10 = (f32[4,512]{1,0:T(4,128)S(1)}, f32[4,512]{1,0:T(4,128)S(1)}, u32[]{:S(2)}, u32[]{:S(2)}) collective-permute-start(f32[4,512]{1,0:T(4,128)S(1)} %constant_dynamic-update-slice_fusion.16), channel_id=1, source_target_pairs={{0,128},{32,160},{64,192},{96,224},{128,0},{160,32},{192,64},{224,... | collective-permute-start | bytes 24584 | tf_op jit(solution)/shard_map/ppermute | solution.py:36
  347.2 5.4 %collective-permute-start.11 = (f32[8,512]{1,0:T(8,128)S(1)}, f32[8,512]{1,0:T(8,128)S(1)}, u32[]{:S(2)}, u32[]{:S(2)}) collective-permute-start(f32[8,512]{1,0:T(8,128)S(1)} %constant_dynamic-update-slice_fusion.14), channel_id=1, source_target_pairs={{0,64},{32,96},{64,0},{96,32},{128,192},{160,224},{192,128},{224,1... | collective-permute-start | bytes 49160 | tf_op jit(solution)/shard_map/ppermute | solution.py:36
  352.6 4.9 %collective-permute-start.12 = (f32[16,512]{1,0:T(8,128)S(1)}, f32[16,512]{1,0:T(8,128)S(1)}, u32[]{:S(2)}, u32[]{:S(2)}) collective-permute-start(f32[16,512]{1,0:T(8,128)S(1)} %constant_dynamic-update-slice_fusion.12), channel_id=1, source_target_pairs={{0,32},{32,0},{64,96},{96,64},{128,160},{160,128},{192,224},{224,1... | collective-permute-start | bytes 98312 | tf_op jit(solution)/shard_map/ppermute | solution.py:36
  357.5 6.5 %collective-permute-start.13 = (f32[32,512]{1,0:T(8,128)S(1)}, f32[32,512]{1,0:T(8,128)S(1)}, u32[]{:S(2)}, u32[]{:S(2)}) collective-permute-start(f32[32,512]{1,0:T(8,128)S(1)} %constant_dynamic-update-slice_fusion.10), channel_id=1, source_target_pairs={{0,16},{1,17},{2,18},{3,19},{4,20},{5,21},{6,22},{7,23},{8,24},{9,... | collective-permute-start | bytes 196616 | tf_op jit(solution)/shard_map/ppermute | solution.py:36
  364.0 6.1 %collective-permute-start.14 = (f32[64,512]{1,0:T(8,128)S(1)}, f32[64,512]{1,0:T(8,128)S(1)}, u32[]{:S(2)}, u32[]{:S(2)}) collective-permute-start(f32[64,512]{1,0:T(8,128)S(1)} %constant_dynamic-update-slice_fusion.8), channel_id=1, source_target_pairs={{0,8},{1,9},{2,10},{3,11},{4,12},{5,13},{6,14},{7,15},{8,0},{9,1},... | collective-permute-start | bytes 393224 | tf_op jit(solution)/shard_map/ppermute | solution.py:36
  370.1 8.6 %collective-permute-start.15 = (f32[128,512]{1,0:T(8,128)S(1)}, f32[128,512]{1,0:T(8,128)S(1)}, u32[]{:S(2)}, u32[]{:S(2)}) collective-permute-start(f32[128,512]{1,0:T(8,128)S(1)} %constant_dynamic-update-slice_fusion.6), channel_id=1, source_target_pairs={{0,4},{1,5},{2,6},{3,7},{4,0},{5,1},{6,2},{7,3},{8,12},{9,13},{10,... | collective-permute-start | bytes 786440 | tf_op jit(solution)/shard_map/ppermute | solution.py:36
  378.8 9.9 %collective-permute-start.16 = (f32[256,512]{1,0:T(8,128)S(1)}, f32[256,512]{1,0:T(8,128)S(1)}, u32[]{:S(2)}, u32[]{:S(2)}) collective-permute-start(f32[256,512]{1,0:T(8,128)S(1)} %constant_dynamic-update-slice_fusion.4), channel_id=1, source_target_pairs={{0,2},{1,3},{2,0},{3,1},{4,6},{5,7},{6,4},{7,5},{8,10},{9,11},{10,... | collective-permute-start | bytes 1572872 | tf_op jit(solution)/shard_map/ppermute | solution.py:36
  388.7 75.7 %collective-permute-start.17 = (f32[512,512]{1,0:T(8,128)S(1)}, f32[512,512]{1,0:T(8,128)S(1)}, u32[]{:S(2)}, u32[]{:S(2)}) collective-permute-start(f32[512,512]{1,0:T(8,128)S(1)} %constant_dynamic-update-slice_fusion.2), channel_id=1, source_target_pairs={{0,1},{1,0},{2,3},{3,2},{4,5},{5,4},{6,7},{7,6},{8,9},{9,8},{10,11... | collective-permute-start | bytes 3145736 | tf_op jit(solution)/shard_map/ppermute | solution.py:36
  409.2 3.1 collective-permute-start.18
  412.3 4.3 collective-permute-start.19
  416.6 5.8 %collective-permute-start.20 = (f32[8,128]{1,0:T(8,128)S(1)}, f32[8,128]{1,0:T(8,128)S(1)}, u32[]{:S(2)}, u32[]{:S(2)}) collective-permute-start(f32[8,128]{1,0:T(8,128)S(1)} %fusion.56), channel_id=1, source_target_pairs={{0,4},{1,5},{2,6},{3,7},{4,0},{5,1},{6,2},{7,3},{8,12},{9,13},{10,... | collective-permute-start | bytes 12296 | tf_op jit(solution)/shard_map/ppermute | solution.py:30
  422.5 4.3 collective-permute-start.21
  426.8 5.8 %collective-permute-start.22 = (f32[8,128]{1,0:T(8,128)S(1)}, f32[8,128]{1,0:T(8,128)S(1)}, u32[]{:S(2)}, u32[]{:S(2)}) collective-permute-start(f32[8,128]{1,0:T(8,128)S(1)} %add.274), channel_id=1, source_target_pairs={{0,16},{1,17},{2,18},{3,19},{4,20},{5,21},{6,22},{7,23},{8,24},{9,... | collective-permute-start | bytes 12296 | tf_op jit(solution)/shard_map/ppermute | solution.py:30
  432.7 4.4 collective-permute-start.23
  437.0 5.2 %collective-permute-start.24 = (f32[8,128]{1,0:T(8,128)S(1)}, f32[8,128]{1,0:T(8,128)S(1)}, u32[]{:S(2)}, u32[]{:S(2)}) collective-permute-start(f32[8,128]{1,0:T(8,128)S(1)} %add.276), channel_id=1, source_target_pairs={{0,64},{32,96},{64,0},{96,32},{128,192},{160,224},{192,128},{224,1... | collective-permute-start | bytes 12296 | tf_op jit(solution)/shard_map/ppermute | solution.py:30
  442.3 8.2 %collective-permute-start.25 = (f32[8,128]{1,0:T(8,128)S(1)}, f32[8,128]{1,0:T(8,128)S(1)}, u32[]{:S(2)}, u32[]{:S(2)}) collective-permute-start(f32[8,128]{1,0:T(8,128)S(1)} %add.277), channel_id=1, source_target_pairs={{0,128},{32,160},{64,192},{96,224},{128,0},{160,32},{192,64},{224,... | collective-permute-start | bytes 12296 | tf_op jit(solution)/shard_map/ppermute | solution.py:30
  450.5 13.1 %collective-permute-start.26 = (f32[8,128]{1,0:T(8,128)S(1)}, f32[8,128]{1,0:T(8,128)S(1)}, u32[]{:S(2)}, u32[]{:S(2)}) collective-permute-start(f32[8,128]{1,0:T(8,128)S(1)} %add.278), channel_id=1, source_target_pairs={{0,256},{32,288},{64,320},{96,352},{128,384},{160,416},{192,448},{... | collective-permute-start | bytes 12296 | tf_op jit(solution)/shard_map/ppermute | solution.py:30
  (7 other events, 14.2 us)
Sparse Core Ops, SparseCore 0:
  11.2 67.0 all-gather.3
  88.1 67.8 all-gather.5
  159.4 70.3 all-gather.7

commit v2 on v1

--- a/solution.py
+++ b/solution.py
@@ -14,12 +14,13 @@
     return [(i, i ^ mask) for i in range(size)]
 
 
-REDUCE_STEPS = (("col", 1), ("col", 2), ("col", 4), ("col", 8), ("col", 16), ("row", 1), ("row", 2), ("row", 4), ("row", 8))
+HALVING = (("col", 1), ("col", 2), ("col", 4), ("col", 8), ("col", 16))
+BUTTERFLY = (("row", 1), ("row", 2), ("row", 4), ("row", 8))
 
 
 def tree_allreduce(buf, extra):
     taken = []
-    for axis, mask in REDUCE_STEPS:
+    for axis, mask in HALVING:
         size = lax.axis_size(axis)
         if mask >= size:
             continue
@@ -27,10 +28,18 @@
         half = buf.shape[0] // 2
         keep = lax.dynamic_slice_in_dim(buf, bit * half, half, 0)
         send = lax.dynamic_slice_in_dim(buf, (1 - bit) * half, half, 0)
-        got, got_extra = lax.ppermute((send, extra), axis, xor_pairs(size, mask))
-        buf = keep + got
-        extra = extra + got_extra
+        got = lax.ppermute(jnp.concatenate([send, extra], 0), axis, xor_pairs(size, mask))
+        buf = keep + got[:half]
+        extra = extra + got[half:]
         taken.append((axis, mask, bit))
+    joined = jnp.concatenate([buf, extra], 0)
+    for axis, mask in BUTTERFLY:
+        size = lax.axis_size(axis)
+        if mask >= size:
+            continue
+        joined = joined + lax.ppermute(joined, axis, xor_pairs(size, mask))
+    rows = buf.shape[0]
+    buf, extra = joined[:rows], joined[rows:]
     for axis, mask, bit in reversed(taken):
         size = lax.axis_size(axis)
         got = lax.ppermute(buf, axis, xor_pairs(size, mask))
@@ -113,7 +122,7 @@
     part_self = jnp.dot(node_feats.T, gpre, preferred_element_type=jnp.float32)
     neighbour_partial = jnp.dot(agg.T, gpre, preferred_element_type=jnp.float32)
     stacked = jnp.concatenate([part_self, neighbour_partial], axis=0)
-    total, loss_tile = tree_allreduce(stacked, jnp.broadcast_to(loss_part, (8, 128)))
+    total, loss_tile = tree_allreduce(stacked, jnp.broadcast_to(loss_part, (8, width)))
     grad_self = total[:width]
     neighbour_weight_gradient = total[width:]
     return (grad_self, neighbour_weight_gradient, loss_tile[0, 0])

time: 482 us -> 394 us (0.82); the launches traced: 473 us -> 391 us
  starting transfers between devices: 138 us -> 81.8 us
  waiting for transfers between devices: 282 us -> 256 us
    ppermute x18 -> x9, starting transfers between devices: 83.5 us -> 49.3 us  [the longest x5 27.1 us: tree_allreduce(): lax.ppermute(jnp.concatenate([send, extra], 0), axis, xor_pairs(size, mask))]
    ppermute x9 -> x5, starting transfers between devices: 54.6 us -> 32.2 us  [tree_allreduce(): got = lax.ppermute(buf, axis, xor_pairs(size, mask))]
    ppermute x18 -> x9, waiting for transfers between devices: 53.3 us -> 37.5 us  [the longest x5 25.3 us: tree_allreduce(): lax.ppermute(jnp.concatenate([send, extra], 0), axis, xor_pairs(size, mask))]
    ppermute x9 -> x5, waiting for transfers between devices: 27.1 us -> 18.1 us  [tree_allreduce(): got = lax.ppermute(buf, axis, xor_pairs(size, mask))]
  transfers between devices with their start and end apart: 30 -> 17, of which waited for: 29 -> 17; matrix products, arithmetic and copies ran while one was open for 2% -> 2% of each run, Pallas kernels for 0% -> 0%
where the time goes in v2:
time: 394 us; the launch traced here: 391 us
  waiting for transfers between devices  256 us (65%)
  starting transfers between devices  81.8 us (21%)
  matrix products  19.8 us (5%)
  between operations  16.3 us (4%)
  local copies, waits for them, and re-layouts  10 us (3%)
  other arithmetic  6.99 us (2%)
    all_gather x1, waiting for transfers between devices, body(): piece = lax.all_gather(source_feats, 'col', axis=0, tiled=True)  68.1 us
    all_gather x1, waiting for transfers between devices, body(): candidates = lax.all_gather(zeta_bf[:NOISE], 'row', axis=0, tiled=True)  66.6 us
    all_gather x1, waiting for transfers between devices, body(): lax.all_gather(dnoise.astype(jnp.bfloat16), 'row', axis=0, tiled=True)  65.2 us
    ppermute x5, starting transfers between devices, tree_allreduce(): got = lax.ppermute(buf, axis, xor_pairs(size, mask))  32.2 us
    ppermute x5, starting transfers between devices, tree_allreduce(): lax.ppermute(jnp.concatenate([send, extra], 0), axis, xor_pairs(size, mask))  27.1 us
    ppermute x5, waiting for transfers between devices, tree_allreduce(): lax.ppermute(jnp.concatenate([send, extra], 0), axis, xor_pairs(size, mask))  25.3 us
    ppermute x4, starting transfers between devices, tree_allreduce(): joined = joined + lax.ppermute(joined, axis, xor_pairs(size, mask))  22.2 us
    ppermute x5, waiting for transfers between devices, tree_allreduce(): got = lax.ppermute(buf, axis, xor_pairs(size, mask))  18.1 us
  transfers between devices with their start and end apart: 17, of which 17 were waited for; matrix products, arithmetic and copies ran while one was open for 2% of the time, Pallas kernels for 0%

profile of v2, /device:TPU:1, one launch (start us, length us, event | category | flops | bytes accessed | tf_op | source)
XLA Modules:
  0.0 391.1 jit_solution(15393055116449600182)
XLA Ops:
  10.2 68.1 %all-gather.4.cloned.1.call-done = bf16[4096,512]{1,0:T(8,128)(2,1)} async-done(((bf16[128,512]{1,0:T(8,128)(2,1)}), bf16[4096,512]{1,0:T(8,128)(2,1)}) %all-gather.4.cloned.1.call-update) | async-done | bytes 4194320 | tf_op jit(solution)/shard_map/all_gather | solution.py:77
  78.3 5.5 %fusion.1 = bf16[4,8,128,512]{3,1,2,0:T(8,128)(2,1)S(1)} fusion(bf16[32,128,512,1]{2,1,0,3:T(8,128)(2,1)} %bitcast.40, s32[4,8]{1,0:T(4,128)S(1)} %copy-done.5), kind=kOutput, calls=%fused_computation.2 | convolution fusion | flops 134218752 | bytes 8388736 | tf_op jit(solution)/shard_map/bkc,cjd->bkjd/dot_general | solution.py:83
  83.9 2.6 fusion.8
  89.5 66.6 %all-gather.6.cloned.1.call-done = bf16[2048,512]{0,1:T(8,128)(2,1)} async-done(((bf16[128,512]{0,1:T(8,128)(2,1)}), bf16[2048,512]{0,1:T(8,128)(2,1)}) %all-gather.6.cloned.1.call-update) | async-done | bytes 2097168 | tf_op jit(solution)/shard_map/all_gather | solution.py:93
  164.6 65.2 %all-gather.8.cloned.1.call-done = bf16[2048,512]{1,0:T(8,128)(2,1)} async-done(((bf16[128,512]{1,0:T(8,128)(2,1)}), bf16[2048,512]{1,0:T(8,128)(2,1)}) %all-gather.8.cloned.1.call-update) | async-done | bytes 2097168 | tf_op jit(solution)/shard_map/all_gather | solution.py:111
  229.8 3.2 reshape.99
  238.7 11.6 %collective-permute-start = (f32[520,512]{1,0:T(8,128)}, f32[520,512]{1,0:T(8,128)}, u32[]{:S(2)}, u32[]{:S(2)}) collective-permute-start(f32[520,512]{1,0:T(8,128)} %concatenate.24), channel_id=1, source_target_pairs={{0,1},{1,0},{2,3},{3,2},{4,5},{5,4},{6,7},{7,6},{8,9},{9,8},{10,11... | collective-permute-start | bytes 3194888 | tf_op jit(solution)/shard_map/ppermute | solution.py:31
  250.4 2.6 collective-permute-done
  256.4 3.1 collective-permute-start.1
  259.5 12.2 %collective-permute-done.1 = f32[264,512]{1,0:T(8,128)S(1)} collective-permute-done((f32[264,512]{1,0:T(8,128)S(1)}, f32[264,512]{1,0:T(8,128)S(1)}, u32[]{:S(2)}, u32[]{:S(2)}) %collective-permute-start.1) | collective-permute-done | bytes 540704 | tf_op jit(solution)/shard_map/ppermute | solution.py:31
  273.7 4.6 %collective-permute-start.2 = (f32[136,512]{1,0:T(8,128)S(1)}, f32[136,512]{1,0:T(8,128)S(1)}, u32[]{:S(2)}, u32[]{:S(2)}) collective-permute-start(f32[136,512]{1,0:T(8,128)S(1)} %pad_maximum_fusion.1), channel_id=1, source_target_pairs={{0,4},{1,5},{2,6},{3,7},{4,0},{5,1},{6,2},{7,3},{8,12},{9,13},{10,... | collective-permute-start | bytes 835592 | tf_op jit(solution)/shard_map/ppermute | solution.py:31
  278.3 5.7 %collective-permute-done.2 = f32[136,512]{1,0:T(8,128)S(1)} collective-permute-done((f32[136,512]{1,0:T(8,128)S(1)}, f32[136,512]{1,0:T(8,128)S(1)}, u32[]{:S(2)}, u32[]{:S(2)}) %collective-permute-start.2) | collective-permute-done | bytes 278560 | tf_op jit(solution)/shard_map/ppermute | solution.py:31
  284.1 3.1 collective-permute-start.3
  287.3 2.7 collective-permute-done.3
  290.1 4.6 %collective-permute-start.4 = (f32[40,512]{1,0:T(8,128)S(1)}, f32[40,512]{1,0:T(8,128)S(1)}, u32[]{:S(2)}, u32[]{:S(2)}) collective-permute-start(f32[40,512]{1,0:T(8,128)S(1)} %pad_maximum_fusion.3), channel_id=1, source_target_pairs={{0,16},{1,17},{2,18},{3,19},{4,20},{5,21},{6,22},{7,23},{8,24},{9,... | collective-permute-start | bytes 245768 | tf_op jit(solution)/shard_map/ppermute | solution.py:31
  294.7 2.0 collective-permute-done.4
  296.8 3.3 collective-permute-start.5
  302.0 3.1 collective-permute-start.6
  305.1 3.0 collective-permute-done.6
  308.1 5.0 %collective-permute-start.7 = (f32[40,512]{1,0:T(8,128)S(1)}, f32[40,512]{1,0:T(8,128)S(1)}, u32[]{:S(2)}, u32[]{:S(2)}) collective-permute-start(f32[40,512]{1,0:T(8,128)S(1)} %add.203), channel_id=1, source_target_pairs={{0,128},{32,160},{64,192},{96,224},{128,0},{160,32},{192,64},{224,... | collective-permute-start | bytes 245768 | tf_op jit(solution)/shard_map/ppermute | solution.py:40
  313.1 4.1 %collective-permute-done.7 = f32[40,512]{1,0:T(8,128)S(1)} collective-permute-done((f32[40,512]{1,0:T(8,128)S(1)}, f32[40,512]{1,0:T(8,128)S(1)}, u32[]{:S(2)}, u32[]{:S(2)}) %collective-permute-start.7) | collective-permute-done | bytes 81952 | tf_op jit(solution)/shard_map/ppermute | solution.py:40
  317.2 10.8 %collective-permute-start.8 = (f32[40,512]{1,0:T(8,128)S(1)}, f32[40,512]{1,0:T(8,128)S(1)}, u32[]{:S(2)}, u32[]{:S(2)}) collective-permute-start(f32[40,512]{1,0:T(8,128)S(1)} %add.204), channel_id=1, source_target_pairs={{0,256},{32,288},{64,320},{96,352},{128,384},{160,416},{192,448},{... | collective-permute-start | bytes 245768 | tf_op jit(solution)/shard_map/ppermute | solution.py:40
  328.0 3.3 collective-permute-done.8
  331.4 4.6 %collective-permute-start.9 = (f32[32,512]{1,0:T(8,128)S(1)}, f32[32,512]{1,0:T(8,128)S(1)}, u32[]{:S(2)}, u32[]{:S(2)}) collective-permute-start(f32[32,512]{1,0:T(8,128)S(1)} %get-tuple-element.17), channel_id=1, source_target_pairs={{0,16},{1,17},{2,18},{3,19},{4,20},{5,21},{6,22},{7,23},{8,24},{9,... | collective-permute-start | bytes 196616 | tf_op jit(solution)/shard_map/ppermute | solution.py:45
  336.0 2.2 collective-permute-done.9
  338.2 3.1 collective-permute-start.10
  341.4 2.5 collective-permute-done.10
  343.9 4.6 %collective-permute-start.11 = (f32[128,512]{1,0:T(8,128)S(1)}, f32[128,512]{1,0:T(8,128)S(1)}, u32[]{:S(2)}, u32[]{:S(2)}) collective-permute-start(f32[128,512]{1,0:T(8,128)S(1)} %constant_dynamic-update-slice_fusion.6), channel_id=1, source_target_pairs={{0,4},{1,5},{2,6},{3,7},{4,0},{5,1},{6,2},{7,3},{8,12},{9,13},{10,... | collective-permute-start | bytes 786440 | tf_op jit(solution)/shard_map/ppermute | solution.py:45
  348.6 3.9 %collective-permute-done.11 = f32[128,512]{1,0:T(8,128)S(1)} collective-permute-done((f32[128,512]{1,0:T(8,128)S(1)}, f32[128,512]{1,0:T(8,128)S(1)}, u32[]{:S(2)}, u32[]{:S(2)}) %collective-permute-start.11) | collective-permute-done | bytes 262176 | tf_op jit(solution)/shard_map/ppermute | solution.py:45
  352.6 3.1 collective-permute-start.12
  355.9 8.1 %collective-permute-done.12 = f32[256,512]{1,0:T(8,128)S(1)} collective-permute-done((f32[256,512]{1,0:T(8,128)S(1)}, f32[256,512]{1,0:T(8,128)S(1)}, u32[]{:S(2)}, u32[]{:S(2)}) %collective-permute-start.12) | collective-permute-done | bytes 524320 | tf_op jit(solution)/shard_map/ppermute | solution.py:45
  364.0 16.7 %collective-permute-start.13 = (f32[512,512]{1,0:T(8,128)S(1)}, f32[512,512]{1,0:T(8,128)S(1)}, u32[]{:S(2)}, u32[]{:S(2)}) collective-permute-start(f32[512,512]{1,0:T(8,128)S(1)} %constant_dynamic-update-slice_fusion.2), channel_id=1, source_target_pairs={{0,1},{1,0},{2,3},{3,2},{4,5},{5,4},{6,7},{7,6},{8,9},{9,8},{10,11... | collective-permute-start | bytes 3145736 | tf_op jit(solution)/shard_map/ppermute | solution.py:45
  (89 shorter events, 29.9 us)
Async XLA Ops:
  7.2 1.5 copy-start
  7.2 71.1 %copy-start.5 = (s32[4,8]{1,0:T(4,128)S(1)}, s32[4,8]{1,0:T(4,128)}, u32[]{:S(2)}) copy-start(s32[4,8]{1,0:T(4,128)} %param.13) | copy-start | bytes 388
  7.2 71.1 %all-gather.4.cloned.1.call-start = ((), (), s32[]{:S(2)}) async-start(), calls=%async_computation | async-start | bytes 4325376 | tf_op jit(solution)/shard_map/all_gather | solution.py:77
  7.9 148.1 %all-gather.6.cloned.1.call-start = ((), (), s32[]{:S(2)}) async-start(), calls=%async_computation.1 | async-start | bytes 2228224 | tf_op jit(solution)/shard_map/all_gather | solution.py:93
  78.3 5.5 %copy-start.8 = (bf16[4,8,128,128]{3,2,1,0:T(8,128)(2,1)S(1)}, bf16[4,8,128,128]{3,2,1,0:T(8,128)(2,1)}, u32[]{:S(2)}) copy-start(bf16[4,8,128,128]{3,2,1,0:T(8,128)(2,1)} %param.15) | copy-start | bytes 3145732
  83.8 2.6 copy-start.4
  86.5 0.8 copy-start.2
  86.5 1.7 copy-start.7
  87.3 72.0 %copy-start.6 = (s32[512]{0:T(512)S(1)}, s32[512]{0:T(512)}, u32[]{:S(2)}) copy-start(s32[512]{0:T(512)} %param.16) | copy-start | bytes 6148
  88.0 141.8 %all-gather.8.cloned.1.call-start = ((), (), s32[]{:S(2)}) async-start(), calls=%async_computation.2 | async-start | bytes 2228224 | tf_op jit(solution)/shard_map/all_gather | solution.py:111
  235.2 1.0 copy-start.3
  238.7 14.3 %collective-permute-start = (f32[520,512]{1,0:T(8,128)}, f32[520,512]{1,0:T(8,128)}, u32[]{:S(2)}, u32[]{:S(2)}) collective-permute-start(f32[520,512]{1,0:T(8,128)} %concatenate.24), channel_id=1, source_target_pairs={{0,1},{1,0},{2,3},{3,2},{4,5},{5,4},{6,7},{7,6},{8,9},{9,8},{10,11... | collective-permute-start | bytes 3194888 | tf_op jit(solution)/shard_map/ppermute | solution.py:31
  254.6 1.0 copy-start.1
  256.4 15.4 %collective-permute-start.1 = (f32[264,512]{1,0:T(8,128)S(1)}, f32[264,512]{1,0:T(8,128)S(1)}, u32[]{:S(2)}, u32[]{:S(2)}) collective-permute-start(f32[264,512]{1,0:T(8,128)S(1)} %pad_maximum_fusion), channel_id=1, source_target_pairs={{0,2},{1,3},{2,0},{3,1},{4,6},{5,7},{6,4},{7,5},{8,10},{9,11},{10,... | collective-permute-start | bytes 1622024 | tf_op jit(solution)/shard_map/ppermute | solution.py:31
  273.7 10.3 %collective-permute-start.2 = (f32[136,512]{1,0:T(8,128)S(1)}, f32[136,512]{1,0:T(8,128)S(1)}, u32[]{:S(2)}, u32[]{:S(2)}) collective-permute-start(f32[136,512]{1,0:T(8,128)S(1)} %pad_maximum_fusion.1), channel_id=1, source_target_pairs={{0,4},{1,5},{2,6},{3,7},{4,0},{5,1},{6,2},{7,3},{8,12},{9,13},{10,... | collective-permute-start | bytes 835592 | tf_op jit(solution)/shard_map/ppermute | solution.py:31
  284.1 5.9 %collective-permute-start.3 = (f32[72,512]{1,0:T(8,128)S(1)}, f32[72,512]{1,0:T(8,128)S(1)}, u32[]{:S(2)}, u32[]{:S(2)}) collective-permute-start(f32[72,512]{1,0:T(8,128)S(1)} %pad_maximum_fusion.2), channel_id=1, source_target_pairs={{0,8},{1,9},{2,10},{3,11},{4,12},{5,13},{6,14},{7,15},{8,0},{9,1},... | collective-permute-start | bytes 442376 | tf_op jit(solution)/shard_map/ppermute | solution.py:31
  290.1 6.7 %collective-permute-start.4 = (f32[40,512]{1,0:T(8,128)S(1)}, f32[40,512]{1,0:T(8,128)S(1)}, u32[]{:S(2)}, u32[]{:S(2)}) collective-permute-start(f32[40,512]{1,0:T(8,128)S(1)} %pad_maximum_fusion.3), channel_id=1, source_target_pairs={{0,16},{1,17},{2,18},{3,19},{4,20},{5,21},{6,22},{7,23},{8,24},{9,... | collective-permute-start | bytes 245768 | tf_op jit(solution)/shard_map/ppermute | solution.py:31
  296.8 5.2 %collective-permute-start.5 = (f32[40,512]{1,0:T(8,128)S(1)}, f32[40,512]{1,0:T(8,128)S(1)}, u32[]{:S(2)}, u32[]{:S(2)}) collective-permute-start(f32[40,512]{1,0:T(8,128)S(1)} %pad_maximum_fusion.4), channel_id=1, source_target_pairs={{0,32},{32,0},{64,96},{96,64},{128,160},{160,128},{192,224},{224,1... | collective-permute-start | bytes 245768 | tf_op jit(solution)/shard_map/ppermute | solution.py:40
  302.0 6.1 %collective-permute-start.6 = (f32[40,512]{1,0:T(8,128)S(1)}, f32[40,512]{1,0:T(8,128)S(1)}, u32[]{:S(2)}, u32[]{:S(2)}) collective-permute-start(f32[40,512]{1,0:T(8,128)S(1)} %fusion.39), channel_id=1, source_target_pairs={{0,64},{32,96},{64,0},{96,32},{128,192},{160,224},{192,128},{224,1... | collective-permute-start | bytes 245768 | tf_op jit(solution)/shard_map/ppermute | solution.py:40
  308.1 9.1 %collective-permute-start.7 = (f32[40,512]{1,0:T(8,128)S(1)}, f32[40,512]{1,0:T(8,128)S(1)}, u32[]{:S(2)}, u32[]{:S(2)}) collective-permute-start(f32[40,512]{1,0:T(8,128)S(1)} %add.203), channel_id=1, source_target_pairs={{0,128},{32,160},{64,192},{96,224},{128,0},{160,32},{192,64},{224,... | collective-permute-start | bytes 245768 | tf_op jit(solution)/shard_map/ppermute | solution.py:40
  317.2 14.1 %collective-permute-start.8 = (f32[40,512]{1,0:T(8,128)S(1)}, f32[40,512]{1,0:T(8,128)S(1)}, u32[]{:S(2)}, u32[]{:S(2)}) collective-permute-start(f32[40,512]{1,0:T(8,128)S(1)} %add.204), channel_id=1, source_target_pairs={{0,256},{32,288},{64,320},{96,352},{128,384},{160,416},{192,448},{... | collective-permute-start | bytes 245768 | tf_op jit(solution)/shard_map/ppermute | solution.py:40
  331.4 6.8 %collective-permute-start.9 = (f32[32,512]{1,0:T(8,128)S(1)}, f32[32,512]{1,0:T(8,128)S(1)}, u32[]{:S(2)}, u32[]{:S(2)}) collective-permute-start(f32[32,512]{1,0:T(8,128)S(1)} %get-tuple-element.17), channel_id=1, source_target_pairs={{0,16},{1,17},{2,18},{3,19},{4,20},{5,21},{6,22},{7,23},{8,24},{9,... | collective-permute-start | bytes 196616 | tf_op jit(solution)/shard_map/ppermute | solution.py:45
  338.2 5.7 %collective-permute-start.10 = (f32[64,512]{1,0:T(8,128)S(1)}, f32[64,512]{1,0:T(8,128)S(1)}, u32[]{:S(2)}, u32[]{:S(2)}) collective-permute-start(f32[64,512]{1,0:T(8,128)S(1)} %constant_dynamic-update-slice_fusion.8), channel_id=1, source_target_pairs={{0,8},{1,9},{2,10},{3,11},{4,12},{5,13},{6,14},{7,15},{8,0},{9,1},... | collective-permute-start | bytes 393224 | tf_op jit(solution)/shard_map/ppermute | solution.py:45
  343.9 8.6 %collective-permute-start.11 = (f32[128,512]{1,0:T(8,128)S(1)}, f32[128,512]{1,0:T(8,128)S(1)}, u32[]{:S(2)}, u32[]{:S(2)}) collective-permute-start(f32[128,512]{1,0:T(8,128)S(1)} %constant_dynamic-update-slice_fusion.6), channel_id=1, source_target_pairs={{0,4},{1,5},{2,6},{3,7},{4,0},{5,1},{6,2},{7,3},{8,12},{9,13},{10,... | collective-permute-start | bytes 786440 | tf_op jit(solution)/shard_map/ppermute | solution.py:45
  352.6 11.4 %collective-permute-start.12 = (f32[256,512]{1,0:T(8,128)S(1)}, f32[256,512]{1,0:T(8,128)S(1)}, u32[]{:S(2)}, u32[]{:S(2)}) collective-permute-start(f32[256,512]{1,0:T(8,128)S(1)} %constant_dynamic-update-slice_fusion.4), channel_id=1, source_target_pairs={{0,2},{1,3},{2,0},{3,1},{4,6},{5,7},{6,4},{7,5},{8,10},{9,11},{10,... | collective-permute-start | bytes 1572872 | tf_op jit(solution)/shard_map/ppermute | solution.py:45
  364.0 19.0 %collective-permute-start.13 = (f32[512,512]{1,0:T(8,128)S(1)}, f32[512,512]{1,0:T(8,128)S(1)}, u32[]{:S(2)}, u32[]{:S(2)}) collective-permute-start(f32[512,512]{1,0:T(8,128)S(1)} %constant_dynamic-update-slice_fusion.2), channel_id=1, source_target_pairs={{0,1},{1,0},{2,3},{3,2},{4,5},{5,4},{6,7},{7,6},{8,9},{9,8},{10,11... | collective-permute-start | bytes 3145736 | tf_op jit(solution)/shard_map/ppermute | solution.py:45
Sparse Core Ops, SparseCore 0:
  11.2 67.0 all-gather.3
  88.1 67.8 all-gather.5
  159.4 70.3 all-gather.7

commit v3 on v2

--- a/solution.py
+++ b/solution.py
@@ -69,32 +69,46 @@
     rows = node_feats.shape[0]
     width = node_feats.shape[1]
     slots = adj_tiles.shape[1]
+    lanes = adj_tiles.shape[3]
     highest = lax.Precision.HIGHEST
-    nodes = rows * lax.axis_size("row") * lax.axis_size("col")
+    groups = lax.axis_size("row")
+    nodes = rows * groups * lax.axis_size("col")
     scale_factor = 1.0 / softness_divisor
     valid = jnp.arange(slots, dtype=jnp.int32)[None, :] < nbr_count[:, None]
     tiles = adj_tiles * valid[:, :, None, None].astype(jnp.bfloat16)
+    id_row = jnp.zeros((8, lanes), jnp.bfloat16).at[0, :slots].set(nbr_blocks[0].astype(jnp.bfloat16))
+    nf_rows = NOISE * width // lanes
+    payload = jnp.concatenate(
+        [node_feats[:NOISE].reshape(nf_rows, lanes), tiles[0].reshape(slots * BLOCK, lanes), id_row], axis=0
+    )
+    fanned = jnp.broadcast_to(payload[None], (groups,) + payload.shape)
+    arrived = lax.all_to_all(fanned, "row", 0, 0, tiled=False)
+    my_row = lax.axis_index("row")
+    fetched = lax.dynamic_index_in_dim(arrived, noise_block_rows[my_row], 0, keepdims=False)
+    noise_feats = fetched[:nf_rows].reshape(NOISE, width)
+    noise_tiles = fetched[nf_rows:nf_rows + slots * BLOCK].reshape(1, slots, BLOCK, BLOCK)
+    noise_ids = fetched[nf_rows + slots * BLOCK, :slots].astype(jnp.int32)
+    all_tiles = jnp.concatenate([tiles, noise_tiles], axis=0)
+    all_ids = jnp.concatenate([nbr_blocks, noise_ids[None]], axis=0)
+    all_feats = jnp.concatenate([node_feats, noise_feats], axis=0)
     piece = lax.all_gather(source_feats, "col", axis=0, tiled=True)
     count = piece.shape[0] // BLOCK
     blocks = piece.reshape(count, BLOCK, width)
     indicator_matrix = (
-        nbr_blocks[:, :, None] == jnp.arange(count, dtype=jnp.int32)[None, None, :]
+        all_ids[:, :, None] == jnp.arange(count, dtype=jnp.int32)[None, None, :]
     ).astype(jnp.bfloat16)
     selected = jnp.einsum(
         "bkc,cjd->bkjd", indicator_matrix, blocks, preferred_element_type=jnp.float32
     ).astype(jnp.bfloat16)
-    summed = jnp.einsum("bkij,bkjd->bid", tiles, selected, preferred_element_type=jnp.float32)
-    agg = summed.reshape(rows, width).astype(jnp.bfloat16)
-    pre = jnp.dot(node_feats, w_self, preferred_element_type=jnp.float32) + jnp.dot(
+    summed = jnp.einsum("bkij,bkjd->bid", all_tiles, selected, preferred_element_type=jnp.float32)
+    agg = summed.reshape(rows + NOISE, width).astype(jnp.bfloat16)
+    pre = jnp.dot(all_feats, w_self, preferred_element_type=jnp.float32) + jnp.dot(
         agg, w_neigh, preferred_element_type=jnp.float32
     )
     emb32, pull = jax.vjp(embed, pre)
     zeta_bf = emb32.astype(jnp.bfloat16)
-    candidates = lax.all_gather(zeta_bf[:NOISE], "row", axis=0, tiled=True)
-    my_row = lax.axis_index("row")
-    my_noise = noise_block_rows[my_row]
-    noise_emb = lax.dynamic_slice_in_dim(candidates, my_noise * NOISE, NOISE, 0).astype(jnp.float32)
-    zeta = zeta_bf.astype(jnp.float32)
+    noise_emb = zeta_bf[rows:].astype(jnp.float32)
+    zeta = zeta_bf[:rows].astype(jnp.float32)
     pairing = (pos_index[:, None] == jnp.arange(rows, dtype=jnp.int32)[None, :]).astype(jnp.float32)
     partner = jnp.dot(pairing, zeta, precision=highest)
     s_pos = jnp.sum(zeta * partner, axis=-1) * scale_factor
@@ -107,19 +121,10 @@
     )
     partner_grad = jnp.dot(pairing.T, scale_factor * grad_pos[:, None] * zeta, precision=highest)
     dnoise = scale_factor * jnp.dot(grad_neg.T, zeta, precision=highest)
-    groups = lax.axis_size("row")
-    collected = lax.all_gather(dnoise.astype(jnp.bfloat16), "row", axis=0, tiled=True)
-    owned = (noise_block_rows == my_row).astype(jnp.float32)
-    returned = jnp.dot(
-        owned[None, :],
-        collected.astype(jnp.float32).reshape(groups, NOISE * width),
-        precision=highest,
-    )
-    returned = returned.reshape(NOISE, width)
-    dzeta = anchor + partner_grad
-    dzeta = dzeta.at[:NOISE].add(returned)
+    dnoise = dnoise.astype(jnp.bfloat16).astype(jnp.float32)
+    dzeta = jnp.concatenate([anchor + partner_grad, dnoise], axis=0)
     gpre = pull(dzeta)[0].astype(jnp.bfloat16)
-    part_self = jnp.dot(node_feats.T, gpre, preferred_element_type=jnp.float32)
+    part_self = jnp.dot(all_feats.T, gpre, preferred_element_type=jnp.float32)
     neighbour_partial = jnp.dot(agg.T, gpre, preferred_element_type=jnp.float32)
     stacked = jnp.concatenate([part_self, neighbour_partial], axis=0)
     total, loss_tile = tree_allreduce(stacked, jnp.broadcast_to(loss_part, (8, width)))

time: 394 us -> 471 us (1.20)
  waiting for transfers between devices: 256 us -> 322 us
  starting transfers between devices: 81.8 us -> 94.5 us
    all_to_all x0 -> x1, waiting for transfers between devices: none -> 270 us  [body(): arrived = lax.all_to_all(fanned, 'row', 0, 0, tiled=False)]
    all_gather x2 -> x0, waiting for transfers between devices: 132 us -> none  [the longest x1 66.6 us: body(): candidates = lax.all_gather(zeta_bf[:NOISE], 'row', axis=0, tiled=True)]
    all_gather x1, waiting for transfers between devices: 68.1 us -> 0.02 us  [body(): piece = lax.all_gather(source_feats, 'col', axis=0, tiled=True)]
    all_to_all x0 -> x1, starting transfers between devices: none -> 15.9 us  [body(): arrived = lax.all_to_all(fanned, 'row', 0, 0, tiled=False)]
    ppermute x5, starting transfers between devices: 27.1 us -> 19.2 us  [tree_allreduce(): lax.ppermute(jnp.concatenate([send, extra], 0), axis, xor_pairs(size, mask))]
  transfers between devices with their start and end apart: 17 -> 16, of which waited for: 17 -> 15; matrix products, arithmetic and copies ran while one was open for 2% -> 1% of each run, Pallas kernels for 0% -> 0%
where the time goes in v3:
time: 471 us; the launch traced here: 469 us
  waiting for transfers between devices  322 us (68%)
  starting transfers between devices  94.5 us (20%)
  between operations  18.1 us (4%)
  matrix products  15.4 us (3%)
  local copies, waits for them, and re-layouts  12.1 us (3%)
  other arithmetic  7.36 us (2%)
    all_to_all x1, waiting for transfers between devices, body(): arrived = lax.all_to_all(fanned, 'row', 0, 0, tiled=False)  270 us
    ppermute x5, starting transfers between devices, tree_allreduce(): got = lax.ppermute(buf, axis, xor_pairs(size, mask))  34.5 us
    ppermute x5, waiting for transfers between devices, tree_allreduce(): lax.ppermute(jnp.concatenate([send, extra], 0), axis, xor_pairs(size, mask))  24.9 us
    ppermute x4, starting transfers between devices, tree_allreduce(): joined = joined + lax.ppermute(joined, axis, xor_pairs(size, mask))  24.9 us
    ppermute x5, starting transfers between devices, tree_allreduce(): lax.ppermute(jnp.concatenate([send, extra], 0), axis, xor_pairs(size, mask))  19.2 us
    ppermute x5, waiting for transfers between devices, tree_allreduce(): got = lax.ppermute(buf, axis, xor_pairs(size, mask))  16.3 us
    all_to_all x1, starting transfers between devices, body(): arrived = lax.all_to_all(fanned, 'row', 0, 0, tiled=False)  15.9 us
    ppermute x4, waiting for transfers between devices, tree_allreduce(): joined = joined + lax.ppermute(joined, axis, xor_pairs(size, mask))  10.2 us
  transfers between devices with their start and end apart: 16, of which 15 were waited for; matrix products, arithmetic and copies ran while one was open for 1% of the time, Pallas kernels for 0%

profile of v3, /device:TPU:1, one launch (start us, length us, event | category | flops | bytes accessed | tf_op | source)
XLA Modules:
  0.0 469.5 jit_solution(4014025064332530206)
XLA Ops:
  9.6 3.4 broadcast_in_dim.21
  13.0 15.9 %all-to-all-start = ((bf16[16,1544,128]{2,1,0:T(8,128)(2,1)}), bf16[16,1544,128]{2,1,0:T(8,128)(2,1)}, u32[]{:S(2)}, u32[]{:S(2)}) async-start(bf16[16,1544,128]{2,1,0:T(8,128)(2,1)} %broadcast_in_dim.21), calls=%async_computation | async-start | bytes 12648448 | tf_op jit(solution)/shard_map/all_to_all | solution.py:85
  32.3 269.7 %all-to-all-done = bf16[16,1544,128]{2,1,0:T(8,128)(2,1)} async-done(((bf16[16,1544,128]{2,1,0:T(8,128)(2,1)}), bf16[16,1544,128]{2,1,0:T(8,128)(2,1)}, u32[]{:S(2)}, u32[]{:S(2)}) %all-to-all-start) | async-done | bytes 6324256 | tf_op jit(solution)/shard_map/all_to_all | solution.py:85
  304.1 5.4 %fusion.1 = bf16[5,8,128,512]{3,1,2,0:T(8,128)(2,1)S(1)} fusion(bf16[32,128,512,1]{2,1,0,3:T(8,128)(2,1)} %bitcast.28, s32[5,8]{1,0:T(8,128)S(1)} %pad_add_fusion), kind=kOutput, calls=%fused_computation.2 | convolution fusion | flops 167773440 | bytes 9437344 | tf_op jit(solution)/shard_map/bkc,cjd->bkjd/dot_general | solution.py:100
  310.6 3.1 fusion.5
  324.7 3.4 collective-permute-start
  328.1 2.6 collective-permute-done
  334.2 3.1 collective-permute-start.1
  337.4 12.2 %collective-permute-done.1 = f32[264,512]{1,0:T(8,128)S(1)} collective-permute-done((f32[264,512]{1,0:T(8,128)S(1)}, f32[264,512]{1,0:T(8,128)S(1)}, u32[]{:S(2)}, u32[]{:S(2)}) %collective-permute-start.1) | collective-permute-done | bytes 540704 | tf_op jit(solution)/shard_map/ppermute | solution.py:31
  350.5 4.6 collective-permute-start.2
  355.1 5.6 %collective-permute-done.2 = f32[136,512]{1,0:T(8,128)S(1)} collective-permute-done((f32[136,512]{1,0:T(8,128)S(1)}, f32[136,512]{1,0:T(8,128)S(1)}, u32[]{:S(2)}, u32[]{:S(2)}) %collective-permute-start.2) | collective-permute-done | bytes 278560 | tf_op jit(solution)/shard_map/ppermute | solution.py:31
  360.9 3.2 collective-permute-start.3
  364.2 2.6 collective-permute-done.3
  366.9 4.8 %collective-permute-start.4 = (f32[40,512]{1,0:T(8,128)S(1)}, f32[40,512]{1,0:T(8,128)S(1)}, u32[]{:S(2)}, u32[]{:S(2)}) collective-permute-start(f32[40,512]{1,0:T(8,128)S(1)} %pad_maximum_fusion.4), channel_id=1, source_target_pairs={{0,16},{1,17},{2,18},{3,19},{4,20},{5,21},{6,22},{7,23},{8,24},{9,... | collective-permute-start | bytes 245768 | tf_op jit(solution)/shard_map/ppermute | solution.py:31
  371.7 1.8 collective-permute-done.4
  373.6 4.3 collective-permute-start.5
  377.9 1.8 collective-permute-done.5
  379.7 4.0 collective-permute-start.6
  383.8 2.0 collective-permute-done.6
  385.8 6.5 %collective-permute-start.7 = (f32[40,512]{1,0:T(8,128)S(1)}, f32[40,512]{1,0:T(8,128)S(1)}, u32[]{:S(2)}, u32[]{:S(2)}) collective-permute-start(f32[40,512]{1,0:T(8,128)S(1)} %add.200), channel_id=1, source_target_pairs={{0,128},{32,160},{64,192},{96,224},{128,0},{160,32},{192,64},{224,... | collective-permute-start | bytes 245768 | tf_op jit(solution)/shard_map/ppermute | solution.py:40
  392.3 2.6 collective-permute-done.7
  394.9 10.1 %collective-permute-start.8 = (f32[40,512]{1,0:T(8,128)S(1)}, f32[40,512]{1,0:T(8,128)S(1)}, u32[]{:S(2)}, u32[]{:S(2)}) collective-permute-start(f32[40,512]{1,0:T(8,128)S(1)} %add.201), channel_id=1, source_target_pairs={{0,256},{32,288},{64,320},{96,352},{128,384},{160,416},{192,448},{... | collective-permute-start | bytes 245768 | tf_op jit(solution)/shard_map/ppermute | solution.py:40
  405.0 3.8 collective-permute-done.8
  408.9 4.8 %collective-permute-start.9 = (f32[32,512]{1,0:T(8,128)S(1)}, f32[32,512]{1,0:T(8,128)S(1)}, u32[]{:S(2)}, u32[]{:S(2)}) collective-permute-start(f32[32,512]{1,0:T(8,128)S(1)} %get-tuple-element.17), channel_id=1, source_target_pairs={{0,16},{1,17},{2,18},{3,19},{4,20},{5,21},{6,22},{7,23},{8,24},{9,... | collective-permute-start | bytes 196616 | tf_op jit(solution)/shard_map/ppermute | solution.py:45
  413.7 2.0 collective-permute-done.9
  415.7 3.2 collective-permute-start.10
  419.0 2.4 collective-permute-done.10
  421.5 4.6 collective-permute-start.11
  426.2 3.9 collective-permute-done.11
  430.1 3.1 collective-permute-start.12
  433.4 6.6 %collective-permute-done.12 = f32[256,512]{1,0:T(8,128)S(1)} collective-permute-done((f32[256,512]{1,0:T(8,128)S(1)}, f32[256,512]{1,0:T(8,128)S(1)}, u32[]{:S(2)}, u32[]{:S(2)}) %collective-permute-start.12) | collective-permute-done | bytes 524320 | tf_op jit(solution)/shard_map/ppermute | solution.py:45
  440.1 18.7 %collective-permute-start.13 = (f32[512,512]{1,0:T(8,128)S(1)}, f32[512,512]{1,0:T(8,128)S(1)}, u32[]{:S(2)}, u32[]{:S(2)}) collective-permute-start(f32[512,512]{1,0:T(8,128)S(1)} %constant_dynamic-update-slice_fusion.2), channel_id=1, source_target_pairs={{0,1},{1,0},{2,3},{3,2},{4,5},{5,4},{6,7},{7,6},{8,9},{9,8},{10,11... | collective-permute-start | bytes 3145736 | tf_op jit(solution)/shard_map/ppermute | solution.py:45
  (95 shorter events, 25.1 us)
Async XLA Ops:
  7.2 307.1 %copy-start = (bf16[512,512]{1,0:T(8,128)(2,1)S(1)}, bf16[512,512]{1,0:T(8,128)(2,1)}, u32[]{:S(2)}) copy-start(bf16[512,512]{1,0:T(8,128)(2,1)} %param.19) | copy-start | bytes 1572868
  8.0 1.4 slice-start
  8.0 1.6 copy-start.5
  13.0 16.7 %copy-start.7 = (s32[16]{0:T(128)S(1)}, s32[16]{0:T(128)}, u32[]{:S(2)}) copy-start(s32[16]{0:T(128)} %param.17) | copy-start | bytes 196
  13.0 19.2 %copy-start.3 = (bf16[512,512]{1,0:T(8,128)(2,1)S(1)}, bf16[512,512]{1,0:T(8,128)(2,1)}, u32[]{:S(2)}) copy-start(bf16[512,512]{1,0:T(8,128)(2,1)} %param.11) | copy-start | bytes 1572868
  13.0 289.0 %all-to-all-start = ((bf16[16,1544,128]{2,1,0:T(8,128)(2,1)}), bf16[16,1544,128]{2,1,0:T(8,128)(2,1)}, u32[]{:S(2)}, u32[]{:S(2)}) async-start(bf16[16,1544,128]{2,1,0:T(8,128)(2,1)} %broadcast_in_dim.21), calls=%async_computation | async-start | bytes 12648448 | tf_op jit(solution)/shard_map/all_to_all | solution.py:85
  29.0 275.2 %all-gather.2.cloned.1.call-start = ((), (), s32[]{:S(2)}) async-start(), calls=%async_computation.1 | async-start | bytes 4325376 | tf_op jit(solution)/shard_map/all_gather | solution.py:94
  310.6 3.1 copy-start.4
  315.0 1.1 copy-start.6
  324.7 6.0 %collective-permute-start = (f32[520,512]{1,0:T(8,128)}, f32[520,512]{1,0:T(8,128)}, u32[]{:S(2)}, u32[]{:S(2)}) collective-permute-start(f32[520,512]{1,0:T(8,128)} %concatenate.44), channel_id=1, source_target_pairs={{0,1},{1,0},{2,3},{3,2},{4,5},{5,4},{6,7},{7,6},{8,9},{9,8},{10,11... | collective-permute-start | bytes 3194888 | tf_op jit(solution)/shard_map/ppermute | solution.py:31
  332.3 1.0 copy-start.1
  333.3 16.2 %copy-start.2 = (f32[512,512]{1,0:T(8,128)S(1)}, f32[512,512]{1,0:T(8,128)}, u32[]{:S(2)}) copy-start(f32[512,512]{1,0:T(8,128)} %copy-done.1) | copy-start | bytes 3145732
  334.2 15.4 %collective-permute-start.1 = (f32[264,512]{1,0:T(8,128)S(1)}, f32[264,512]{1,0:T(8,128)S(1)}, u32[]{:S(2)}, u32[]{:S(2)}) collective-permute-start(f32[264,512]{1,0:T(8,128)S(1)} %pad_maximum_fusion.1), channel_id=1, source_target_pairs={{0,2},{1,3},{2,0},{3,1},{4,6},{5,7},{6,4},{7,5},{8,10},{9,11},{10,... | collective-permute-start | bytes 1622024 | tf_op jit(solution)/shard_map/ppermute | solution.py:31
  350.5 10.3 %collective-permute-start.2 = (f32[136,512]{1,0:T(8,128)S(1)}, f32[136,512]{1,0:T(8,128)S(1)}, u32[]{:S(2)}, u32[]{:S(2)}) collective-permute-start(f32[136,512]{1,0:T(8,128)S(1)} %pad_maximum_fusion.2), channel_id=1, source_target_pairs={{0,4},{1,5},{2,6},{3,7},{4,0},{5,1},{6,2},{7,3},{8,12},{9,13},{10,... | collective-permute-start | bytes 835592 | tf_op jit(solution)/shard_map/ppermute | solution.py:31
  360.9 5.9 %collective-permute-start.3 = (f32[72,512]{1,0:T(8,128)S(1)}, f32[72,512]{1,0:T(8,128)S(1)}, u32[]{:S(2)}, u32[]{:S(2)}) collective-permute-start(f32[72,512]{1,0:T(8,128)S(1)} %pad_maximum_fusion.3), channel_id=1, source_target_pairs={{0,8},{1,9},{2,10},{3,11},{4,12},{5,13},{6,14},{7,15},{8,0},{9,1},... | collective-permute-start | bytes 442376 | tf_op jit(solution)/shard_map/ppermute | solution.py:31
  366.9 6.7 %collective-permute-start.4 = (f32[40,512]{1,0:T(8,128)S(1)}, f32[40,512]{1,0:T(8,128)S(1)}, u32[]{:S(2)}, u32[]{:S(2)}) collective-permute-start(f32[40,512]{1,0:T(8,128)S(1)} %pad_maximum_fusion.4), channel_id=1, source_target_pairs={{0,16},{1,17},{2,18},{3,19},{4,20},{5,21},{6,22},{7,23},{8,24},{9,... | collective-permute-start | bytes 245768 | tf_op jit(solution)/shard_map/ppermute | solution.py:31
  373.6 6.1 %collective-permute-start.5 = (f32[40,512]{1,0:T(8,128)S(1)}, f32[40,512]{1,0:T(8,128)S(1)}, u32[]{:S(2)}, u32[]{:S(2)}) collective-permute-start(f32[40,512]{1,0:T(8,128)S(1)} %pad_maximum_fusion.5), channel_id=1, source_target_pairs={{0,32},{32,0},{64,96},{96,64},{128,160},{160,128},{192,224},{224,1... | collective-permute-start | bytes 245768 | tf_op jit(solution)/shard_map/ppermute | solution.py:40
  379.7 6.1 %collective-permute-start.6 = (f32[40,512]{1,0:T(8,128)S(1)}, f32[40,512]{1,0:T(8,128)S(1)}, u32[]{:S(2)}, u32[]{:S(2)}) collective-permute-start(f32[40,512]{1,0:T(8,128)S(1)} %fusion.39), channel_id=1, source_target_pairs={{0,64},{32,96},{64,0},{96,32},{128,192},{160,224},{192,128},{224,1... | collective-permute-start | bytes 245768 | tf_op jit(solution)/shard_map/ppermute | solution.py:40
  385.8 9.1 %collective-permute-start.7 = (f32[40,512]{1,0:T(8,128)S(1)}, f32[40,512]{1,0:T(8,128)S(1)}, u32[]{:S(2)}, u32[]{:S(2)}) collective-permute-start(f32[40,512]{1,0:T(8,128)S(1)} %add.200), channel_id=1, source_target_pairs={{0,128},{32,160},{64,192},{96,224},{128,0},{160,32},{192,64},{224,... | collective-permute-start | bytes 245768 | tf_op jit(solution)/shard_map/ppermute | solution.py:40
  394.9 13.9 %collective-permute-start.8 = (f32[40,512]{1,0:T(8,128)S(1)}, f32[40,512]{1,0:T(8,128)S(1)}, u32[]{:S(2)}, u32[]{:S(2)}) collective-permute-start(f32[40,512]{1,0:T(8,128)S(1)} %add.201), channel_id=1, source_target_pairs={{0,256},{32,288},{64,320},{96,352},{128,384},{160,416},{192,448},{... | collective-permute-start | bytes 245768 | tf_op jit(solution)/shard_map/ppermute | solution.py:40
  408.9 6.8 %collective-permute-start.9 = (f32[32,512]{1,0:T(8,128)S(1)}, f32[32,512]{1,0:T(8,128)S(1)}, u32[]{:S(2)}, u32[]{:S(2)}) collective-permute-start(f32[32,512]{1,0:T(8,128)S(1)} %get-tuple-element.17), channel_id=1, source_target_pairs={{0,16},{1,17},{2,18},{3,19},{4,20},{5,21},{6,22},{7,23},{8,24},{9,... | collective-permute-start | bytes 196616 | tf_op jit(solution)/shard_map/ppermute | solution.py:45
  415.7 5.7 %collective-permute-start.10 = (f32[64,512]{1,0:T(8,128)S(1)}, f32[64,512]{1,0:T(8,128)S(1)}, u32[]{:S(2)}, u32[]{:S(2)}) collective-permute-start(f32[64,512]{1,0:T(8,128)S(1)} %constant_dynamic-update-slice_fusion.8), channel_id=1, source_target_pairs={{0,8},{1,9},{2,10},{3,11},{4,12},{5,13},{6,14},{7,15},{8,0},{9,1},... | collective-permute-start | bytes 393224 | tf_op jit(solution)/shard_map/ppermute | solution.py:45
  421.5 8.6 %collective-permute-start.11 = (f32[128,512]{1,0:T(8,128)S(1)}, f32[128,512]{1,0:T(8,128)S(1)}, u32[]{:S(2)}, u32[]{:S(2)}) collective-permute-start(f32[128,512]{1,0:T(8,128)S(1)} %constant_dynamic-update-slice_fusion.6), channel_id=1, source_target_pairs={{0,4},{1,5},{2,6},{3,7},{4,0},{5,1},{6,2},{7,3},{8,12},{9,13},{10,... | collective-permute-start | bytes 786440 | tf_op jit(solution)/shard_map/ppermute | solution.py:45
  430.1 9.9 %collective-permute-start.12 = (f32[256,512]{1,0:T(8,128)S(1)}, f32[256,512]{1,0:T(8,128)S(1)}, u32[]{:S(2)}, u32[]{:S(2)}) collective-permute-start(f32[256,512]{1,0:T(8,128)S(1)} %constant_dynamic-update-slice_fusion.4), channel_id=1, source_target_pairs={{0,2},{1,3},{2,0},{3,1},{4,6},{5,7},{6,4},{7,5},{8,10},{9,11},{10,... | collective-permute-start | bytes 1572872 | tf_op jit(solution)/shard_map/ppermute | solution.py:45
  440.1 21.0 %collective-permute-start.13 = (f32[512,512]{1,0:T(8,128)S(1)}, f32[512,512]{1,0:T(8,128)S(1)}, u32[]{:S(2)}, u32[]{:S(2)}) collective-permute-start(f32[512,512]{1,0:T(8,128)S(1)} %constant_dynamic-update-slice_fusion.2), channel_id=1, source_target_pairs={{0,1},{1,0},{2,3},{3,2},{4,5},{5,4},{6,7},{7,6},{8,9},{9,8},{10,11... | collective-permute-start | bytes 3145736 | tf_op jit(solution)/shard_map/ppermute | solution.py:45
Sparse Core Ops, SparseCore 0:
  32.9 63.3 all-gather.1

commit v4 on v0

--- a/solution.py
+++ b/solution.py
@@ -8,6 +8,40 @@
 
 
 softness_divisor = 0.2
+
+
+def xor_pairs(size, mask):
+    return [(i, i ^ mask) for i in range(size)]
+
+
+DOUBLING = (("col", 16), ("col", 8), ("col", 4), ("col", 2), ("col", 1))
+BUTTERFLY = (("row", 1), ("row", 2), ("row", 4), ("row", 8))
+
+
+def tree_allreduce(buf, extra):
+    ways = lax.axis_size("col")
+    me = lax.axis_index("col")
+    masks = [mask for axis, mask in DOUBLING if mask < ways]
+    position = [sum(((j // mask) % 2) << t for t, mask in enumerate(masks)) for j in range(ways)]
+    rows = buf.shape[0] // ways
+    chunks = buf.reshape(ways, rows, buf.shape[1])[jnp.array(position, jnp.int32)]
+    chunks = jnp.concatenate([chunks, jnp.broadcast_to(extra[None], (ways,) + extra.shape)], axis=1)
+    joined = lax.all_to_all(chunks, "col", 0, 0, tiled=False).sum(axis=0)
+    for axis, mask in BUTTERFLY:
+        size = lax.axis_size(axis)
+        if mask >= size:
+            continue
+        joined = joined + lax.ppermute(joined, axis, xor_pairs(size, mask))
+    buf, extra = joined[:rows], joined[rows:]
+    for mask in masks:
+        bit = (me // mask) % 2
+        got = lax.ppermute(buf, "col", xor_pairs(ways, mask))
+        held = buf.shape[0]
+        out = jnp.zeros((2 * held,) + buf.shape[1:], buf.dtype)
+        out = lax.dynamic_update_slice_in_dim(out, buf, bit * held, 0)
+        out = lax.dynamic_update_slice_in_dim(out, got, (1 - bit) * held, 0)
+        buf = out
+    return buf, extra
 
 
 def embed(pre):
@@ -55,9 +89,9 @@
     noise_emb = lax.dynamic_slice_in_dim(candidates, my_noise * NOISE, NOISE, 0).astype(jnp.float32)
     zeta = zeta_bf.astype(jnp.float32)
     pairing = (pos_index[:, None] == jnp.arange(rows, dtype=jnp.int32)[None, :]).astype(jnp.float32)
-    partner = jnp.dot(pairing, zeta, precision=highest)
+    partner = jnp.dot(pairing.astype(jnp.bfloat16), zeta_bf, preferred_element_type=jnp.float32)
     s_pos = jnp.sum(zeta * partner, axis=-1) * scale_factor
-    s_neg = jnp.dot(zeta, noise_emb.T, precision=highest) * scale_factor
+    s_neg = jnp.dot(zeta_bf, noise_emb.astype(jnp.bfloat16).T, preferred_element_type=jnp.float32) * scale_factor
     loss_part = (jnp.sum(jax.nn.softplus(-s_pos)) + jnp.sum(jax.nn.softplus(s_neg)) / NOISE) / nodes
     grad_pos = -jax.nn.sigmoid(-s_pos) / nodes
     grad_neg = jax.nn.sigmoid(s_neg) / (NOISE * nodes)
@@ -69,21 +103,19 @@
     groups = lax.axis_size("row")
     collected = lax.all_gather(dnoise.astype(jnp.bfloat16), "row", axis=0, tiled=True)
     owned = (noise_block_rows == my_row).astype(jnp.float32)
-    returned = jnp.dot(
-        owned[None, :],
-        collected.astype(jnp.float32).reshape(groups, NOISE * width),
-        precision=highest,
+    returned = jnp.sum(
+        owned[:, None, None] * collected.astype(jnp.float32).reshape(groups, NOISE, width), axis=0
     )
-    returned = returned.reshape(NOISE, width)
     dzeta = anchor + partner_grad
     dzeta = dzeta.at[:NOISE].add(returned)
     gpre = pull(dzeta)[0].astype(jnp.bfloat16)
     part_self = jnp.dot(node_feats.T, gpre, preferred_element_type=jnp.float32)
     neighbour_partial = jnp.dot(agg.T, gpre, preferred_element_type=jnp.float32)
-    grad_self, neighbour_weight_gradient, loss = lax.psum(
-        (part_self, neighbour_partial, loss_part), ("row", "col")
-    )
-    return (grad_self, neighbour_weight_gradient, loss)
+    stacked = jnp.concatenate([part_self, neighbour_partial], axis=0)
+    total, loss_tile = tree_allreduce(stacked, jnp.broadcast_to(loss_part, (8, width)))
+    grad_self = total[:width]
+    neighbour_weight_gradient = total[width:]
+    return (grad_self, neighbour_weight_gradient, loss_tile[0, 0])
 
 
 def solution(mesh):

time: 734 us -> 385 us (0.52)
  waiting for transfers between devices: 572 us -> 232 us
  blocking collectives: 111 us -> 50.4 us
  starting transfers between devices: 0.34 us -> 54.6 us
    psum x1 -> x0, waiting for transfers between devices: 371 us -> none  [body(): lax.psum((part_self, neighbour_partial, loss_part), ('row', 'col'))]
    psum x1 -> x0, blocking collectives: 111 us -> none  [body(): lax.psum((part_self, neighbour_partial, loss_part), ('row', 'col'))]
    ppermute x0 -> x9, starting transfers between devices: none -> 54.3 us  [the longest x5 28.4 us: tree_allreduce(): got = lax.ppermute(buf, 'col', xor_pairs(ways, mask))]
    all_to_all x0 -> x1, blocking collectives: none -> 50.4 us  [tree_allreduce(): joined = lax.all_to_all(chunks, 'col', 0, 0, tiled=False).sum(axis=0)]
    ppermute x0 -> x9, waiting for transfers between devices: none -> 31.3 us  [the longest x5 21.3 us: tree_allreduce(): got = lax.ppermute(buf, 'col', xor_pairs(ways, mask))]
  transfers between devices with their start and end apart: 4 -> 12, of which waited for: 4 -> 12; matrix products, arithmetic and copies ran while one was open for 1% -> 2% of each run, Pallas kernels for 0% -> 0%
where the time goes in v4:
time: 385 us; the launch traced here: 384 us
  waiting for transfers between devices  232 us (60%)
  starting transfers between devices  54.6 us (14%)
  blocking collectives  50.4 us (13%)
  matrix products  17.9 us (5%)
  between operations  16.3 us (4%)
  local copies, waits for them, and re-layouts  7.16 us (2%)
  other arithmetic  5.97 us (2%)
    all_gather x1, waiting for transfers between devices, body(): piece = lax.all_gather(source_feats, 'col', axis=0, tiled=True)  68.1 us
    all_gather x1, waiting for transfers between devices, body(): candidates = lax.all_gather(zeta_bf[:NOISE], 'row', axis=0, tiled=True)  66.6 us
    all_gather x1, waiting for transfers between devices, body(): lax.all_gather(dnoise.astype(jnp.bfloat16), 'row', axis=0, tiled=True)  65.1 us
    all_to_all x1, blocking collectives, tree_allreduce(): joined = lax.all_to_all(chunks, 'col', 0, 0, tiled=False).sum(axis=0)  50.4 us
    ppermute x5, starting transfers between devices, tree_allreduce(): got = lax.ppermute(buf, 'col', xor_pairs(ways, mask))  28.4 us
    ppermute x4, starting transfers between devices, tree_allreduce(): joined = joined + lax.ppermute(joined, axis, xor_pairs(size, mask))  25.9 us
    ppermute x5, waiting for transfers between devices, tree_allreduce(): got = lax.ppermute(buf, 'col', xor_pairs(ways, mask))  21.3 us
    ppermute x4, waiting for transfers between devices, tree_allreduce(): joined = joined + lax.ppermute(joined, axis, xor_pairs(size, mask))  10 us
  transfers between devices with their start and end apart: 12, of which 12 were waited for; matrix products, arithmetic and copies ran while one was open for 2% of the time, Pallas kernels for 0%

profile of v4, /device:TPU:1, one launch (start us, length us, event | category | flops | bytes accessed | tf_op | source)
XLA Modules:
  0.0 384.0 jit_solution(16159899819602484493)
XLA Ops:
  8.7 1.5 fusion.33
  10.2 68.1 %all-gather.4.cloned.1.call-done = bf16[4096,512]{1,0:T(8,128)(2,1)} async-done(((bf16[128,512]{1,0:T(8,128)(2,1)}), bf16[4096,512]{1,0:T(8,128)(2,1)}) %all-gather.4.cloned.1.call-update) | async-done | bytes 4194320 | tf_op jit(solution)/shard_map/all_gather | solution.py:70
  78.3 5.5 %fusion.2 = bf16[4,8,128,512]{3,1,2,0:T(8,128)(2,1)S(1)} fusion(bf16[32,128,512,1]{2,1,0,3:T(8,128)(2,1)} %bitcast.33, s32[4,8]{1,0:T(4,128)S(1)} %copy-done.4), kind=kOutput, calls=%fused_computation.5 | convolution fusion | flops 134218752 | bytes 8388736 | tf_op jit(solution)/shard_map/bkc,cjd->bkjd/dot_general | solution.py:76
  83.9 2.6 fusion.6
  89.5 66.6 %all-gather.6.cloned.1.call-done = bf16[2048,512]{0,1:T(8,128)(2,1)} async-done(((bf16[128,512]{0,1:T(8,128)(2,1)}), bf16[2048,512]{0,1:T(8,128)(2,1)}) %all-gather.6.cloned.1.call-update) | async-done | bytes 2097168 | tf_op jit(solution)/shard_map/all_gather | solution.py:86
  156.0 2.0 fusion.16
  158.0 1.4 fusion.7
  162.0 1.6 fusion.5
  164.8 65.1 %all-gather.8.cloned.1.call-done = bf16[2048,512]{1,0:T(8,128)(2,1)} async-done(((bf16[128,512]{1,0:T(8,128)(2,1)}), bf16[2048,512]{1,0:T(8,128)(2,1)}) %all-gather.8.cloned.1.call-update) | async-done | bytes 2097168 | tf_op jit(solution)/shard_map/all_gather | solution.py:104
  229.9 2.1 fusion.1
  234.0 1.5 pad_maximum_fusion
  235.5 2.3 gather_fusion
  238.1 50.4 %all_to_all.5 = f32[32,40,512]{2,1,0:T(8,128)S(1)} all-to-all(f32[32,40,512]{2,1,0:T(8,128)S(1)} %concatenate.9), channel_id=1, replica_groups=mesh['row'=16,'col'=32] {'col'}, dimensions={0} | all-to-all | bytes 5242880 | tf_op jit(solution)/shard_map/all_to_all | solution.py:29
  288.7 3.4 collective-permute-start
  292.1 1.8 collective-permute-done
  293.9 3.1 collective-permute-start.1
  297.0 3.0 collective-permute-done.1
  300.0 5.6 %collective-permute-start.2 = (f32[40,512]{1,0:T(8,128)S(1)}, f32[40,512]{1,0:T(8,128)S(1)}, u32[]{:S(2)}, u32[]{:S(2)}) collective-permute-start(f32[40,512]{1,0:T(8,128)S(1)} %add.146), channel_id=1, source_target_pairs={{0,128},{32,160},{64,192},{96,224},{128,0},{160,32},{192,64},{224,... | collective-permute-start | bytes 245768 | tf_op jit(solution)/shard_map/ppermute | solution.py:34
  305.6 3.5 collective-permute-done.2
  309.1 13.8 %collective-permute-start.3 = (f32[40,512]{1,0:T(8,128)S(1)}, f32[40,512]{1,0:T(8,128)S(1)}, u32[]{:S(2)}, u32[]{:S(2)}) collective-permute-start(f32[40,512]{1,0:T(8,128)S(1)} %add.147), channel_id=1, source_target_pairs={{0,256},{32,288},{64,320},{96,352},{128,384},{160,416},{192,448},{... | collective-permute-start | bytes 245768 | tf_op jit(solution)/shard_map/ppermute | solution.py:34
  323.0 1.8 collective-permute-done.3
  324.8 5.7 %collective-permute-start.4 = (f32[32,512]{1,0:T(8,128)S(1)}, f32[32,512]{1,0:T(8,128)S(1)}, u32[]{:S(2)}, u32[]{:S(2)}) collective-permute-start(f32[32,512]{1,0:T(8,128)S(1)} %get-tuple-element.17), channel_id=1, source_target_pairs={{0,16},{1,17},{2,18},{3,19},{4,20},{5,21},{6,22},{7,23},{8,24},{9,... | collective-permute-start | bytes 196616 | tf_op jit(solution)/shard_map/ppermute | solution.py:38
  330.5 1.9 collective-permute-done.4
  332.5 4.1 %collective-permute-start.5 = (f32[64,512]{1,0:T(8,128)S(1)}, f32[64,512]{1,0:T(8,128)S(1)}, u32[]{:S(2)}, u32[]{:S(2)}) collective-permute-start(f32[64,512]{1,0:T(8,128)S(1)} %constant_dynamic-update-slice_fusion.7), channel_id=1, source_target_pairs={{0,8},{1,9},{2,10},{3,11},{4,12},{5,13},{6,14},{7,15},{8,0},{9,1},... | collective-permute-start | bytes 393224 | tf_op jit(solution)/shard_map/ppermute | solution.py:38
  336.7 2.3 collective-permute-done.5
  339.0 1.9 collective-permute-start.6
  341.1 6.6 %collective-permute-done.6 = f32[128,512]{1,0:T(8,128)S(1)} collective-permute-done((f32[128,512]{1,0:T(8,128)S(1)}, f32[128,512]{1,0:T(8,128)S(1)}, u32[]{:S(2)}, u32[]{:S(2)}) %collective-permute-start.6) | collective-permute-done | bytes 262176 | tf_op jit(solution)/shard_map/ppermute | solution.py:38
  347.6 4.2 %collective-permute-start.7 = (f32[256,512]{1,0:T(8,128)S(1)}, f32[256,512]{1,0:T(8,128)S(1)}, u32[]{:S(2)}, u32[]{:S(2)}) collective-permute-start(f32[256,512]{1,0:T(8,128)S(1)} %constant_dynamic-update-slice_fusion.3), channel_id=1, source_target_pairs={{0,2},{1,3},{2,0},{3,1},{4,6},{5,7},{6,4},{7,5},{8,10},{9,11},{10,... | collective-permute-start | bytes 1572872 | tf_op jit(solution)/shard_map/ppermute | solution.py:38
  352.1 9.1 %collective-permute-done.7 = f32[256,512]{1,0:T(8,128)S(1)} collective-permute-done((f32[256,512]{1,0:T(8,128)S(1)}, f32[256,512]{1,0:T(8,128)S(1)}, u32[]{:S(2)}, u32[]{:S(2)}) %collective-permute-start.7) | collective-permute-done | bytes 524320 | tf_op jit(solution)/shard_map/ppermute | solution.py:38
  361.3 12.4 %collective-permute-start.8 = (f32[512,512]{1,0:T(8,128)S(1)}, f32[512,512]{1,0:T(8,128)S(1)}, u32[]{:S(2)}, u32[]{:S(2)}) collective-permute-start(f32[512,512]{1,0:T(8,128)S(1)} %constant_dynamic-update-slice_fusion.1), channel_id=1, source_target_pairs={{0,1},{1,0},{2,3},{3,2},{4,5},{5,4},{6,7},{7,6},{8,9},{9,8},{10,11... | collective-permute-start | bytes 3145736 | tf_op jit(solution)/shard_map/ppermute | solution.py:38
  374.5 1.4 collective-permute-done.8
  376.0 1.5 fusion.31
  (64 shorter events, 10.0 us)
Async XLA Ops:
  7.2 1.5 copy-start
  7.2 71.1 %copy-start.4 = (s32[4,8]{1,0:T(4,128)S(1)}, s32[4,8]{1,0:T(4,128)}, u32[]{:S(2)}) copy-start(s32[4,8]{1,0:T(4,128)} %param.14) | copy-start | bytes 388
  7.2 71.1 %all-gather.4.cloned.1.call-start = ((), (), s32[]{:S(2)}) async-start(), calls=%async_computation.1 | async-start | bytes 4325376 | tf_op jit(solution)/shard_map/all_gather | solution.py:70
  7.9 148.1 %all-gather.6.cloned.1.call-start = ((), (), s32[]{:S(2)}) async-start(), calls=%async_computation.2 | async-start | bytes 2228224 | tf_op jit(solution)/shard_map/all_gather | solution.py:86
  78.3 5.5 %copy-start.7 = (bf16[4,8,128,128]{3,2,1,0:T(8,128)(2,1)S(1)}, bf16[4,8,128,128]{3,2,1,0:T(8,128)(2,1)}, u32[]{:S(2)}) copy-start(bf16[4,8,128,128]{3,2,1,0:T(8,128)(2,1)} %param.16) | copy-start | bytes 3145732
  83.8 2.6 copy-start.3
  86.5 0.8 copy-start.1
  86.5 1.7 copy-start.8
  87.3 72.1 %copy-start.6 = (s32[32]{0:T(128)S(1)}, s32[32]{0:T(128)}, u32[]{:S(2)}) copy-start(s32[32]{0:T(128)} %constant.185) | copy-start | bytes 388
  87.3 72.2 %copy-start.5 = (s32[512]{0:T(512)S(1)}, s32[512]{0:T(512)}, u32[]{:S(2)}) copy-start(s32[512]{0:T(512)} %param.17) | copy-start | bytes 6148
  88.0 141.9 %all-gather.8.cloned.1.call-start = ((), (), s32[]{:S(2)}) async-start(), calls=%async_computation.3 | async-start | bytes 2228224 | tf_op jit(solution)/shard_map/all_gather | solution.py:104
  232.5 1.0 copy-start.2
  288.7 5.2 %collective-permute-start = (f32[40,512]{1,0:T(8,128)S(1)}, f32[40,512]{1,0:T(8,128)S(1)}, u32[]{:S(2)}, u32[]{:S(2)}) collective-permute-start(f32[40,512]{1,0:T(8,128)S(1)} %reduce_sum.73), channel_id=1, source_target_pairs={{0,32},{32,0},{64,96},{96,64},{128,160},{160,128},{192,224},{224,1... | collective-permute-start | bytes 245768 | tf_op jit(solution)/shard_map/ppermute | solution.py:34
  293.9 6.1 %collective-permute-start.1 = (f32[40,512]{1,0:T(8,128)S(1)}, f32[40,512]{1,0:T(8,128)S(1)}, u32[]{:S(2)}, u32[]{:S(2)}) collective-permute-start(f32[40,512]{1,0:T(8,128)S(1)} %add.145), channel_id=1, source_target_pairs={{0,64},{32,96},{64,0},{96,32},{128,192},{160,224},{192,128},{224,1... | collective-permute-start | bytes 245768 | tf_op jit(solution)/shard_map/ppermute | solution.py:34
  300.0 9.1 %collective-permute-start.2 = (f32[40,512]{1,0:T(8,128)S(1)}, f32[40,512]{1,0:T(8,128)S(1)}, u32[]{:S(2)}, u32[]{:S(2)}) collective-permute-start(f32[40,512]{1,0:T(8,128)S(1)} %add.146), channel_id=1, source_target_pairs={{0,128},{32,160},{64,192},{96,224},{128,0},{160,32},{192,64},{224,... | collective-permute-start | bytes 245768 | tf_op jit(solution)/shard_map/ppermute | solution.py:34
  309.1 15.6 %collective-permute-start.3 = (f32[40,512]{1,0:T(8,128)S(1)}, f32[40,512]{1,0:T(8,128)S(1)}, u32[]{:S(2)}, u32[]{:S(2)}) collective-permute-start(f32[40,512]{1,0:T(8,128)S(1)} %add.147), channel_id=1, source_target_pairs={{0,256},{32,288},{64,320},{96,352},{128,384},{160,416},{192,448},{... | collective-permute-start | bytes 245768 | tf_op jit(solution)/shard_map/ppermute | solution.py:34
  324.8 7.7 %collective-permute-start.4 = (f32[32,512]{1,0:T(8,128)S(1)}, f32[32,512]{1,0:T(8,128)S(1)}, u32[]{:S(2)}, u32[]{:S(2)}) collective-permute-start(f32[32,512]{1,0:T(8,128)S(1)} %get-tuple-element.17), channel_id=1, source_target_pairs={{0,16},{1,17},{2,18},{3,19},{4,20},{5,21},{6,22},{7,23},{8,24},{9,... | collective-permute-start | bytes 196616 | tf_op jit(solution)/shard_map/ppermute | solution.py:38
  332.5 6.5 %collective-permute-start.5 = (f32[64,512]{1,0:T(8,128)S(1)}, f32[64,512]{1,0:T(8,128)S(1)}, u32[]{:S(2)}, u32[]{:S(2)}) collective-permute-start(f32[64,512]{1,0:T(8,128)S(1)} %constant_dynamic-update-slice_fusion.7), channel_id=1, source_target_pairs={{0,8},{1,9},{2,10},{3,11},{4,12},{5,13},{6,14},{7,15},{8,0},{9,1},... | collective-permute-start | bytes 393224 | tf_op jit(solution)/shard_map/ppermute | solution.py:38
  339.0 8.6 %collective-permute-start.6 = (f32[128,512]{1,0:T(8,128)S(1)}, f32[128,512]{1,0:T(8,128)S(1)}, u32[]{:S(2)}, u32[]{:S(2)}) collective-permute-start(f32[128,512]{1,0:T(8,128)S(1)} %constant_dynamic-update-slice_fusion.5), channel_id=1, source_target_pairs={{0,4},{1,5},{2,6},{3,7},{4,0},{5,1},{6,2},{7,3},{8,12},{9,13},{10,... | collective-permute-start | bytes 786440 | tf_op jit(solution)/shard_map/ppermute | solution.py:38
  347.6 13.6 %collective-permute-start.7 = (f32[256,512]{1,0:T(8,128)S(1)}, f32[256,512]{1,0:T(8,128)S(1)}, u32[]{:S(2)}, u32[]{:S(2)}) collective-permute-start(f32[256,512]{1,0:T(8,128)S(1)} %constant_dynamic-update-slice_fusion.3), channel_id=1, source_target_pairs={{0,2},{1,3},{2,0},{3,1},{4,6},{5,7},{6,4},{7,5},{8,10},{9,11},{10,... | collective-permute-start | bytes 1572872 | tf_op jit(solution)/shard_map/ppermute | solution.py:38
  361.3 14.7 %collective-permute-start.8 = (f32[512,512]{1,0:T(8,128)S(1)}, f32[512,512]{1,0:T(8,128)S(1)}, u32[]{:S(2)}, u32[]{:S(2)}) collective-permute-start(f32[512,512]{1,0:T(8,128)S(1)} %constant_dynamic-update-slice_fusion.1), channel_id=1, source_target_pairs={{0,1},{1,0},{2,3},{3,2},{4,5},{5,4},{6,7},{7,6},{8,9},{9,8},{10,11... | collective-permute-start | bytes 3145736 | tf_op jit(solution)/shard_map/ppermute | solution.py:38
Sparse Core Ops, SparseCore 0:
  11.2 67.0 all-gather.3
  88.1 67.8 all-gather.5
  159.5 70.3 all-gather.7

commit v5 on v4

--- a/solution.py
+++ b/solution.py
@@ -44,6 +44,76 @@
     return buf, extra
 
 
+def route_plan(table):
+    size = lax.axis_size("row")
+    n = size.bit_length() - 1
+    masks = [1 << (n - 1 - i) for i in range(n)]
+    h = n // 2
+    me = lax.axis_index("row")
+    high = sum(masks[:h])
+    wide = 1 << (n - h)
+    j = jnp.arange(wide, dtype=jnp.int32)
+    dest = (me & high) + sum(((j >> i) & 1) * masks[h + i] for i in range(n - h))
+    src = table[dest]
+    slots = sum(((src // masks[i]) % 2) << i for i in range(h))
+    conds = []
+    for u in range(n - h):
+        m = masks[h + u]
+        k = jnp.arange(wide >> (u + 1), dtype=jnp.int32)
+        done_bits = high + sum(masks[h:h + u + 1])
+        kept = (me & done_bits) + sum(((k >> i) & 1) * masks[h + u + 1 + i] for i in range(n - h - u - 1))
+        conds.append((table[kept] // m) % 2 == (me // m) % 2)
+    return masks, h, slots, conds
+
+
+def route_forward(x, plan):
+    masks, h, slots, conds = plan
+    size = lax.axis_size("row")
+    me = lax.axis_index("row")
+    held = x[None]
+    for t in range(h):
+        m = masks[t]
+        got = lax.ppermute(held, "row", xor_pairs(size, m))
+        first = (me // m) % 2 == 0
+        held = jnp.where(first, jnp.concatenate([held, got], 0), jnp.concatenate([got, held], 0))
+    d = jnp.take(held, slots, axis=0)
+    for u, c in enumerate(conds):
+        m = masks[h + u]
+        first = (me // m) % 2 == 0
+        pair = d.reshape((-1, 2) + d.shape[1:])
+        keep = jnp.where(first, pair[:, 0], pair[:, 1])
+        send = jnp.where(first, pair[:, 1], pair[:, 0])
+        got = lax.ppermute(send, "row", xor_pairs(size, m))
+        d = jnp.where(c.reshape((-1,) + (1,) * (d.ndim - 1)), keep, got)
+    return d[0]
+
+
+def route_backward(g, plan):
+    masks, h, slots, conds = plan
+    size = lax.axis_size("row")
+    me = lax.axis_index("row")
+    dbar = g[None]
+    for u in reversed(range(len(conds))):
+        m = masks[h + u]
+        first = (me // m) % 2 == 0
+        c = conds[u].reshape((-1,) + (1,) * (dbar.ndim - 1))
+        kbar = jnp.where(c, dbar, 0.0)
+        rbar = jnp.where(c, 0.0, dbar)
+        sbar = lax.ppermute(rbar.astype(jnp.bfloat16), "row", xor_pairs(size, m)).astype(jnp.float32)
+        pair = jnp.where(first, jnp.stack([kbar, sbar], 1), jnp.stack([sbar, kbar], 1))
+        dbar = pair.reshape((-1,) + dbar.shape[1:])
+    pick = (slots[:, None] == jnp.arange(1 << h, dtype=jnp.int32)[None, :]).astype(jnp.float32)
+    hbar = jnp.sum(pick.reshape(pick.shape + (1,) * (dbar.ndim - 1)) * dbar[:, None], axis=0)
+    for t in reversed(range(h)):
+        m = masks[t]
+        first = (me // m) % 2 == 0
+        half = hbar.shape[0] // 2
+        mine = jnp.where(first, hbar[:half], hbar[half:])
+        other = jnp.where(first, hbar[half:], hbar[:half])
+        hbar = mine + lax.ppermute(other.astype(jnp.bfloat16), "row", xor_pairs(size, m)).astype(jnp.float32)
+    return hbar[0]
+
+
 def embed(pre):
     return pre * lax.rsqrt(jnp.sum(pre * pre, axis=-1, keepdims=True) + 1e-06)
 
@@ -83,10 +153,8 @@
     )
     emb32, pull = jax.vjp(embed, pre)
     zeta_bf = emb32.astype(jnp.bfloat16)
-    candidates = lax.all_gather(zeta_bf[:NOISE], "row", axis=0, tiled=True)
-    my_row = lax.axis_index("row")
-    my_noise = noise_block_rows[my_row]
-    noise_emb = lax.dynamic_slice_in_dim(candidates, my_noise * NOISE, NOISE, 0).astype(jnp.float32)
+    plan = route_plan(noise_block_rows)
+    noise_emb = route_forward(zeta_bf[:NOISE], plan).astype(jnp.float32)
     zeta = zeta_bf.astype(jnp.float32)
     pairing = (pos_index[:, None] == jnp.arange(rows, dtype=jnp.int32)[None, :]).astype(jnp.float32)
     partner = jnp.dot(pairing.astype(jnp.bfloat16), zeta_bf, preferred_element_type=jnp.float32)
@@ -100,12 +168,7 @@
     )
     partner_grad = jnp.dot(pairing.T, scale_factor * grad_pos[:, None] * zeta, precision=highest)
     dnoise = scale_factor * jnp.dot(grad_neg.T, zeta, precision=highest)
-    groups = lax.axis_size("row")
-    collected = lax.all_gather(dnoise.astype(jnp.bfloat16), "row", axis=0, tiled=True)
-    owned = (noise_block_rows == my_row).astype(jnp.float32)
-    returned = jnp.sum(
-        owned[:, None, None] * collected.astype(jnp.float32).reshape(groups, NOISE, width), axis=0
-    )
+    returned = route_backward(dnoise.astype(jnp.bfloat16).astype(jnp.float32), plan)
     dzeta = anchor + partner_grad
     dzeta = dzeta.at[:NOISE].add(returned)
     gpre = pull(dzeta)[0].astype(jnp.bfloat16)

time: 385 us -> 372 us (0.966)
  waiting for transfers between devices: 232 us -> 192 us
  starting transfers between devices: 54.6 us -> 83.3 us
  blocking collectives: 50.4 us -> 39.4 us
  local copies, waits for them, and re-layouts: 7.16 us -> 12.6 us
    all_gather x2 -> x0, waiting for transfers between devices: 132 us -> none  [the longest x1 66.6 us: body(): candidates = lax.all_gather(zeta_bf[:NOISE], 'row', axis=0, tiled=True)]
    ppermute x0 -> x8, waiting for transfers between devices: none -> 77.6 us  [the longest x2 31.3 us: route_backward(): lax.ppermute(other.astype(jnp.bfloat16), 'row', xor_pairs(size, m))]
    ppermute x0 -> x8, starting transfers between devices: none -> 46.5 us  [the longest x2 25.5 us: route_forward(): got = lax.ppermute(held, 'row', xor_pairs(size, m))]
    ppermute x4, waiting for transfers between devices: 10 us -> 26.4 us  [tree_allreduce(): joined = joined + lax.ppermute(joined, axis, xor_pairs(size, mask))]
    all_to_all x1, blocking collectives: 50.4 us -> 39.4 us  [tree_allreduce(): joined = lax.all_to_all(chunks, 'col', 0, 0, tiled=False).sum(axis=0)]
    ppermute x5, starting transfers between devices: 28.4 us -> 18.6 us  [tree_allreduce(): got = lax.ppermute(buf, 'col', xor_pairs(ways, mask))]
    ppermute x4, starting transfers between devices: 25.9 us -> 18.2 us  [tree_allreduce(): joined = joined + lax.ppermute(joined, axis, xor_pairs(size, mask))]
  transfers between devices with their start and end apart: 12 -> 18, of which waited for: 12 -> 18; matrix products, arithmetic and copies ran while one was open for 2% -> 4% of each run, Pallas kernels for 0% -> 0%
where the time goes in v5:
time: 372 us; the launch traced here: 371 us
  waiting for transfers between devices  192 us (52%)
  starting transfers between devices  83.3 us (22%)
  blocking collectives  39.4 us (11%)
  between operations  18.1 us (5%)
  matrix products  17 us (5%)
  local copies, waits for them, and re-layouts  12.6 us (3%)
  other arithmetic  8.18 us (2%)
    all_gather x1, waiting for transfers between devices, body(): piece = lax.all_gather(source_feats, 'col', axis=0, tiled=True)  65.3 us
    all_to_all x1, blocking collectives, tree_allreduce(): joined = lax.all_to_all(chunks, 'col', 0, 0, tiled=False).sum(axis=0)  39.4 us
    ppermute x2, waiting for transfers between devices, route_backward(): lax.ppermute(other.astype(jnp.bfloat16), 'row', xor_pairs(size, m))  31.3 us
    ppermute x4, waiting for transfers between devices, tree_allreduce(): joined = joined + lax.ppermute(joined, axis, xor_pairs(size, mask))  26.4 us
    ppermute x2, starting transfers between devices, route_forward(): got = lax.ppermute(held, 'row', xor_pairs(size, m))  25.5 us
    ppermute x5, waiting for transfers between devices, tree_allreduce(): got = lax.ppermute(buf, 'col', xor_pairs(ways, mask))  22.4 us
    ppermute x2, waiting for transfers between devices, route_forward(): got = lax.ppermute(held, 'row', xor_pairs(size, m))  20.5 us
    ppermute x5, starting transfers between devices, tree_allreduce(): got = lax.ppermute(buf, 'col', xor_pairs(ways, mask))  18.6 us
  transfers between devices with their start and end apart: 18, of which 18 were waited for; matrix products, arithmetic and copies ran while one was open for 4% of the time, Pallas kernels for 0%

profile of v5, /device:TPU:1, one launch (start us, length us, event | category | flops | bytes accessed | tf_op | source)
XLA Modules:
  0.0 371.1 jit_solution(2980097555326524101)
XLA Ops:
  13.0 65.3 %all-gather.2.cloned.1.call-done = bf16[4096,512]{1,0:T(8,128)(2,1)} async-done(((bf16[128,512]{1,0:T(8,128)(2,1)}), bf16[4096,512]{1,0:T(8,128)(2,1)}) %all-gather.2.cloned.1.call-update) | async-done | bytes 4194320 | tf_op jit(solution)/shard_map/all_gather | solution.py:140
  78.3 5.5 %fusion.5 = bf16[4,8,128,512]{3,1,2,0:T(8,128)(2,1)S(1)} fusion(bf16[32,128,512]{2,1,0:T(8,128)(2,1)} %bitcast.94, s32[4,8]{1,0:T(4,128)S(1)} %copy-done.6), kind=kOutput, calls=%fused_computation.10 | convolution fusion | flops 136315904 | bytes 8388736 | tf_op jit(solution)/shard_map/bkc,cjd->bkjd/dot_general | solution.py:146
  83.9 2.6 fusion.13
  87.4 12.5 %collective-permute-start = (bf16[1,128,512]{1,2,0:T(8,128)(2,1)S(1)}, bf16[1,128,512]{1,2,0:T(8,128)(2,1)S(1)}, u32[]{:S(2)}, u32[]{:S(2)}) collective-permute-start(bf16[1,128,512]{1,2,0:T(8,128)(2,1)S(1)} %slice_bitcast_fusion), channel_id=1, source_target_pairs={{0,256},{32,288},{64,320},{96,352},{128,384},{160,416},{192,448},{... | collective-permute-start | bytes 393224 | tf_op jit(solution)/shard_map/ppermute | solution.py:76
  100.0 3.6 collective-permute-done
  103.7 13.0 %collective-permute-start.1 = (bf16[2,128,512]{1,2,0:T(8,128)(2,1)S(1)}, bf16[2,128,512]{1,2,0:T(8,128)(2,1)S(1)}, u32[]{:S(2)}, u32[]{:S(2)}) collective-permute-start(bf16[2,128,512]{1,2,0:T(8,128)(2,1)S(1)} %maximum_select_fusion.4), channel_id=1, source_target_pairs={{0,128},{32,160},{64,192},{96,224},{128,0},{160,32},{192,64},{224,... | collective-permute-start | bytes 786440 | tf_op jit(solution)/shard_map/ppermute | solution.py:76
  120.0 16.9 %collective-permute-done.1 = bf16[2,128,512]{1,2,0:T(8,128)(2,1)S(1)} collective-permute-done((bf16[2,128,512]{1,2,0:T(8,128)(2,1)S(1)}, bf16[2,128,512]{1,2,0:T(8,128)(2,1)S(1)}, u32[]{:S(2)}, u32[]{:S(2)}) %collective-permute-start.1) | collective-permute-done | bytes 262176 | tf_op jit(solution)/shard_map/ppermute | solution.py:76
  141.5 6.6 %collective-permute-done.2 = bf16[2,128,512]{2,1,0:T(8,128)(2,1)S(1)} collective-permute-done((bf16[2,128,512]{2,1,0:T(8,128)(2,1)S(1)}, bf16[2,128,512]{2,1,0:T(8,128)(2,1)S(1)}, u32[]{:S(2)}, u32[]{:S(2)}) %collective-permute-start.2) | collective-permute-done | bytes 262176 | tf_op jit(solution)/shard_map/ppermute | solution.py:86
  151.4 2.6 collective-permute-done.3
  157.7 3.8 %collective-permute-done.4 = bf16[1,128,512]{2,1,0:T(8,128)(2,1)S(1)} collective-permute-done((bf16[1,128,512]{2,1,0:T(8,128)(2,1)S(1)}, bf16[1,128,512]{2,1,0:T(8,128)(2,1)S(1)}, u32[]{:S(2)}, u32[]{:S(2)}) %collective-permute-start.4) | collective-permute-done | bytes 131104 | tf_op jit(solution)/shard_map/ppermute | solution.py:102
  161.6 2.2 collective-permute-start.5
  164.0 12.8 %collective-permute-done.5 = bf16[2,128,512]{2,1,0:T(8,128)(2,1)S(1)} collective-permute-done((bf16[2,128,512]{2,1,0:T(8,128)(2,1)S(1)}, bf16[2,128,512]{2,1,0:T(8,128)(2,1)S(1)}, u32[]{:S(2)}, u32[]{:S(2)}) %collective-permute-start.5) | collective-permute-done | bytes 262176 | tf_op jit(solution)/shard_map/ppermute | solution.py:102
  179.8 6.3 %collective-permute-start.6 = (bf16[2,128,512]{1,2,0:T(8,128)(2,1)S(1)}, bf16[2,128,512]{1,2,0:T(8,128)(2,1)S(1)}, u32[]{:S(2)}, u32[]{:S(2)}) collective-permute-start(bf16[2,128,512]{1,2,0:T(8,128)(2,1)S(1)} %select_convert_fusion), channel_id=1, source_target_pairs={{0,128},{32,160},{64,192},{96,224},{128,0},{160,32},{192,64},{224,... | collective-permute-start | bytes 786440 | tf_op jit(solution)/shard_map/ppermute | solution.py:113
  188.0 20.7 %collective-permute-done.6 = bf16[2,128,512]{1,2,0:T(8,128)(2,1)S(1)} collective-permute-done((bf16[2,128,512]{1,2,0:T(8,128)(2,1)S(1)}, bf16[2,128,512]{1,2,0:T(8,128)(2,1)S(1)}, u32[]{:S(2)}, u32[]{:S(2)}) %collective-permute-start.6) | collective-permute-done | bytes 262176 | tf_op jit(solution)/shard_map/ppermute | solution.py:113
  209.5 6.6 %collective-permute-start.7 = (bf16[1,128,512]{1,2,0:T(8,128)(2,1)}, bf16[1,128,512]{1,2,0:T(8,128)(2,1)}, u32[]{:S(2)}, u32[]{:S(2)}) collective-permute-start(bf16[1,128,512]{1,2,0:T(8,128)(2,1)} %select_convert_fusion.1), channel_id=1, source_target_pairs={{0,256},{32,288},{64,320},{96,352},{128,384},{160,416},{192,448},{... | collective-permute-start | bytes 393224 | tf_op jit(solution)/shard_map/ppermute | solution.py:113
  218.1 10.6 %collective-permute-done.7 = bf16[1,128,512]{1,2,0:T(8,128)(2,1)} collective-permute-done((bf16[1,128,512]{1,2,0:T(8,128)(2,1)}, bf16[1,128,512]{1,2,0:T(8,128)(2,1)}, u32[]{:S(2)}, u32[]{:S(2)}) %collective-permute-start.7) | collective-permute-done | bytes 131104 | tf_op jit(solution)/shard_map/ppermute | solution.py:113
  233.0 2.4 gather_fusion.3
  235.7 39.4 %all_to_all.5 = f32[32,40,512]{2,1,0:T(8,128)S(1)} all-to-all(f32[32,40,512]{2,1,0:T(8,128)S(1)} %concatenate.45), channel_id=1, replica_groups=mesh['row'=16,'col'=32] {'col'}, dimensions={0} | all-to-all | bytes 5242880 | tf_op jit(solution)/shard_map/all_to_all | solution.py:29
  277.3 3.3 collective-permute-done.8
  282.5 5.0 %collective-permute-done.9 = f32[40,512]{1,0:T(8,128)S(1)} collective-permute-done((f32[40,512]{1,0:T(8,128)S(1)}, f32[40,512]{1,0:T(8,128)S(1)}, u32[]{:S(2)}, u32[]{:S(2)}) %collective-permute-start.9) | collective-permute-done | bytes 81952 | tf_op jit(solution)/shard_map/ppermute | solution.py:34
  287.5 5.6 %collective-permute-start.10 = (f32[40,512]{1,0:T(8,128)S(1)}, f32[40,512]{1,0:T(8,128)S(1)}, u32[]{:S(2)}, u32[]{:S(2)}) collective-permute-start(f32[40,512]{1,0:T(8,128)S(1)} %add.379), channel_id=1, source_target_pairs={{0,128},{32,160},{64,192},{96,224},{128,0},{160,32},{192,64},{224,... | collective-permute-start | bytes 245768 | tf_op jit(solution)/shard_map/ppermute | solution.py:34
  293.2 9.1 %collective-permute-done.10 = f32[40,512]{1,0:T(8,128)S(1)} collective-permute-done((f32[40,512]{1,0:T(8,128)S(1)}, f32[40,512]{1,0:T(8,128)S(1)}, u32[]{:S(2)}, u32[]{:S(2)}) %collective-permute-start.10) | collective-permute-done | bytes 81952 | tf_op jit(solution)/shard_map/ppermute | solution.py:34
  302.3 8.7 %collective-permute-start.11 = (f32[40,512]{1,0:T(8,128)S(1)}, f32[40,512]{1,0:T(8,128)S(1)}, u32[]{:S(2)}, u32[]{:S(2)}) collective-permute-start(f32[40,512]{1,0:T(8,128)S(1)} %add.380), channel_id=1, source_target_pairs={{0,256},{32,288},{64,320},{96,352},{128,384},{160,416},{192,448},{... | collective-permute-start | bytes 245768 | tf_op jit(solution)/shard_map/ppermute | solution.py:34
  311.0 9.0 %collective-permute-done.11 = f32[40,512]{1,0:T(8,128)S(1)} collective-permute-done((f32[40,512]{1,0:T(8,128)S(1)}, f32[40,512]{1,0:T(8,128)S(1)}, u32[]{:S(2)}, u32[]{:S(2)}) %collective-permute-start.11) | collective-permute-done | bytes 81952 | tf_op jit(solution)/shard_map/ppermute | solution.py:34
  322.0 4.6 %collective-permute-done.12 = f32[32,512]{1,0:T(8,128)S(1)} collective-permute-done((f32[32,512]{1,0:T(8,128)S(1)}, f32[32,512]{1,0:T(8,128)S(1)}, u32[]{:S(2)}, u32[]{:S(2)}) %collective-permute-start.12) | collective-permute-done | bytes 65568 | tf_op jit(solution)/shard_map/ppermute | solution.py:38
  326.6 2.1 collective-permute-start.13
  328.8 3.5 collective-permute-done.13
  332.4 3.0 collective-permute-start.14
  335.5 5.5 %collective-permute-done.14 = f32[128,512]{1,0:T(8,128)S(1)} collective-permute-done((f32[128,512]{1,0:T(8,128)S(1)}, f32[128,512]{1,0:T(8,128)S(1)}, u32[]{:S(2)}, u32[]{:S(2)}) %collective-permute-start.14) | collective-permute-done | bytes 262176 | tf_op jit(solution)/shard_map/ppermute | solution.py:38
  341.0 4.5 %collective-permute-start.15 = (f32[256,512]{1,0:T(8,128)S(1)}, f32[256,512]{1,0:T(8,128)S(1)}, u32[]{:S(2)}, u32[]{:S(2)}) collective-permute-start(f32[256,512]{1,0:T(8,128)S(1)} %constant_dynamic-update-slice_fusion.3), channel_id=1, source_target_pairs={{0,2},{1,3},{2,0},{3,1},{4,6},{5,7},{6,4},{7,5},{8,10},{9,11},{10,... | collective-permute-start | bytes 1572872 | tf_op jit(solution)/shard_map/ppermute | solution.py:38
  345.8 7.4 %collective-permute-done.15 = f32[256,512]{1,0:T(8,128)S(1)} collective-permute-done((f32[256,512]{1,0:T(8,128)S(1)}, f32[256,512]{1,0:T(8,128)S(1)}, u32[]{:S(2)}, u32[]{:S(2)}) %collective-permute-start.15) | collective-permute-done | bytes 524320 | tf_op jit(solution)/shard_map/ppermute | solution.py:38
  353.2 7.2 %collective-permute-start.16 = (f32[512,512]{1,0:T(8,128)S(1)}, f32[512,512]{1,0:T(8,128)S(1)}, u32[]{:S(2)}, u32[]{:S(2)}) collective-permute-start(f32[512,512]{1,0:T(8,128)S(1)} %constant_dynamic-update-slice_fusion.1), channel_id=1, source_target_pairs={{0,1},{1,0},{2,3},{3,2},{4,5},{5,4},{6,7},{7,6},{8,9},{9,8},{10,11... | collective-permute-start | bytes 3145736 | tf_op jit(solution)/shard_map/ppermute | solution.py:38
  (117 shorter events, 40.9 us)
Async XLA Ops:
  7.2 4.3 %copy-start = (bf16[512,512]{1,0:T(8,128)(2,1)S(1)}, bf16[512,512]{1,0:T(8,128)(2,1)}, u32[]{:S(2)}) copy-start(bf16[512,512]{1,0:T(8,128)(2,1)} %param.12) | copy-start | bytes 1572868
  7.2 71.1 %copy-start.6 = (s32[4,8]{1,0:T(4,128)S(1)}, s32[4,8]{1,0:T(4,128)}, u32[]{:S(2)}) copy-start(s32[4,8]{1,0:T(4,128)} %param.14) | copy-start | bytes 388
  7.2 71.1 %all-gather.2.cloned.1.call-start = ((), (), s32[]{:S(2)}) async-start(), calls=%async_computation.1 | async-start | bytes 4325376 | tf_op jit(solution)/shard_map/all_gather | solution.py:140
  78.3 5.5 %copy-start.12 = (bf16[4,8,128,128]{3,2,1,0:T(8,128)(2,1)S(1)}, bf16[4,8,128,128]{3,2,1,0:T(8,128)(2,1)}, u32[]{:S(2)}) copy-start(bf16[4,8,128,128]{3,2,1,0:T(8,128)(2,1)} %param.16) | copy-start | bytes 3145732
  83.8 2.6 copy-start.5
  86.5 0.8 copy-start.2
  86.5 30.2 %copy-start.11 = (s32[32]{0:T(128)S(1)}, s32[32]{0:T(128)}, u32[]{:S(2)}) copy-start(s32[32]{0:T(128)} %constant.335) | copy-start | bytes 388
  86.5 30.8 %copy-start.1 = (s32[16]{0:T(128)S(1)}, s32[16]{0:T(128)}, u32[]{:S(2)}) copy-start(s32[16]{0:T(128)} %param.18) | copy-start | bytes 196
  87.4 16.2 %collective-permute-start = (bf16[1,128,512]{1,2,0:T(8,128)(2,1)S(1)}, bf16[1,128,512]{1,2,0:T(8,128)(2,1)S(1)}, u32[]{:S(2)}, u32[]{:S(2)}) collective-permute-start(bf16[1,128,512]{1,2,0:T(8,128)(2,1)S(1)} %slice_bitcast_fusion), channel_id=1, source_target_pairs={{0,256},{32,288},{64,320},{96,352},{128,384},{160,416},{192,448},{... | collective-permute-start | bytes 393224 | tf_op jit(solution)/shard_map/ppermute | solution.py:76
  100.0 48.2 %copy-start.8 = (pred[2]{0:T(512)(128)(4,1)}, pred[2]{0:T(512)(128)(4,1)S(1)}, u32[]{:S(2)}) copy-start(pred[2]{0:T(512)(128)(4,1)S(1)} %fusion.53) | copy-start | bytes 10
  103.7 36.3 %copy-start.10 = (s32[512]{0:T(512)S(1)}, s32[512]{0:T(512)}, u32[]{:S(2)}) copy-start(s32[512]{0:T(512)} %param.17) | copy-start | bytes 6148
  103.7 33.2 %collective-permute-start.1 = (bf16[2,128,512]{1,2,0:T(8,128)(2,1)S(1)}, bf16[2,128,512]{1,2,0:T(8,128)(2,1)S(1)}, u32[]{:S(2)}, u32[]{:S(2)}) collective-permute-start(bf16[2,128,512]{1,2,0:T(8,128)(2,1)S(1)} %maximum_select_fusion.4), channel_id=1, source_target_pairs={{0,128},{32,160},{64,192},{96,224},{128,0},{160,32},{192,64},{224,... | collective-permute-start | bytes 786440 | tf_op jit(solution)/shard_map/ppermute | solution.py:76
  138.0 10.1 %collective-permute-start.2 = (bf16[2,128,512]{2,1,0:T(8,128)(2,1)S(1)}, bf16[2,128,512]{2,1,0:T(8,128)(2,1)S(1)}, u32[]{:S(2)}, u32[]{:S(2)}) collective-permute-start(bf16[2,128,512]{2,1,0:T(8,128)(2,1)S(1)} %select_bitcast_fusion), channel_id=1, source_target_pairs={{0,64},{32,96},{64,0},{96,32},{128,192},{160,224},{192,128},{224,1... | collective-permute-start | bytes 786440 | tf_op jit(solution)/shard_map/ppermute | solution.py:86
  148.2 13.2 %copy-start.9 = (pred[2]{0:T(512)(128)(4,1)S(1)}, pred[2]{0:T(512)(128)(4,1)}, u32[]{:S(2)}) copy-start(pred[2]{0:T(512)(128)(4,1)} %copy-done.8) | copy-start | bytes 10
  148.3 5.7 %collective-permute-start.3 = (bf16[1,128,512]{2,1,0:T(8,128)(2,1)S(1)}, bf16[1,128,512]{2,1,0:T(8,128)(2,1)S(1)}, u32[]{:S(2)}, u32[]{:S(2)}) collective-permute-start(bf16[1,128,512]{2,1,0:T(8,128)(2,1)S(1)} %select_bitcast_fusion.3), channel_id=1, source_target_pairs={{0,32},{32,0},{64,96},{96,64},{128,160},{160,128},{192,224},{224,1... | collective-permute-start | bytes 393224 | tf_op jit(solution)/shard_map/ppermute | solution.py:86
  155.8 5.7 %collective-permute-start.4 = (bf16[1,128,512]{2,1,0:T(8,128)(2,1)S(1)}, bf16[1,128,512]{2,1,0:T(8,128)(2,1)S(1)}, u32[]{:S(2)}, u32[]{:S(2)}) collective-permute-start(bf16[1,128,512]{2,1,0:T(8,128)(2,1)S(1)} %get-tuple-element.20), channel_id=1, source_target_pairs={{0,32},{32,0},{64,96},{96,64},{128,160},{160,128},{192,224},{224,1... | collective-permute-start | bytes 393224 | tf_op jit(solution)/shard_map/ppermute | solution.py:102
  161.6 15.2 %collective-permute-start.5 = (bf16[2,128,512]{2,1,0:T(8,128)(2,1)S(1)}, bf16[2,128,512]{2,1,0:T(8,128)(2,1)S(1)}, u32[]{:S(2)}, u32[]{:S(2)}) collective-permute-start(bf16[2,128,512]{2,1,0:T(8,128)(2,1)S(1)} %fusion.25), channel_id=1, source_target_pairs={{0,64},{32,96},{64,0},{96,32},{128,192},{160,224},{192,128},{224,1... | collective-permute-start | bytes 786440 | tf_op jit(solution)/shard_map/ppermute | solution.py:102
  177.4 8.7 %copy-start.7 = (f32[512]{0:T(512)S(1)}, f32[512]{0:T(512)}, u32[]{:S(2)}) copy-start(f32[512]{0:T(512)} %get-tuple-element.24) | copy-start | bytes 6148
  179.7 36.4 %copy-start.4 = (f32[512,512]{0,1:T(8,128)S(1)}, f32[512,512]{0,1:T(8,128)}, u32[]{:S(2)}) copy-start(f32[512,512]{0,1:T(8,128)} %get-tuple-element.29) | copy-start | bytes 3145732
  179.8 28.9 %collective-permute-start.6 = (bf16[2,128,512]{1,2,0:T(8,128)(2,1)S(1)}, bf16[2,128,512]{1,2,0:T(8,128)(2,1)S(1)}, u32[]{:S(2)}, u32[]{:S(2)}) collective-permute-start(bf16[2,128,512]{1,2,0:T(8,128)(2,1)S(1)} %select_convert_fusion), channel_id=1, source_target_pairs={{0,128},{32,160},{64,192},{96,224},{128,0},{160,32},{192,64},{224,... | collective-permute-start | bytes 786440 | tf_op jit(solution)/shard_map/ppermute | solution.py:113
  209.5 19.2 %collective-permute-start.7 = (bf16[1,128,512]{1,2,0:T(8,128)(2,1)}, bf16[1,128,512]{1,2,0:T(8,128)(2,1)}, u32[]{:S(2)}, u32[]{:S(2)}) collective-permute-start(bf16[1,128,512]{1,2,0:T(8,128)(2,1)} %select_convert_fusion.1), channel_id=1, source_target_pairs={{0,256},{32,288},{64,320},{96,352},{128,384},{160,416},{192,448},{... | collective-permute-start | bytes 393224 | tf_op jit(solution)/shard_map/ppermute | solution.py:113
  230.0 1.0 copy-start.3
  275.4 5.2 %collective-permute-start.8 = (f32[40,512]{1,0:T(8,128)S(1)}, f32[40,512]{1,0:T(8,128)S(1)}, u32[]{:S(2)}, u32[]{:S(2)}) collective-permute-start(f32[40,512]{1,0:T(8,128)S(1)} %reduce_sum.73), channel_id=1, source_target_pairs={{0,32},{32,0},{64,96},{96,64},{128,160},{160,128},{192,224},{224,1... | collective-permute-start | bytes 245768 | tf_op jit(solution)/shard_map/ppermute | solution.py:34
  280.6 7.0 %collective-permute-start.9 = (f32[40,512]{1,0:T(8,128)S(1)}, f32[40,512]{1,0:T(8,128)S(1)}, u32[]{:S(2)}, u32[]{:S(2)}) collective-permute-start(f32[40,512]{1,0:T(8,128)S(1)} %add.378), channel_id=1, source_target_pairs={{0,64},{32,96},{64,0},{96,32},{128,192},{160,224},{192,128},{224,1... | collective-permute-start | bytes 245768 | tf_op jit(solution)/shard_map/ppermute | solution.py:34
  287.5 14.7 %collective-permute-start.10 = (f32[40,512]{1,0:T(8,128)S(1)}, f32[40,512]{1,0:T(8,128)S(1)}, u32[]{:S(2)}, u32[]{:S(2)}) collective-permute-start(f32[40,512]{1,0:T(8,128)S(1)} %add.379), channel_id=1, source_target_pairs={{0,128},{32,160},{64,192},{96,224},{128,0},{160,32},{192,64},{224,... | collective-permute-start | bytes 245768 | tf_op jit(solution)/shard_map/ppermute | solution.py:34
  302.3 17.8 %collective-permute-start.11 = (f32[40,512]{1,0:T(8,128)S(1)}, f32[40,512]{1,0:T(8,128)S(1)}, u32[]{:S(2)}, u32[]{:S(2)}) collective-permute-start(f32[40,512]{1,0:T(8,128)S(1)} %add.380), channel_id=1, source_target_pairs={{0,256},{32,288},{64,320},{96,352},{128,384},{160,416},{192,448},{... | collective-permute-start | bytes 245768 | tf_op jit(solution)/shard_map/ppermute | solution.py:34
  320.1 6.5 %collective-permute-start.12 = (f32[32,512]{1,0:T(8,128)S(1)}, f32[32,512]{1,0:T(8,128)S(1)}, u32[]{:S(2)}, u32[]{:S(2)}) collective-permute-start(f32[32,512]{1,0:T(8,128)S(1)} %get-tuple-element.21), channel_id=1, source_target_pairs={{0,16},{1,17},{2,18},{3,19},{4,20},{5,21},{6,22},{7,23},{8,24},{9,... | collective-permute-start | bytes 196616 | tf_op jit(solution)/shard_map/ppermute | solution.py:38
  326.6 5.7 %collective-permute-start.13 = (f32[64,512]{1,0:T(8,128)S(1)}, f32[64,512]{1,0:T(8,128)S(1)}, u32[]{:S(2)}, u32[]{:S(2)}) collective-permute-start(f32[64,512]{1,0:T(8,128)S(1)} %constant_dynamic-update-slice_fusion.7), channel_id=1, source_target_pairs={{0,8},{1,9},{2,10},{3,11},{4,12},{5,13},{6,14},{7,15},{8,0},{9,1},... | collective-permute-start | bytes 393224 | tf_op jit(solution)/shard_map/ppermute | solution.py:38
  332.4 8.6 %collective-permute-start.14 = (f32[128,512]{1,0:T(8,128)S(1)}, f32[128,512]{1,0:T(8,128)S(1)}, u32[]{:S(2)}, u32[]{:S(2)}) collective-permute-start(f32[128,512]{1,0:T(8,128)S(1)} %constant_dynamic-update-slice_fusion.5), channel_id=1, source_target_pairs={{0,4},{1,5},{2,6},{3,7},{4,0},{5,1},{6,2},{7,3},{8,12},{9,13},{10,... | collective-permute-start | bytes 786440 | tf_op jit(solution)/shard_map/ppermute | solution.py:38
  341.0 12.2 %collective-permute-start.15 = (f32[256,512]{1,0:T(8,128)S(1)}, f32[256,512]{1,0:T(8,128)S(1)}, u32[]{:S(2)}, u32[]{:S(2)}) collective-permute-start(f32[256,512]{1,0:T(8,128)S(1)} %constant_dynamic-update-slice_fusion.3), channel_id=1, source_target_pairs={{0,2},{1,3},{2,0},{3,1},{4,6},{5,7},{6,4},{7,5},{8,10},{9,11},{10,... | collective-permute-start | bytes 1572872 | tf_op jit(solution)/shard_map/ppermute | solution.py:38
  353.2 9.4 %collective-permute-start.16 = (f32[512,512]{1,0:T(8,128)S(1)}, f32[512,512]{1,0:T(8,128)S(1)}, u32[]{:S(2)}, u32[]{:S(2)}) collective-permute-start(f32[512,512]{1,0:T(8,128)S(1)} %constant_dynamic-update-slice_fusion.1), channel_id=1, source_target_pairs={{0,1},{1,0},{2,3},{3,2},{4,5},{5,4},{6,7},{7,6},{8,9},{9,8},{10,11... | collective-permute-start | bytes 3145736 | tf_op jit(solution)/shard_map/ppermute | solution.py:38
Sparse Core Ops, SparseCore 0:
  11.2 67.0 all-gather.1

commit v6 on v5

--- a/solution.py
+++ b/solution.py
@@ -47,7 +47,7 @@
 def route_plan(table):
     size = lax.axis_size("row")
     n = size.bit_length() - 1
-    masks = [1 << (n - 1 - i) for i in range(n)]
+    masks = [1 << (n - 1)] + [1 << i for i in range(n - 1)]
     h = n // 2
     me = lax.axis_index("row")
     high = sum(masks[:h])

time: 372 us -> 365 us (0.981)
  waiting for transfers between devices: 192 us -> 183 us
  blocking collectives: 39.4 us -> 43.6 us
    ppermute x2, waiting for transfers between devices: 31.3 us -> 14.9 us  [route_backward(): lax.ppermute(other.astype(jnp.bfloat16), 'row', xor_pairs(size, m))]
    ppermute x2, waiting for transfers between devices: 20.5 us -> 6.02 us  [route_forward(): got = lax.ppermute(held, 'row', xor_pairs(size, m))]
    ppermute x2, starting transfers between devices: 3.84 us -> 16 us  [route_forward(): got = lax.ppermute(send, 'row', xor_pairs(size, m))]
    ppermute x2, waiting for transfers between devices: 9.22 us -> 19.9 us  [route_forward(): got = lax.ppermute(send, 'row', xor_pairs(size, m))]
    ppermute x2, waiting for transfers between devices: 16.6 us -> 25.4 us  [route_backward(): lax.ppermute(rbar.astype(jnp.bfloat16), 'row', xor_pairs(size, m))]
    ppermute x2, starting transfers between devices: 25.5 us -> 17.7 us  [route_forward(): got = lax.ppermute(held, 'row', xor_pairs(size, m))]
    all_to_all x1, blocking collectives: 39.4 us -> 43.6 us  [tree_allreduce(): joined = lax.all_to_all(chunks, 'col', 0, 0, tiled=False).sum(axis=0)]
where the time goes in v6:
time: 365 us
  waiting for transfers between devices  183 us (50%)
  starting transfers between devices  81.6 us (22%)
  blocking collectives  43.6 us (12%)
  between operations  18.8 us (5%)
  matrix products  17 us (5%)
  local copies, waits for them, and re-layouts  12.6 us (3%)
  other arithmetic  8.24 us (2%)
    all_gather x1, waiting for transfers between devices, body(): piece = lax.all_gather(source_feats, 'col', axis=0, tiled=True)  65.3 us
    all_to_all x1, blocking collectives, tree_allreduce(): joined = lax.all_to_all(chunks, 'col', 0, 0, tiled=False).sum(axis=0)  43.6 us
    ppermute x4, waiting for transfers between devices, tree_allreduce(): joined = joined + lax.ppermute(joined, axis, xor_pairs(size, mask))  26.4 us
    ppermute x2, waiting for transfers between devices, route_backward(): lax.ppermute(rbar.astype(jnp.bfloat16), 'row', xor_pairs(size, m))  25.4 us
    ppermute x5, waiting for transfers between devices, tree_allreduce(): got = lax.ppermute(buf, 'col', xor_pairs(ways, mask))  24.2 us
    ppermute x2, waiting for transfers between devices, route_forward(): got = lax.ppermute(send, 'row', xor_pairs(size, m))  19.9 us
    ppermute x4, starting transfers between devices, tree_allreduce(): joined = joined + lax.ppermute(joined, axis, xor_pairs(size, mask))  17.8 us
    ppermute x2, starting transfers between devices, route_forward(): got = lax.ppermute(held, 'row', xor_pairs(size, m))  17.7 us
  transfers between devices with their start and end apart: 18, of which 18 were waited for; matrix products, arithmetic and copies ran while one was open for 4% of the time, Pallas kernels for 0%

profile of v6, /device:TPU:1, one launch (start us, length us, event | category | flops | bytes accessed | tf_op | source)
XLA Modules:
  0.0 364.5 jit_solution(8719064179355596097)
XLA Ops:
  13.0 65.3 %all-gather.2.cloned.1.call-done = bf16[4096,512]{1,0:T(8,128)(2,1)} async-done(((bf16[128,512]{1,0:T(8,128)(2,1)}), bf16[4096,512]{1,0:T(8,128)(2,1)}) %all-gather.2.cloned.1.call-update) | async-done | bytes 4194320 | tf_op jit(solution)/shard_map/all_gather | solution.py:140
  78.3 5.5 %fusion.5 = bf16[4,8,128,512]{3,1,2,0:T(8,128)(2,1)S(1)} fusion(bf16[32,128,512]{2,1,0:T(8,128)(2,1)} %bitcast.92, s32[4,8]{1,0:T(4,128)S(1)} %copy-done.6), kind=kOutput, calls=%fused_computation.10 | convolution fusion | flops 136315904 | bytes 8388736 | tf_op jit(solution)/shard_map/bkc,cjd->bkjd/dot_general | solution.py:146
  83.9 2.6 fusion.13
  87.4 12.5 %collective-permute-start = (bf16[1,128,512]{1,2,0:T(8,128)(2,1)S(1)}, bf16[1,128,512]{1,2,0:T(8,128)(2,1)S(1)}, u32[]{:S(2)}, u32[]{:S(2)}) collective-permute-start(bf16[1,128,512]{1,2,0:T(8,128)(2,1)S(1)} %slice_bitcast_fusion), channel_id=1, source_target_pairs={{0,256},{32,288},{64,320},{96,352},{128,384},{160,416},{192,448},{... | collective-permute-start | bytes 393224 | tf_op jit(solution)/shard_map/ppermute | solution.py:76
  100.0 3.6 collective-permute-done
  103.7 5.2 %collective-permute-start.1 = (bf16[2,128,512]{1,2,0:T(8,128)(2,1)S(1)}, bf16[2,128,512]{1,2,0:T(8,128)(2,1)S(1)}, u32[]{:S(2)}, u32[]{:S(2)}) collective-permute-start(bf16[2,128,512]{1,2,0:T(8,128)(2,1)S(1)} %maximum_select_fusion.4), channel_id=1, source_target_pairs={{0,32},{32,0},{64,96},{96,64},{128,160},{160,128},{192,224},{224,1... | collective-permute-start | bytes 786440 | tf_op jit(solution)/shard_map/ppermute | solution.py:76
  112.9 2.4 collective-permute-done.1
  116.4 8.2 %collective-permute-start.2 = (bf16[2,128,512]{2,1,0:T(8,128)(2,1)S(1)}, bf16[2,128,512]{2,1,0:T(8,128)(2,1)S(1)}, u32[]{:S(2)}, u32[]{:S(2)}) collective-permute-start(bf16[2,128,512]{2,1,0:T(8,128)(2,1)S(1)} %select_bitcast_fusion), channel_id=1, source_target_pairs={{0,64},{32,96},{64,0},{96,32},{128,192},{160,224},{192,128},{224,1... | collective-permute-start | bytes 786440 | tf_op jit(solution)/shard_map/ppermute | solution.py:86
  126.1 10.8 %collective-permute-done.2 = bf16[2,128,512]{2,1,0:T(8,128)(2,1)S(1)} collective-permute-done((bf16[2,128,512]{2,1,0:T(8,128)(2,1)S(1)}, bf16[2,128,512]{2,1,0:T(8,128)(2,1)S(1)}, u32[]{:S(2)}, u32[]{:S(2)}) %collective-permute-start.2) | collective-permute-done | bytes 262176 | tf_op jit(solution)/shard_map/ppermute | solution.py:86
  137.0 7.8 %collective-permute-start.3 = (bf16[1,128,512]{2,1,0:T(8,128)(2,1)S(1)}, bf16[1,128,512]{2,1,0:T(8,128)(2,1)S(1)}, u32[]{:S(2)}, u32[]{:S(2)}) collective-permute-start(bf16[1,128,512]{2,1,0:T(8,128)(2,1)S(1)} %select_bitcast_fusion.3), channel_id=1, source_target_pairs={{0,128},{32,160},{64,192},{96,224},{128,0},{160,32},{192,64},{224,... | collective-permute-start | bytes 393224 | tf_op jit(solution)/shard_map/ppermute | solution.py:86
  146.1 9.1 %collective-permute-done.3 = bf16[1,128,512]{2,1,0:T(8,128)(2,1)S(1)} collective-permute-done((bf16[1,128,512]{2,1,0:T(8,128)(2,1)S(1)}, bf16[1,128,512]{2,1,0:T(8,128)(2,1)S(1)}, u32[]{:S(2)}, u32[]{:S(2)}) %collective-permute-start.3) | collective-permute-done | bytes 131104 | tf_op jit(solution)/shard_map/ppermute | solution.py:86
  158.9 13.7 %collective-permute-done.4 = bf16[1,128,512]{2,1,0:T(8,128)(2,1)S(1)} collective-permute-done((bf16[1,128,512]{2,1,0:T(8,128)(2,1)S(1)}, bf16[1,128,512]{2,1,0:T(8,128)(2,1)S(1)}, u32[]{:S(2)}, u32[]{:S(2)}) %collective-permute-start.4) | collective-permute-done | bytes 131104 | tf_op jit(solution)/shard_map/ppermute | solution.py:102
  174.8 11.6 %collective-permute-done.5 = bf16[2,128,512]{2,1,0:T(8,128)(2,1)S(1)} collective-permute-done((bf16[2,128,512]{2,1,0:T(8,128)(2,1)S(1)}, bf16[2,128,512]{2,1,0:T(8,128)(2,1)S(1)}, u32[]{:S(2)}, u32[]{:S(2)}) %collective-permute-start.5) | collective-permute-done | bytes 262176 | tf_op jit(solution)/shard_map/ppermute | solution.py:102
  189.5 2.1 collective-permute-start.6
  193.4 5.5 %collective-permute-done.6 = bf16[2,128,512]{1,2,0:T(8,128)(2,1)S(1)} collective-permute-done((bf16[2,128,512]{1,2,0:T(8,128)(2,1)S(1)}, bf16[2,128,512]{1,2,0:T(8,128)(2,1)S(1)}, u32[]{:S(2)}, u32[]{:S(2)}) %collective-permute-start.6) | collective-permute-done | bytes 262176 | tf_op jit(solution)/shard_map/ppermute | solution.py:113
  199.7 8.4 %collective-permute-start.7 = (bf16[1,128,512]{1,2,0:T(8,128)(2,1)}, bf16[1,128,512]{1,2,0:T(8,128)(2,1)}, u32[]{:S(2)}, u32[]{:S(2)}) collective-permute-start(bf16[1,128,512]{1,2,0:T(8,128)(2,1)} %select_convert_fusion.1), channel_id=1, source_target_pairs={{0,256},{32,288},{64,320},{96,352},{128,384},{160,416},{192,448},{... | collective-permute-start | bytes 393224 | tf_op jit(solution)/shard_map/ppermute | solution.py:113
  210.0 9.4 %collective-permute-done.7 = bf16[1,128,512]{1,2,0:T(8,128)(2,1)} collective-permute-done((bf16[1,128,512]{1,2,0:T(8,128)(2,1)}, bf16[1,128,512]{1,2,0:T(8,128)(2,1)}, u32[]{:S(2)}, u32[]{:S(2)}) %collective-permute-start.7) | collective-permute-done | bytes 131104 | tf_op jit(solution)/shard_map/ppermute | solution.py:113
  223.8 2.4 gather_fusion.3
  226.5 43.6 %all_to_all.5 = f32[32,40,512]{2,1,0:T(8,128)S(1)} all-to-all(f32[32,40,512]{2,1,0:T(8,128)S(1)} %concatenate.45), channel_id=1, replica_groups=mesh['row'=16,'col'=32] {'col'}, dimensions={0} | all-to-all | bytes 5242880 | tf_op jit(solution)/shard_map/all_to_all | solution.py:29
  270.3 1.9 collective-permute-start.8
  272.3 3.2 collective-permute-done.8
  277.4 4.8 %collective-permute-done.9 = f32[40,512]{1,0:T(8,128)S(1)} collective-permute-done((f32[40,512]{1,0:T(8,128)S(1)}, f32[40,512]{1,0:T(8,128)S(1)}, u32[]{:S(2)}, u32[]{:S(2)}) %collective-permute-start.9) | collective-permute-done | bytes 81952 | tf_op jit(solution)/shard_map/ppermute | solution.py:34
  282.2 5.8 %collective-permute-start.10 = (f32[40,512]{1,0:T(8,128)S(1)}, f32[40,512]{1,0:T(8,128)S(1)}, u32[]{:S(2)}, u32[]{:S(2)}) collective-permute-start(f32[40,512]{1,0:T(8,128)S(1)} %add.370), channel_id=1, source_target_pairs={{0,128},{32,160},{64,192},{96,224},{128,0},{160,32},{192,64},{224,... | collective-permute-start | bytes 245768 | tf_op jit(solution)/shard_map/ppermute | solution.py:34
  288.0 8.5 %collective-permute-done.10 = f32[40,512]{1,0:T(8,128)S(1)} collective-permute-done((f32[40,512]{1,0:T(8,128)S(1)}, f32[40,512]{1,0:T(8,128)S(1)}, u32[]{:S(2)}, u32[]{:S(2)}) %collective-permute-start.10) | collective-permute-done | bytes 81952 | tf_op jit(solution)/shard_map/ppermute | solution.py:34
  296.5 8.2 %collective-permute-start.11 = (f32[40,512]{1,0:T(8,128)S(1)}, f32[40,512]{1,0:T(8,128)S(1)}, u32[]{:S(2)}, u32[]{:S(2)}) collective-permute-start(f32[40,512]{1,0:T(8,128)S(1)} %add.371), channel_id=1, source_target_pairs={{0,256},{32,288},{64,320},{96,352},{128,384},{160,416},{192,448},{... | collective-permute-start | bytes 245768 | tf_op jit(solution)/shard_map/ppermute | solution.py:34
  304.7 9.9 %collective-permute-done.11 = f32[40,512]{1,0:T(8,128)S(1)} collective-permute-done((f32[40,512]{1,0:T(8,128)S(1)}, f32[40,512]{1,0:T(8,128)S(1)}, u32[]{:S(2)}, u32[]{:S(2)}) %collective-permute-start.11) | collective-permute-done | bytes 81952 | tf_op jit(solution)/shard_map/ppermute | solution.py:34
  316.7 4.6 %collective-permute-done.12 = f32[32,512]{1,0:T(8,128)S(1)} collective-permute-done((f32[32,512]{1,0:T(8,128)S(1)}, f32[32,512]{1,0:T(8,128)S(1)}, u32[]{:S(2)}, u32[]{:S(2)}) %collective-permute-start.12) | collective-permute-done | bytes 65568 | tf_op jit(solution)/shard_map/ppermute | solution.py:38
  323.3 3.7 %collective-permute-done.13 = f32[64,512]{1,0:T(8,128)S(1)} collective-permute-done((f32[64,512]{1,0:T(8,128)S(1)}, f32[64,512]{1,0:T(8,128)S(1)}, u32[]{:S(2)}, u32[]{:S(2)}) %collective-permute-start.13) | collective-permute-done | bytes 131104 | tf_op jit(solution)/shard_map/ppermute | solution.py:38
  327.0 2.9 collective-permute-start.14
  330.0 5.6 %collective-permute-done.14 = f32[128,512]{1,0:T(8,128)S(1)} collective-permute-done((f32[128,512]{1,0:T(8,128)S(1)}, f32[128,512]{1,0:T(8,128)S(1)}, u32[]{:S(2)}, u32[]{:S(2)}) %collective-permute-start.14) | collective-permute-done | bytes 262176 | tf_op jit(solution)/shard_map/ppermute | solution.py:38
  337.8 8.9 %collective-permute-done.15 = f32[256,512]{1,0:T(8,128)S(1)} collective-permute-done((f32[256,512]{1,0:T(8,128)S(1)}, f32[256,512]{1,0:T(8,128)S(1)}, u32[]{:S(2)}, u32[]{:S(2)}) %collective-permute-start.15) | collective-permute-done | bytes 524320 | tf_op jit(solution)/shard_map/ppermute | solution.py:38
  346.7 7.1 %collective-permute-start.16 = (f32[512,512]{1,0:T(8,128)S(1)}, f32[512,512]{1,0:T(8,128)S(1)}, u32[]{:S(2)}, u32[]{:S(2)}) collective-permute-start(f32[512,512]{1,0:T(8,128)S(1)} %constant_dynamic-update-slice_fusion.1), channel_id=1, source_target_pairs={{0,1},{1,0},{2,3},{3,2},{4,5},{5,4},{6,7},{7,6},{8,9},{9,8},{10,11... | collective-permute-start | bytes 3145736 | tf_op jit(solution)/shard_map/ppermute | solution.py:38
  (117 shorter events, 40.9 us)
Async XLA Ops:
  7.2 4.3 %copy-start = (bf16[512,512]{1,0:T(8,128)(2,1)S(1)}, bf16[512,512]{1,0:T(8,128)(2,1)}, u32[]{:S(2)}) copy-start(bf16[512,512]{1,0:T(8,128)(2,1)} %param.12) | copy-start | bytes 1572868
  7.2 71.1 %copy-start.6 = (s32[4,8]{1,0:T(4,128)S(1)}, s32[4,8]{1,0:T(4,128)}, u32[]{:S(2)}) copy-start(s32[4,8]{1,0:T(4,128)} %param.14) | copy-start | bytes 388
  7.2 71.1 %all-gather.2.cloned.1.call-start = ((), (), s32[]{:S(2)}) async-start(), calls=%async_computation.1 | async-start | bytes 4325376 | tf_op jit(solution)/shard_map/all_gather | solution.py:140
  78.3 5.5 %copy-start.12 = (bf16[4,8,128,128]{3,2,1,0:T(8,128)(2,1)S(1)}, bf16[4,8,128,128]{3,2,1,0:T(8,128)(2,1)}, u32[]{:S(2)}) copy-start(bf16[4,8,128,128]{3,2,1,0:T(8,128)(2,1)} %param.16) | copy-start | bytes 3145732
  83.8 2.6 copy-start.5
  86.5 0.8 copy-start.2
  86.5 22.4 %copy-start.11 = (s32[32]{0:T(128)S(1)}, s32[32]{0:T(128)}, u32[]{:S(2)}) copy-start(s32[32]{0:T(128)} %constant.340) | copy-start | bytes 388
  86.5 23.0 %copy-start.1 = (s32[16]{0:T(128)S(1)}, s32[16]{0:T(128)}, u32[]{:S(2)}) copy-start(s32[16]{0:T(128)} %param.18) | copy-start | bytes 196
  87.4 16.2 %collective-permute-start = (bf16[1,128,512]{1,2,0:T(8,128)(2,1)S(1)}, bf16[1,128,512]{1,2,0:T(8,128)(2,1)S(1)}, u32[]{:S(2)}, u32[]{:S(2)}) collective-permute-start(bf16[1,128,512]{1,2,0:T(8,128)(2,1)S(1)} %slice_bitcast_fusion), channel_id=1, source_target_pairs={{0,256},{32,288},{64,320},{96,352},{128,384},{160,416},{192,448},{... | collective-permute-start | bytes 393224 | tf_op jit(solution)/shard_map/ppermute | solution.py:76
  100.0 36.9 %copy-start.8 = (pred[2]{0:T(512)(128)(4,1)}, pred[2]{0:T(512)(128)(4,1)S(1)}, u32[]{:S(2)}) copy-start(pred[2]{0:T(512)(128)(4,1)S(1)} %fusion.52) | copy-start | bytes 10
  103.7 20.9 %copy-start.10 = (s32[512]{0:T(512)S(1)}, s32[512]{0:T(512)}, u32[]{:S(2)}) copy-start(s32[512]{0:T(512)} %param.17) | copy-start | bytes 6148
  103.7 11.6 %collective-permute-start.1 = (bf16[2,128,512]{1,2,0:T(8,128)(2,1)S(1)}, bf16[2,128,512]{1,2,0:T(8,128)(2,1)S(1)}, u32[]{:S(2)}, u32[]{:S(2)}) collective-permute-start(bf16[2,128,512]{1,2,0:T(8,128)(2,1)S(1)} %maximum_select_fusion.4), channel_id=1, source_target_pairs={{0,32},{32,0},{64,96},{96,64},{128,160},{160,128},{192,224},{224,1... | collective-permute-start | bytes 786440 | tf_op jit(solution)/shard_map/ppermute | solution.py:76
  116.4 20.5 %collective-permute-start.2 = (bf16[2,128,512]{2,1,0:T(8,128)(2,1)S(1)}, bf16[2,128,512]{2,1,0:T(8,128)(2,1)S(1)}, u32[]{:S(2)}, u32[]{:S(2)}) collective-permute-start(bf16[2,128,512]{2,1,0:T(8,128)(2,1)S(1)} %select_bitcast_fusion), channel_id=1, source_target_pairs={{0,64},{32,96},{64,0},{96,32},{128,192},{160,224},{192,128},{224,1... | collective-permute-start | bytes 786440 | tf_op jit(solution)/shard_map/ppermute | solution.py:86
  137.0 35.6 %copy-start.9 = (pred[2]{0:T(512)(128)(4,1)S(1)}, pred[2]{0:T(512)(128)(4,1)}, u32[]{:S(2)}) copy-start(pred[2]{0:T(512)(128)(4,1)} %copy-done.8) | copy-start | bytes 10
  137.0 18.1 %collective-permute-start.3 = (bf16[1,128,512]{2,1,0:T(8,128)(2,1)S(1)}, bf16[1,128,512]{2,1,0:T(8,128)(2,1)S(1)}, u32[]{:S(2)}, u32[]{:S(2)}) collective-permute-start(bf16[1,128,512]{2,1,0:T(8,128)(2,1)S(1)} %select_bitcast_fusion.3), channel_id=1, source_target_pairs={{0,128},{32,160},{64,192},{96,224},{128,0},{160,32},{192,64},{224,... | collective-permute-start | bytes 393224 | tf_op jit(solution)/shard_map/ppermute | solution.py:86
  156.9 15.7 %collective-permute-start.4 = (bf16[1,128,512]{2,1,0:T(8,128)(2,1)S(1)}, bf16[1,128,512]{2,1,0:T(8,128)(2,1)S(1)}, u32[]{:S(2)}, u32[]{:S(2)}) collective-permute-start(bf16[1,128,512]{2,1,0:T(8,128)(2,1)S(1)} %get-tuple-element.20), channel_id=1, source_target_pairs={{0,128},{32,160},{64,192},{96,224},{128,0},{160,32},{192,64},{224,... | collective-permute-start | bytes 393224 | tf_op jit(solution)/shard_map/ppermute | solution.py:102
  172.7 13.7 %collective-permute-start.5 = (bf16[2,128,512]{2,1,0:T(8,128)(2,1)S(1)}, bf16[2,128,512]{2,1,0:T(8,128)(2,1)S(1)}, u32[]{:S(2)}, u32[]{:S(2)}) collective-permute-start(bf16[2,128,512]{2,1,0:T(8,128)(2,1)S(1)} %fusion.25), channel_id=1, source_target_pairs={{0,64},{32,96},{64,0},{96,32},{128,192},{160,224},{192,128},{224,1... | collective-permute-start | bytes 786440 | tf_op jit(solution)/shard_map/ppermute | solution.py:102
  187.1 4.5 %copy-start.7 = (f32[512]{0:T(512)S(1)}, f32[512]{0:T(512)}, u32[]{:S(2)}) copy-start(f32[512]{0:T(512)} %get-tuple-element.24) | copy-start | bytes 6148
  189.4 18.6 %copy-start.4 = (f32[512,512]{0,1:T(8,128)S(1)}, f32[512,512]{0,1:T(8,128)}, u32[]{:S(2)}) copy-start(f32[512,512]{0,1:T(8,128)} %get-tuple-element.29) | copy-start | bytes 3145732
  189.5 9.4 %collective-permute-start.6 = (bf16[2,128,512]{1,2,0:T(8,128)(2,1)S(1)}, bf16[2,128,512]{1,2,0:T(8,128)(2,1)S(1)}, u32[]{:S(2)}, u32[]{:S(2)}) collective-permute-start(bf16[2,128,512]{1,2,0:T(8,128)(2,1)S(1)} %select_convert_fusion), channel_id=1, source_target_pairs={{0,32},{32,0},{64,96},{96,64},{128,160},{160,128},{192,224},{224,1... | collective-permute-start | bytes 786440 | tf_op jit(solution)/shard_map/ppermute | solution.py:113
  199.7 19.8 %collective-permute-start.7 = (bf16[1,128,512]{1,2,0:T(8,128)(2,1)}, bf16[1,128,512]{1,2,0:T(8,128)(2,1)}, u32[]{:S(2)}, u32[]{:S(2)}) collective-permute-start(bf16[1,128,512]{1,2,0:T(8,128)(2,1)} %select_convert_fusion.1), channel_id=1, source_target_pairs={{0,256},{32,288},{64,320},{96,352},{128,384},{160,416},{192,448},{... | collective-permute-start | bytes 393224 | tf_op jit(solution)/shard_map/ppermute | solution.py:113
  220.8 1.0 copy-start.3
  270.3 5.2 %collective-permute-start.8 = (f32[40,512]{1,0:T(8,128)S(1)}, f32[40,512]{1,0:T(8,128)S(1)}, u32[]{:S(2)}, u32[]{:S(2)}) collective-permute-start(f32[40,512]{1,0:T(8,128)S(1)} %reduce_sum.73), channel_id=1, source_target_pairs={{0,32},{32,0},{64,96},{96,64},{128,160},{160,128},{192,224},{224,1... | collective-permute-start | bytes 245768 | tf_op jit(solution)/shard_map/ppermute | solution.py:34
  275.5 6.7 %collective-permute-start.9 = (f32[40,512]{1,0:T(8,128)S(1)}, f32[40,512]{1,0:T(8,128)S(1)}, u32[]{:S(2)}, u32[]{:S(2)}) collective-permute-start(f32[40,512]{1,0:T(8,128)S(1)} %add.369), channel_id=1, source_target_pairs={{0,64},{32,96},{64,0},{96,32},{128,192},{160,224},{192,128},{224,1... | collective-permute-start | bytes 245768 | tf_op jit(solution)/shard_map/ppermute | solution.py:34
  282.2 14.3 %collective-permute-start.10 = (f32[40,512]{1,0:T(8,128)S(1)}, f32[40,512]{1,0:T(8,128)S(1)}, u32[]{:S(2)}, u32[]{:S(2)}) collective-permute-start(f32[40,512]{1,0:T(8,128)S(1)} %add.370), channel_id=1, source_target_pairs={{0,128},{32,160},{64,192},{96,224},{128,0},{160,32},{192,64},{224,... | collective-permute-start | bytes 245768 | tf_op jit(solution)/shard_map/ppermute | solution.py:34
  296.5 18.1 %collective-permute-start.11 = (f32[40,512]{1,0:T(8,128)S(1)}, f32[40,512]{1,0:T(8,128)S(1)}, u32[]{:S(2)}, u32[]{:S(2)}) collective-permute-start(f32[40,512]{1,0:T(8,128)S(1)} %add.371), channel_id=1, source_target_pairs={{0,256},{32,288},{64,320},{96,352},{128,384},{160,416},{192,448},{... | collective-permute-start | bytes 245768 | tf_op jit(solution)/shard_map/ppermute | solution.py:34
  314.7 6.5 %collective-permute-start.12 = (f32[32,512]{1,0:T(8,128)S(1)}, f32[32,512]{1,0:T(8,128)S(1)}, u32[]{:S(2)}, u32[]{:S(2)}) collective-permute-start(f32[32,512]{1,0:T(8,128)S(1)} %get-tuple-element.21), channel_id=1, source_target_pairs={{0,16},{1,17},{2,18},{3,19},{4,20},{5,21},{6,22},{7,23},{8,24},{9,... | collective-permute-start | bytes 196616 | tf_op jit(solution)/shard_map/ppermute | solution.py:38
  321.3 5.7 %collective-permute-start.13 = (f32[64,512]{1,0:T(8,128)S(1)}, f32[64,512]{1,0:T(8,128)S(1)}, u32[]{:S(2)}, u32[]{:S(2)}) collective-permute-start(f32[64,512]{1,0:T(8,128)S(1)} %constant_dynamic-update-slice_fusion.7), channel_id=1, source_target_pairs={{0,8},{1,9},{2,10},{3,11},{4,12},{5,13},{6,14},{7,15},{8,0},{9,1},... | collective-permute-start | bytes 393224 | tf_op jit(solution)/shard_map/ppermute | solution.py:38
  327.0 8.6 %collective-permute-start.14 = (f32[128,512]{1,0:T(8,128)S(1)}, f32[128,512]{1,0:T(8,128)S(1)}, u32[]{:S(2)}, u32[]{:S(2)}) collective-permute-start(f32[128,512]{1,0:T(8,128)S(1)} %constant_dynamic-update-slice_fusion.5), channel_id=1, source_target_pairs={{0,4},{1,5},{2,6},{3,7},{4,0},{5,1},{6,2},{7,3},{8,12},{9,13},{10,... | collective-permute-start | bytes 786440 | tf_op jit(solution)/shard_map/ppermute | solution.py:38
  335.6 11.0 %collective-permute-start.15 = (f32[256,512]{1,0:T(8,128)S(1)}, f32[256,512]{1,0:T(8,128)S(1)}, u32[]{:S(2)}, u32[]{:S(2)}) collective-permute-start(f32[256,512]{1,0:T(8,128)S(1)} %constant_dynamic-update-slice_fusion.3), channel_id=1, source_target_pairs={{0,2},{1,3},{2,0},{3,1},{4,6},{5,7},{6,4},{7,5},{8,10},{9,11},{10,... | collective-permute-start | bytes 1572872 | tf_op jit(solution)/shard_map/ppermute | solution.py:38
  346.7 9.4 %collective-permute-start.16 = (f32[512,512]{1,0:T(8,128)S(1)}, f32[512,512]{1,0:T(8,128)S(1)}, u32[]{:S(2)}, u32[]{:S(2)}) collective-permute-start(f32[512,512]{1,0:T(8,128)S(1)} %constant_dynamic-update-slice_fusion.1), channel_id=1, source_target_pairs={{0,1},{1,0},{2,3},{3,2},{4,5},{5,4},{6,7},{7,6},{8,9},{9,8},{10,11... | collective-permute-start | bytes 3145736 | tf_op jit(solution)/shard_map/ppermute | solution.py:38
Sparse Core Ops, SparseCore 0:
  11.2 67.0 all-gather.1

commit v7 on v6

--- a/solution.py
+++ b/solution.py
@@ -148,18 +148,22 @@
     ).astype(jnp.bfloat16)
     summed = jnp.einsum("bkij,bkjd->bid", tiles, selected, preferred_element_type=jnp.float32)
     agg = summed.reshape(rows, width).astype(jnp.bfloat16)
-    pre = jnp.dot(node_feats, w_self, preferred_element_type=jnp.float32) + jnp.dot(
-        agg, w_neigh, preferred_element_type=jnp.float32
+    plan = route_plan(noise_block_rows)
+    fetched = route_forward(jnp.concatenate([node_feats[:NOISE], agg[:NOISE]], axis=0), plan)
+    all_feats = jnp.concatenate([node_feats, fetched[:NOISE]], axis=0)
+    all_agg = jnp.concatenate([agg, fetched[NOISE:]], axis=0)
+    pre = jnp.dot(all_feats, w_self, preferred_element_type=jnp.float32) + jnp.dot(
+        all_agg, w_neigh, preferred_element_type=jnp.float32
     )
     emb32, pull = jax.vjp(embed, pre)
-    zeta_bf = emb32.astype(jnp.bfloat16)
-    plan = route_plan(noise_block_rows)
-    noise_emb = route_forward(zeta_bf[:NOISE], plan).astype(jnp.float32)
+    all_bf = emb32.astype(jnp.bfloat16)
+    zeta_bf = all_bf[:rows]
+    noise_emb = all_bf[rows:].astype(jnp.float32)
     zeta = zeta_bf.astype(jnp.float32)
     pairing = (pos_index[:, None] == jnp.arange(rows, dtype=jnp.int32)[None, :]).astype(jnp.float32)
     partner = jnp.dot(pairing.astype(jnp.bfloat16), zeta_bf, preferred_element_type=jnp.float32)
     s_pos = jnp.sum(zeta * partner, axis=-1) * scale_factor
-    s_neg = jnp.dot(zeta_bf, noise_emb.astype(jnp.bfloat16).T, preferred_element_type=jnp.float32) * scale_factor
+    s_neg = jnp.dot(zeta_bf, all_bf[rows:].T, preferred_element_type=jnp.float32) * scale_factor
     loss_part = (jnp.sum(jax.nn.softplus(-s_pos)) + jnp.sum(jax.nn.softplus(s_neg)) / NOISE) / nodes
     grad_pos = -jax.nn.sigmoid(-s_pos) / nodes
     grad_neg = jax.nn.sigmoid(s_neg) / (NOISE * nodes)
@@ -168,12 +172,11 @@
     )
     partner_grad = jnp.dot(pairing.T, scale_factor * grad_pos[:, None] * zeta, precision=highest)
     dnoise = scale_factor * jnp.dot(grad_neg.T, zeta, precision=highest)
-    returned = route_backward(dnoise.astype(jnp.bfloat16).astype(jnp.float32), plan)
-    dzeta = anchor + partner_grad
-    dzeta = dzeta.at[:NOISE].add(returned)
+    dnoise = dnoise.astype(jnp.bfloat16).astype(jnp.float32)
+    dzeta = jnp.concatenate([anchor + partner_grad, dnoise], axis=0)
     gpre = pull(dzeta)[0].astype(jnp.bfloat16)
-    part_self = jnp.dot(node_feats.T, gpre, preferred_element_type=jnp.float32)
-    neighbour_partial = jnp.dot(agg.T, gpre, preferred_element_type=jnp.float32)
+    part_self = jnp.dot(all_feats.T, gpre, preferred_element_type=jnp.float32)
+    neighbour_partial = jnp.dot(all_agg.T, gpre, preferred_element_type=jnp.float32)
     stacked = jnp.concatenate([part_self, neighbour_partial], axis=0)
     total, loss_tile = tree_allreduce(stacked, jnp.broadcast_to(loss_part, (8, width)))
     grad_self = total[:width]

time: 365 us -> 344 us (0.942)
  starting transfers between devices: 81.6 us -> 71.1 us
  local copies, waits for them, and re-layouts: 12.6 us -> 8.1 us
  blocking collectives: 43.6 us -> 39.3 us
  waiting for transfers between devices: 183 us -> 187 us
  other arithmetic: 8.24 us -> 4.45 us
    ppermute x4 -> x0, waiting for transfers between devices: 40.3 us -> none  [the longest x2 25.4 us: route_backward(): lax.ppermute(rbar.astype(jnp.bfloat16), 'row', xor_pairs(size, m))]
    ppermute x2, waiting for transfers between devices: 19.9 us -> 40.8 us  [route_forward(): got = lax.ppermute(send, 'row', xor_pairs(size, m))]
    ppermute x2, waiting for transfers between devices: 6.02 us -> 25.7 us  [route_forward(): got = lax.ppermute(held, 'row', xor_pairs(size, m))]
    ppermute x4 -> x0, starting transfers between devices: 14.3 us -> none  [the longest x2 10.4 us: route_backward(): lax.ppermute(other.astype(jnp.bfloat16), 'row', xor_pairs(size, m))]
    all_gather x1, waiting for transfers between devices: 65.3 us -> 69.6 us  [body(): piece = lax.all_gather(source_feats, 'col', axis=0, tiled=True)]
    all_to_all x1, blocking collectives: 43.6 us -> 39.3 us  [tree_allreduce(): joined = lax.all_to_all(chunks, 'col', 0, 0, tiled=False).sum(axis=0)]
  transfers between devices with their start and end apart: 18 -> 14, of which waited for: 18 -> 14; matrix products, arithmetic and copies ran while one was open for 4% -> 1% of each run, Pallas kernels for 0% -> 0%
where the time goes in v7:
time: 344 us; the launch traced here: 343 us
  waiting for transfers between devices  187 us (54%)
  starting transfers between devices  71.1 us (21%)
  blocking collectives  39.3 us (11%)
  between operations  18.8 us (5%)
  matrix products  14.8 us (4%)
  local copies, waits for them, and re-layouts  8.1 us (2%)
  other arithmetic  4.45 us (1%)
    all_gather x1, waiting for transfers between devices, body(): piece = lax.all_gather(source_feats, 'col', axis=0, tiled=True)  69.6 us
    ppermute x2, waiting for transfers between devices, route_forward(): got = lax.ppermute(send, 'row', xor_pairs(size, m))  40.8 us
    all_to_all x1, blocking collectives, tree_allreduce(): joined = lax.all_to_all(chunks, 'col', 0, 0, tiled=False).sum(axis=0)  39.3 us
    ppermute x4, waiting for transfers between devices, tree_allreduce(): joined = joined + lax.ppermute(joined, axis, xor_pairs(size, mask))  26.4 us
    ppermute x2, waiting for transfers between devices, route_forward(): got = lax.ppermute(held, 'row', xor_pairs(size, m))  25.7 us
    ppermute x5, waiting for transfers between devices, tree_allreduce(): got = lax.ppermute(buf, 'col', xor_pairs(ways, mask))  23.3 us
    ppermute x4, starting transfers between devices, tree_allreduce(): joined = joined + lax.ppermute(joined, axis, xor_pairs(size, mask))  19.6 us
    ppermute x2, starting transfers between devices, route_forward(): got = lax.ppermute(held, 'row', xor_pairs(size, m))  18.6 us
  transfers between devices with their start and end apart: 14, of which 14 were waited for; matrix products, arithmetic and copies ran while one was open for 1% of the time, Pallas kernels for 0%

profile of v7, /device:TPU:1, one launch (start us, length us, event | category | flops | bytes accessed | tf_op | source)
XLA Modules:
  0.0 343.1 jit_solution(13993342624538797826)
XLA Ops:
  8.6 69.6 %all-gather.2.cloned.1.call-done = bf16[4096,512]{1,0:T(8,128)(2,1)} async-done(((bf16[128,512]{1,0:T(8,128)(2,1)}), bf16[4096,512]{1,0:T(8,128)(2,1)}) %all-gather.2.cloned.1.call-update) | async-done | bytes 4194320 | tf_op jit(solution)/shard_map/all_gather | solution.py:140
  78.3 5.6 %fusion.1 = bf16[4,8,128,512]{3,1,2,0:T(8,128)(2,1)S(1)} fusion(bf16[32,128,512,1]{2,1,0,3:T(8,128)(2,1)} %bitcast.65, s32[4,8]{1,0:T(4,128)} %param.12), kind=kOutput, calls=%fused_computation.6 | convolution fusion | flops 134218752 | bytes 8388736 | tf_op jit(solution)/shard_map/bkc,cjd->bkjd/dot_general | solution.py:146
  83.9 2.6 fusion.6
  86.5 12.5 %collective-permute-start = (bf16[1,256,512]{2,1,0:T(8,128)(2,1)S(1)}, bf16[1,256,512]{2,1,0:T(8,128)(2,1)S(1)}, u32[]{:S(2)}, u32[]{:S(2)}) collective-permute-start(bf16[1,256,512]{2,1,0:T(8,128)(2,1)S(1)} %maximum_bitcast_fusion), channel_id=1, source_target_pairs={{0,256},{32,288},{64,320},{96,352},{128,384},{160,416},{192,448},{... | collective-permute-start | bytes 786440 | tf_op jit(solution)/shard_map/ppermute | solution.py:76
  99.9 12.1 %collective-permute-done = bf16[1,256,512]{2,1,0:T(8,128)(2,1)S(1)} collective-permute-done((bf16[1,256,512]{2,1,0:T(8,128)(2,1)S(1)}, bf16[1,256,512]{2,1,0:T(8,128)(2,1)S(1)}, u32[]{:S(2)}, u32[]{:S(2)}) %collective-permute-start) | collective-permute-done | bytes 262176 | tf_op jit(solution)/shard_map/ppermute | solution.py:76
  112.1 6.1 %collective-permute-start.1 = (bf16[2,256,512]{2,1,0:T(8,128)(2,1)S(1)}, bf16[2,256,512]{2,1,0:T(8,128)(2,1)S(1)}, u32[]{:S(2)}, u32[]{:S(2)}) collective-permute-start(bf16[2,256,512]{2,1,0:T(8,128)(2,1)S(1)} %maximum_select_fusion.1), channel_id=1, source_target_pairs={{0,32},{32,0},{64,96},{96,64},{128,160},{160,128},{192,224},{224,1... | collective-permute-start | bytes 1572872 | tf_op jit(solution)/shard_map/ppermute | solution.py:76
  118.4 13.6 %collective-permute-done.1 = bf16[2,256,512]{2,1,0:T(8,128)(2,1)S(1)} collective-permute-done((bf16[2,256,512]{2,1,0:T(8,128)(2,1)S(1)}, bf16[2,256,512]{2,1,0:T(8,128)(2,1)S(1)}, u32[]{:S(2)}, u32[]{:S(2)}) %collective-permute-start.1) | collective-permute-done | bytes 524320 | tf_op jit(solution)/shard_map/ppermute | solution.py:76
  133.0 6.7 %collective-permute-start.2 = (bf16[2,256,512]{2,1,0:T(8,128)(2,1)S(1)}, bf16[2,256,512]{2,1,0:T(8,128)(2,1)S(1)}, u32[]{:S(2)}, u32[]{:S(2)}) collective-permute-start(bf16[2,256,512]{2,1,0:T(8,128)(2,1)S(1)} %select_bitcast_fusion), channel_id=1, source_target_pairs={{0,64},{32,96},{64,0},{96,32},{128,192},{160,224},{192,128},{224,1... | collective-permute-start | bytes 1572872 | tf_op jit(solution)/shard_map/ppermute | solution.py:86
  140.5 22.8 %collective-permute-done.2 = bf16[2,256,512]{2,1,0:T(8,128)(2,1)S(1)} collective-permute-done((bf16[2,256,512]{2,1,0:T(8,128)(2,1)S(1)}, bf16[2,256,512]{2,1,0:T(8,128)(2,1)S(1)}, u32[]{:S(2)}, u32[]{:S(2)}) %collective-permute-start.2) | collective-permute-done | bytes 524320 | tf_op jit(solution)/shard_map/ppermute | solution.py:86
  163.5 9.5 %collective-permute-start.3 = (bf16[1,256,512]{2,1,0:T(8,128)(2,1)S(1)}, bf16[1,256,512]{2,1,0:T(8,128)(2,1)S(1)}, u32[]{:S(2)}, u32[]{:S(2)}) collective-permute-start(bf16[1,256,512]{2,1,0:T(8,128)(2,1)S(1)} %select_bitcast_fusion.1), channel_id=1, source_target_pairs={{0,128},{32,160},{64,192},{96,224},{128,0},{160,32},{192,64},{224,... | collective-permute-start | bytes 786440 | tf_op jit(solution)/shard_map/ppermute | solution.py:86
  176.2 18.0 %collective-permute-done.3 = bf16[1,256,512]{2,1,0:T(8,128)(2,1)S(1)} collective-permute-done((bf16[1,256,512]{2,1,0:T(8,128)(2,1)S(1)}, bf16[1,256,512]{2,1,0:T(8,128)(2,1)S(1)}, u32[]{:S(2)}, u32[]{:S(2)}) %collective-permute-start.3) | collective-permute-done | bytes 262176 | tf_op jit(solution)/shard_map/ppermute | solution.py:86
  203.5 1.5 pad_maximum_fusion
  205.0 2.3 gather_fusion.3
  207.6 39.3 %all_to_all.5 = f32[32,40,512]{2,1,0:T(8,128)S(1)} all-to-all(f32[32,40,512]{2,1,0:T(8,128)S(1)} %concatenate.39), channel_id=1, replica_groups=mesh['row'=16,'col'=32] {'col'}, dimensions={0} | all-to-all | bytes 5242880 | tf_op jit(solution)/shard_map/all_to_all | solution.py:29
  247.1 1.9 collective-permute-start.4
  249.0 3.3 collective-permute-done.4
  252.3 2.7 collective-permute-start.5
  255.0 4.3 %collective-permute-done.5 = f32[40,512]{1,0:T(8,128)S(1)} collective-permute-done((f32[40,512]{1,0:T(8,128)S(1)}, f32[40,512]{1,0:T(8,128)S(1)}, u32[]{:S(2)}, u32[]{:S(2)}) %collective-permute-start.5) | collective-permute-done | bytes 81952 | tf_op jit(solution)/shard_map/ppermute | solution.py:34
  259.3 6.9 %collective-permute-start.6 = (f32[40,512]{1,0:T(8,128)S(1)}, f32[40,512]{1,0:T(8,128)S(1)}, u32[]{:S(2)}, u32[]{:S(2)}) collective-permute-start(f32[40,512]{1,0:T(8,128)S(1)} %add.328), channel_id=1, source_target_pairs={{0,128},{32,160},{64,192},{96,224},{128,0},{160,32},{192,64},{224,... | collective-permute-start | bytes 245768 | tf_op jit(solution)/shard_map/ppermute | solution.py:34
  266.2 7.6 %collective-permute-done.6 = f32[40,512]{1,0:T(8,128)S(1)} collective-permute-done((f32[40,512]{1,0:T(8,128)S(1)}, f32[40,512]{1,0:T(8,128)S(1)}, u32[]{:S(2)}, u32[]{:S(2)}) %collective-permute-start.6) | collective-permute-done | bytes 81952 | tf_op jit(solution)/shard_map/ppermute | solution.py:34
  273.8 8.1 %collective-permute-start.7 = (f32[40,512]{1,0:T(8,128)S(1)}, f32[40,512]{1,0:T(8,128)S(1)}, u32[]{:S(2)}, u32[]{:S(2)}) collective-permute-start(f32[40,512]{1,0:T(8,128)S(1)} %add.329), channel_id=1, source_target_pairs={{0,256},{32,288},{64,320},{96,352},{128,384},{160,416},{192,448},{... | collective-permute-start | bytes 245768 | tf_op jit(solution)/shard_map/ppermute | solution.py:34
  282.0 11.2 %collective-permute-done.7 = f32[40,512]{1,0:T(8,128)S(1)} collective-permute-done((f32[40,512]{1,0:T(8,128)S(1)}, f32[40,512]{1,0:T(8,128)S(1)}, u32[]{:S(2)}, u32[]{:S(2)}) %collective-permute-start.7) | collective-permute-done | bytes 81952 | tf_op jit(solution)/shard_map/ppermute | solution.py:34
  293.3 1.9 collective-permute-start.8
  295.2 4.6 %collective-permute-done.8 = f32[32,512]{1,0:T(8,128)S(1)} collective-permute-done((f32[32,512]{1,0:T(8,128)S(1)}, f32[32,512]{1,0:T(8,128)S(1)}, u32[]{:S(2)}, u32[]{:S(2)}) %collective-permute-start.8) | collective-permute-done | bytes 65568 | tf_op jit(solution)/shard_map/ppermute | solution.py:38
  299.8 1.9 collective-permute-start.9
  301.8 3.7 %collective-permute-done.9 = f32[64,512]{1,0:T(8,128)S(1)} collective-permute-done((f32[64,512]{1,0:T(8,128)S(1)}, f32[64,512]{1,0:T(8,128)S(1)}, u32[]{:S(2)}, u32[]{:S(2)}) %collective-permute-start.9) | collective-permute-done | bytes 131104 | tf_op jit(solution)/shard_map/ppermute | solution.py:38
  305.5 2.8 collective-permute-start.10
  308.5 5.6 %collective-permute-done.10 = f32[128,512]{1,0:T(8,128)S(1)} collective-permute-done((f32[128,512]{1,0:T(8,128)S(1)}, f32[128,512]{1,0:T(8,128)S(1)}, u32[]{:S(2)}, u32[]{:S(2)}) %collective-permute-start.10) | collective-permute-done | bytes 262176 | tf_op jit(solution)/shard_map/ppermute | solution.py:38
  314.2 3.1 collective-permute-start.11
  317.6 8.0 %collective-permute-done.11 = f32[256,512]{1,0:T(8,128)S(1)} collective-permute-done((f32[256,512]{1,0:T(8,128)S(1)}, f32[256,512]{1,0:T(8,128)S(1)}, u32[]{:S(2)}, u32[]{:S(2)}) %collective-permute-start.11) | collective-permute-done | bytes 524320 | tf_op jit(solution)/shard_map/ppermute | solution.py:38
  325.6 6.8 %collective-permute-start.12 = (f32[512,512]{1,0:T(8,128)S(1)}, f32[512,512]{1,0:T(8,128)S(1)}, u32[]{:S(2)}, u32[]{:S(2)}) collective-permute-start(f32[512,512]{1,0:T(8,128)S(1)} %constant_dynamic-update-slice_fusion.1), channel_id=1, source_target_pairs={{0,1},{1,0},{2,3},{3,2},{4,5},{5,4},{6,7},{7,6},{8,9},{9,8},{10,11... | collective-permute-start | bytes 3145736 | tf_op jit(solution)/shard_map/ppermute | solution.py:38
  334.7 1.5 fusion.58
  (82 shorter events, 16.1 us)
Async XLA Ops:
  7.2 187.8 %copy-start = (bf16[512,512]{1,0:T(8,128)(2,1)S(1)}, bf16[512,512]{1,0:T(8,128)(2,1)}, u32[]{:S(2)}) copy-start(bf16[512,512]{1,0:T(8,128)(2,1)} %param.18) | copy-start | bytes 1572868
  7.2 71.1 %all-gather.2.cloned.1.call-start = ((), (), s32[]{:S(2)}) async-start(), calls=%async_computation.1 | async-start | bytes 4325376 | tf_op jit(solution)/shard_map/all_gather | solution.py:140
  78.3 5.6 %copy-start.6 = (bf16[4,8,128,128]{3,2,1,0:T(8,128)(2,1)S(1)}, bf16[4,8,128,128]{3,2,1,0:T(8,128)(2,1)}, u32[]{:S(2)}) copy-start(bf16[4,8,128,128]{3,2,1,0:T(8,128)(2,1)} %param.14) | copy-start | bytes 3145732
  83.9 2.7 slice-start
  83.9 15.3 %copy-start.1 = (s32[16]{0:T(128)S(1)}, s32[16]{0:T(128)}, u32[]{:S(2)}) copy-start(s32[16]{0:T(128)} %param.16) | copy-start | bytes 196
  86.5 25.5 %collective-permute-start = (bf16[1,256,512]{2,1,0:T(8,128)(2,1)S(1)}, bf16[1,256,512]{2,1,0:T(8,128)(2,1)S(1)}, u32[]{:S(2)}, u32[]{:S(2)}) collective-permute-start(bf16[1,256,512]{2,1,0:T(8,128)(2,1)S(1)} %maximum_bitcast_fusion), channel_id=1, source_target_pairs={{0,256},{32,288},{64,320},{96,352},{128,384},{160,416},{192,448},{... | collective-permute-start | bytes 786440 | tf_op jit(solution)/shard_map/ppermute | solution.py:76
  112.1 19.8 %collective-permute-start.1 = (bf16[2,256,512]{2,1,0:T(8,128)(2,1)S(1)}, bf16[2,256,512]{2,1,0:T(8,128)(2,1)S(1)}, u32[]{:S(2)}, u32[]{:S(2)}) collective-permute-start(bf16[2,256,512]{2,1,0:T(8,128)(2,1)S(1)} %maximum_select_fusion.1), channel_id=1, source_target_pairs={{0,32},{32,0},{64,96},{96,64},{128,160},{160,128},{192,224},{224,1... | collective-permute-start | bytes 1572872 | tf_op jit(solution)/shard_map/ppermute | solution.py:76
  133.0 30.3 %collective-permute-start.2 = (bf16[2,256,512]{2,1,0:T(8,128)(2,1)S(1)}, bf16[2,256,512]{2,1,0:T(8,128)(2,1)S(1)}, u32[]{:S(2)}, u32[]{:S(2)}) collective-permute-start(bf16[2,256,512]{2,1,0:T(8,128)(2,1)S(1)} %select_bitcast_fusion), channel_id=1, source_target_pairs={{0,64},{32,96},{64,0},{96,32},{128,192},{160,224},{192,128},{224,1... | collective-permute-start | bytes 1572872 | tf_op jit(solution)/shard_map/ppermute | solution.py:86
  140.4 35.7 %copy-start.5 = (s32[32]{0:T(128)S(1)}, s32[32]{0:T(128)}, u32[]{:S(2)}) copy-start(s32[32]{0:T(128)} %constant.296) | copy-start | bytes 388
  163.4 30.9 %copy-start.2 = (bf16[512,512]{1,0:T(8,128)(2,1)S(1)}, bf16[512,512]{1,0:T(8,128)(2,1)}, u32[]{:S(2)}) copy-start(bf16[512,512]{1,0:T(8,128)(2,1)} %param.10) | copy-start | bytes 1572868
  163.4 30.9 %copy-start.3 = (bf16[512,512]{1,0:T(8,128)(2,1)S(1)}, bf16[512,512]{1,0:T(8,128)(2,1)}, u32[]{:S(2)}) copy-start(bf16[512,512]{1,0:T(8,128)(2,1)} %param.17) | copy-start | bytes 1572868
  163.5 30.7 %collective-permute-start.3 = (bf16[1,256,512]{2,1,0:T(8,128)(2,1)S(1)}, bf16[1,256,512]{2,1,0:T(8,128)(2,1)S(1)}, u32[]{:S(2)}, u32[]{:S(2)}) collective-permute-start(bf16[1,256,512]{2,1,0:T(8,128)(2,1)S(1)} %select_bitcast_fusion.1), channel_id=1, source_target_pairs={{0,128},{32,160},{64,192},{96,224},{128,0},{160,32},{192,64},{224,... | collective-permute-start | bytes 786440 | tf_op jit(solution)/shard_map/ppermute | solution.py:86
  195.6 1.1 copy-start.4
  247.1 5.2 %collective-permute-start.4 = (f32[40,512]{1,0:T(8,128)S(1)}, f32[40,512]{1,0:T(8,128)S(1)}, u32[]{:S(2)}, u32[]{:S(2)}) collective-permute-start(f32[40,512]{1,0:T(8,128)S(1)} %reduce_sum.63), channel_id=1, source_target_pairs={{0,32},{32,0},{64,96},{96,64},{128,160},{160,128},{192,224},{224,1... | collective-permute-start | bytes 245768 | tf_op jit(solution)/shard_map/ppermute | solution.py:34
  252.3 7.0 %collective-permute-start.5 = (f32[40,512]{1,0:T(8,128)S(1)}, f32[40,512]{1,0:T(8,128)S(1)}, u32[]{:S(2)}, u32[]{:S(2)}) collective-permute-start(f32[40,512]{1,0:T(8,128)S(1)} %add.327), channel_id=1, source_target_pairs={{0,64},{32,96},{64,0},{96,32},{128,192},{160,224},{192,128},{224,1... | collective-permute-start | bytes 245768 | tf_op jit(solution)/shard_map/ppermute | solution.py:34
  259.3 14.5 %collective-permute-start.6 = (f32[40,512]{1,0:T(8,128)S(1)}, f32[40,512]{1,0:T(8,128)S(1)}, u32[]{:S(2)}, u32[]{:S(2)}) collective-permute-start(f32[40,512]{1,0:T(8,128)S(1)} %add.328), channel_id=1, source_target_pairs={{0,128},{32,160},{64,192},{96,224},{128,0},{160,32},{192,64},{224,... | collective-permute-start | bytes 245768 | tf_op jit(solution)/shard_map/ppermute | solution.py:34
  273.8 19.4 %collective-permute-start.7 = (f32[40,512]{1,0:T(8,128)S(1)}, f32[40,512]{1,0:T(8,128)S(1)}, u32[]{:S(2)}, u32[]{:S(2)}) collective-permute-start(f32[40,512]{1,0:T(8,128)S(1)} %add.329), channel_id=1, source_target_pairs={{0,256},{32,288},{64,320},{96,352},{128,384},{160,416},{192,448},{... | collective-permute-start | bytes 245768 | tf_op jit(solution)/shard_map/ppermute | solution.py:34
  293.3 6.5 %collective-permute-start.8 = (f32[32,512]{1,0:T(8,128)S(1)}, f32[32,512]{1,0:T(8,128)S(1)}, u32[]{:S(2)}, u32[]{:S(2)}) collective-permute-start(f32[32,512]{1,0:T(8,128)S(1)} %get-tuple-element.7), channel_id=1, source_target_pairs={{0,16},{1,17},{2,18},{3,19},{4,20},{5,21},{6,22},{7,23},{8,24},{9,... | collective-permute-start | bytes 196616 | tf_op jit(solution)/shard_map/ppermute | solution.py:38
  299.8 5.7 %collective-permute-start.9 = (f32[64,512]{1,0:T(8,128)S(1)}, f32[64,512]{1,0:T(8,128)S(1)}, u32[]{:S(2)}, u32[]{:S(2)}) collective-permute-start(f32[64,512]{1,0:T(8,128)S(1)} %constant_dynamic-update-slice_fusion.7), channel_id=1, source_target_pairs={{0,8},{1,9},{2,10},{3,11},{4,12},{5,13},{6,14},{7,15},{8,0},{9,1},... | collective-permute-start | bytes 393224 | tf_op jit(solution)/shard_map/ppermute | solution.py:38
  305.5 8.6 %collective-permute-start.10 = (f32[128,512]{1,0:T(8,128)S(1)}, f32[128,512]{1,0:T(8,128)S(1)}, u32[]{:S(2)}, u32[]{:S(2)}) collective-permute-start(f32[128,512]{1,0:T(8,128)S(1)} %constant_dynamic-update-slice_fusion.5), channel_id=1, source_target_pairs={{0,4},{1,5},{2,6},{3,7},{4,0},{5,1},{6,2},{7,3},{8,12},{9,13},{10,... | collective-permute-start | bytes 786440 | tf_op jit(solution)/shard_map/ppermute | solution.py:38
  314.2 11.4 %collective-permute-start.11 = (f32[256,512]{1,0:T(8,128)S(1)}, f32[256,512]{1,0:T(8,128)S(1)}, u32[]{:S(2)}, u32[]{:S(2)}) collective-permute-start(f32[256,512]{1,0:T(8,128)S(1)} %constant_dynamic-update-slice_fusion.3), channel_id=1, source_target_pairs={{0,2},{1,3},{2,0},{3,1},{4,6},{5,7},{6,4},{7,5},{8,10},{9,11},{10,... | collective-permute-start | bytes 1572872 | tf_op jit(solution)/shard_map/ppermute | solution.py:38
  325.6 9.0 %collective-permute-start.12 = (f32[512,512]{1,0:T(8,128)S(1)}, f32[512,512]{1,0:T(8,128)S(1)}, u32[]{:S(2)}, u32[]{:S(2)}) collective-permute-start(f32[512,512]{1,0:T(8,128)S(1)} %constant_dynamic-update-slice_fusion.1), channel_id=1, source_target_pairs={{0,1},{1,0},{2,3},{3,2},{4,5},{5,4},{6,7},{7,6},{8,9},{9,8},{10,11... | collective-permute-start | bytes 3145736 | tf_op jit(solution)/shard_map/ppermute | solution.py:38
Sparse Core Ops, SparseCore 0:
  11.2 67.0 all-gather.1

commit v8 on v7

--- a/solution.py
+++ b/solution.py
@@ -137,21 +137,29 @@
     scale_factor = 1.0 / softness_divisor
     valid = jnp.arange(slots, dtype=jnp.int32)[None, :] < nbr_count[:, None]
     tiles = adj_tiles * valid[:, :, None, None].astype(jnp.bfloat16)
+    plan = route_plan(noise_block_rows)
+    noise_feats = route_forward(node_feats[:NOISE], plan)
     piece = lax.all_gather(source_feats, "col", axis=0, tiled=True)
+    piece, noise_feats = lax.optimization_barrier((piece, noise_feats))
     count = piece.shape[0] // BLOCK
     blocks = piece.reshape(count, BLOCK, width)
-    indicator_matrix = (
-        nbr_blocks[:, :, None] == jnp.arange(count, dtype=jnp.int32)[None, None, :]
-    ).astype(jnp.bfloat16)
-    selected = jnp.einsum(
-        "bkc,cjd->bkjd", indicator_matrix, blocks, preferred_element_type=jnp.float32
-    ).astype(jnp.bfloat16)
-    summed = jnp.einsum("bkij,bkjd->bid", tiles, selected, preferred_element_type=jnp.float32)
-    agg = summed.reshape(rows, width).astype(jnp.bfloat16)
-    plan = route_plan(noise_block_rows)
-    fetched = route_forward(jnp.concatenate([node_feats[:NOISE], agg[:NOISE]], axis=0), plan)
-    all_feats = jnp.concatenate([node_feats, fetched[:NOISE]], axis=0)
-    all_agg = jnp.concatenate([agg, fetched[NOISE:]], axis=0)
+
+    def aggregate(part_tiles, part_ids):
+        indicator_matrix = (
+            part_ids[:, :, None] == jnp.arange(count, dtype=jnp.int32)[None, None, :]
+        ).astype(jnp.bfloat16)
+        selected = jnp.einsum(
+            "bkc,cjd->bkjd", indicator_matrix, blocks, preferred_element_type=jnp.float32
+        ).astype(jnp.bfloat16)
+        summed = jnp.einsum("bkij,bkjd->bid", part_tiles, selected, preferred_element_type=jnp.float32)
+        return summed.reshape(-1, width).astype(jnp.bfloat16)
+
+    head = NOISE // BLOCK
+    agg_head = aggregate(tiles[:head], nbr_blocks[:head])
+    noise_agg = route_forward(agg_head, plan)
+    agg = jnp.concatenate([agg_head, aggregate(tiles[head:], nbr_blocks[head:])], axis=0)
+    all_feats = jnp.concatenate([node_feats, noise_feats], axis=0)
+    all_agg = jnp.concatenate([agg, noise_agg], axis=0)
     pre = jnp.dot(all_feats, w_self, preferred_element_type=jnp.float32) + jnp.dot(
         all_agg, w_neigh, preferred_element_type=jnp.float32
     )

time: 344 us -> 304 us (0.88)
  waiting for transfers between devices: 187 us -> 97.9 us
  starting transfers between devices: 71.1 us -> 107 us
  matrix products: 14.8 us -> 20.9 us
  blocking collectives: 39.3 us -> 44.4 us
    all_gather x1, waiting for transfers between devices: 69.6 us -> 0.02 us  [body(): piece = lax.all_gather(source_feats, 'col', axis=0, tiled=True)]
    ppermute x2 -> x4, starting transfers between devices: 18.6 us -> 43.3 us  [route_forward(): got = lax.ppermute(held, 'row', xor_pairs(size, m))]
    ppermute x2 -> x4, waiting for transfers between devices: 25.7 us -> 7.97 us  [route_forward(): got = lax.ppermute(held, 'row', xor_pairs(size, m))]
    ppermute x2 -> x4, starting transfers between devices: 16.2 us -> 26.9 us  [route_forward(): got = lax.ppermute(send, 'row', xor_pairs(size, m))]
    dot_general x2 -> x4, matrix products: 8.16 us -> 14.2 us  [the longest x2 9.51 us: aggregate(): jnp.einsum('bkc,cjd->bkjd', indicator_matrix, blocks, preferred_element_t...]
    all_to_all x1, blocking collectives: 39.3 us -> 44.4 us  [tree_allreduce(): joined = lax.all_to_all(chunks, 'col', 0, 0, tiled=False).sum(axis=0)]
    ppermute x2 -> x4, waiting for transfers between devices: 40.8 us -> 40.4 us  [route_forward(): got = lax.ppermute(send, 'row', xor_pairs(size, m))]
  transfers between devices with their start and end apart: 14 -> 18, of which waited for: 14 -> 17; matrix products, arithmetic and copies ran while one was open for 1% -> 5% of each run, Pallas kernels for 0% -> 0%
where the time goes in v8:
time: 304 us; the launch traced here: 303 us
  starting transfers between devices  107 us (35%)
  waiting for transfers between devices  97.9 us (32%)
  blocking collectives  44.4 us (15%)
  matrix products  20.9 us (7%)
  between operations  18.9 us (6%)
  local copies, waits for them, and re-layouts  10.1 us (3%)
  other arithmetic  4 us (1%)
    all_to_all x1, blocking collectives, tree_allreduce(): joined = lax.all_to_all(chunks, 'col', 0, 0, tiled=False).sum(axis=0)  44.4 us
    ppermute x4, starting transfers between devices, route_forward(): got = lax.ppermute(held, 'row', xor_pairs(size, m))  43.3 us
    ppermute x4, waiting for transfers between devices, route_forward(): got = lax.ppermute(send, 'row', xor_pairs(size, m))  40.4 us
    ppermute x4, waiting for transfers between devices, tree_allreduce(): joined = joined + lax.ppermute(joined, axis, xor_pairs(size, mask))  27.1 us
    ppermute x4, starting transfers between devices, route_forward(): got = lax.ppermute(send, 'row', xor_pairs(size, m))  26.9 us
    ppermute x5, waiting for transfers between devices, tree_allreduce(): got = lax.ppermute(buf, 'col', xor_pairs(ways, mask))  21.7 us
    ppermute x5, starting transfers between devices, tree_allreduce(): got = lax.ppermute(buf, 'col', xor_pairs(ways, mask))  19.3 us
    ppermute x4, starting transfers between devices, tree_allreduce(): joined = joined + lax.ppermute(joined, axis, xor_pairs(size, mask))  17.5 us
  transfers between devices with their start and end apart: 18, of which 17 were waited for; matrix products, arithmetic and copies ran while one was open for 5% of the time, Pallas kernels for 0%

profile of v8, /device:TPU:1, one launch (start us, length us, event | category | flops | bytes accessed | tf_op | source)
XLA Modules:
  0.0 303.4 jit_solution(15217126742418558460)
XLA Ops:
  8.9 16.3 %collective-permute-start = (bf16[1,128,512]{2,1,0:T(8,128)(2,1)S(1)}, bf16[1,128,512]{2,1,0:T(8,128)(2,1)S(1)}, u32[]{:S(2)}, u32[]{:S(2)}) collective-permute-start(bf16[1,128,512]{2,1,0:T(8,128)(2,1)S(1)} %slice_bitcast_fusion.6), channel_id=1, source_target_pairs={{0,256},{32,288},{64,320},{96,352},{128,384},{160,416},{192,448},{... | collective-permute-start | bytes 393224 | tf_op jit(solution)/shard_map/ppermute | solution.py:76
  27.8 11.6 %collective-permute-start.1 = (bf16[2,128,512]{2,1,0:T(8,128)(2,1)S(1)}, bf16[2,128,512]{2,1,0:T(8,128)(2,1)S(1)}, u32[]{:S(2)}, u32[]{:S(2)}) collective-permute-start(bf16[2,128,512]{2,1,0:T(8,128)(2,1)S(1)} %maximum_select_fusion.2), channel_id=1, source_target_pairs={{0,32},{32,0},{64,96},{96,64},{128,160},{160,128},{192,224},{224,1... | collective-permute-start | bytes 786440 | tf_op jit(solution)/shard_map/ppermute | solution.py:76
  42.8 1.9 collective-permute-done.1
  47.7 13.5 %collective-permute-done.2 = bf16[2,128,512]{2,1,0:T(8,128)(2,1)S(1)} collective-permute-done((bf16[2,128,512]{2,1,0:T(8,128)(2,1)S(1)}, bf16[2,128,512]{2,1,0:T(8,128)(2,1)S(1)}, u32[]{:S(2)}, u32[]{:S(2)}) %collective-permute-start.2) | collective-permute-done | bytes 262176 | tf_op jit(solution)/shard_map/ppermute | solution.py:86
  61.3 8.1 %collective-permute-start.3 = (bf16[1,128,512]{2,1,0:T(8,128)(2,1)S(1)}, bf16[1,128,512]{2,1,0:T(8,128)(2,1)S(1)}, u32[]{:S(2)}, u32[]{:S(2)}) collective-permute-start(bf16[1,128,512]{2,1,0:T(8,128)(2,1)S(1)} %select_bitcast_fusion.3), channel_id=1, source_target_pairs={{0,128},{32,160},{64,192},{96,224},{128,0},{160,32},{192,64},{224,... | collective-permute-start | bytes 393224 | tf_op jit(solution)/shard_map/ppermute | solution.py:86
  69.5 10.8 %collective-permute-done.3 = bf16[1,128,512]{2,1,0:T(8,128)(2,1)S(1)} collective-permute-done((bf16[1,128,512]{2,1,0:T(8,128)(2,1)S(1)}, bf16[1,128,512]{2,1,0:T(8,128)(2,1)S(1)}, u32[]{:S(2)}, u32[]{:S(2)}) %collective-permute-start.3) | collective-permute-done | bytes 131104 | tf_op jit(solution)/shard_map/ppermute | solution.py:86
  80.3 4.7 %fusion.2 = bf16[8,128,512]{2,0,1:T(8,128)(2,1)S(1)} fusion(bf16[32,128,512]{2,1,0:T(8,128)(2,1)} %bitcast.103, s32[8]{0:T(128)S(1)} %slice_bitcast_fusion.7), kind=kOutput, calls=%fused_computation.8 | convolution fusion | flops 33554688 | bytes 5242912 | tf_op jit(solution)/shard_map/bkc,cjd->bkjd/dot_general | solution.py:151
  85.8 11.2 %collective-permute-start.4 = (bf16[1,128,512]{2,1,0:T(8,128)(2,1)S(1)}, bf16[1,128,512]{2,1,0:T(8,128)(2,1)S(1)}, u32[]{:S(2)}, u32[]{:S(2)}) collective-permute-start(bf16[1,128,512]{2,1,0:T(8,128)(2,1)S(1)} %bitcast.110), channel_id=1, source_target_pairs={{0,256},{32,288},{64,320},{96,352},{128,384},{160,416},{192,448},{... | collective-permute-start | bytes 393224 | tf_op jit(solution)/shard_map/ppermute | solution.py:76
  97.1 3.9 %collective-permute-done.4 = bf16[1,128,512]{2,1,0:T(8,128)(2,1)S(1)} collective-permute-done((bf16[1,128,512]{2,1,0:T(8,128)(2,1)S(1)}, bf16[1,128,512]{2,1,0:T(8,128)(2,1)S(1)}, u32[]{:S(2)}, u32[]{:S(2)}) %collective-permute-start.4) | collective-permute-done | bytes 131104 | tf_op jit(solution)/shard_map/ppermute | solution.py:76
  101.0 4.2 %collective-permute-start.5 = (bf16[2,128,512]{2,1,0:T(8,128)(2,1)S(1)}, bf16[2,128,512]{2,1,0:T(8,128)(2,1)S(1)}, u32[]{:S(2)}, u32[]{:S(2)}) collective-permute-start(bf16[2,128,512]{2,1,0:T(8,128)(2,1)S(1)} %maximum_select_fusion.3), channel_id=1, source_target_pairs={{0,32},{32,0},{64,96},{96,64},{128,160},{160,128},{192,224},{224,1... | collective-permute-start | bytes 786440 | tf_op jit(solution)/shard_map/ppermute | solution.py:76
  105.3 4.8 %fusion = bf16[3,8,128,512]{3,1,2,0:T(8,128)(2,1)} fusion(bf16[32,128,512,1]{2,1,0,3:T(8,128)(2,1)S(1)} %bitcast.104, s32[3,8]{1,0:T(4,128)S(1)} %slice.79), kind=kOutput, calls=%fused_computation.6 | convolution fusion | flops 100664064 | bytes 7340128 | tf_op jit(solution)/shard_map/bkc,cjd->bkjd/dot_general | solution.py:151
  112.5 7.1 %collective-permute-start.6 = (bf16[2,128,512]{2,1,0:T(8,128)(2,1)S(1)}, bf16[2,128,512]{2,1,0:T(8,128)(2,1)S(1)}, u32[]{:S(2)}, u32[]{:S(2)}) collective-permute-start(bf16[2,128,512]{2,1,0:T(8,128)(2,1)S(1)} %select_bitcast_fusion), channel_id=1, source_target_pairs={{0,64},{32,96},{64,0},{96,32},{128,192},{160,224},{192,128},{224,1... | collective-permute-start | bytes 786440 | tf_op jit(solution)/shard_map/ppermute | solution.py:86
  119.6 4.0 %fusion.8 = bf16[3,128,512]{2,1,0:T(8,128)(2,1)S(1)} fusion(bf16[4,8,128,128]{3,2,1,0:T(8,128)(2,1)S(1)} %copy-done.5, bf16[3,8,128,512]{3,1,2,0:T(8,128)(2,1)} %fusion), kind=kOutput, calls=%fused_computation.26 | convolution fusion | flops 402849792 | bytes 4587520 | tf_op jit(solution)/shard_map/bkij,bkjd->bid/dot_general | solution.py:154
  123.6 6.9 %collective-permute-done.6 = bf16[2,128,512]{2,1,0:T(8,128)(2,1)S(1)} collective-permute-done((bf16[2,128,512]{2,1,0:T(8,128)(2,1)S(1)}, bf16[2,128,512]{2,1,0:T(8,128)(2,1)S(1)}, u32[]{:S(2)}, u32[]{:S(2)}) %collective-permute-start.6) | collective-permute-done | bytes 262176 | tf_op jit(solution)/shard_map/ppermute | solution.py:86
  130.7 9.8 %collective-permute-start.7 = (bf16[1,128,512]{2,1,0:T(8,128)(2,1)S(1)}, bf16[1,128,512]{2,1,0:T(8,128)(2,1)S(1)}, u32[]{:S(2)}, u32[]{:S(2)}) collective-permute-start(bf16[1,128,512]{2,1,0:T(8,128)(2,1)S(1)} %select_bitcast_fusion.2), channel_id=1, source_target_pairs={{0,128},{32,160},{64,192},{96,224},{128,0},{160,32},{192,64},{224,... | collective-permute-start | bytes 393224 | tf_op jit(solution)/shard_map/ppermute | solution.py:86
  141.2 9.2 %collective-permute-done.7 = bf16[1,128,512]{2,1,0:T(8,128)(2,1)S(1)} collective-permute-done((bf16[1,128,512]{2,1,0:T(8,128)(2,1)S(1)}, bf16[1,128,512]{2,1,0:T(8,128)(2,1)S(1)}, u32[]{:S(2)}, u32[]{:S(2)}) %collective-permute-start.7) | collective-permute-done | bytes 131104 | tf_op jit(solution)/shard_map/ppermute | solution.py:86
  160.5 2.3 gather_fusion.2
  163.1 44.4 %all_to_all.5 = f32[32,40,512]{2,1,0:T(8,128)S(1)} all-to-all(f32[32,40,512]{2,1,0:T(8,128)S(1)} %concatenate.51), channel_id=1, replica_groups=mesh['row'=16,'col'=32] {'col'}, dimensions={0} | all-to-all | bytes 5242880 | tf_op jit(solution)/shard_map/all_to_all | solution.py:29
  209.6 3.3 %collective-permute-done.8 = f32[40,512]{1,0:T(8,128)S(1)} collective-permute-done((f32[40,512]{1,0:T(8,128)S(1)}, f32[40,512]{1,0:T(8,128)S(1)}, u32[]{:S(2)}, u32[]{:S(2)}) %collective-permute-start.8) | collective-permute-done | bytes 81952 | tf_op jit(solution)/shard_map/ppermute | solution.py:34
  212.8 2.1 collective-permute-start.9
  215.0 4.8 %collective-permute-done.9 = f32[40,512]{1,0:T(8,128)S(1)} collective-permute-done((f32[40,512]{1,0:T(8,128)S(1)}, f32[40,512]{1,0:T(8,128)S(1)}, u32[]{:S(2)}, u32[]{:S(2)}) %collective-permute-start.9) | collective-permute-done | bytes 81952 | tf_op jit(solution)/shard_map/ppermute | solution.py:34
  219.8 6.4 %collective-permute-start.10 = (f32[40,512]{1,0:T(8,128)S(1)}, f32[40,512]{1,0:T(8,128)S(1)}, u32[]{:S(2)}, u32[]{:S(2)}) collective-permute-start(f32[40,512]{1,0:T(8,128)S(1)} %add.265), channel_id=1, source_target_pairs={{0,128},{32,160},{64,192},{96,224},{128,0},{160,32},{192,64},{224,... | collective-permute-start | bytes 245768 | tf_op jit(solution)/shard_map/ppermute | solution.py:34
  226.2 8.6 %collective-permute-done.10 = f32[40,512]{1,0:T(8,128)S(1)} collective-permute-done((f32[40,512]{1,0:T(8,128)S(1)}, f32[40,512]{1,0:T(8,128)S(1)}, u32[]{:S(2)}, u32[]{:S(2)}) %collective-permute-start.10) | collective-permute-done | bytes 81952 | tf_op jit(solution)/shard_map/ppermute | solution.py:34
  234.8 7.1 %collective-permute-start.11 = (f32[40,512]{1,0:T(8,128)S(1)}, f32[40,512]{1,0:T(8,128)S(1)}, u32[]{:S(2)}, u32[]{:S(2)}) collective-permute-start(f32[40,512]{1,0:T(8,128)S(1)} %add.266), channel_id=1, source_target_pairs={{0,256},{32,288},{64,320},{96,352},{128,384},{160,416},{192,448},{... | collective-permute-start | bytes 245768 | tf_op jit(solution)/shard_map/ppermute | solution.py:34
  241.9 10.4 %collective-permute-done.11 = f32[40,512]{1,0:T(8,128)S(1)} collective-permute-done((f32[40,512]{1,0:T(8,128)S(1)}, f32[40,512]{1,0:T(8,128)S(1)}, u32[]{:S(2)}, u32[]{:S(2)}) %collective-permute-start.11) | collective-permute-done | bytes 81952 | tf_op jit(solution)/shard_map/ppermute | solution.py:34
  252.4 5.5 %collective-permute-start.12 = (f32[32,512]{1,0:T(8,128)S(1)}, f32[32,512]{1,0:T(8,128)S(1)}, u32[]{:S(2)}, u32[]{:S(2)}) collective-permute-start(f32[32,512]{1,0:T(8,128)S(1)} %get-tuple-element.12), channel_id=1, source_target_pairs={{0,16},{1,17},{2,18},{3,19},{4,20},{5,21},{6,22},{7,23},{8,24},{9,... | collective-permute-start | bytes 196616 | tf_op jit(solution)/shard_map/ppermute | solution.py:38
  258.0 2.0 collective-permute-done.12
  260.0 3.4 %collective-permute-start.13 = (f32[64,512]{1,0:T(8,128)S(1)}, f32[64,512]{1,0:T(8,128)S(1)}, u32[]{:S(2)}, u32[]{:S(2)}) collective-permute-start(f32[64,512]{1,0:T(8,128)S(1)} %constant_dynamic-update-slice_fusion.9), channel_id=1, source_target_pairs={{0,8},{1,9},{2,10},{3,11},{4,12},{5,13},{6,14},{7,15},{8,0},{9,1},... | collective-permute-start | bytes 393224 | tf_op jit(solution)/shard_map/ppermute | solution.py:38
  263.6 2.3 collective-permute-done.13
  267.9 6.6 %collective-permute-done.14 = f32[128,512]{1,0:T(8,128)S(1)} collective-permute-done((f32[128,512]{1,0:T(8,128)S(1)}, f32[128,512]{1,0:T(8,128)S(1)}, u32[]{:S(2)}, u32[]{:S(2)}) %collective-permute-start.14) | collective-permute-done | bytes 262176 | tf_op jit(solution)/shard_map/ppermute | solution.py:38
  276.6 9.5 %collective-permute-done.15 = f32[256,512]{1,0:T(8,128)S(1)} collective-permute-done((f32[256,512]{1,0:T(8,128)S(1)}, f32[256,512]{1,0:T(8,128)S(1)}, u32[]{:S(2)}, u32[]{:S(2)}) %collective-permute-start.15) | collective-permute-done | bytes 524320 | tf_op jit(solution)/shard_map/ppermute | solution.py:38
  286.2 6.5 %collective-permute-start.16 = (f32[512,512]{1,0:T(8,128)S(1)}, f32[512,512]{1,0:T(8,128)S(1)}, u32[]{:S(2)}, u32[]{:S(2)}) collective-permute-start(f32[512,512]{1,0:T(8,128)S(1)} %constant_dynamic-update-slice_fusion.3), channel_id=1, source_target_pairs={{0,1},{1,0},{2,3},{3,2},{4,5},{5,4},{6,7},{7,6},{8,9},{9,8},{10,11... | collective-permute-start | bytes 3145736 | tf_op jit(solution)/shard_map/ppermute | solution.py:38
  (108 shorter events, 31.2 us)
Async XLA Ops:
  7.2 143.2 %copy-start = (bf16[512,512]{1,0:T(8,128)(2,1)S(1)}, bf16[512,512]{1,0:T(8,128)(2,1)}, u32[]{:S(2)}) copy-start(bf16[512,512]{1,0:T(8,128)(2,1)} %param.20) | copy-start | bytes 1572868
  7.2 19.4 %copy-start.1 = (s32[16]{0:T(128)S(1)}, s32[16]{0:T(128)}, u32[]{:S(2)}) copy-start(s32[16]{0:T(128)} %param.18) | copy-start | bytes 196
  7.2 35.5 %copy-start.11 = (s32[4]{0:T(128)S(1)}, s32[4]{0:T(128)}, u32[]{:S(2)}) copy-start(s32[4]{0:T(128)} %param.15) | copy-start | bytes 52
  7.2 73.1 %all-gather.2.cloned.1.call-start = ((), (), s32[]{:S(2)}) async-start(), calls=%async_computation.1 | async-start | bytes 4325376 | tf_op jit(solution)/shard_map/all_gather | solution.py:142
  8.9 18.9 %collective-permute-start = (bf16[1,128,512]{2,1,0:T(8,128)(2,1)S(1)}, bf16[1,128,512]{2,1,0:T(8,128)(2,1)S(1)}, u32[]{:S(2)}, u32[]{:S(2)}) collective-permute-start(bf16[1,128,512]{2,1,0:T(8,128)(2,1)S(1)} %slice_bitcast_fusion.6), channel_id=1, source_target_pairs={{0,256},{32,288},{64,320},{96,352},{128,384},{160,416},{192,448},{... | collective-permute-start | bytes 393224 | tf_op jit(solution)/shard_map/ppermute | solution.py:76
  27.8 16.9 %collective-permute-start.1 = (bf16[2,128,512]{2,1,0:T(8,128)(2,1)S(1)}, bf16[2,128,512]{2,1,0:T(8,128)(2,1)S(1)}, u32[]{:S(2)}, u32[]{:S(2)}) collective-permute-start(bf16[2,128,512]{2,1,0:T(8,128)(2,1)S(1)} %maximum_select_fusion.2), channel_id=1, source_target_pairs={{0,32},{32,0},{64,96},{96,64},{128,160},{160,128},{192,224},{224,1... | collective-permute-start | bytes 786440 | tf_op jit(solution)/shard_map/ppermute | solution.py:76
  44.8 2.7 copy-start.3
  45.6 23.9 %copy-start.9 = (s32[4,8]{1,0:T(4,128)S(1)}, s32[4,8]{1,0:T(4,128)}, u32[]{:S(2)}) copy-start(s32[4,8]{1,0:T(4,128)} %param.14) | copy-start | bytes 388
  45.6 15.6 %collective-permute-start.2 = (bf16[2,128,512]{2,1,0:T(8,128)(2,1)S(1)}, bf16[2,128,512]{2,1,0:T(8,128)(2,1)S(1)}, u32[]{:S(2)}, u32[]{:S(2)}) collective-permute-start(bf16[2,128,512]{2,1,0:T(8,128)(2,1)S(1)} %select_bitcast_fusion.1), channel_id=1, source_target_pairs={{0,64},{32,96},{64,0},{96,32},{128,192},{160,224},{192,128},{224,1... | collective-permute-start | bytes 786440 | tf_op jit(solution)/shard_map/ppermute | solution.py:86
  47.7 37.4 %copy-start.4 = (bf16[4,8,128,128]{3,2,1,0:T(8,128)(2,1)}, bf16[4,8,128,128]{3,2,1,0:T(8,128)(2,1)S(1)}, u32[]{:S(2)}) copy-start(bf16[4,8,128,128]{3,2,1,0:T(8,128)(2,1)S(1)} %broadcast_multiply_fusion) | copy-start | bytes 3145732
  61.3 18.9 %collective-permute-start.3 = (bf16[1,128,512]{2,1,0:T(8,128)(2,1)S(1)}, bf16[1,128,512]{2,1,0:T(8,128)(2,1)S(1)}, u32[]{:S(2)}, u32[]{:S(2)}) collective-permute-start(bf16[1,128,512]{2,1,0:T(8,128)(2,1)S(1)} %select_bitcast_fusion.3), channel_id=1, source_target_pairs={{0,128},{32,160},{64,192},{96,224},{128,0},{160,32},{192,64},{224,... | collective-permute-start | bytes 393224 | tf_op jit(solution)/shard_map/ppermute | solution.py:86
  80.3 24.9 %copy-start.2 = (bf16[4096,512]{1,0:T(8,128)(2,1)S(1)}, bf16[4096,512]{1,0:T(8,128)(2,1)}, u32[]{:S(2)}) copy-start(bf16[4096,512]{1,0:T(8,128)(2,1)} %all-gather.2.cloned.1.call-done) | copy-start | bytes 12582916
  85.0 11.9 %copy-start.10 = (s32[32]{0:T(128)S(1)}, s32[32]{0:T(128)}, u32[]{:S(2)}) copy-start(s32[32]{0:T(128)} %constant.303) | copy-start | bytes 388
  85.1 12.0 %copy-start.6 = (bf16[512,512]{1,0:T(8,128)(2,1)S(1)}, bf16[512,512]{1,0:T(8,128)(2,1)}, u32[]{:S(2)}) copy-start(bf16[512,512]{1,0:T(8,128)(2,1)} %param.12) | copy-start | bytes 1572868
  85.8 15.2 %collective-permute-start.4 = (bf16[1,128,512]{2,1,0:T(8,128)(2,1)S(1)}, bf16[1,128,512]{2,1,0:T(8,128)(2,1)S(1)}, u32[]{:S(2)}, u32[]{:S(2)}) collective-permute-start(bf16[1,128,512]{2,1,0:T(8,128)(2,1)S(1)} %bitcast.110), channel_id=1, source_target_pairs={{0,256},{32,288},{64,320},{96,352},{128,384},{160,416},{192,448},{... | collective-permute-start | bytes 393224 | tf_op jit(solution)/shard_map/ppermute | solution.py:76
  101.0 10.7 %collective-permute-start.5 = (bf16[2,128,512]{2,1,0:T(8,128)(2,1)S(1)}, bf16[2,128,512]{2,1,0:T(8,128)(2,1)S(1)}, u32[]{:S(2)}, u32[]{:S(2)}) collective-permute-start(bf16[2,128,512]{2,1,0:T(8,128)(2,1)S(1)} %maximum_select_fusion.3), channel_id=1, source_target_pairs={{0,32},{32,0},{64,96},{96,64},{128,160},{160,128},{192,224},{224,1... | collective-permute-start | bytes 786440 | tf_op jit(solution)/shard_map/ppermute | solution.py:76
  111.8 7.8 %copy-start.5 = (bf16[4,8,128,128]{3,2,1,0:T(8,128)(2,1)S(1)}, bf16[4,8,128,128]{3,2,1,0:T(8,128)(2,1)}, u32[]{:S(2)}) copy-start(bf16[4,8,128,128]{3,2,1,0:T(8,128)(2,1)} %copy-done.4) | copy-start | bytes 3145732
  112.5 18.0 %collective-permute-start.6 = (bf16[2,128,512]{2,1,0:T(8,128)(2,1)S(1)}, bf16[2,128,512]{2,1,0:T(8,128)(2,1)S(1)}, u32[]{:S(2)}, u32[]{:S(2)}) collective-permute-start(bf16[2,128,512]{2,1,0:T(8,128)(2,1)S(1)} %select_bitcast_fusion), channel_id=1, source_target_pairs={{0,64},{32,96},{64,0},{96,32},{128,192},{160,224},{192,128},{224,1... | collective-permute-start | bytes 786440 | tf_op jit(solution)/shard_map/ppermute | solution.py:86
  123.6 16.9 %copy-start.7 = (bf16[512,512]{1,0:T(8,128)(2,1)S(1)}, bf16[512,512]{1,0:T(8,128)(2,1)}, u32[]{:S(2)}) copy-start(bf16[512,512]{1,0:T(8,128)(2,1)} %param.19) | copy-start | bytes 1572868
  130.7 19.6 %collective-permute-start.7 = (bf16[1,128,512]{2,1,0:T(8,128)(2,1)S(1)}, bf16[1,128,512]{2,1,0:T(8,128)(2,1)S(1)}, u32[]{:S(2)}, u32[]{:S(2)}) collective-permute-start(bf16[1,128,512]{2,1,0:T(8,128)(2,1)S(1)} %select_bitcast_fusion.2), channel_id=1, source_target_pairs={{0,128},{32,160},{64,192},{96,224},{128,0},{160,32},{192,64},{224,... | collective-permute-start | bytes 393224 | tf_op jit(solution)/shard_map/ppermute | solution.py:86
  151.0 1.1 copy-start.8
  207.6 5.2 %collective-permute-start.8 = (f32[40,512]{1,0:T(8,128)S(1)}, f32[40,512]{1,0:T(8,128)S(1)}, u32[]{:S(2)}, u32[]{:S(2)}) collective-permute-start(f32[40,512]{1,0:T(8,128)S(1)} %reduce_sum.63), channel_id=1, source_target_pairs={{0,32},{32,0},{64,96},{96,64},{128,160},{160,128},{192,224},{224,1... | collective-permute-start | bytes 245768 | tf_op jit(solution)/shard_map/ppermute | solution.py:34
  212.8 7.0 %collective-permute-start.9 = (f32[40,512]{1,0:T(8,128)S(1)}, f32[40,512]{1,0:T(8,128)S(1)}, u32[]{:S(2)}, u32[]{:S(2)}) collective-permute-start(f32[40,512]{1,0:T(8,128)S(1)} %add.264), channel_id=1, source_target_pairs={{0,64},{32,96},{64,0},{96,32},{128,192},{160,224},{192,128},{224,1... | collective-permute-start | bytes 245768 | tf_op jit(solution)/shard_map/ppermute | solution.py:34
  219.8 15.0 %collective-permute-start.10 = (f32[40,512]{1,0:T(8,128)S(1)}, f32[40,512]{1,0:T(8,128)S(1)}, u32[]{:S(2)}, u32[]{:S(2)}) collective-permute-start(f32[40,512]{1,0:T(8,128)S(1)} %add.265), channel_id=1, source_target_pairs={{0,128},{32,160},{64,192},{96,224},{128,0},{160,32},{192,64},{224,... | collective-permute-start | bytes 245768 | tf_op jit(solution)/shard_map/ppermute | solution.py:34
  234.8 17.5 %collective-permute-start.11 = (f32[40,512]{1,0:T(8,128)S(1)}, f32[40,512]{1,0:T(8,128)S(1)}, u32[]{:S(2)}, u32[]{:S(2)}) collective-permute-start(f32[40,512]{1,0:T(8,128)S(1)} %add.266), channel_id=1, source_target_pairs={{0,256},{32,288},{64,320},{96,352},{128,384},{160,416},{192,448},{... | collective-permute-start | bytes 245768 | tf_op jit(solution)/shard_map/ppermute | solution.py:34
  252.4 7.6 %collective-permute-start.12 = (f32[32,512]{1,0:T(8,128)S(1)}, f32[32,512]{1,0:T(8,128)S(1)}, u32[]{:S(2)}, u32[]{:S(2)}) collective-permute-start(f32[32,512]{1,0:T(8,128)S(1)} %get-tuple-element.12), channel_id=1, source_target_pairs={{0,16},{1,17},{2,18},{3,19},{4,20},{5,21},{6,22},{7,23},{8,24},{9,... | collective-permute-start | bytes 196616 | tf_op jit(solution)/shard_map/ppermute | solution.py:38
  260.0 5.8 %collective-permute-start.13 = (f32[64,512]{1,0:T(8,128)S(1)}, f32[64,512]{1,0:T(8,128)S(1)}, u32[]{:S(2)}, u32[]{:S(2)}) collective-permute-start(f32[64,512]{1,0:T(8,128)S(1)} %constant_dynamic-update-slice_fusion.9), channel_id=1, source_target_pairs={{0,8},{1,9},{2,10},{3,11},{4,12},{5,13},{6,14},{7,15},{8,0},{9,1},... | collective-permute-start | bytes 393224 | tf_op jit(solution)/shard_map/ppermute | solution.py:38
  265.8 8.6 %collective-permute-start.14 = (f32[128,512]{1,0:T(8,128)S(1)}, f32[128,512]{1,0:T(8,128)S(1)}, u32[]{:S(2)}, u32[]{:S(2)}) collective-permute-start(f32[128,512]{1,0:T(8,128)S(1)} %constant_dynamic-update-slice_fusion.7), channel_id=1, source_target_pairs={{0,4},{1,5},{2,6},{3,7},{4,0},{5,1},{6,2},{7,3},{8,12},{9,13},{10,... | collective-permute-start | bytes 786440 | tf_op jit(solution)/shard_map/ppermute | solution.py:38
  274.5 11.7 %collective-permute-start.15 = (f32[256,512]{1,0:T(8,128)S(1)}, f32[256,512]{1,0:T(8,128)S(1)}, u32[]{:S(2)}, u32[]{:S(2)}) collective-permute-start(f32[256,512]{1,0:T(8,128)S(1)} %constant_dynamic-update-slice_fusion.5), channel_id=1, source_target_pairs={{0,2},{1,3},{2,0},{3,1},{4,6},{5,7},{6,4},{7,5},{8,10},{9,11},{10,... | collective-permute-start | bytes 1572872 | tf_op jit(solution)/shard_map/ppermute | solution.py:38
  286.2 8.8 %collective-permute-start.16 = (f32[512,512]{1,0:T(8,128)S(1)}, f32[512,512]{1,0:T(8,128)S(1)}, u32[]{:S(2)}, u32[]{:S(2)}) collective-permute-start(f32[512,512]{1,0:T(8,128)S(1)} %constant_dynamic-update-slice_fusion.3), channel_id=1, source_target_pairs={{0,1},{1,0},{2,3},{3,2},{4,5},{5,4},{6,7},{7,6},{8,9},{9,8},{10,11... | collective-permute-start | bytes 3145736 | tf_op jit(solution)/shard_map/ppermute | solution.py:38
Sparse Core Ops, SparseCore 0:
  11.2 67.0 all-gather.1

commit v9 on v8

--- a/solution.py
+++ b/solution.py
@@ -25,8 +25,8 @@
     position = [sum(((j // mask) % 2) << t for t, mask in enumerate(masks)) for j in range(ways)]
     rows = buf.shape[0] // ways
     chunks = buf.reshape(ways, rows, buf.shape[1])[jnp.array(position, jnp.int32)]
-    chunks = jnp.concatenate([chunks, jnp.broadcast_to(extra[None], (ways,) + extra.shape)], axis=1)
-    joined = lax.all_to_all(chunks, "col", 0, 0, tiled=False).sum(axis=0)
+    scattered = lax.all_to_all(chunks, "col", 0, 0, tiled=False).sum(axis=0)
+    joined = jnp.concatenate([scattered, extra], axis=0)
     for axis, mask in BUTTERFLY:
         size = lax.axis_size(axis)
         if mask >= size:
@@ -35,11 +35,12 @@
     buf, extra = joined[:rows], joined[rows:]
     for mask in masks:
         bit = (me // mask) % 2
-        got = lax.ppermute(buf, "col", xor_pairs(ways, mask))
         held = buf.shape[0]
+        got = lax.ppermute(jnp.concatenate([buf, extra], axis=0), "col", xor_pairs(ways, mask))
+        extra = extra + got[held:]
         out = jnp.zeros((2 * held,) + buf.shape[1:], buf.dtype)
         out = lax.dynamic_update_slice_in_dim(out, buf, bit * held, 0)
-        out = lax.dynamic_update_slice_in_dim(out, got, (1 - bit) * held, 0)
+        out = lax.dynamic_update_slice_in_dim(out, got[:held], (1 - bit) * held, 0)
         buf = out
     return buf, extra
 

time: 304 us -> 302 us (level)
  blocking collectives: 44.4 us -> 0 us
  waiting for transfers between devices: 97.9 us -> 120 us
  starting transfers between devices: 107 us -> 123 us
    all_to_all x1 -> x0, blocking collectives: 44.4 us -> none  [tree_allreduce(): joined = lax.all_to_all(chunks, 'col', 0, 0, tiled=False).sum(axis=0)]
    all_to_all x0 -> x1, waiting for transfers between devices: none -> 26.5 us  [tree_allreduce(): scattered = lax.all_to_all(chunks, 'col', 0, 0, tiled=False).sum(axis=0)]
    all_to_all x0 -> x1, starting transfers between devices: none -> 10.6 us  [tree_allreduce(): scattered = lax.all_to_all(chunks, 'col', 0, 0, tiled=False).sum(axis=0)]
    ppermute x5, starting transfers between devices: 19.3 us -> 27 us  [tree_allreduce(): lax.ppermute(jnp.concatenate([buf, extra], axis=0), 'col', xor_pairs(ways...]
    ppermute x4, waiting for transfers between devices: 27.1 us -> 23.6 us  [tree_allreduce(): joined = joined + lax.ppermute(joined, axis, xor_pairs(size, mask))]
  transfers between devices with their start and end apart: 18 -> 19, of which waited for: 17 -> 18; matrix products, arithmetic and copies ran while one was open for 5% -> 5% of each run, Pallas kernels for 0% -> 0%
where the time goes in v9:
time: 302 us; the launch traced here: 301 us
  starting transfers between devices  123 us (41%)
  waiting for transfers between devices  120 us (40%)
  between operations  21.4 us (7%)
  matrix products  20.9 us (7%)
  local copies, waits for them, and re-layouts  12 us (4%)
    ppermute x4, starting transfers between devices, route_forward(): got = lax.ppermute(held, 'row', xor_pairs(size, m))  43.3 us
    ppermute x4, waiting for transfers between devices, route_forward(): got = lax.ppermute(send, 'row', xor_pairs(size, m))  40.4 us
    ppermute x5, starting transfers between devices, tree_allreduce(): lax.ppermute(jnp.concatenate([buf, extra], axis=0), 'col', xor_pairs(ways...  27 us
    ppermute x4, starting transfers between devices, route_forward(): got = lax.ppermute(send, 'row', xor_pairs(size, m))  26.9 us
    all_to_all x1, waiting for transfers between devices, tree_allreduce(): scattered = lax.all_to_all(chunks, 'col', 0, 0, tiled=False).sum(axis=0)  26.5 us
    ppermute x4, waiting for transfers between devices, tree_allreduce(): joined = joined + lax.ppermute(joined, axis, xor_pairs(size, mask))  23.6 us
    ppermute x5, waiting for transfers between devices, tree_allreduce(): lax.ppermute(jnp.concatenate([buf, extra], axis=0), 'col', xor_pairs(ways...  21.1 us
    ppermute x4, starting transfers between devices, tree_allreduce(): joined = joined + lax.ppermute(joined, axis, xor_pairs(size, mask))  15.5 us
  transfers between devices with their start and end apart: 19, of which 18 were waited for; matrix products, arithmetic and copies ran while one was open for 5% of the time, Pallas kernels for 0%

profile of v9, /device:TPU:1, one launch (start us, length us, event | category | flops | bytes accessed | tf_op | source)
XLA Modules:
  0.0 300.7 jit_solution(5294569851676545023)
XLA Ops:
  8.9 16.3 %collective-permute-start = (bf16[1,128,512]{2,1,0:T(8,128)(2,1)S(1)}, bf16[1,128,512]{2,1,0:T(8,128)(2,1)S(1)}, u32[]{:S(2)}, u32[]{:S(2)}) collective-permute-start(bf16[1,128,512]{2,1,0:T(8,128)(2,1)S(1)} %slice_bitcast_fusion.6), channel_id=1, source_target_pairs={{0,256},{32,288},{64,320},{96,352},{128,384},{160,416},{192,448},{... | collective-permute-start | bytes 393224 | tf_op jit(solution)/shard_map/ppermute | solution.py:77
  27.8 11.6 %collective-permute-start.1 = (bf16[2,128,512]{2,1,0:T(8,128)(2,1)S(1)}, bf16[2,128,512]{2,1,0:T(8,128)(2,1)S(1)}, u32[]{:S(2)}, u32[]{:S(2)}) collective-permute-start(bf16[2,128,512]{2,1,0:T(8,128)(2,1)S(1)} %maximum_select_fusion.2), channel_id=1, source_target_pairs={{0,32},{32,0},{64,96},{96,64},{128,160},{160,128},{192,224},{224,1... | collective-permute-start | bytes 786440 | tf_op jit(solution)/shard_map/ppermute | solution.py:77
  42.8 1.9 collective-permute-done.1
  47.7 13.5 %collective-permute-done.2 = bf16[2,128,512]{2,1,0:T(8,128)(2,1)S(1)} collective-permute-done((bf16[2,128,512]{2,1,0:T(8,128)(2,1)S(1)}, bf16[2,128,512]{2,1,0:T(8,128)(2,1)S(1)}, u32[]{:S(2)}, u32[]{:S(2)}) %collective-permute-start.2) | collective-permute-done | bytes 262176 | tf_op jit(solution)/shard_map/ppermute | solution.py:87
  61.3 8.1 %collective-permute-start.3 = (bf16[1,128,512]{2,1,0:T(8,128)(2,1)S(1)}, bf16[1,128,512]{2,1,0:T(8,128)(2,1)S(1)}, u32[]{:S(2)}, u32[]{:S(2)}) collective-permute-start(bf16[1,128,512]{2,1,0:T(8,128)(2,1)S(1)} %select_bitcast_fusion.3), channel_id=1, source_target_pairs={{0,128},{32,160},{64,192},{96,224},{128,0},{160,32},{192,64},{224,... | collective-permute-start | bytes 393224 | tf_op jit(solution)/shard_map/ppermute | solution.py:87
  69.5 10.8 %collective-permute-done.3 = bf16[1,128,512]{2,1,0:T(8,128)(2,1)S(1)} collective-permute-done((bf16[1,128,512]{2,1,0:T(8,128)(2,1)S(1)}, bf16[1,128,512]{2,1,0:T(8,128)(2,1)S(1)}, u32[]{:S(2)}, u32[]{:S(2)}) %collective-permute-start.3) | collective-permute-done | bytes 131104 | tf_op jit(solution)/shard_map/ppermute | solution.py:87
  80.3 4.7 %fusion.2 = bf16[8,128,512]{2,0,1:T(8,128)(2,1)S(1)} fusion(bf16[32,128,512]{2,1,0:T(8,128)(2,1)} %bitcast.103, s32[8]{0:T(128)S(1)} %slice_bitcast_fusion.7), kind=kOutput, calls=%fused_computation.8 | convolution fusion | flops 33554688 | bytes 5242912 | tf_op jit(solution)/shard_map/bkc,cjd->bkjd/dot_general | solution.py:152
  85.8 11.2 %collective-permute-start.4 = (bf16[1,128,512]{2,1,0:T(8,128)(2,1)S(1)}, bf16[1,128,512]{2,1,0:T(8,128)(2,1)S(1)}, u32[]{:S(2)}, u32[]{:S(2)}) collective-permute-start(bf16[1,128,512]{2,1,0:T(8,128)(2,1)S(1)} %bitcast.110), channel_id=1, source_target_pairs={{0,256},{32,288},{64,320},{96,352},{128,384},{160,416},{192,448},{... | collective-permute-start | bytes 393224 | tf_op jit(solution)/shard_map/ppermute | solution.py:77
  97.1 3.9 %collective-permute-done.4 = bf16[1,128,512]{2,1,0:T(8,128)(2,1)S(1)} collective-permute-done((bf16[1,128,512]{2,1,0:T(8,128)(2,1)S(1)}, bf16[1,128,512]{2,1,0:T(8,128)(2,1)S(1)}, u32[]{:S(2)}, u32[]{:S(2)}) %collective-permute-start.4) | collective-permute-done | bytes 131104 | tf_op jit(solution)/shard_map/ppermute | solution.py:77
  101.0 4.2 %collective-permute-start.5 = (bf16[2,128,512]{2,1,0:T(8,128)(2,1)S(1)}, bf16[2,128,512]{2,1,0:T(8,128)(2,1)S(1)}, u32[]{:S(2)}, u32[]{:S(2)}) collective-permute-start(bf16[2,128,512]{2,1,0:T(8,128)(2,1)S(1)} %maximum_select_fusion.3), channel_id=1, source_target_pairs={{0,32},{32,0},{64,96},{96,64},{128,160},{160,128},{192,224},{224,1... | collective-permute-start | bytes 786440 | tf_op jit(solution)/shard_map/ppermute | solution.py:77
  105.3 4.8 %fusion = bf16[3,8,128,512]{3,1,2,0:T(8,128)(2,1)} fusion(bf16[32,128,512,1]{2,1,0,3:T(8,128)(2,1)S(1)} %bitcast.104, s32[3,8]{1,0:T(4,128)S(1)} %slice.111), kind=kOutput, calls=%fused_computation.6 | convolution fusion | flops 100664064 | bytes 7340128 | tf_op jit(solution)/shard_map/bkc,cjd->bkjd/dot_general | solution.py:152
  112.5 7.1 %collective-permute-start.6 = (bf16[2,128,512]{2,1,0:T(8,128)(2,1)S(1)}, bf16[2,128,512]{2,1,0:T(8,128)(2,1)S(1)}, u32[]{:S(2)}, u32[]{:S(2)}) collective-permute-start(bf16[2,128,512]{2,1,0:T(8,128)(2,1)S(1)} %select_bitcast_fusion), channel_id=1, source_target_pairs={{0,64},{32,96},{64,0},{96,32},{128,192},{160,224},{192,128},{224,1... | collective-permute-start | bytes 786440 | tf_op jit(solution)/shard_map/ppermute | solution.py:87
  119.6 4.0 %fusion.8 = bf16[3,128,512]{2,1,0:T(8,128)(2,1)S(1)} fusion(bf16[4,8,128,128]{3,2,1,0:T(8,128)(2,1)S(1)} %copy-done.5, bf16[3,8,128,512]{3,1,2,0:T(8,128)(2,1)} %fusion), kind=kOutput, calls=%fused_computation.26 | convolution fusion | flops 402849792 | bytes 4587520 | tf_op jit(solution)/shard_map/bkij,bkjd->bid/dot_general | solution.py:155
  123.6 6.9 %collective-permute-done.6 = bf16[2,128,512]{2,1,0:T(8,128)(2,1)S(1)} collective-permute-done((bf16[2,128,512]{2,1,0:T(8,128)(2,1)S(1)}, bf16[2,128,512]{2,1,0:T(8,128)(2,1)S(1)}, u32[]{:S(2)}, u32[]{:S(2)}) %collective-permute-start.6) | collective-permute-done | bytes 262176 | tf_op jit(solution)/shard_map/ppermute | solution.py:87
  130.7 9.8 %collective-permute-start.7 = (bf16[1,128,512]{2,1,0:T(8,128)(2,1)S(1)}, bf16[1,128,512]{2,1,0:T(8,128)(2,1)S(1)}, u32[]{:S(2)}, u32[]{:S(2)}) collective-permute-start(bf16[1,128,512]{2,1,0:T(8,128)(2,1)S(1)} %select_bitcast_fusion.2), channel_id=1, source_target_pairs={{0,128},{32,160},{64,192},{96,224},{128,0},{160,32},{192,64},{224,... | collective-permute-start | bytes 393224 | tf_op jit(solution)/shard_map/ppermute | solution.py:87
  141.2 9.2 %collective-permute-done.7 = bf16[1,128,512]{2,1,0:T(8,128)(2,1)S(1)} collective-permute-done((bf16[1,128,512]{2,1,0:T(8,128)(2,1)S(1)}, bf16[1,128,512]{2,1,0:T(8,128)(2,1)S(1)}, u32[]{:S(2)}, u32[]{:S(2)}) %collective-permute-start.7) | collective-permute-done | bytes 131104 | tf_op jit(solution)/shard_map/ppermute | solution.py:87
  157.9 2.0 gather_fusion.2
  159.9 10.6 %all-to-all-start = ((f32[32,32,512]{2,1,0:T(8,128)}), f32[32,32,512]{2,1,0:T(8,128)S(1)}, u32[]{:S(2)}, u32[]{:S(2)}) async-start(f32[32,32,512]{2,1,0:T(8,128)} %gather_fusion.2), calls=%async_computation | async-start | bytes 4194304 | tf_op jit(solution)/shard_map/all_to_all | solution.py:28
  171.8 26.5 %all-to-all-done = f32[32,32,512]{2,1,0:T(8,128)S(1)} async-done(((f32[32,32,512]{2,1,0:T(8,128)}), f32[32,32,512]{2,1,0:T(8,128)S(1)}, u32[]{:S(2)}, u32[]{:S(2)}) %all-to-all-start) | async-done | bytes 2097184 | tf_op jit(solution)/shard_map/all_to_all | solution.py:28
  200.4 3.3 %collective-permute-done.8 = f32[40,512]{1,0:T(8,128)S(1)} collective-permute-done((f32[40,512]{1,0:T(8,128)S(1)}, f32[40,512]{1,0:T(8,128)S(1)}, u32[]{:S(2)}, u32[]{:S(2)}) %collective-permute-start.8) | collective-permute-done | bytes 81952 | tf_op jit(solution)/shard_map/ppermute | solution.py:34
  205.6 4.8 %collective-permute-done.9 = f32[40,512]{1,0:T(8,128)S(1)} collective-permute-done((f32[40,512]{1,0:T(8,128)S(1)}, f32[40,512]{1,0:T(8,128)S(1)}, u32[]{:S(2)}, u32[]{:S(2)}) %collective-permute-start.9) | collective-permute-done | bytes 81952 | tf_op jit(solution)/shard_map/ppermute | solution.py:34
  210.4 4.7 %collective-permute-start.10 = (f32[40,512]{1,0:T(8,128)S(1)}, f32[40,512]{1,0:T(8,128)S(1)}, u32[]{:S(2)}, u32[]{:S(2)}) collective-permute-start(f32[40,512]{1,0:T(8,128)S(1)} %add.280), channel_id=1, source_target_pairs={{0,128},{32,160},{64,192},{96,224},{128,0},{160,32},{192,64},{224,... | collective-permute-start | bytes 245768 | tf_op jit(solution)/shard_map/ppermute | solution.py:34
  215.1 6.2 %collective-permute-done.10 = f32[40,512]{1,0:T(8,128)S(1)} collective-permute-done((f32[40,512]{1,0:T(8,128)S(1)}, f32[40,512]{1,0:T(8,128)S(1)}, u32[]{:S(2)}, u32[]{:S(2)}) %collective-permute-start.10) | collective-permute-done | bytes 81952 | tf_op jit(solution)/shard_map/ppermute | solution.py:34
  221.3 7.0 %collective-permute-start.11 = (f32[40,512]{1,0:T(8,128)S(1)}, f32[40,512]{1,0:T(8,128)S(1)}, u32[]{:S(2)}, u32[]{:S(2)}) collective-permute-start(f32[40,512]{1,0:T(8,128)S(1)} %add.281), channel_id=1, source_target_pairs={{0,256},{32,288},{64,320},{96,352},{128,384},{160,416},{192,448},{... | collective-permute-start | bytes 245768 | tf_op jit(solution)/shard_map/ppermute | solution.py:34
  228.4 9.3 %collective-permute-done.11 = f32[40,512]{1,0:T(8,128)S(1)} collective-permute-done((f32[40,512]{1,0:T(8,128)S(1)}, f32[40,512]{1,0:T(8,128)S(1)}, u32[]{:S(2)}, u32[]{:S(2)}) %collective-permute-start.11) | collective-permute-done | bytes 81952 | tf_op jit(solution)/shard_map/ppermute | solution.py:34
  237.7 10.3 %collective-permute-start.12 = (f32[40,512]{1,0:T(8,128)S(1)}, f32[40,512]{1,0:T(8,128)S(1)}, u32[]{:S(2)}, u32[]{:S(2)}) collective-permute-start(f32[40,512]{1,0:T(8,128)S(1)} %add.282), channel_id=1, source_target_pairs={{0,16},{1,17},{2,18},{3,19},{4,20},{5,21},{6,22},{7,23},{8,24},{9,... | collective-permute-start | bytes 245768 | tf_op jit(solution)/shard_map/ppermute | solution.py:39
  249.8 5.1 %collective-permute-start.13 = (f32[72,512]{1,0:T(8,128)S(1)}, f32[72,512]{1,0:T(8,128)S(1)}, u32[]{:S(2)}, u32[]{:S(2)}) collective-permute-start(f32[72,512]{1,0:T(8,128)S(1)} %pad_maximum_fusion.8), channel_id=1, source_target_pairs={{0,8},{1,9},{2,10},{3,11},{4,12},{5,13},{6,14},{7,15},{8,0},{9,1},... | collective-permute-start | bytes 442376 | tf_op jit(solution)/shard_map/ppermute | solution.py:39
  255.1 2.4 collective-permute-done.13
  259.6 6.7 %collective-permute-done.14 = f32[136,512]{1,0:T(8,128)S(1)} collective-permute-done((f32[136,512]{1,0:T(8,128)S(1)}, f32[136,512]{1,0:T(8,128)S(1)}, u32[]{:S(2)}, u32[]{:S(2)}) %collective-permute-start.14) | collective-permute-done | bytes 278560 | tf_op jit(solution)/shard_map/ppermute | solution.py:39
  266.4 3.2 %collective-permute-start.15 = (f32[264,512]{1,0:T(8,128)S(1)}, f32[264,512]{1,0:T(8,128)S(1)}, u32[]{:S(2)}, u32[]{:S(2)}) collective-permute-start(f32[264,512]{1,0:T(8,128)S(1)} %pad_maximum_fusion.4), channel_id=1, source_target_pairs={{0,2},{1,3},{2,0},{3,1},{4,6},{5,7},{6,4},{7,5},{8,10},{9,11},{10,... | collective-permute-start | bytes 1622024 | tf_op jit(solution)/shard_map/ppermute | solution.py:39
  269.8 8.6 %collective-permute-done.15 = f32[264,512]{1,0:T(8,128)S(1)} collective-permute-done((f32[264,512]{1,0:T(8,128)S(1)}, f32[264,512]{1,0:T(8,128)S(1)}, u32[]{:S(2)}, u32[]{:S(2)}) %collective-permute-start.15) | collective-permute-done | bytes 540704 | tf_op jit(solution)/shard_map/ppermute | solution.py:39
  278.6 6.5 %collective-permute-start.16 = (f32[520,512]{1,0:T(8,128)S(1)}, f32[520,512]{1,0:T(8,128)}, u32[]{:S(2)}, u32[]{:S(2)}) collective-permute-start(f32[520,512]{1,0:T(8,128)S(1)} %pad_maximum_fusion.2), channel_id=1, source_target_pairs={{0,1},{1,0},{2,3},{3,2},{4,5},{5,4},{6,7},{7,6},{8,9},{9,8},{10,11... | collective-permute-start | bytes 3194888 | tf_op jit(solution)/shard_map/ppermute | solution.py:39
  (118 shorter events, 34.0 us)
Async XLA Ops:
  7.2 143.2 %copy-start = (bf16[512,512]{1,0:T(8,128)(2,1)S(1)}, bf16[512,512]{1,0:T(8,128)(2,1)}, u32[]{:S(2)}) copy-start(bf16[512,512]{1,0:T(8,128)(2,1)} %param.20) | copy-start | bytes 1572868
  7.2 19.4 %copy-start.1 = (s32[16]{0:T(128)S(1)}, s32[16]{0:T(128)}, u32[]{:S(2)}) copy-start(s32[16]{0:T(128)} %param.18) | copy-start | bytes 196
  7.2 35.5 %copy-start.11 = (s32[4]{0:T(128)S(1)}, s32[4]{0:T(128)}, u32[]{:S(2)}) copy-start(s32[4]{0:T(128)} %param.15) | copy-start | bytes 52
  7.2 73.1 %all-gather.2.cloned.1.call-start = ((), (), s32[]{:S(2)}) async-start(), calls=%async_computation.1 | async-start | bytes 4325376 | tf_op jit(solution)/shard_map/all_gather | solution.py:143
  8.9 18.9 %collective-permute-start = (bf16[1,128,512]{2,1,0:T(8,128)(2,1)S(1)}, bf16[1,128,512]{2,1,0:T(8,128)(2,1)S(1)}, u32[]{:S(2)}, u32[]{:S(2)}) collective-permute-start(bf16[1,128,512]{2,1,0:T(8,128)(2,1)S(1)} %slice_bitcast_fusion.6), channel_id=1, source_target_pairs={{0,256},{32,288},{64,320},{96,352},{128,384},{160,416},{192,448},{... | collective-permute-start | bytes 393224 | tf_op jit(solution)/shard_map/ppermute | solution.py:77
  27.8 16.9 %collective-permute-start.1 = (bf16[2,128,512]{2,1,0:T(8,128)(2,1)S(1)}, bf16[2,128,512]{2,1,0:T(8,128)(2,1)S(1)}, u32[]{:S(2)}, u32[]{:S(2)}) collective-permute-start(bf16[2,128,512]{2,1,0:T(8,128)(2,1)S(1)} %maximum_select_fusion.2), channel_id=1, source_target_pairs={{0,32},{32,0},{64,96},{96,64},{128,160},{160,128},{192,224},{224,1... | collective-permute-start | bytes 786440 | tf_op jit(solution)/shard_map/ppermute | solution.py:77
  44.8 2.7 copy-start.3
  45.6 23.9 %copy-start.9 = (s32[4,8]{1,0:T(4,128)S(1)}, s32[4,8]{1,0:T(4,128)}, u32[]{:S(2)}) copy-start(s32[4,8]{1,0:T(4,128)} %param.14) | copy-start | bytes 388
  45.6 15.6 %collective-permute-start.2 = (bf16[2,128,512]{2,1,0:T(8,128)(2,1)S(1)}, bf16[2,128,512]{2,1,0:T(8,128)(2,1)S(1)}, u32[]{:S(2)}, u32[]{:S(2)}) collective-permute-start(bf16[2,128,512]{2,1,0:T(8,128)(2,1)S(1)} %select_bitcast_fusion.1), channel_id=1, source_target_pairs={{0,64},{32,96},{64,0},{96,32},{128,192},{160,224},{192,128},{224,1... | collective-permute-start | bytes 786440 | tf_op jit(solution)/shard_map/ppermute | solution.py:87
  47.7 37.4 %copy-start.4 = (bf16[4,8,128,128]{3,2,1,0:T(8,128)(2,1)}, bf16[4,8,128,128]{3,2,1,0:T(8,128)(2,1)S(1)}, u32[]{:S(2)}) copy-start(bf16[4,8,128,128]{3,2,1,0:T(8,128)(2,1)S(1)} %broadcast_multiply_fusion) | copy-start | bytes 3145732
  61.3 18.9 %collective-permute-start.3 = (bf16[1,128,512]{2,1,0:T(8,128)(2,1)S(1)}, bf16[1,128,512]{2,1,0:T(8,128)(2,1)S(1)}, u32[]{:S(2)}, u32[]{:S(2)}) collective-permute-start(bf16[1,128,512]{2,1,0:T(8,128)(2,1)S(1)} %select_bitcast_fusion.3), channel_id=1, source_target_pairs={{0,128},{32,160},{64,192},{96,224},{128,0},{160,32},{192,64},{224,... | collective-permute-start | bytes 393224 | tf_op jit(solution)/shard_map/ppermute | solution.py:87
  80.3 24.9 %copy-start.2 = (bf16[4096,512]{1,0:T(8,128)(2,1)S(1)}, bf16[4096,512]{1,0:T(8,128)(2,1)}, u32[]{:S(2)}) copy-start(bf16[4096,512]{1,0:T(8,128)(2,1)} %all-gather.2.cloned.1.call-done) | copy-start | bytes 12582916
  85.0 11.9 %copy-start.10 = (s32[32]{0:T(128)S(1)}, s32[32]{0:T(128)}, u32[]{:S(2)}) copy-start(s32[32]{0:T(128)} %constant.303) | copy-start | bytes 388
  85.1 12.0 %copy-start.6 = (bf16[512,512]{1,0:T(8,128)(2,1)S(1)}, bf16[512,512]{1,0:T(8,128)(2,1)}, u32[]{:S(2)}) copy-start(bf16[512,512]{1,0:T(8,128)(2,1)} %param.12) | copy-start | bytes 1572868
  85.8 15.2 %collective-permute-start.4 = (bf16[1,128,512]{2,1,0:T(8,128)(2,1)S(1)}, bf16[1,128,512]{2,1,0:T(8,128)(2,1)S(1)}, u32[]{:S(2)}, u32[]{:S(2)}) collective-permute-start(bf16[1,128,512]{2,1,0:T(8,128)(2,1)S(1)} %bitcast.110), channel_id=1, source_target_pairs={{0,256},{32,288},{64,320},{96,352},{128,384},{160,416},{192,448},{... | collective-permute-start | bytes 393224 | tf_op jit(solution)/shard_map/ppermute | solution.py:77
  101.0 10.7 %collective-permute-start.5 = (bf16[2,128,512]{2,1,0:T(8,128)(2,1)S(1)}, bf16[2,128,512]{2,1,0:T(8,128)(2,1)S(1)}, u32[]{:S(2)}, u32[]{:S(2)}) collective-permute-start(bf16[2,128,512]{2,1,0:T(8,128)(2,1)S(1)} %maximum_select_fusion.3), channel_id=1, source_target_pairs={{0,32},{32,0},{64,96},{96,64},{128,160},{160,128},{192,224},{224,1... | collective-permute-start | bytes 786440 | tf_op jit(solution)/shard_map/ppermute | solution.py:77
  111.8 7.8 %copy-start.5 = (bf16[4,8,128,128]{3,2,1,0:T(8,128)(2,1)S(1)}, bf16[4,8,128,128]{3,2,1,0:T(8,128)(2,1)}, u32[]{:S(2)}) copy-start(bf16[4,8,128,128]{3,2,1,0:T(8,128)(2,1)} %copy-done.4) | copy-start | bytes 3145732
  112.5 18.0 %collective-permute-start.6 = (bf16[2,128,512]{2,1,0:T(8,128)(2,1)S(1)}, bf16[2,128,512]{2,1,0:T(8,128)(2,1)S(1)}, u32[]{:S(2)}, u32[]{:S(2)}) collective-permute-start(bf16[2,128,512]{2,1,0:T(8,128)(2,1)S(1)} %select_bitcast_fusion), channel_id=1, source_target_pairs={{0,64},{32,96},{64,0},{96,32},{128,192},{160,224},{192,128},{224,1... | collective-permute-start | bytes 786440 | tf_op jit(solution)/shard_map/ppermute | solution.py:87
  123.6 16.9 %copy-start.7 = (bf16[512,512]{1,0:T(8,128)(2,1)S(1)}, bf16[512,512]{1,0:T(8,128)(2,1)}, u32[]{:S(2)}) copy-start(bf16[512,512]{1,0:T(8,128)(2,1)} %param.19) | copy-start | bytes 1572868
  130.7 19.6 %collective-permute-start.7 = (bf16[1,128,512]{2,1,0:T(8,128)(2,1)S(1)}, bf16[1,128,512]{2,1,0:T(8,128)(2,1)S(1)}, u32[]{:S(2)}, u32[]{:S(2)}) collective-permute-start(bf16[1,128,512]{2,1,0:T(8,128)(2,1)S(1)} %select_bitcast_fusion.2), channel_id=1, source_target_pairs={{0,128},{32,160},{64,192},{96,224},{128,0},{160,32},{192,64},{224,... | collective-permute-start | bytes 393224 | tf_op jit(solution)/shard_map/ppermute | solution.py:87
  151.0 1.1 copy-start.8
  159.9 38.4 %all-to-all-start = ((f32[32,32,512]{2,1,0:T(8,128)}), f32[32,32,512]{2,1,0:T(8,128)S(1)}, u32[]{:S(2)}, u32[]{:S(2)}) async-start(f32[32,32,512]{2,1,0:T(8,128)} %gather_fusion.2), calls=%async_computation | async-start | bytes 4194304 | tf_op jit(solution)/shard_map/all_to_all | solution.py:28
  198.5 5.2 %collective-permute-start.8 = (f32[40,512]{1,0:T(8,128)S(1)}, f32[40,512]{1,0:T(8,128)S(1)}, u32[]{:S(2)}, u32[]{:S(2)}) collective-permute-start(f32[40,512]{1,0:T(8,128)S(1)} %concatenate.64), channel_id=1, source_target_pairs={{0,32},{32,0},{64,96},{96,64},{128,160},{160,128},{192,224},{224,1... | collective-permute-start | bytes 245768 | tf_op jit(solution)/shard_map/ppermute | solution.py:34
  203.7 6.7 %collective-permute-start.9 = (f32[40,512]{1,0:T(8,128)S(1)}, f32[40,512]{1,0:T(8,128)S(1)}, u32[]{:S(2)}, u32[]{:S(2)}) collective-permute-start(f32[40,512]{1,0:T(8,128)S(1)} %pad_add_fusion), channel_id=1, source_target_pairs={{0,64},{32,96},{64,0},{96,32},{128,192},{160,224},{192,128},{224,1... | collective-permute-start | bytes 245768 | tf_op jit(solution)/shard_map/ppermute | solution.py:34
  210.4 10.9 %collective-permute-start.10 = (f32[40,512]{1,0:T(8,128)S(1)}, f32[40,512]{1,0:T(8,128)S(1)}, u32[]{:S(2)}, u32[]{:S(2)}) collective-permute-start(f32[40,512]{1,0:T(8,128)S(1)} %add.280), channel_id=1, source_target_pairs={{0,128},{32,160},{64,192},{96,224},{128,0},{160,32},{192,64},{224,... | collective-permute-start | bytes 245768 | tf_op jit(solution)/shard_map/ppermute | solution.py:34
  221.3 16.4 %collective-permute-start.11 = (f32[40,512]{1,0:T(8,128)S(1)}, f32[40,512]{1,0:T(8,128)S(1)}, u32[]{:S(2)}, u32[]{:S(2)}) collective-permute-start(f32[40,512]{1,0:T(8,128)S(1)} %add.281), channel_id=1, source_target_pairs={{0,256},{32,288},{64,320},{96,352},{128,384},{160,416},{192,448},{... | collective-permute-start | bytes 245768 | tf_op jit(solution)/shard_map/ppermute | solution.py:34
  237.7 12.1 %collective-permute-start.12 = (f32[40,512]{1,0:T(8,128)S(1)}, f32[40,512]{1,0:T(8,128)S(1)}, u32[]{:S(2)}, u32[]{:S(2)}) collective-permute-start(f32[40,512]{1,0:T(8,128)S(1)} %add.282), channel_id=1, source_target_pairs={{0,16},{1,17},{2,18},{3,19},{4,20},{5,21},{6,22},{7,23},{8,24},{9,... | collective-permute-start | bytes 245768 | tf_op jit(solution)/shard_map/ppermute | solution.py:39
  249.8 7.7 %collective-permute-start.13 = (f32[72,512]{1,0:T(8,128)S(1)}, f32[72,512]{1,0:T(8,128)S(1)}, u32[]{:S(2)}, u32[]{:S(2)}) collective-permute-start(f32[72,512]{1,0:T(8,128)S(1)} %pad_maximum_fusion.8), channel_id=1, source_target_pairs={{0,8},{1,9},{2,10},{3,11},{4,12},{5,13},{6,14},{7,15},{8,0},{9,1},... | collective-permute-start | bytes 442376 | tf_op jit(solution)/shard_map/ppermute | solution.py:39
  257.6 8.8 %collective-permute-start.14 = (f32[136,512]{1,0:T(8,128)S(1)}, f32[136,512]{1,0:T(8,128)S(1)}, u32[]{:S(2)}, u32[]{:S(2)}) collective-permute-start(f32[136,512]{1,0:T(8,128)S(1)} %pad_maximum_fusion.5), channel_id=1, source_target_pairs={{0,4},{1,5},{2,6},{3,7},{4,0},{5,1},{6,2},{7,3},{8,12},{9,13},{10,... | collective-permute-start | bytes 835592 | tf_op jit(solution)/shard_map/ppermute | solution.py:39
  266.4 12.0 %collective-permute-start.15 = (f32[264,512]{1,0:T(8,128)S(1)}, f32[264,512]{1,0:T(8,128)S(1)}, u32[]{:S(2)}, u32[]{:S(2)}) collective-permute-start(f32[264,512]{1,0:T(8,128)S(1)} %pad_maximum_fusion.4), channel_id=1, source_target_pairs={{0,2},{1,3},{2,0},{3,1},{4,6},{5,7},{6,4},{7,5},{8,10},{9,11},{10,... | collective-permute-start | bytes 1622024 | tf_op jit(solution)/shard_map/ppermute | solution.py:39
  278.6 8.9 %collective-permute-start.16 = (f32[520,512]{1,0:T(8,128)S(1)}, f32[520,512]{1,0:T(8,128)}, u32[]{:S(2)}, u32[]{:S(2)}) collective-permute-start(f32[520,512]{1,0:T(8,128)S(1)} %pad_maximum_fusion.2), channel_id=1, source_target_pairs={{0,1},{1,0},{2,3},{3,2},{4,5},{5,4},{6,7},{7,6},{8,9},{9,8},{10,11... | collective-permute-start | bytes 3194888 | tf_op jit(solution)/shard_map/ppermute | solution.py:39
Sparse Core Ops, SparseCore 0:
  11.2 67.0 all-gather.1

commit v10 on v9

--- a/solution.py
+++ b/solution.py
@@ -146,12 +146,7 @@
     blocks = piece.reshape(count, BLOCK, width)
 
     def aggregate(part_tiles, part_ids):
-        indicator_matrix = (
-            part_ids[:, :, None] == jnp.arange(count, dtype=jnp.int32)[None, None, :]
-        ).astype(jnp.bfloat16)
-        selected = jnp.einsum(
-            "bkc,cjd->bkjd", indicator_matrix, blocks, preferred_element_type=jnp.float32
-        ).astype(jnp.bfloat16)
+        selected = jnp.take(blocks, part_ids, axis=0, mode="clip")
         summed = jnp.einsum("bkij,bkjd->bid", part_tiles, selected, preferred_element_type=jnp.float32)
         return summed.reshape(-1, width).astype(jnp.bfloat16)
 

time: 302 us -> 299 us (0.990)
  matrix products: 20.9 us -> 9.86 us
  local copies, waits for them, and re-layouts: 12 us -> 20.6 us
  starting transfers between devices: 123 us -> 115 us
  waiting for transfers between devices: 120 us -> 128 us
    dot_general x2 -> x0, matrix products: 9.51 us -> none  [aggregate(): jnp.einsum('bkc,cjd->bkjd', indicator_matrix, blocks, preferred_element_t...]
    ppermute x4, waiting for transfers between devices: 7.97 us -> 15.8 us  [route_forward(): got = lax.ppermute(held, 'row', xor_pairs(size, m))]
    gather x0 -> x2, local copies, waits for them, and re-layouts: none -> 7.53 us  [aggregate(): selected = jnp.take(blocks, part_ids, axis=0, mode='clip')]
    ppermute x4, starting transfers between devices: 26.9 us -> 22.1 us  [route_forward(): got = lax.ppermute(send, 'row', xor_pairs(size, m))]
  transfers between devices with their start and end apart: 19 -> 19, of which waited for: 18 -> 17; matrix products, arithmetic and copies ran while one was open for 5% -> 5% of each run, Pallas kernels for 0% -> 0%
where the time goes in v10:
time: 299 us
  waiting for transfers between devices  128 us (43%)
  starting transfers between devices  115 us (38%)
  between operations  21.3 us (7%)
  local copies, waits for them, and re-layouts  20.6 us (7%)
  matrix products  9.86 us (3%)
    ppermute x4, starting transfers between devices, route_forward(): got = lax.ppermute(held, 'row', xor_pairs(size, m))  41 us
    ppermute x4, waiting for transfers between devices, route_forward(): got = lax.ppermute(send, 'row', xor_pairs(size, m))  40.8 us
    ppermute x5, starting transfers between devices, tree_allreduce(): lax.ppermute(jnp.concatenate([buf, extra], axis=0), 'col', xor_pairs(ways...  27 us
    all_to_all x1, waiting for transfers between devices, tree_allreduce(): scattered = lax.all_to_all(chunks, 'col', 0, 0, tiled=False).sum(axis=0)  26.5 us
    ppermute x4, waiting for transfers between devices, tree_allreduce(): joined = joined + lax.ppermute(joined, axis, xor_pairs(size, mask))  23.5 us
    ppermute x4, starting transfers between devices, route_forward(): got = lax.ppermute(send, 'row', xor_pairs(size, m))  22.1 us
    ppermute x5, waiting for transfers between devices, tree_allreduce(): lax.ppermute(jnp.concatenate([buf, extra], axis=0), 'col', xor_pairs(ways...  21.1 us
    ppermute x4, waiting for transfers between devices, route_forward(): got = lax.ppermute(held, 'row', xor_pairs(size, m))  15.8 us
  transfers between devices with their start and end apart: 19, of which 17 were waited for; matrix products, arithmetic and copies ran while one was open for 5% of the time, Pallas kernels for 0%

profile of v10, /device:TPU:1, one launch (start us, length us, event | category | flops | bytes accessed | tf_op | source)
XLA Modules:
  0.0 298.5 jit_solution(5889711460628727698)
XLA Ops:
  8.9 16.3 %collective-permute-start = (bf16[1,128,512]{2,1,0:T(8,128)(2,1)S(1)}, bf16[1,128,512]{2,1,0:T(8,128)(2,1)S(1)}, u32[]{:S(2)}, u32[]{:S(2)}) collective-permute-start(bf16[1,128,512]{2,1,0:T(8,128)(2,1)S(1)} %slice_bitcast_fusion.6), channel_id=1, source_target_pairs={{0,256},{32,288},{64,320},{96,352},{128,384},{160,416},{192,448},{... | collective-permute-start | bytes 393224 | tf_op jit(solution)/shard_map/ppermute | solution.py:77
  27.8 11.6 %collective-permute-start.1 = (bf16[2,128,512]{2,1,0:T(8,128)(2,1)S(1)}, bf16[2,128,512]{2,1,0:T(8,128)(2,1)S(1)}, u32[]{:S(2)}, u32[]{:S(2)}) collective-permute-start(bf16[2,128,512]{2,1,0:T(8,128)(2,1)S(1)} %maximum_select_fusion.2), channel_id=1, source_target_pairs={{0,32},{32,0},{64,96},{96,64},{128,160},{160,128},{192,224},{224,1... | collective-permute-start | bytes 786440 | tf_op jit(solution)/shard_map/ppermute | solution.py:77
  39.6 5.1 %collective-permute-done.1 = bf16[2,128,512]{2,1,0:T(8,128)(2,1)S(1)} collective-permute-done((bf16[2,128,512]{2,1,0:T(8,128)(2,1)S(1)}, bf16[2,128,512]{2,1,0:T(8,128)(2,1)S(1)}, u32[]{:S(2)}, u32[]{:S(2)}) %collective-permute-start.1) | collective-permute-done | bytes 262176 | tf_op jit(solution)/shard_map/ppermute | solution.py:77
  45.6 2.1 collective-permute-start.2
  47.8 13.5 %collective-permute-done.2 = bf16[2,128,512]{2,1,0:T(8,128)(2,1)S(1)} collective-permute-done((bf16[2,128,512]{2,1,0:T(8,128)(2,1)S(1)}, bf16[2,128,512]{2,1,0:T(8,128)(2,1)S(1)}, u32[]{:S(2)}, u32[]{:S(2)}) %collective-permute-start.2) | collective-permute-done | bytes 262176 | tf_op jit(solution)/shard_map/ppermute | solution.py:87
  61.5 8.1 %collective-permute-start.3 = (bf16[1,128,512]{2,1,0:T(8,128)(2,1)S(1)}, bf16[1,128,512]{2,1,0:T(8,128)(2,1)S(1)}, u32[]{:S(2)}, u32[]{:S(2)}) collective-permute-start(bf16[1,128,512]{2,1,0:T(8,128)(2,1)S(1)} %select_bitcast_fusion.3), channel_id=1, source_target_pairs={{0,128},{32,160},{64,192},{96,224},{128,0},{160,32},{192,64},{224,... | collective-permute-start | bytes 393224 | tf_op jit(solution)/shard_map/ppermute | solution.py:87
  72.9 7.5 %collective-permute-done.3 = bf16[1,128,512]{2,1,0:T(8,128)(2,1)S(1)} collective-permute-done((bf16[1,128,512]{2,1,0:T(8,128)(2,1)S(1)}, bf16[1,128,512]{2,1,0:T(8,128)(2,1)S(1)}, u32[]{:S(2)}, u32[]{:S(2)}) %collective-permute-start.3) | collective-permute-done | bytes 131104 | tf_op jit(solution)/shard_map/ppermute | solution.py:87
  80.5 2.8 gather_fusion.2
  83.6 11.2 %collective-permute-start.4 = (bf16[1,128,512]{2,1,0:T(8,128)(2,1)S(1)}, bf16[1,128,512]{2,1,0:T(8,128)(2,1)S(1)}, u32[]{:S(2)}, u32[]{:S(2)}) collective-permute-start(bf16[1,128,512]{2,1,0:T(8,128)(2,1)S(1)} %bitcast.102), channel_id=1, source_target_pairs={{0,256},{32,288},{64,320},{96,352},{128,384},{160,416},{192,448},{... | collective-permute-start | bytes 393224 | tf_op jit(solution)/shard_map/ppermute | solution.py:77
  94.8 10.2 %collective-permute-done.4 = bf16[1,128,512]{2,1,0:T(8,128)(2,1)S(1)} collective-permute-done((bf16[1,128,512]{2,1,0:T(8,128)(2,1)S(1)}, bf16[1,128,512]{2,1,0:T(8,128)(2,1)S(1)}, u32[]{:S(2)}, u32[]{:S(2)}) %collective-permute-start.4) | collective-permute-done | bytes 131104 | tf_op jit(solution)/shard_map/ppermute | solution.py:77
  108.1 4.7 %gather_fusion.3 = bf16[24,128,512]{2,1,0:T(8,128)(2,1)} fusion(bf16[32,128,512]{2,1,0:T(8,128)(2,1)} %bitcast.100, s32[1024]{0:T(1024)S(1)} %get-tuple-element.22), kind=kCustom, calls=%fused_computation.5 | custom fusion | bytes 6291552 | tf_op jit(solution)/shard_map/jit(_take)/gather | solution.py:149
  113.6 3.5 %collective-permute-start.6 = (bf16[2,128,512]{2,1,0:T(8,128)(2,1)S(1)}, bf16[2,128,512]{2,1,0:T(8,128)(2,1)S(1)}, u32[]{:S(2)}, u32[]{:S(2)}) collective-permute-start(bf16[2,128,512]{2,1,0:T(8,128)(2,1)S(1)} %select_bitcast_fusion), channel_id=1, source_target_pairs={{0,64},{32,96},{64,0},{96,32},{128,192},{160,224},{192,128},{224,1... | collective-permute-start | bytes 786440 | tf_op jit(solution)/shard_map/ppermute | solution.py:87
  117.1 2.9 fusion.2
  120.0 9.0 %collective-permute-done.6 = bf16[2,128,512]{2,1,0:T(8,128)(2,1)S(1)} collective-permute-done((bf16[2,128,512]{2,1,0:T(8,128)(2,1)S(1)}, bf16[2,128,512]{2,1,0:T(8,128)(2,1)S(1)}, u32[]{:S(2)}, u32[]{:S(2)}) %collective-permute-start.6) | collective-permute-done | bytes 262176 | tf_op jit(solution)/shard_map/ppermute | solution.py:87
  129.2 8.4 %collective-permute-start.7 = (bf16[1,128,512]{2,1,0:T(8,128)(2,1)S(1)}, bf16[1,128,512]{2,1,0:T(8,128)(2,1)S(1)}, u32[]{:S(2)}, u32[]{:S(2)}) collective-permute-start(bf16[1,128,512]{2,1,0:T(8,128)(2,1)S(1)} %select_bitcast_fusion.2), channel_id=1, source_target_pairs={{0,128},{32,160},{64,192},{96,224},{128,0},{160,32},{192,64},{224,... | collective-permute-start | bytes 393224 | tf_op jit(solution)/shard_map/ppermute | solution.py:87
  138.2 10.7 %collective-permute-done.7 = bf16[1,128,512]{2,1,0:T(8,128)(2,1)S(1)} collective-permute-done((bf16[1,128,512]{2,1,0:T(8,128)(2,1)S(1)}, bf16[1,128,512]{2,1,0:T(8,128)(2,1)S(1)}, u32[]{:S(2)}, u32[]{:S(2)}) %collective-permute-start.7) | collective-permute-done | bytes 131104 | tf_op jit(solution)/shard_map/ppermute | solution.py:87
  156.5 2.0 gather_fusion.4
  158.5 9.5 %all-to-all-start = ((f32[32,32,512]{2,1,0:T(8,128)}), f32[32,32,512]{2,1,0:T(8,128)S(1)}, u32[]{:S(2)}, u32[]{:S(2)}) async-start(f32[32,32,512]{2,1,0:T(8,128)} %gather_fusion.4), calls=%async_computation | async-start | bytes 4194304 | tf_op jit(solution)/shard_map/all_to_all | solution.py:28
  169.4 26.5 %all-to-all-done = f32[32,32,512]{2,1,0:T(8,128)S(1)} async-done(((f32[32,32,512]{2,1,0:T(8,128)}), f32[32,32,512]{2,1,0:T(8,128)S(1)}, u32[]{:S(2)}, u32[]{:S(2)}) %all-to-all-start) | async-done | bytes 2097184 | tf_op jit(solution)/shard_map/all_to_all | solution.py:28
  198.0 3.3 %collective-permute-done.8 = f32[40,512]{1,0:T(8,128)S(1)} collective-permute-done((f32[40,512]{1,0:T(8,128)S(1)}, f32[40,512]{1,0:T(8,128)S(1)}, u32[]{:S(2)}, u32[]{:S(2)}) %collective-permute-start.8) | collective-permute-done | bytes 81952 | tf_op jit(solution)/shard_map/ppermute | solution.py:34
  203.2 4.8 %collective-permute-done.9 = f32[40,512]{1,0:T(8,128)S(1)} collective-permute-done((f32[40,512]{1,0:T(8,128)S(1)}, f32[40,512]{1,0:T(8,128)S(1)}, u32[]{:S(2)}, u32[]{:S(2)}) %collective-permute-start.9) | collective-permute-done | bytes 81952 | tf_op jit(solution)/shard_map/ppermute | solution.py:34
  208.0 4.8 %collective-permute-start.10 = (f32[40,512]{1,0:T(8,128)S(1)}, f32[40,512]{1,0:T(8,128)S(1)}, u32[]{:S(2)}, u32[]{:S(2)}) collective-permute-start(f32[40,512]{1,0:T(8,128)S(1)} %add.280), channel_id=1, source_target_pairs={{0,128},{32,160},{64,192},{96,224},{128,0},{160,32},{192,64},{224,... | collective-permute-start | bytes 245768 | tf_op jit(solution)/shard_map/ppermute | solution.py:34
  212.8 6.1 %collective-permute-done.10 = f32[40,512]{1,0:T(8,128)S(1)} collective-permute-done((f32[40,512]{1,0:T(8,128)S(1)}, f32[40,512]{1,0:T(8,128)S(1)}, u32[]{:S(2)}, u32[]{:S(2)}) %collective-permute-start.10) | collective-permute-done | bytes 81952 | tf_op jit(solution)/shard_map/ppermute | solution.py:34
  218.9 7.1 %collective-permute-start.11 = (f32[40,512]{1,0:T(8,128)S(1)}, f32[40,512]{1,0:T(8,128)S(1)}, u32[]{:S(2)}, u32[]{:S(2)}) collective-permute-start(f32[40,512]{1,0:T(8,128)S(1)} %add.281), channel_id=1, source_target_pairs={{0,256},{32,288},{64,320},{96,352},{128,384},{160,416},{192,448},{... | collective-permute-start | bytes 245768 | tf_op jit(solution)/shard_map/ppermute | solution.py:34
  226.1 9.3 %collective-permute-done.11 = f32[40,512]{1,0:T(8,128)S(1)} collective-permute-done((f32[40,512]{1,0:T(8,128)S(1)}, f32[40,512]{1,0:T(8,128)S(1)}, u32[]{:S(2)}, u32[]{:S(2)}) %collective-permute-start.11) | collective-permute-done | bytes 81952 | tf_op jit(solution)/shard_map/ppermute | solution.py:34
  235.4 10.3 %collective-permute-start.12 = (f32[40,512]{1,0:T(8,128)S(1)}, f32[40,512]{1,0:T(8,128)S(1)}, u32[]{:S(2)}, u32[]{:S(2)}) collective-permute-start(f32[40,512]{1,0:T(8,128)S(1)} %add.282), channel_id=1, source_target_pairs={{0,16},{1,17},{2,18},{3,19},{4,20},{5,21},{6,22},{7,23},{8,24},{9,... | collective-permute-start | bytes 245768 | tf_op jit(solution)/shard_map/ppermute | solution.py:39
  247.6 5.1 %collective-permute-start.13 = (f32[72,512]{1,0:T(8,128)S(1)}, f32[72,512]{1,0:T(8,128)S(1)}, u32[]{:S(2)}, u32[]{:S(2)}) collective-permute-start(f32[72,512]{1,0:T(8,128)S(1)} %pad_maximum_fusion.8), channel_id=1, source_target_pairs={{0,8},{1,9},{2,10},{3,11},{4,12},{5,13},{6,14},{7,15},{8,0},{9,1},... | collective-permute-start | bytes 442376 | tf_op jit(solution)/shard_map/ppermute | solution.py:39
  252.8 2.4 collective-permute-done.13
  257.3 6.7 %collective-permute-done.14 = f32[136,512]{1,0:T(8,128)S(1)} collective-permute-done((f32[136,512]{1,0:T(8,128)S(1)}, f32[136,512]{1,0:T(8,128)S(1)}, u32[]{:S(2)}, u32[]{:S(2)}) %collective-permute-start.14) | collective-permute-done | bytes 278560 | tf_op jit(solution)/shard_map/ppermute | solution.py:39
  264.2 3.2 %collective-permute-start.15 = (f32[264,512]{1,0:T(8,128)S(1)}, f32[264,512]{1,0:T(8,128)S(1)}, u32[]{:S(2)}, u32[]{:S(2)}) collective-permute-start(f32[264,512]{1,0:T(8,128)S(1)} %pad_maximum_fusion.4), channel_id=1, source_target_pairs={{0,2},{1,3},{2,0},{3,1},{4,6},{5,7},{6,4},{7,5},{8,10},{9,11},{10,... | collective-permute-start | bytes 1622024 | tf_op jit(solution)/shard_map/ppermute | solution.py:39
  267.5 8.6 %collective-permute-done.15 = f32[264,512]{1,0:T(8,128)S(1)} collective-permute-done((f32[264,512]{1,0:T(8,128)S(1)}, f32[264,512]{1,0:T(8,128)S(1)}, u32[]{:S(2)}, u32[]{:S(2)}) %collective-permute-start.15) | collective-permute-done | bytes 540704 | tf_op jit(solution)/shard_map/ppermute | solution.py:39
  276.3 6.5 %collective-permute-start.16 = (f32[520,512]{1,0:T(8,128)S(1)}, f32[520,512]{1,0:T(8,128)}, u32[]{:S(2)}, u32[]{:S(2)}) collective-permute-start(f32[520,512]{1,0:T(8,128)S(1)} %pad_maximum_fusion.2), channel_id=1, source_target_pairs={{0,1},{1,0},{2,3},{3,2},{4,5},{5,4},{6,7},{7,6},{8,9},{9,8},{10,11... | collective-permute-start | bytes 3194888 | tf_op jit(solution)/shard_map/ppermute | solution.py:39
  (112 shorter events, 33.2 us)
Async XLA Ops:
  7.2 141.8 %copy-start = (bf16[512,512]{1,0:T(8,128)(2,1)S(1)}, bf16[512,512]{1,0:T(8,128)(2,1)}, u32[]{:S(2)}) copy-start(bf16[512,512]{1,0:T(8,128)(2,1)} %param.20) | copy-start | bytes 1572868
  7.2 19.4 %copy-start.1 = (s32[16]{0:T(128)S(1)}, s32[16]{0:T(128)}, u32[]{:S(2)}) copy-start(s32[16]{0:T(128)} %param.18) | copy-start | bytes 196
  7.2 32.3 %copy-start.7 = (s32[4]{0:T(128)S(1)}, s32[4]{0:T(128)}, u32[]{:S(2)}) copy-start(s32[4]{0:T(128)} %param.15) | copy-start | bytes 52
  7.2 73.2 %all-gather.2.cloned.1.call-start = ((), (), s32[]{:S(2)}) async-start(), calls=%async_computation.1 | async-start | bytes 4325376 | tf_op jit(solution)/shard_map/all_gather | solution.py:143
  8.9 18.9 %collective-permute-start = (bf16[1,128,512]{2,1,0:T(8,128)(2,1)S(1)}, bf16[1,128,512]{2,1,0:T(8,128)(2,1)S(1)}, u32[]{:S(2)}, u32[]{:S(2)}) collective-permute-start(bf16[1,128,512]{2,1,0:T(8,128)(2,1)S(1)} %slice_bitcast_fusion.6), channel_id=1, source_target_pairs={{0,256},{32,288},{64,320},{96,352},{128,384},{160,416},{192,448},{... | collective-permute-start | bytes 393224 | tf_op jit(solution)/shard_map/ppermute | solution.py:77
  27.8 16.9 %collective-permute-start.1 = (bf16[2,128,512]{2,1,0:T(8,128)(2,1)S(1)}, bf16[2,128,512]{2,1,0:T(8,128)(2,1)S(1)}, u32[]{:S(2)}, u32[]{:S(2)}) collective-permute-start(bf16[2,128,512]{2,1,0:T(8,128)(2,1)S(1)} %maximum_select_fusion.2), channel_id=1, source_target_pairs={{0,32},{32,0},{64,96},{96,64},{128,160},{160,128},{192,224},{224,1... | collective-permute-start | bytes 786440 | tf_op jit(solution)/shard_map/ppermute | solution.py:77
  45.4 2.2 copy-start.2
  45.6 24.0 %copy-start.5 = (s32[4,8]{1,0:T(4,128)S(1)}, s32[4,8]{1,0:T(4,128)}, u32[]{:S(2)}) copy-start(s32[4,8]{1,0:T(4,128)} %param.14) | copy-start | bytes 388
  45.6 15.8 %collective-permute-start.2 = (bf16[2,128,512]{2,1,0:T(8,128)(2,1)S(1)}, bf16[2,128,512]{2,1,0:T(8,128)(2,1)S(1)}, u32[]{:S(2)}, u32[]{:S(2)}) collective-permute-start(bf16[2,128,512]{2,1,0:T(8,128)(2,1)S(1)} %select_bitcast_fusion.1), channel_id=1, source_target_pairs={{0,64},{32,96},{64,0},{96,32},{128,192},{160,224},{192,128},{224,1... | collective-permute-start | bytes 786440 | tf_op jit(solution)/shard_map/ppermute | solution.py:87
  61.5 18.9 %collective-permute-start.3 = (bf16[1,128,512]{2,1,0:T(8,128)(2,1)S(1)}, bf16[1,128,512]{2,1,0:T(8,128)(2,1)S(1)}, u32[]{:S(2)}, u32[]{:S(2)}) collective-permute-start(bf16[1,128,512]{2,1,0:T(8,128)(2,1)S(1)} %select_bitcast_fusion.3), channel_id=1, source_target_pairs={{0,128},{32,160},{64,192},{96,224},{128,0},{160,32},{192,64},{224,... | collective-permute-start | bytes 393224 | tf_op jit(solution)/shard_map/ppermute | solution.py:87
  83.3 23.7 %copy-start.6 = (s32[32]{0:T(128)S(1)}, s32[32]{0:T(128)}, u32[]{:S(2)}) copy-start(s32[32]{0:T(128)} %constant.303) | copy-start | bytes 388
  83.6 21.3 %collective-permute-start.4 = (bf16[1,128,512]{2,1,0:T(8,128)(2,1)S(1)}, bf16[1,128,512]{2,1,0:T(8,128)(2,1)S(1)}, u32[]{:S(2)}, u32[]{:S(2)}) collective-permute-start(bf16[1,128,512]{2,1,0:T(8,128)(2,1)S(1)} %bitcast.102), channel_id=1, source_target_pairs={{0,256},{32,288},{64,320},{96,352},{128,384},{160,416},{192,448},{... | collective-permute-start | bytes 393224 | tf_op jit(solution)/shard_map/ppermute | solution.py:77
  105.0 7.8 %collective-permute-start.5 = (bf16[2,128,512]{2,1,0:T(8,128)(2,1)S(1)}, bf16[2,128,512]{2,1,0:T(8,128)(2,1)S(1)}, u32[]{:S(2)}, u32[]{:S(2)}) collective-permute-start(bf16[2,128,512]{2,1,0:T(8,128)(2,1)S(1)} %maximum_select_fusion.3), channel_id=1, source_target_pairs={{0,32},{32,0},{64,96},{96,64},{128,160},{160,128},{192,224},{224,1... | collective-permute-start | bytes 786440 | tf_op jit(solution)/shard_map/ppermute | solution.py:77
  113.6 15.4 %collective-permute-start.6 = (bf16[2,128,512]{2,1,0:T(8,128)(2,1)S(1)}, bf16[2,128,512]{2,1,0:T(8,128)(2,1)S(1)}, u32[]{:S(2)}, u32[]{:S(2)}) collective-permute-start(bf16[2,128,512]{2,1,0:T(8,128)(2,1)S(1)} %select_bitcast_fusion), channel_id=1, source_target_pairs={{0,64},{32,96},{64,0},{96,32},{128,192},{160,224},{192,128},{224,1... | collective-permute-start | bytes 786440 | tf_op jit(solution)/shard_map/ppermute | solution.py:87
  120.0 17.6 %copy-start.3 = (bf16[512,512]{1,0:T(8,128)(2,1)S(1)}, bf16[512,512]{1,0:T(8,128)(2,1)}, u32[]{:S(2)}) copy-start(bf16[512,512]{1,0:T(8,128)(2,1)} %param.19) | copy-start | bytes 1572868
  129.2 19.8 %collective-permute-start.7 = (bf16[1,128,512]{2,1,0:T(8,128)(2,1)S(1)}, bf16[1,128,512]{2,1,0:T(8,128)(2,1)S(1)}, u32[]{:S(2)}, u32[]{:S(2)}) collective-permute-start(bf16[1,128,512]{2,1,0:T(8,128)(2,1)S(1)} %select_bitcast_fusion.2), channel_id=1, source_target_pairs={{0,128},{32,160},{64,192},{96,224},{128,0},{160,32},{192,64},{224,... | collective-permute-start | bytes 393224 | tf_op jit(solution)/shard_map/ppermute | solution.py:87
  149.7 1.1 copy-start.4
  158.5 37.4 %all-to-all-start = ((f32[32,32,512]{2,1,0:T(8,128)}), f32[32,32,512]{2,1,0:T(8,128)S(1)}, u32[]{:S(2)}, u32[]{:S(2)}) async-start(f32[32,32,512]{2,1,0:T(8,128)} %gather_fusion.4), calls=%async_computation | async-start | bytes 4194304 | tf_op jit(solution)/shard_map/all_to_all | solution.py:28
  196.1 5.2 %collective-permute-start.8 = (f32[40,512]{1,0:T(8,128)S(1)}, f32[40,512]{1,0:T(8,128)S(1)}, u32[]{:S(2)}, u32[]{:S(2)}) collective-permute-start(f32[40,512]{1,0:T(8,128)S(1)} %concatenate.64), channel_id=1, source_target_pairs={{0,32},{32,0},{64,96},{96,64},{128,160},{160,128},{192,224},{224,1... | collective-permute-start | bytes 245768 | tf_op jit(solution)/shard_map/ppermute | solution.py:34
  201.3 6.7 %collective-permute-start.9 = (f32[40,512]{1,0:T(8,128)S(1)}, f32[40,512]{1,0:T(8,128)S(1)}, u32[]{:S(2)}, u32[]{:S(2)}) collective-permute-start(f32[40,512]{1,0:T(8,128)S(1)} %pad_add_fusion), channel_id=1, source_target_pairs={{0,64},{32,96},{64,0},{96,32},{128,192},{160,224},{192,128},{224,1... | collective-permute-start | bytes 245768 | tf_op jit(solution)/shard_map/ppermute | solution.py:34
  208.0 10.9 %collective-permute-start.10 = (f32[40,512]{1,0:T(8,128)S(1)}, f32[40,512]{1,0:T(8,128)S(1)}, u32[]{:S(2)}, u32[]{:S(2)}) collective-permute-start(f32[40,512]{1,0:T(8,128)S(1)} %add.280), channel_id=1, source_target_pairs={{0,128},{32,160},{64,192},{96,224},{128,0},{160,32},{192,64},{224,... | collective-permute-start | bytes 245768 | tf_op jit(solution)/shard_map/ppermute | solution.py:34
  218.9 16.5 %collective-permute-start.11 = (f32[40,512]{1,0:T(8,128)S(1)}, f32[40,512]{1,0:T(8,128)S(1)}, u32[]{:S(2)}, u32[]{:S(2)}) collective-permute-start(f32[40,512]{1,0:T(8,128)S(1)} %add.281), channel_id=1, source_target_pairs={{0,256},{32,288},{64,320},{96,352},{128,384},{160,416},{192,448},{... | collective-permute-start | bytes 245768 | tf_op jit(solution)/shard_map/ppermute | solution.py:34
  235.4 12.1 %collective-permute-start.12 = (f32[40,512]{1,0:T(8,128)S(1)}, f32[40,512]{1,0:T(8,128)S(1)}, u32[]{:S(2)}, u32[]{:S(2)}) collective-permute-start(f32[40,512]{1,0:T(8,128)S(1)} %add.282), channel_id=1, source_target_pairs={{0,16},{1,17},{2,18},{3,19},{4,20},{5,21},{6,22},{7,23},{8,24},{9,... | collective-permute-start | bytes 245768 | tf_op jit(solution)/shard_map/ppermute | solution.py:39
  247.6 7.7 %collective-permute-start.13 = (f32[72,512]{1,0:T(8,128)S(1)}, f32[72,512]{1,0:T(8,128)S(1)}, u32[]{:S(2)}, u32[]{:S(2)}) collective-permute-start(f32[72,512]{1,0:T(8,128)S(1)} %pad_maximum_fusion.8), channel_id=1, source_target_pairs={{0,8},{1,9},{2,10},{3,11},{4,12},{5,13},{6,14},{7,15},{8,0},{9,1},... | collective-permute-start | bytes 442376 | tf_op jit(solution)/shard_map/ppermute | solution.py:39
  255.3 8.8 %collective-permute-start.14 = (f32[136,512]{1,0:T(8,128)S(1)}, f32[136,512]{1,0:T(8,128)S(1)}, u32[]{:S(2)}, u32[]{:S(2)}) collective-permute-start(f32[136,512]{1,0:T(8,128)S(1)} %pad_maximum_fusion.5), channel_id=1, source_target_pairs={{0,4},{1,5},{2,6},{3,7},{4,0},{5,1},{6,2},{7,3},{8,12},{9,13},{10,... | collective-permute-start | bytes 835592 | tf_op jit(solution)/shard_map/ppermute | solution.py:39
  264.2 12.0 %collective-permute-start.15 = (f32[264,512]{1,0:T(8,128)S(1)}, f32[264,512]{1,0:T(8,128)S(1)}, u32[]{:S(2)}, u32[]{:S(2)}) collective-permute-start(f32[264,512]{1,0:T(8,128)S(1)} %pad_maximum_fusion.4), channel_id=1, source_target_pairs={{0,2},{1,3},{2,0},{3,1},{4,6},{5,7},{6,4},{7,5},{8,10},{9,11},{10,... | collective-permute-start | bytes 1622024 | tf_op jit(solution)/shard_map/ppermute | solution.py:39
  276.3 8.9 %collective-permute-start.16 = (f32[520,512]{1,0:T(8,128)S(1)}, f32[520,512]{1,0:T(8,128)}, u32[]{:S(2)}, u32[]{:S(2)}) collective-permute-start(f32[520,512]{1,0:T(8,128)S(1)} %pad_maximum_fusion.2), channel_id=1, source_target_pairs={{0,1},{1,0},{2,3},{3,2},{4,5},{5,4},{6,7},{7,6},{8,9},{9,8},{10,11... | collective-permute-start | bytes 3194888 | tf_op jit(solution)/shard_map/ppermute | solution.py:39
Sparse Core Ops, SparseCore 0:
  11.2 67.0 all-gather.1

commit v11 on v10

--- a/solution.py
+++ b/solution.py
@@ -156,18 +156,22 @@
     agg = jnp.concatenate([agg_head, aggregate(tiles[head:], nbr_blocks[head:])], axis=0)
     all_feats = jnp.concatenate([node_feats, noise_feats], axis=0)
     all_agg = jnp.concatenate([agg, noise_agg], axis=0)
-    pre = jnp.dot(all_feats, w_self, preferred_element_type=jnp.float32) + jnp.dot(
-        all_agg, w_neigh, preferred_element_type=jnp.float32
+    pre = jnp.dot(node_feats, w_self, preferred_element_type=jnp.float32) + jnp.dot(
+        agg, w_neigh, preferred_element_type=jnp.float32
     )
     emb32, pull = jax.vjp(embed, pre)
-    all_bf = emb32.astype(jnp.bfloat16)
-    zeta_bf = all_bf[:rows]
-    noise_emb = all_bf[rows:].astype(jnp.float32)
+    noise_pre = jnp.dot(noise_feats, w_self, preferred_element_type=jnp.float32) + jnp.dot(
+        noise_agg, w_neigh, preferred_element_type=jnp.float32
+    )
+    noise_emb32, noise_pull = jax.vjp(embed, noise_pre)
+    zeta_bf = emb32.astype(jnp.bfloat16)
+    noise_bf = noise_emb32.astype(jnp.bfloat16)
+    noise_emb = noise_bf.astype(jnp.float32)
     zeta = zeta_bf.astype(jnp.float32)
     pairing = (pos_index[:, None] == jnp.arange(rows, dtype=jnp.int32)[None, :]).astype(jnp.float32)
     partner = jnp.dot(pairing.astype(jnp.bfloat16), zeta_bf, preferred_element_type=jnp.float32)
     s_pos = jnp.sum(zeta * partner, axis=-1) * scale_factor
-    s_neg = jnp.dot(zeta_bf, all_bf[rows:].T, preferred_element_type=jnp.float32) * scale_factor
+    s_neg = jnp.dot(zeta_bf, noise_bf.T, preferred_element_type=jnp.float32) * scale_factor
     loss_part = (jnp.sum(jax.nn.softplus(-s_pos)) + jnp.sum(jax.nn.softplus(s_neg)) / NOISE) / nodes
     grad_pos = -jax.nn.sigmoid(-s_pos) / nodes
     grad_neg = jax.nn.sigmoid(s_neg) / (NOISE * nodes)
@@ -177,8 +181,7 @@
     partner_grad = jnp.dot(pairing.T, scale_factor * grad_pos[:, None] * zeta, precision=highest)
     dnoise = scale_factor * jnp.dot(grad_neg.T, zeta, precision=highest)
     dnoise = dnoise.astype(jnp.bfloat16).astype(jnp.float32)
-    dzeta = jnp.concatenate([anchor + partner_grad, dnoise], axis=0)
-    gpre = pull(dzeta)[0].astype(jnp.bfloat16)
+    gpre = jnp.concatenate([pull(anchor + partner_grad)[0], noise_pull(dnoise)[0]], axis=0).astype(jnp.bfloat16)
     part_self = jnp.dot(all_feats.T, gpre, preferred_element_type=jnp.float32)
     neighbour_partial = jnp.dot(all_agg.T, gpre, preferred_element_type=jnp.float32)
     stacked = jnp.concatenate([part_self, neighbour_partial], axis=0)

time: 299 us -> 304 us (1.017)
  starting transfers between devices: 115 us -> 120 us
  waiting for transfers between devices: 128 us -> 124 us
    ppermute x4, waiting for transfers between devices: 15.8 us -> 11 us  [route_forward(): got = lax.ppermute(held, 'row', xor_pairs(size, m))]
    ppermute x4, starting transfers between devices: 22.1 us -> 26.5 us  [route_forward(): got = lax.ppermute(send, 'row', xor_pairs(size, m))]
where the time goes in v11:
time: 304 us; the launch traced here: 303 us
  waiting for transfers between devices  124 us (41%)
  starting transfers between devices  120 us (39%)
  local copies, waits for them, and re-layouts  22.2 us (7%)
  between operations  21.2 us (7%)
  matrix products  11.5 us (4%)
  other arithmetic  4.22 us (1%)
    ppermute x4, starting transfers between devices, route_forward(): got = lax.ppermute(held, 'row', xor_pairs(size, m))  40.9 us
    ppermute x4, waiting for transfers between devices, route_forward(): got = lax.ppermute(send, 'row', xor_pairs(size, m))  40.7 us
    ppermute x5, starting transfers between devices, tree_allreduce(): lax.ppermute(jnp.concatenate([buf, extra], axis=0), 'col', xor_pairs(ways...  27.1 us
    all_to_all x1, waiting for transfers between devices, tree_allreduce(): scattered = lax.all_to_all(chunks, 'col', 0, 0, tiled=False).sum(axis=0)  26.5 us
    ppermute x4, starting transfers between devices, route_forward(): got = lax.ppermute(send, 'row', xor_pairs(size, m))  26.5 us
    ppermute x4, waiting for transfers between devices, tree_allreduce(): joined = joined + lax.ppermute(joined, axis, xor_pairs(size, mask))  23.5 us
    ppermute x5, waiting for transfers between devices, tree_allreduce(): lax.ppermute(jnp.concatenate([buf, extra], axis=0), 'col', xor_pairs(ways...  21.1 us
    ppermute x4, starting transfers between devices, tree_allreduce(): joined = joined + lax.ppermute(joined, axis, xor_pairs(size, mask))  15.6 us
  transfers between devices with their start and end apart: 19, of which 17 were waited for; matrix products, arithmetic and copies ran while one was open for 5% of the time, Pallas kernels for 0%

profile of v11, /device:TPU:1, one launch (start us, length us, event | category | flops | bytes accessed | tf_op | source)
XLA Modules:
  0.0 303.1 jit_solution(9802921010705520060)
XLA Ops:
  8.8 16.3 %collective-permute-start = (bf16[1,128,512]{2,1,0:T(8,128)(2,1)S(1)}, bf16[1,128,512]{2,1,0:T(8,128)(2,1)S(1)}, u32[]{:S(2)}, u32[]{:S(2)}) collective-permute-start(bf16[1,128,512]{2,1,0:T(8,128)(2,1)S(1)} %slice_bitcast_fusion.6), channel_id=1, source_target_pairs={{0,256},{32,288},{64,320},{96,352},{128,384},{160,416},{192,448},{... | collective-permute-start | bytes 393224 | tf_op jit(solution)/shard_map/ppermute | solution.py:77
  30.1 9.4 %collective-permute-start.1 = (bf16[2,128,512]{2,1,0:T(8,128)(2,1)S(1)}, bf16[2,128,512]{2,1,0:T(8,128)(2,1)S(1)}, u32[]{:S(2)}, u32[]{:S(2)}) collective-permute-start(bf16[2,128,512]{2,1,0:T(8,128)(2,1)S(1)} %maximum_select_fusion.2), channel_id=1, source_target_pairs={{0,32},{32,0},{64,96},{96,64},{128,160},{160,128},{192,224},{224,1... | collective-permute-start | bytes 786440 | tf_op jit(solution)/shard_map/ppermute | solution.py:77
  40.6 4.2 %collective-permute-done.1 = bf16[2,128,512]{2,1,0:T(8,128)(2,1)S(1)} collective-permute-done((bf16[2,128,512]{2,1,0:T(8,128)(2,1)S(1)}, bf16[2,128,512]{2,1,0:T(8,128)(2,1)S(1)}, u32[]{:S(2)}, u32[]{:S(2)}) %collective-permute-start.1) | collective-permute-done | bytes 262176 | tf_op jit(solution)/shard_map/ppermute | solution.py:77
  48.0 13.2 %collective-permute-done.2 = bf16[2,128,512]{2,1,0:T(8,128)(2,1)S(1)} collective-permute-done((bf16[2,128,512]{2,1,0:T(8,128)(2,1)S(1)}, bf16[2,128,512]{2,1,0:T(8,128)(2,1)S(1)}, u32[]{:S(2)}, u32[]{:S(2)}) %collective-permute-start.2) | collective-permute-done | bytes 262176 | tf_op jit(solution)/shard_map/ppermute | solution.py:87
  61.3 8.1 %collective-permute-start.3 = (bf16[1,128,512]{2,1,0:T(8,128)(2,1)S(1)}, bf16[1,128,512]{2,1,0:T(8,128)(2,1)S(1)}, u32[]{:S(2)}, u32[]{:S(2)}) collective-permute-start(bf16[1,128,512]{2,1,0:T(8,128)(2,1)S(1)} %select_bitcast_fusion.3), channel_id=1, source_target_pairs={{0,128},{32,160},{64,192},{96,224},{128,0},{160,32},{192,64},{224,... | collective-permute-start | bytes 393224 | tf_op jit(solution)/shard_map/ppermute | solution.py:87
  72.7 7.5 %collective-permute-done.3 = bf16[1,128,512]{2,1,0:T(8,128)(2,1)S(1)} collective-permute-done((bf16[1,128,512]{2,1,0:T(8,128)(2,1)S(1)}, bf16[1,128,512]{2,1,0:T(8,128)(2,1)S(1)}, u32[]{:S(2)}, u32[]{:S(2)}) %collective-permute-start.3) | collective-permute-done | bytes 131104 | tf_op jit(solution)/shard_map/ppermute | solution.py:87
  80.3 4.7 %gather_fusion.3 = bf16[24,128,512]{2,1,0:T(8,128)(2,1)} fusion(bf16[32,128,512]{2,1,0:T(8,128)(2,1)} %bitcast.100, s32[1024]{0:T(1024)S(1)} %pad_clamp_fusion.1), kind=kCustom, calls=%fused_computation.5 | custom fusion | bytes 6291552 | tf_op jit(solution)/shard_map/jit(_take)/gather | solution.py:149
  85.0 2.8 gather_fusion.2
  89.1 11.2 %collective-permute-start.4 = (bf16[1,128,512]{2,1,0:T(8,128)(2,1)S(1)}, bf16[1,128,512]{2,1,0:T(8,128)(2,1)S(1)}, u32[]{:S(2)}, u32[]{:S(2)}) collective-permute-start(bf16[1,128,512]{2,1,0:T(8,128)(2,1)S(1)} %bitcast.103), channel_id=1, source_target_pairs={{0,256},{32,288},{64,320},{96,352},{128,384},{160,416},{192,448},{... | collective-permute-start | bytes 393224 | tf_op jit(solution)/shard_map/ppermute | solution.py:77
  100.3 3.1 %fusion.1 = bf16[3,128,512]{2,1,0:T(8,128)(2,1)S(1)} fusion(bf16[4,8,128,128]{3,2,1,0:T(8,128)(2,1)} %broadcast_multiply_fusion, bf16[3,8,128,512]{3,2,1,0:T(8,128)(2,1)} %bitcast.102), kind=kOutput, calls=%fused_computation.16 | convolution fusion | flops 402849792 | bytes 4587520 | tf_op jit(solution)/shard_map/bkij,bkjd->bid/dot_general | solution.py:150
  104.5 4.1 %collective-permute-start.5 = (bf16[2,128,512]{2,1,0:T(8,128)(2,1)S(1)}, bf16[2,128,512]{2,1,0:T(8,128)(2,1)S(1)}, u32[]{:S(2)}, u32[]{:S(2)}) collective-permute-start(bf16[2,128,512]{2,1,0:T(8,128)(2,1)S(1)} %maximum_select_fusion.3), channel_id=1, source_target_pairs={{0,32},{32,0},{64,96},{96,64},{128,160},{160,128},{192,224},{224,1... | collective-permute-start | bytes 786440 | tf_op jit(solution)/shard_map/ppermute | solution.py:77
  109.1 5.9 %collective-permute-done.5 = bf16[2,128,512]{2,1,0:T(8,128)(2,1)S(1)} collective-permute-done((bf16[2,128,512]{2,1,0:T(8,128)(2,1)S(1)}, bf16[2,128,512]{2,1,0:T(8,128)(2,1)S(1)}, u32[]{:S(2)}, u32[]{:S(2)}) %collective-permute-start.5) | collective-permute-done | bytes 262176 | tf_op jit(solution)/shard_map/ppermute | solution.py:77
  115.8 7.1 %collective-permute-start.6 = (bf16[2,128,512]{2,1,0:T(8,128)(2,1)S(1)}, bf16[2,128,512]{2,1,0:T(8,128)(2,1)S(1)}, u32[]{:S(2)}, u32[]{:S(2)}) collective-permute-start(bf16[2,128,512]{2,1,0:T(8,128)(2,1)S(1)} %select_bitcast_fusion), channel_id=1, source_target_pairs={{0,64},{32,96},{64,0},{96,32},{128,192},{160,224},{192,128},{224,1... | collective-permute-start | bytes 786440 | tf_op jit(solution)/shard_map/ppermute | solution.py:87
  123.8 10.7 %collective-permute-done.6 = bf16[2,128,512]{2,1,0:T(8,128)(2,1)S(1)} collective-permute-done((bf16[2,128,512]{2,1,0:T(8,128)(2,1)S(1)}, bf16[2,128,512]{2,1,0:T(8,128)(2,1)S(1)}, u32[]{:S(2)}, u32[]{:S(2)}) %collective-permute-start.6) | collective-permute-done | bytes 262176 | tf_op jit(solution)/shard_map/ppermute | solution.py:87
  134.6 9.4 %collective-permute-start.7 = (bf16[1,128,512]{2,1,0:T(8,128)(2,1)S(1)}, bf16[1,128,512]{2,1,0:T(8,128)(2,1)S(1)}, u32[]{:S(2)}, u32[]{:S(2)}) collective-permute-start(bf16[1,128,512]{2,1,0:T(8,128)(2,1)S(1)} %select_bitcast_fusion.2), channel_id=1, source_target_pairs={{0,128},{32,160},{64,192},{96,224},{128,0},{160,32},{192,64},{224,... | collective-permute-start | bytes 393224 | tf_op jit(solution)/shard_map/ppermute | solution.py:87
  144.6 9.4 %collective-permute-done.7 = bf16[1,128,512]{2,1,0:T(8,128)(2,1)S(1)} collective-permute-done((bf16[1,128,512]{2,1,0:T(8,128)(2,1)S(1)}, bf16[1,128,512]{2,1,0:T(8,128)(2,1)S(1)}, u32[]{:S(2)}, u32[]{:S(2)}) %collective-permute-start.7) | collective-permute-done | bytes 131104 | tf_op jit(solution)/shard_map/ppermute | solution.py:87
  160.6 2.0 gather_fusion.4
  162.6 10.2 %all-to-all-start = ((f32[32,32,512]{2,1,0:T(8,128)}), f32[32,32,512]{2,1,0:T(8,128)S(1)}, u32[]{:S(2)}, u32[]{:S(2)}) async-start(f32[32,32,512]{2,1,0:T(8,128)} %gather_fusion.4), calls=%async_computation | async-start | bytes 4194304 | tf_op jit(solution)/shard_map/all_to_all | solution.py:28
  174.1 26.5 %all-to-all-done = f32[32,32,512]{2,1,0:T(8,128)S(1)} async-done(((f32[32,32,512]{2,1,0:T(8,128)}), f32[32,32,512]{2,1,0:T(8,128)S(1)}, u32[]{:S(2)}, u32[]{:S(2)}) %all-to-all-start) | async-done | bytes 2097184 | tf_op jit(solution)/shard_map/all_to_all | solution.py:28
  202.7 3.3 %collective-permute-done.8 = f32[40,512]{1,0:T(8,128)S(1)} collective-permute-done((f32[40,512]{1,0:T(8,128)S(1)}, f32[40,512]{1,0:T(8,128)S(1)}, u32[]{:S(2)}, u32[]{:S(2)}) %collective-permute-start.8) | collective-permute-done | bytes 81952 | tf_op jit(solution)/shard_map/ppermute | solution.py:34
  207.9 4.8 %collective-permute-done.9 = f32[40,512]{1,0:T(8,128)S(1)} collective-permute-done((f32[40,512]{1,0:T(8,128)S(1)}, f32[40,512]{1,0:T(8,128)S(1)}, u32[]{:S(2)}, u32[]{:S(2)}) %collective-permute-start.9) | collective-permute-done | bytes 81952 | tf_op jit(solution)/shard_map/ppermute | solution.py:34
  212.7 4.7 %collective-permute-start.10 = (f32[40,512]{1,0:T(8,128)S(1)}, f32[40,512]{1,0:T(8,128)S(1)}, u32[]{:S(2)}, u32[]{:S(2)}) collective-permute-start(f32[40,512]{1,0:T(8,128)S(1)} %add.299), channel_id=1, source_target_pairs={{0,128},{32,160},{64,192},{96,224},{128,0},{160,32},{192,64},{224,... | collective-permute-start | bytes 245768 | tf_op jit(solution)/shard_map/ppermute | solution.py:34
  217.4 6.2 %collective-permute-done.10 = f32[40,512]{1,0:T(8,128)S(1)} collective-permute-done((f32[40,512]{1,0:T(8,128)S(1)}, f32[40,512]{1,0:T(8,128)S(1)}, u32[]{:S(2)}, u32[]{:S(2)}) %collective-permute-start.10) | collective-permute-done | bytes 81952 | tf_op jit(solution)/shard_map/ppermute | solution.py:34
  223.6 7.1 %collective-permute-start.11 = (f32[40,512]{1,0:T(8,128)S(1)}, f32[40,512]{1,0:T(8,128)S(1)}, u32[]{:S(2)}, u32[]{:S(2)}) collective-permute-start(f32[40,512]{1,0:T(8,128)S(1)} %add.300), channel_id=1, source_target_pairs={{0,256},{32,288},{64,320},{96,352},{128,384},{160,416},{192,448},{... | collective-permute-start | bytes 245768 | tf_op jit(solution)/shard_map/ppermute | solution.py:34
  230.8 9.2 %collective-permute-done.11 = f32[40,512]{1,0:T(8,128)S(1)} collective-permute-done((f32[40,512]{1,0:T(8,128)S(1)}, f32[40,512]{1,0:T(8,128)S(1)}, u32[]{:S(2)}, u32[]{:S(2)}) %collective-permute-start.11) | collective-permute-done | bytes 81952 | tf_op jit(solution)/shard_map/ppermute | solution.py:34
  240.0 10.4 %collective-permute-start.12 = (f32[40,512]{1,0:T(8,128)S(1)}, f32[40,512]{1,0:T(8,128)S(1)}, u32[]{:S(2)}, u32[]{:S(2)}) collective-permute-start(f32[40,512]{1,0:T(8,128)S(1)} %add.301), channel_id=1, source_target_pairs={{0,16},{1,17},{2,18},{3,19},{4,20},{5,21},{6,22},{7,23},{8,24},{9,... | collective-permute-start | bytes 245768 | tf_op jit(solution)/shard_map/ppermute | solution.py:39
  252.3 5.1 %collective-permute-start.13 = (f32[72,512]{1,0:T(8,128)S(1)}, f32[72,512]{1,0:T(8,128)S(1)}, u32[]{:S(2)}, u32[]{:S(2)}) collective-permute-start(f32[72,512]{1,0:T(8,128)S(1)} %pad_maximum_fusion.7), channel_id=1, source_target_pairs={{0,8},{1,9},{2,10},{3,11},{4,12},{5,13},{6,14},{7,15},{8,0},{9,1},... | collective-permute-start | bytes 442376 | tf_op jit(solution)/shard_map/ppermute | solution.py:39
  257.5 2.4 collective-permute-done.13
  262.0 6.7 %collective-permute-done.14 = f32[136,512]{1,0:T(8,128)S(1)} collective-permute-done((f32[136,512]{1,0:T(8,128)S(1)}, f32[136,512]{1,0:T(8,128)S(1)}, u32[]{:S(2)}, u32[]{:S(2)}) %collective-permute-start.14) | collective-permute-done | bytes 278560 | tf_op jit(solution)/shard_map/ppermute | solution.py:39
  268.8 3.2 %collective-permute-start.15 = (f32[264,512]{1,0:T(8,128)S(1)}, f32[264,512]{1,0:T(8,128)S(1)}, u32[]{:S(2)}, u32[]{:S(2)}) collective-permute-start(f32[264,512]{1,0:T(8,128)S(1)} %pad_maximum_fusion.3), channel_id=1, source_target_pairs={{0,2},{1,3},{2,0},{3,1},{4,6},{5,7},{6,4},{7,5},{8,10},{9,11},{10,... | collective-permute-start | bytes 1622024 | tf_op jit(solution)/shard_map/ppermute | solution.py:39
  272.2 8.6 %collective-permute-done.15 = f32[264,512]{1,0:T(8,128)S(1)} collective-permute-done((f32[264,512]{1,0:T(8,128)S(1)}, f32[264,512]{1,0:T(8,128)S(1)}, u32[]{:S(2)}, u32[]{:S(2)}) %collective-permute-start.15) | collective-permute-done | bytes 540704 | tf_op jit(solution)/shard_map/ppermute | solution.py:39
  281.0 6.5 %collective-permute-start.16 = (f32[520,512]{1,0:T(8,128)S(1)}, f32[520,512]{1,0:T(8,128)}, u32[]{:S(2)}, u32[]{:S(2)}) collective-permute-start(f32[520,512]{1,0:T(8,128)S(1)} %pad_maximum_fusion.1), channel_id=1, source_target_pairs={{0,1},{1,0},{2,3},{3,2},{4,5},{5,4},{6,7},{7,6},{8,9},{9,8},{10,11... | collective-permute-start | bytes 3194888 | tf_op jit(solution)/shard_map/ppermute | solution.py:39
  (118 shorter events, 38.0 us)
Async XLA Ops:
  7.2 101.4 %copy-start = (bf16[512,512]{1,0:T(8,128)(2,1)S(1)}, bf16[512,512]{1,0:T(8,128)(2,1)}, u32[]{:S(2)}) copy-start(bf16[512,512]{1,0:T(8,128)(2,1)} %param.20) | copy-start | bytes 1572868
  7.2 32.3 %copy-start.3 = (bf16[4,8,128,128]{3,2,1,0:T(8,128)(2,1)S(1)}, bf16[4,8,128,128]{3,2,1,0:T(8,128)(2,1)}, u32[]{:S(2)}) copy-start(bf16[4,8,128,128]{3,2,1,0:T(8,128)(2,1)} %param.16) | copy-start | bytes 3145732
  7.2 73.1 %all-gather.2.cloned.1.call-start = ((), (), s32[]{:S(2)}) async-start(), calls=%async_computation.1 | async-start | bytes 4325376 | tf_op jit(solution)/shard_map/all_gather | solution.py:143
  8.8 21.2 %collective-permute-start = (bf16[1,128,512]{2,1,0:T(8,128)(2,1)S(1)}, bf16[1,128,512]{2,1,0:T(8,128)(2,1)S(1)}, u32[]{:S(2)}, u32[]{:S(2)}) collective-permute-start(bf16[1,128,512]{2,1,0:T(8,128)(2,1)S(1)} %slice_bitcast_fusion.6), channel_id=1, source_target_pairs={{0,256},{32,288},{64,320},{96,352},{128,384},{160,416},{192,448},{... | collective-permute-start | bytes 393224 | tf_op jit(solution)/shard_map/ppermute | solution.py:77
  30.1 14.6 %collective-permute-start.1 = (bf16[2,128,512]{2,1,0:T(8,128)(2,1)S(1)}, bf16[2,128,512]{2,1,0:T(8,128)(2,1)S(1)}, u32[]{:S(2)}, u32[]{:S(2)}) collective-permute-start(bf16[2,128,512]{2,1,0:T(8,128)(2,1)S(1)} %maximum_select_fusion.2), channel_id=1, source_target_pairs={{0,32},{32,0},{64,96},{96,64},{128,160},{160,128},{192,224},{224,1... | collective-permute-start | bytes 786440 | tf_op jit(solution)/shard_map/ppermute | solution.py:77
  40.6 6.9 %copy-start.2 = (bf16[512,512]{1,0:T(8,128)(2,1)S(1)}, bf16[512,512]{1,0:T(8,128)(2,1)}, u32[]{:S(2)}) copy-start(bf16[512,512]{1,0:T(8,128)(2,1)} %param.19) | copy-start | bytes 1572868
  40.6 7.0 %copy-start.4 = (bf16[512,512]{1,0:T(8,128)(2,1)S(1)}, bf16[512,512]{1,0:T(8,128)(2,1)}, u32[]{:S(2)}) copy-start(bf16[512,512]{1,0:T(8,128)(2,1)} %param.12) | copy-start | bytes 1572868
  45.5 24.0 %copy-start.1 = (s32[16]{0:T(128)S(1)}, s32[16]{0:T(128)}, u32[]{:S(2)}) copy-start(s32[16]{0:T(128)} %param.18) | copy-start | bytes 196
  45.5 27.2 %copy-start.9 = (s32[32]{0:T(128)S(1)}, s32[32]{0:T(128)}, u32[]{:S(2)}) copy-start(s32[32]{0:T(128)} %constant.305) | copy-start | bytes 388
  45.6 15.6 %collective-permute-start.2 = (bf16[2,128,512]{2,1,0:T(8,128)(2,1)S(1)}, bf16[2,128,512]{2,1,0:T(8,128)(2,1)S(1)}, u32[]{:S(2)}, u32[]{:S(2)}) collective-permute-start(bf16[2,128,512]{2,1,0:T(8,128)(2,1)S(1)} %select_bitcast_fusion.1), channel_id=1, source_target_pairs={{0,64},{32,96},{64,0},{96,32},{128,192},{160,224},{192,128},{224,1... | collective-permute-start | bytes 786440 | tf_op jit(solution)/shard_map/ppermute | solution.py:87
  61.3 18.9 %collective-permute-start.3 = (bf16[1,128,512]{2,1,0:T(8,128)(2,1)S(1)}, bf16[1,128,512]{2,1,0:T(8,128)(2,1)S(1)}, u32[]{:S(2)}, u32[]{:S(2)}) collective-permute-start(bf16[1,128,512]{2,1,0:T(8,128)(2,1)S(1)} %select_bitcast_fusion.3), channel_id=1, source_target_pairs={{0,128},{32,160},{64,192},{96,224},{128,0},{160,32},{192,64},{224,... | collective-permute-start | bytes 393224 | tf_op jit(solution)/shard_map/ppermute | solution.py:87
  89.1 15.3 %collective-permute-start.4 = (bf16[1,128,512]{2,1,0:T(8,128)(2,1)S(1)}, bf16[1,128,512]{2,1,0:T(8,128)(2,1)S(1)}, u32[]{:S(2)}, u32[]{:S(2)}) collective-permute-start(bf16[1,128,512]{2,1,0:T(8,128)(2,1)S(1)} %bitcast.103), channel_id=1, source_target_pairs={{0,256},{32,288},{64,320},{96,352},{128,384},{160,416},{192,448},{... | collective-permute-start | bytes 393224 | tf_op jit(solution)/shard_map/ppermute | solution.py:77
  103.4 11.6 %copy-start.6 = (bf16[3,128,512]{2,1,0:T(8,128)(2,1)}, bf16[3,128,512]{2,1,0:T(8,128)(2,1)S(1)}, u32[]{:S(2)}) copy-start(bf16[3,128,512]{2,1,0:T(8,128)(2,1)S(1)} %fusion.1) | copy-start | bytes 1179652
  104.5 10.5 %collective-permute-start.5 = (bf16[2,128,512]{2,1,0:T(8,128)(2,1)S(1)}, bf16[2,128,512]{2,1,0:T(8,128)(2,1)S(1)}, u32[]{:S(2)}, u32[]{:S(2)}) collective-permute-start(bf16[2,128,512]{2,1,0:T(8,128)(2,1)S(1)} %maximum_select_fusion.3), channel_id=1, source_target_pairs={{0,32},{32,0},{64,96},{96,64},{128,160},{160,128},{192,224},{224,1... | collective-permute-start | bytes 786440 | tf_op jit(solution)/shard_map/ppermute | solution.py:77
  109.1 13.8 %copy-start.8 = (s32[512]{0:T(512)S(1)}, s32[512]{0:T(512)}, u32[]{:S(2)}) copy-start(s32[512]{0:T(512)} %param.17) | copy-start | bytes 6148
  115.8 18.7 %collective-permute-start.6 = (bf16[2,128,512]{2,1,0:T(8,128)(2,1)S(1)}, bf16[2,128,512]{2,1,0:T(8,128)(2,1)S(1)}, u32[]{:S(2)}, u32[]{:S(2)}) collective-permute-start(bf16[2,128,512]{2,1,0:T(8,128)(2,1)S(1)} %select_bitcast_fusion), channel_id=1, source_target_pairs={{0,64},{32,96},{64,0},{96,32},{128,192},{160,224},{192,128},{224,1... | collective-permute-start | bytes 786440 | tf_op jit(solution)/shard_map/ppermute | solution.py:87
  134.6 19.4 %collective-permute-start.7 = (bf16[1,128,512]{2,1,0:T(8,128)(2,1)S(1)}, bf16[1,128,512]{2,1,0:T(8,128)(2,1)S(1)}, u32[]{:S(2)}, u32[]{:S(2)}) collective-permute-start(bf16[1,128,512]{2,1,0:T(8,128)(2,1)S(1)} %select_bitcast_fusion.2), channel_id=1, source_target_pairs={{0,128},{32,160},{64,192},{96,224},{128,0},{160,32},{192,64},{224,... | collective-permute-start | bytes 393224 | tf_op jit(solution)/shard_map/ppermute | solution.py:87
  158.1 1.0 copy-start.5
  158.4 1.4 copy-start.7
  162.6 38.1 %all-to-all-start = ((f32[32,32,512]{2,1,0:T(8,128)}), f32[32,32,512]{2,1,0:T(8,128)S(1)}, u32[]{:S(2)}, u32[]{:S(2)}) async-start(f32[32,32,512]{2,1,0:T(8,128)} %gather_fusion.4), calls=%async_computation | async-start | bytes 4194304 | tf_op jit(solution)/shard_map/all_to_all | solution.py:28
  200.8 5.2 %collective-permute-start.8 = (f32[40,512]{1,0:T(8,128)S(1)}, f32[40,512]{1,0:T(8,128)S(1)}, u32[]{:S(2)}, u32[]{:S(2)}) collective-permute-start(f32[40,512]{1,0:T(8,128)S(1)} %concatenate.70), channel_id=1, source_target_pairs={{0,32},{32,0},{64,96},{96,64},{128,160},{160,128},{192,224},{224,1... | collective-permute-start | bytes 245768 | tf_op jit(solution)/shard_map/ppermute | solution.py:34
  206.0 6.7 %collective-permute-start.9 = (f32[40,512]{1,0:T(8,128)S(1)}, f32[40,512]{1,0:T(8,128)S(1)}, u32[]{:S(2)}, u32[]{:S(2)}) collective-permute-start(f32[40,512]{1,0:T(8,128)S(1)} %pad_add_fusion), channel_id=1, source_target_pairs={{0,64},{32,96},{64,0},{96,32},{128,192},{160,224},{192,128},{224,1... | collective-permute-start | bytes 245768 | tf_op jit(solution)/shard_map/ppermute | solution.py:34
  212.7 10.9 %collective-permute-start.10 = (f32[40,512]{1,0:T(8,128)S(1)}, f32[40,512]{1,0:T(8,128)S(1)}, u32[]{:S(2)}, u32[]{:S(2)}) collective-permute-start(f32[40,512]{1,0:T(8,128)S(1)} %add.299), channel_id=1, source_target_pairs={{0,128},{32,160},{64,192},{96,224},{128,0},{160,32},{192,64},{224,... | collective-permute-start | bytes 245768 | tf_op jit(solution)/shard_map/ppermute | solution.py:34
  223.6 16.4 %collective-permute-start.11 = (f32[40,512]{1,0:T(8,128)S(1)}, f32[40,512]{1,0:T(8,128)S(1)}, u32[]{:S(2)}, u32[]{:S(2)}) collective-permute-start(f32[40,512]{1,0:T(8,128)S(1)} %add.300), channel_id=1, source_target_pairs={{0,256},{32,288},{64,320},{96,352},{128,384},{160,416},{192,448},{... | collective-permute-start | bytes 245768 | tf_op jit(solution)/shard_map/ppermute | solution.py:34
  240.0 12.2 %collective-permute-start.12 = (f32[40,512]{1,0:T(8,128)S(1)}, f32[40,512]{1,0:T(8,128)S(1)}, u32[]{:S(2)}, u32[]{:S(2)}) collective-permute-start(f32[40,512]{1,0:T(8,128)S(1)} %add.301), channel_id=1, source_target_pairs={{0,16},{1,17},{2,18},{3,19},{4,20},{5,21},{6,22},{7,23},{8,24},{9,... | collective-permute-start | bytes 245768 | tf_op jit(solution)/shard_map/ppermute | solution.py:39
  252.3 7.7 %collective-permute-start.13 = (f32[72,512]{1,0:T(8,128)S(1)}, f32[72,512]{1,0:T(8,128)S(1)}, u32[]{:S(2)}, u32[]{:S(2)}) collective-permute-start(f32[72,512]{1,0:T(8,128)S(1)} %pad_maximum_fusion.7), channel_id=1, source_target_pairs={{0,8},{1,9},{2,10},{3,11},{4,12},{5,13},{6,14},{7,15},{8,0},{9,1},... | collective-permute-start | bytes 442376 | tf_op jit(solution)/shard_map/ppermute | solution.py:39
  260.0 8.8 %collective-permute-start.14 = (f32[136,512]{1,0:T(8,128)S(1)}, f32[136,512]{1,0:T(8,128)S(1)}, u32[]{:S(2)}, u32[]{:S(2)}) collective-permute-start(f32[136,512]{1,0:T(8,128)S(1)} %pad_maximum_fusion.6), channel_id=1, source_target_pairs={{0,4},{1,5},{2,6},{3,7},{4,0},{5,1},{6,2},{7,3},{8,12},{9,13},{10,... | collective-permute-start | bytes 835592 | tf_op jit(solution)/shard_map/ppermute | solution.py:39
  268.8 12.0 %collective-permute-start.15 = (f32[264,512]{1,0:T(8,128)S(1)}, f32[264,512]{1,0:T(8,128)S(1)}, u32[]{:S(2)}, u32[]{:S(2)}) collective-permute-start(f32[264,512]{1,0:T(8,128)S(1)} %pad_maximum_fusion.3), channel_id=1, source_target_pairs={{0,2},{1,3},{2,0},{3,1},{4,6},{5,7},{6,4},{7,5},{8,10},{9,11},{10,... | collective-permute-start | bytes 1622024 | tf_op jit(solution)/shard_map/ppermute | solution.py:39
  281.0 8.9 %collective-permute-start.16 = (f32[520,512]{1,0:T(8,128)S(1)}, f32[520,512]{1,0:T(8,128)}, u32[]{:S(2)}, u32[]{:S(2)}) collective-permute-start(f32[520,512]{1,0:T(8,128)S(1)} %pad_maximum_fusion.1), channel_id=1, source_target_pairs={{0,1},{1,0},{2,3},{3,2},{4,5},{5,4},{6,7},{7,6},{8,9},{9,8},{10,11... | collective-permute-start | bytes 3194888 | tf_op jit(solution)/shard_map/ppermute | solution.py:39
Sparse Core Ops, SparseCore 0:
  11.2 67.0 all-gather.1

commit v12 on v10

--- a/solution.py
+++ b/solution.py
@@ -14,15 +14,15 @@
     return [(i, i ^ mask) for i in range(size)]
 
 
-DOUBLING = (("col", 16), ("col", 8), ("col", 4), ("col", 2), ("col", 1))
+DOUBLING = ((16, 8, 4, 2, 1), (4, 2, 16, 8, 1))
 BUTTERFLY = (("row", 1), ("row", 2), ("row", 4), ("row", 8))
 
 
 def tree_allreduce(buf, extra):
     ways = lax.axis_size("col")
     me = lax.axis_index("col")
-    masks = [mask for axis, mask in DOUBLING if mask < ways]
-    position = [sum(((j // mask) % 2) << t for t, mask in enumerate(masks)) for j in range(ways)]
+    orders = [[mask for mask in order if mask < ways] for order in DOUBLING]
+    position = [sum(((j // mask) % 2) << t for t, mask in enumerate(orders[j % 2])) for j in range(ways)]
     rows = buf.shape[0] // ways
     chunks = buf.reshape(ways, rows, buf.shape[1])[jnp.array(position, jnp.int32)]
     scattered = lax.all_to_all(chunks, "col", 0, 0, tiled=False).sum(axis=0)
@@ -33,10 +33,13 @@
             continue
         joined = joined + lax.ppermute(joined, axis, xor_pairs(size, mask))
     buf, extra = joined[:rows], joined[rows:]
-    for mask in masks:
+    odd = me % 2 == 1
+    for even_mask, odd_mask in zip(*orders):
+        mask = jnp.where(odd, odd_mask, even_mask)
         bit = (me // mask) % 2
         held = buf.shape[0]
-        got = lax.ppermute(jnp.concatenate([buf, extra], axis=0), "col", xor_pairs(ways, mask))
+        pairs = [(i, i ^ (odd_mask if i % 2 else even_mask)) for i in range(ways)]
+        got = lax.ppermute(jnp.concatenate([buf, extra], axis=0), "col", pairs)
         extra = extra + got[held:]
         out = jnp.zeros((2 * held,) + buf.shape[1:], buf.dtype)
         out = lax.dynamic_update_slice_in_dim(out, buf, bit * held, 0)

time: 299 us -> 298 us (level)
  waiting for transfers between devices: 128 us -> 124 us
  starting transfers between devices: 115 us -> 118 us
    ppermute x5, waiting for transfers between devices: 21.1 us -> 16.4 us  [tree_allreduce(): got = lax.ppermute(jnp.concatenate([buf, extra], axis=0), 'col', pairs)]
where the time goes in v12:
time: 298 us; the launch traced here: 297 us
  waiting for transfers between devices  124 us (42%)
  starting transfers between devices  118 us (40%)
  between operations  21.4 us (7%)
  local copies, waits for them, and re-layouts  20.6 us (7%)
  matrix products  9.86 us (3%)
    ppermute x4, starting transfers between devices, route_forward(): got = lax.ppermute(held, 'row', xor_pairs(size, m))  41 us
    ppermute x4, waiting for transfers between devices, route_forward(): got = lax.ppermute(send, 'row', xor_pairs(size, m))  40.8 us
    ppermute x5, starting transfers between devices, tree_allreduce(): got = lax.ppermute(jnp.concatenate([buf, extra], axis=0), 'col', pairs)  30 us
    all_to_all x1, waiting for transfers between devices, tree_allreduce(): scattered = lax.all_to_all(chunks, 'col', 0, 0, tiled=False).sum(axis=0)  26.5 us
    ppermute x4, waiting for transfers between devices, tree_allreduce(): joined = joined + lax.ppermute(joined, axis, xor_pairs(size, mask))  23.4 us
    ppermute x4, starting transfers between devices, route_forward(): got = lax.ppermute(send, 'row', xor_pairs(size, m))  22.1 us
    ppermute x5, waiting for transfers between devices, tree_allreduce(): got = lax.ppermute(jnp.concatenate([buf, extra], axis=0), 'col', pairs)  16.4 us
    ppermute x4, waiting for transfers between devices, route_forward(): got = lax.ppermute(held, 'row', xor_pairs(size, m))  15.8 us
  transfers between devices with their start and end apart: 19, of which 17 were waited for; matrix products, arithmetic and copies ran while one was open for 5% of the time, Pallas kernels for 0%

profile of v12, /device:TPU:1, one launch (start us, length us, event | category | flops | bytes accessed | tf_op | source)
XLA Modules:
  0.0 296.8 jit_solution(2716741444444118183)
XLA Ops:
  8.9 16.3 %collective-permute-start = (bf16[1,128,512]{2,1,0:T(8,128)(2,1)S(1)}, bf16[1,128,512]{2,1,0:T(8,128)(2,1)S(1)}, u32[]{:S(2)}, u32[]{:S(2)}) collective-permute-start(bf16[1,128,512]{2,1,0:T(8,128)(2,1)S(1)} %slice_bitcast_fusion.6), channel_id=1, source_target_pairs={{0,256},{32,288},{64,320},{96,352},{128,384},{160,416},{192,448},{... | collective-permute-start | bytes 393224 | tf_op jit(solution)/shard_map/ppermute | solution.py:80
  27.8 11.6 %collective-permute-start.1 = (bf16[2,128,512]{2,1,0:T(8,128)(2,1)S(1)}, bf16[2,128,512]{2,1,0:T(8,128)(2,1)S(1)}, u32[]{:S(2)}, u32[]{:S(2)}) collective-permute-start(bf16[2,128,512]{2,1,0:T(8,128)(2,1)S(1)} %maximum_select_fusion.2), channel_id=1, source_target_pairs={{0,32},{32,0},{64,96},{96,64},{128,160},{160,128},{192,224},{224,1... | collective-permute-start | bytes 786440 | tf_op jit(solution)/shard_map/ppermute | solution.py:80
  39.6 5.1 %collective-permute-done.1 = bf16[2,128,512]{2,1,0:T(8,128)(2,1)S(1)} collective-permute-done((bf16[2,128,512]{2,1,0:T(8,128)(2,1)S(1)}, bf16[2,128,512]{2,1,0:T(8,128)(2,1)S(1)}, u32[]{:S(2)}, u32[]{:S(2)}) %collective-permute-start.1) | collective-permute-done | bytes 262176 | tf_op jit(solution)/shard_map/ppermute | solution.py:80
  45.6 2.1 collective-permute-start.2
  47.8 13.5 %collective-permute-done.2 = bf16[2,128,512]{2,1,0:T(8,128)(2,1)S(1)} collective-permute-done((bf16[2,128,512]{2,1,0:T(8,128)(2,1)S(1)}, bf16[2,128,512]{2,1,0:T(8,128)(2,1)S(1)}, u32[]{:S(2)}, u32[]{:S(2)}) %collective-permute-start.2) | collective-permute-done | bytes 262176 | tf_op jit(solution)/shard_map/ppermute | solution.py:90
  61.5 8.1 %collective-permute-start.3 = (bf16[1,128,512]{2,1,0:T(8,128)(2,1)S(1)}, bf16[1,128,512]{2,1,0:T(8,128)(2,1)S(1)}, u32[]{:S(2)}, u32[]{:S(2)}) collective-permute-start(bf16[1,128,512]{2,1,0:T(8,128)(2,1)S(1)} %select_bitcast_fusion.3), channel_id=1, source_target_pairs={{0,128},{32,160},{64,192},{96,224},{128,0},{160,32},{192,64},{224,... | collective-permute-start | bytes 393224 | tf_op jit(solution)/shard_map/ppermute | solution.py:90
  72.9 7.5 %collective-permute-done.3 = bf16[1,128,512]{2,1,0:T(8,128)(2,1)S(1)} collective-permute-done((bf16[1,128,512]{2,1,0:T(8,128)(2,1)S(1)}, bf16[1,128,512]{2,1,0:T(8,128)(2,1)S(1)}, u32[]{:S(2)}, u32[]{:S(2)}) %collective-permute-start.3) | collective-permute-done | bytes 131104 | tf_op jit(solution)/shard_map/ppermute | solution.py:90
  80.5 2.8 gather_fusion.2
  83.6 11.2 %collective-permute-start.4 = (bf16[1,128,512]{2,1,0:T(8,128)(2,1)S(1)}, bf16[1,128,512]{2,1,0:T(8,128)(2,1)S(1)}, u32[]{:S(2)}, u32[]{:S(2)}) collective-permute-start(bf16[1,128,512]{2,1,0:T(8,128)(2,1)S(1)} %bitcast.102), channel_id=1, source_target_pairs={{0,256},{32,288},{64,320},{96,352},{128,384},{160,416},{192,448},{... | collective-permute-start | bytes 393224 | tf_op jit(solution)/shard_map/ppermute | solution.py:80
  94.8 10.2 %collective-permute-done.4 = bf16[1,128,512]{2,1,0:T(8,128)(2,1)S(1)} collective-permute-done((bf16[1,128,512]{2,1,0:T(8,128)(2,1)S(1)}, bf16[1,128,512]{2,1,0:T(8,128)(2,1)S(1)}, u32[]{:S(2)}, u32[]{:S(2)}) %collective-permute-start.4) | collective-permute-done | bytes 131104 | tf_op jit(solution)/shard_map/ppermute | solution.py:80
  108.1 4.7 %gather_fusion.3 = bf16[24,128,512]{2,1,0:T(8,128)(2,1)} fusion(bf16[32,128,512]{2,1,0:T(8,128)(2,1)} %bitcast.100, s32[1024]{0:T(1024)S(1)} %get-tuple-element.22), kind=kCustom, calls=%fused_computation.5 | custom fusion | bytes 6291552 | tf_op jit(solution)/shard_map/jit(_take)/gather | solution.py:152
  113.6 3.5 %collective-permute-start.6 = (bf16[2,128,512]{2,1,0:T(8,128)(2,1)S(1)}, bf16[2,128,512]{2,1,0:T(8,128)(2,1)S(1)}, u32[]{:S(2)}, u32[]{:S(2)}) collective-permute-start(bf16[2,128,512]{2,1,0:T(8,128)(2,1)S(1)} %select_bitcast_fusion), channel_id=1, source_target_pairs={{0,64},{32,96},{64,0},{96,32},{128,192},{160,224},{192,128},{224,1... | collective-permute-start | bytes 786440 | tf_op jit(solution)/shard_map/ppermute | solution.py:90
  117.1 2.9 fusion.2
  120.0 9.0 %collective-permute-done.6 = bf16[2,128,512]{2,1,0:T(8,128)(2,1)S(1)} collective-permute-done((bf16[2,128,512]{2,1,0:T(8,128)(2,1)S(1)}, bf16[2,128,512]{2,1,0:T(8,128)(2,1)S(1)}, u32[]{:S(2)}, u32[]{:S(2)}) %collective-permute-start.6) | collective-permute-done | bytes 262176 | tf_op jit(solution)/shard_map/ppermute | solution.py:90
  129.2 8.4 %collective-permute-start.7 = (bf16[1,128,512]{2,1,0:T(8,128)(2,1)S(1)}, bf16[1,128,512]{2,1,0:T(8,128)(2,1)S(1)}, u32[]{:S(2)}, u32[]{:S(2)}) collective-permute-start(bf16[1,128,512]{2,1,0:T(8,128)(2,1)S(1)} %select_bitcast_fusion.2), channel_id=1, source_target_pairs={{0,128},{32,160},{64,192},{96,224},{128,0},{160,32},{192,64},{224,... | collective-permute-start | bytes 393224 | tf_op jit(solution)/shard_map/ppermute | solution.py:90
  138.2 10.7 %collective-permute-done.7 = bf16[1,128,512]{2,1,0:T(8,128)(2,1)S(1)} collective-permute-done((bf16[1,128,512]{2,1,0:T(8,128)(2,1)S(1)}, bf16[1,128,512]{2,1,0:T(8,128)(2,1)S(1)}, u32[]{:S(2)}, u32[]{:S(2)}) %collective-permute-start.7) | collective-permute-done | bytes 131104 | tf_op jit(solution)/shard_map/ppermute | solution.py:90
  158.5 9.5 %all-to-all-start = ((f32[32,32,512]{2,1,0:T(8,128)}), f32[32,32,512]{2,1,0:T(8,128)S(1)}, u32[]{:S(2)}, u32[]{:S(2)}) async-start(f32[32,32,512]{2,1,0:T(8,128)} %gather_fusion.4), calls=%async_computation | async-start | bytes 4194304 | tf_op jit(solution)/shard_map/all_to_all | solution.py:28
  169.4 26.5 %all-to-all-done = f32[32,32,512]{2,1,0:T(8,128)S(1)} async-done(((f32[32,32,512]{2,1,0:T(8,128)}), f32[32,32,512]{2,1,0:T(8,128)S(1)}, u32[]{:S(2)}, u32[]{:S(2)}) %all-to-all-start) | async-done | bytes 2097184 | tf_op jit(solution)/shard_map/all_to_all | solution.py:28
  198.0 3.3 %collective-permute-done.8 = f32[40,512]{1,0:T(8,128)S(1)} collective-permute-done((f32[40,512]{1,0:T(8,128)S(1)}, f32[40,512]{1,0:T(8,128)S(1)}, u32[]{:S(2)}, u32[]{:S(2)}) %collective-permute-start.8) | collective-permute-done | bytes 81952 | tf_op jit(solution)/shard_map/ppermute | solution.py:34
  203.2 4.8 %collective-permute-done.9 = f32[40,512]{1,0:T(8,128)S(1)} collective-permute-done((f32[40,512]{1,0:T(8,128)S(1)}, f32[40,512]{1,0:T(8,128)S(1)}, u32[]{:S(2)}, u32[]{:S(2)}) %collective-permute-start.9) | collective-permute-done | bytes 81952 | tf_op jit(solution)/shard_map/ppermute | solution.py:34
  208.0 4.8 %collective-permute-start.10 = (f32[40,512]{1,0:T(8,128)S(1)}, f32[40,512]{1,0:T(8,128)S(1)}, u32[]{:S(2)}, u32[]{:S(2)}) collective-permute-start(f32[40,512]{1,0:T(8,128)S(1)} %add.281), channel_id=1, source_target_pairs={{0,128},{32,160},{64,192},{96,224},{128,0},{160,32},{192,64},{224,... | collective-permute-start | bytes 245768 | tf_op jit(solution)/shard_map/ppermute | solution.py:34
  212.8 6.1 %collective-permute-done.10 = f32[40,512]{1,0:T(8,128)S(1)} collective-permute-done((f32[40,512]{1,0:T(8,128)S(1)}, f32[40,512]{1,0:T(8,128)S(1)}, u32[]{:S(2)}, u32[]{:S(2)}) %collective-permute-start.10) | collective-permute-done | bytes 81952 | tf_op jit(solution)/shard_map/ppermute | solution.py:34
  218.9 7.1 %collective-permute-start.11 = (f32[40,512]{1,0:T(8,128)S(1)}, f32[40,512]{1,0:T(8,128)S(1)}, u32[]{:S(2)}, u32[]{:S(2)}) collective-permute-start(f32[40,512]{1,0:T(8,128)S(1)} %add.282), channel_id=1, source_target_pairs={{0,256},{32,288},{64,320},{96,352},{128,384},{160,416},{192,448},{... | collective-permute-start | bytes 245768 | tf_op jit(solution)/shard_map/ppermute | solution.py:34
  226.1 9.3 %collective-permute-done.11 = f32[40,512]{1,0:T(8,128)S(1)} collective-permute-done((f32[40,512]{1,0:T(8,128)S(1)}, f32[40,512]{1,0:T(8,128)S(1)}, u32[]{:S(2)}, u32[]{:S(2)}) %collective-permute-start.11) | collective-permute-done | bytes 81952 | tf_op jit(solution)/shard_map/ppermute | solution.py:34
  235.4 8.9 %collective-permute-start.12 = (f32[40,512]{1,0:T(8,128)S(1)}, f32[40,512]{1,0:T(8,128)S(1)}, u32[]{:S(2)}, u32[]{:S(2)}) collective-permute-start(f32[40,512]{1,0:T(8,128)S(1)} %add.283), channel_id=1, source_target_pairs={{0,16},{1,5},{2,18},{3,7},{4,20},{5,1},{6,22},{7,3},{8,24},{9,13},... | collective-permute-start | bytes 245768 | tf_op jit(solution)/shard_map/ppermute | solution.py:42
  246.2 4.8 %collective-permute-start.13 = (f32[72,512]{1,0:T(8,128)S(1)}, f32[72,512]{1,0:T(8,128)S(1)}, u32[]{:S(2)}, u32[]{:S(2)}) collective-permute-start(f32[72,512]{1,0:T(8,128)S(1)} %pad_maximum_fusion.8), channel_id=1, source_target_pairs={{0,8},{1,3},{2,10},{3,1},{4,12},{5,7},{6,14},{7,5},{8,0},{9,11},{1... | collective-permute-start | bytes 442376 | tf_op jit(solution)/shard_map/ppermute | solution.py:42
  251.1 2.4 collective-permute-done.13
  253.6 4.8 %collective-permute-start.14 = (f32[136,512]{1,0:T(8,128)S(1)}, f32[136,512]{1,0:T(8,128)S(1)}, u32[]{:S(2)}, u32[]{:S(2)}) collective-permute-start(f32[136,512]{1,0:T(8,128)S(1)} %pad_maximum_fusion.5), channel_id=1, source_target_pairs={{0,4},{1,17},{2,6},{3,19},{4,0},{5,21},{6,2},{7,23},{8,12},{9,25},... | collective-permute-start | bytes 835592 | tf_op jit(solution)/shard_map/ppermute | solution.py:42
  258.5 3.9 %collective-permute-done.14 = f32[136,512]{1,0:T(8,128)S(1)} collective-permute-done((f32[136,512]{1,0:T(8,128)S(1)}, f32[136,512]{1,0:T(8,128)S(1)}, u32[]{:S(2)}, u32[]{:S(2)}) %collective-permute-start.14) | collective-permute-done | bytes 278560 | tf_op jit(solution)/shard_map/ppermute | solution.py:42
  262.5 5.0 %collective-permute-start.15 = (f32[264,512]{1,0:T(8,128)S(1)}, f32[264,512]{1,0:T(8,128)S(1)}, u32[]{:S(2)}, u32[]{:S(2)}) collective-permute-start(f32[264,512]{1,0:T(8,128)S(1)} %pad_maximum_fusion.4), channel_id=1, source_target_pairs={{0,2},{1,9},{2,0},{3,11},{4,6},{5,13},{6,4},{7,15},{8,10},{9,1},{1... | collective-permute-start | bytes 1622024 | tf_op jit(solution)/shard_map/ppermute | solution.py:42
  267.8 6.8 %collective-permute-done.15 = f32[264,512]{1,0:T(8,128)S(1)} collective-permute-done((f32[264,512]{1,0:T(8,128)S(1)}, f32[264,512]{1,0:T(8,128)S(1)}, u32[]{:S(2)}, u32[]{:S(2)}) %collective-permute-start.15) | collective-permute-done | bytes 540704 | tf_op jit(solution)/shard_map/ppermute | solution.py:42
  274.7 6.4 %collective-permute-start.16 = (f32[520,512]{1,0:T(8,128)S(1)}, f32[520,512]{1,0:T(8,128)}, u32[]{:S(2)}, u32[]{:S(2)}) collective-permute-start(f32[520,512]{1,0:T(8,128)S(1)} %pad_maximum_fusion.2), channel_id=1, source_target_pairs={{0,1},{1,0},{2,3},{3,2},{4,5},{5,4},{6,7},{7,6},{8,9},{9,8},{10,11... | collective-permute-start | bytes 3194888 | tf_op jit(solution)/shard_map/ppermute | solution.py:42
  (112 shorter events, 33.3 us)
Async XLA Ops:
  7.2 141.8 %copy-start = (bf16[512,512]{1,0:T(8,128)(2,1)S(1)}, bf16[512,512]{1,0:T(8,128)(2,1)}, u32[]{:S(2)}) copy-start(bf16[512,512]{1,0:T(8,128)(2,1)} %param.20) | copy-start | bytes 1572868
  7.2 19.4 %copy-start.1 = (s32[16]{0:T(128)S(1)}, s32[16]{0:T(128)}, u32[]{:S(2)}) copy-start(s32[16]{0:T(128)} %param.18) | copy-start | bytes 196
  7.2 32.3 %copy-start.7 = (s32[4]{0:T(128)S(1)}, s32[4]{0:T(128)}, u32[]{:S(2)}) copy-start(s32[4]{0:T(128)} %param.15) | copy-start | bytes 52
  7.2 73.2 %all-gather.2.cloned.1.call-start = ((), (), s32[]{:S(2)}) async-start(), calls=%async_computation.1 | async-start | bytes 4325376 | tf_op jit(solution)/shard_map/all_gather | solution.py:146
  8.9 18.9 %collective-permute-start = (bf16[1,128,512]{2,1,0:T(8,128)(2,1)S(1)}, bf16[1,128,512]{2,1,0:T(8,128)(2,1)S(1)}, u32[]{:S(2)}, u32[]{:S(2)}) collective-permute-start(bf16[1,128,512]{2,1,0:T(8,128)(2,1)S(1)} %slice_bitcast_fusion.6), channel_id=1, source_target_pairs={{0,256},{32,288},{64,320},{96,352},{128,384},{160,416},{192,448},{... | collective-permute-start | bytes 393224 | tf_op jit(solution)/shard_map/ppermute | solution.py:80
  27.8 16.9 %collective-permute-start.1 = (bf16[2,128,512]{2,1,0:T(8,128)(2,1)S(1)}, bf16[2,128,512]{2,1,0:T(8,128)(2,1)S(1)}, u32[]{:S(2)}, u32[]{:S(2)}) collective-permute-start(bf16[2,128,512]{2,1,0:T(8,128)(2,1)S(1)} %maximum_select_fusion.2), channel_id=1, source_target_pairs={{0,32},{32,0},{64,96},{96,64},{128,160},{160,128},{192,224},{224,1... | collective-permute-start | bytes 786440 | tf_op jit(solution)/shard_map/ppermute | solution.py:80
  45.4 2.2 copy-start.2
  45.6 24.0 %copy-start.5 = (s32[4,8]{1,0:T(4,128)S(1)}, s32[4,8]{1,0:T(4,128)}, u32[]{:S(2)}) copy-start(s32[4,8]{1,0:T(4,128)} %param.14) | copy-start | bytes 388
  45.6 15.8 %collective-permute-start.2 = (bf16[2,128,512]{2,1,0:T(8,128)(2,1)S(1)}, bf16[2,128,512]{2,1,0:T(8,128)(2,1)S(1)}, u32[]{:S(2)}, u32[]{:S(2)}) collective-permute-start(bf16[2,128,512]{2,1,0:T(8,128)(2,1)S(1)} %select_bitcast_fusion.1), channel_id=1, source_target_pairs={{0,64},{32,96},{64,0},{96,32},{128,192},{160,224},{192,128},{224,1... | collective-permute-start | bytes 786440 | tf_op jit(solution)/shard_map/ppermute | solution.py:90
  61.5 18.9 %collective-permute-start.3 = (bf16[1,128,512]{2,1,0:T(8,128)(2,1)S(1)}, bf16[1,128,512]{2,1,0:T(8,128)(2,1)S(1)}, u32[]{:S(2)}, u32[]{:S(2)}) collective-permute-start(bf16[1,128,512]{2,1,0:T(8,128)(2,1)S(1)} %select_bitcast_fusion.3), channel_id=1, source_target_pairs={{0,128},{32,160},{64,192},{96,224},{128,0},{160,32},{192,64},{224,... | collective-permute-start | bytes 393224 | tf_op jit(solution)/shard_map/ppermute | solution.py:90
  83.3 23.7 %copy-start.6 = (s32[32]{0:T(128)S(1)}, s32[32]{0:T(128)}, u32[]{:S(2)}) copy-start(s32[32]{0:T(128)} %constant.294) | copy-start | bytes 388
  83.6 21.3 %collective-permute-start.4 = (bf16[1,128,512]{2,1,0:T(8,128)(2,1)S(1)}, bf16[1,128,512]{2,1,0:T(8,128)(2,1)S(1)}, u32[]{:S(2)}, u32[]{:S(2)}) collective-permute-start(bf16[1,128,512]{2,1,0:T(8,128)(2,1)S(1)} %bitcast.102), channel_id=1, source_target_pairs={{0,256},{32,288},{64,320},{96,352},{128,384},{160,416},{192,448},{... | collective-permute-start | bytes 393224 | tf_op jit(solution)/shard_map/ppermute | solution.py:80
  105.0 7.8 %collective-permute-start.5 = (bf16[2,128,512]{2,1,0:T(8,128)(2,1)S(1)}, bf16[2,128,512]{2,1,0:T(8,128)(2,1)S(1)}, u32[]{:S(2)}, u32[]{:S(2)}) collective-permute-start(bf16[2,128,512]{2,1,0:T(8,128)(2,1)S(1)} %maximum_select_fusion.3), channel_id=1, source_target_pairs={{0,32},{32,0},{64,96},{96,64},{128,160},{160,128},{192,224},{224,1... | collective-permute-start | bytes 786440 | tf_op jit(solution)/shard_map/ppermute | solution.py:80
  113.6 15.4 %collective-permute-start.6 = (bf16[2,128,512]{2,1,0:T(8,128)(2,1)S(1)}, bf16[2,128,512]{2,1,0:T(8,128)(2,1)S(1)}, u32[]{:S(2)}, u32[]{:S(2)}) collective-permute-start(bf16[2,128,512]{2,1,0:T(8,128)(2,1)S(1)} %select_bitcast_fusion), channel_id=1, source_target_pairs={{0,64},{32,96},{64,0},{96,32},{128,192},{160,224},{192,128},{224,1... | collective-permute-start | bytes 786440 | tf_op jit(solution)/shard_map/ppermute | solution.py:90
  120.0 17.6 %copy-start.3 = (bf16[512,512]{1,0:T(8,128)(2,1)S(1)}, bf16[512,512]{1,0:T(8,128)(2,1)}, u32[]{:S(2)}) copy-start(bf16[512,512]{1,0:T(8,128)(2,1)} %param.19) | copy-start | bytes 1572868
  129.2 19.8 %collective-permute-start.7 = (bf16[1,128,512]{2,1,0:T(8,128)(2,1)S(1)}, bf16[1,128,512]{2,1,0:T(8,128)(2,1)S(1)}, u32[]{:S(2)}, u32[]{:S(2)}) collective-permute-start(bf16[1,128,512]{2,1,0:T(8,128)(2,1)S(1)} %select_bitcast_fusion.2), channel_id=1, source_target_pairs={{0,128},{32,160},{64,192},{96,224},{128,0},{160,32},{192,64},{224,... | collective-permute-start | bytes 393224 | tf_op jit(solution)/shard_map/ppermute | solution.py:90
  149.7 1.1 copy-start.4
  158.5 37.4 %all-to-all-start = ((f32[32,32,512]{2,1,0:T(8,128)}), f32[32,32,512]{2,1,0:T(8,128)S(1)}, u32[]{:S(2)}, u32[]{:S(2)}) async-start(f32[32,32,512]{2,1,0:T(8,128)} %gather_fusion.4), calls=%async_computation | async-start | bytes 4194304 | tf_op jit(solution)/shard_map/all_to_all | solution.py:28
  196.1 5.2 %collective-permute-start.8 = (f32[40,512]{1,0:T(8,128)S(1)}, f32[40,512]{1,0:T(8,128)S(1)}, u32[]{:S(2)}, u32[]{:S(2)}) collective-permute-start(f32[40,512]{1,0:T(8,128)S(1)} %concatenate.64), channel_id=1, source_target_pairs={{0,32},{32,0},{64,96},{96,64},{128,160},{160,128},{192,224},{224,1... | collective-permute-start | bytes 245768 | tf_op jit(solution)/shard_map/ppermute | solution.py:34
  201.3 6.7 %collective-permute-start.9 = (f32[40,512]{1,0:T(8,128)S(1)}, f32[40,512]{1,0:T(8,128)S(1)}, u32[]{:S(2)}, u32[]{:S(2)}) collective-permute-start(f32[40,512]{1,0:T(8,128)S(1)} %pad_add_fusion), channel_id=1, source_target_pairs={{0,64},{32,96},{64,0},{96,32},{128,192},{160,224},{192,128},{224,1... | collective-permute-start | bytes 245768 | tf_op jit(solution)/shard_map/ppermute | solution.py:34
  208.0 10.9 %collective-permute-start.10 = (f32[40,512]{1,0:T(8,128)S(1)}, f32[40,512]{1,0:T(8,128)S(1)}, u32[]{:S(2)}, u32[]{:S(2)}) collective-permute-start(f32[40,512]{1,0:T(8,128)S(1)} %add.281), channel_id=1, source_target_pairs={{0,128},{32,160},{64,192},{96,224},{128,0},{160,32},{192,64},{224,... | collective-permute-start | bytes 245768 | tf_op jit(solution)/shard_map/ppermute | solution.py:34
  218.9 16.5 %collective-permute-start.11 = (f32[40,512]{1,0:T(8,128)S(1)}, f32[40,512]{1,0:T(8,128)S(1)}, u32[]{:S(2)}, u32[]{:S(2)}) collective-permute-start(f32[40,512]{1,0:T(8,128)S(1)} %add.282), channel_id=1, source_target_pairs={{0,256},{32,288},{64,320},{96,352},{128,384},{160,416},{192,448},{... | collective-permute-start | bytes 245768 | tf_op jit(solution)/shard_map/ppermute | solution.py:34
  235.4 10.8 %collective-permute-start.12 = (f32[40,512]{1,0:T(8,128)S(1)}, f32[40,512]{1,0:T(8,128)S(1)}, u32[]{:S(2)}, u32[]{:S(2)}) collective-permute-start(f32[40,512]{1,0:T(8,128)S(1)} %add.283), channel_id=1, source_target_pairs={{0,16},{1,5},{2,18},{3,7},{4,20},{5,1},{6,22},{7,3},{8,24},{9,13},... | collective-permute-start | bytes 245768 | tf_op jit(solution)/shard_map/ppermute | solution.py:42
  246.2 7.4 %collective-permute-start.13 = (f32[72,512]{1,0:T(8,128)S(1)}, f32[72,512]{1,0:T(8,128)S(1)}, u32[]{:S(2)}, u32[]{:S(2)}) collective-permute-start(f32[72,512]{1,0:T(8,128)S(1)} %pad_maximum_fusion.8), channel_id=1, source_target_pairs={{0,8},{1,3},{2,10},{3,1},{4,12},{5,7},{6,14},{7,5},{8,0},{9,11},{1... | collective-permute-start | bytes 442376 | tf_op jit(solution)/shard_map/ppermute | solution.py:42
  253.6 8.8 %collective-permute-start.14 = (f32[136,512]{1,0:T(8,128)S(1)}, f32[136,512]{1,0:T(8,128)S(1)}, u32[]{:S(2)}, u32[]{:S(2)}) collective-permute-start(f32[136,512]{1,0:T(8,128)S(1)} %pad_maximum_fusion.5), channel_id=1, source_target_pairs={{0,4},{1,17},{2,6},{3,19},{4,0},{5,21},{6,2},{7,23},{8,12},{9,25},... | collective-permute-start | bytes 835592 | tf_op jit(solution)/shard_map/ppermute | solution.py:42
  262.5 12.1 %collective-permute-start.15 = (f32[264,512]{1,0:T(8,128)S(1)}, f32[264,512]{1,0:T(8,128)S(1)}, u32[]{:S(2)}, u32[]{:S(2)}) collective-permute-start(f32[264,512]{1,0:T(8,128)S(1)} %pad_maximum_fusion.4), channel_id=1, source_target_pairs={{0,2},{1,9},{2,0},{3,11},{4,6},{5,13},{6,4},{7,15},{8,10},{9,1},{1... | collective-permute-start | bytes 1622024 | tf_op jit(solution)/shard_map/ppermute | solution.py:42
  274.7 8.8 %collective-permute-start.16 = (f32[520,512]{1,0:T(8,128)S(1)}, f32[520,512]{1,0:T(8,128)}, u32[]{:S(2)}, u32[]{:S(2)}) collective-permute-start(f32[520,512]{1,0:T(8,128)S(1)} %pad_maximum_fusion.2), channel_id=1, source_target_pairs={{0,1},{1,0},{2,3},{3,2},{4,5},{5,4},{6,7},{7,6},{8,9},{9,8},{10,11... | collective-permute-start | bytes 3194888 | tf_op jit(solution)/shard_map/ppermute | solution.py:42
Sparse Core Ops, SparseCore 0:
  11.2 67.0 all-gather.1

commit v13 on v12

--- a/solution.py
+++ b/solution.py
@@ -24,7 +24,7 @@
     orders = [[mask for mask in order if mask < ways] for order in DOUBLING]
     position = [sum(((j // mask) % 2) << t for t, mask in enumerate(orders[j % 2])) for j in range(ways)]
     rows = buf.shape[0] // ways
-    chunks = buf.reshape(ways, rows, buf.shape[1])[jnp.array(position, jnp.int32)]
+    chunks = buf.reshape(ways, rows, buf.shape[1])
     scattered = lax.all_to_all(chunks, "col", 0, 0, tiled=False).sum(axis=0)
     joined = jnp.concatenate([scattered, extra], axis=0)
     for axis, mask in BUTTERFLY:
@@ -45,6 +45,7 @@
         out = lax.dynamic_update_slice_in_dim(out, buf, bit * held, 0)
         out = lax.dynamic_update_slice_in_dim(out, got[:held], (1 - bit) * held, 0)
         buf = out
+    buf = buf.reshape(ways, rows, buf.shape[1])[jnp.array(position, jnp.int32)].reshape(-1, buf.shape[1])
     return buf, extra
 
 

time: 298 us -> 301 us (1.010)
  transfers between devices with their start and end apart: 19 -> 19, of which waited for: 17 -> 18; matrix products, arithmetic and copies ran while one was open for 5% -> 5% of each run, Pallas kernels for 0% -> 0%
where the time goes in v13:
time: 301 us; the launch traced here: 300 us
  waiting for transfers between devices  122 us (41%)
  starting transfers between devices  121 us (40%)
  between operations  21.4 us (7%)
  local copies, waits for them, and re-layouts  21.2 us (7%)
  matrix products  9.86 us (3%)
  other arithmetic  4.15 us (1%)
    ppermute x4, starting transfers between devices, route_forward(): got = lax.ppermute(held, 'row', xor_pairs(size, m))  41 us
    ppermute x4, waiting for transfers between devices, route_forward(): got = lax.ppermute(send, 'row', xor_pairs(size, m))  38.3 us
    ppermute x5, starting transfers between devices, tree_allreduce(): got = lax.ppermute(jnp.concatenate([buf, extra], axis=0), 'col', pairs)  30 us
    all_to_all x1, waiting for transfers between devices, tree_allreduce(): scattered = lax.all_to_all(chunks, 'col', 0, 0, tiled=False).sum(axis=0)  26.5 us
    ppermute x4, starting transfers between devices, route_forward(): got = lax.ppermute(send, 'row', xor_pairs(size, m))  24.2 us
    ppermute x4, waiting for transfers between devices, tree_allreduce(): joined = joined + lax.ppermute(joined, axis, xor_pairs(size, mask))  23.6 us
    ppermute x5, waiting for transfers between devices, tree_allreduce(): got = lax.ppermute(jnp.concatenate([buf, extra], axis=0), 'col', pairs)  16.4 us
    ppermute x4, waiting for transfers between devices, route_forward(): got = lax.ppermute(held, 'row', xor_pairs(size, m))  16.2 us
  transfers between devices with their start and end apart: 19, of which 18 were waited for; matrix products, arithmetic and copies ran while one was open for 5% of the time, Pallas kernels for 0%

profile of v13, /device:TPU:1, one launch (start us, length us, event | category | flops | bytes accessed | tf_op | source)
XLA Modules:
  0.0 299.7 jit_solution(6933164374018431480)
XLA Ops:
  8.9 16.3 %collective-permute-start = (bf16[1,128,512]{2,1,0:T(8,128)(2,1)S(1)}, bf16[1,128,512]{2,1,0:T(8,128)(2,1)S(1)}, u32[]{:S(2)}, u32[]{:S(2)}) collective-permute-start(bf16[1,128,512]{2,1,0:T(8,128)(2,1)S(1)} %slice_bitcast_fusion.6), channel_id=1, source_target_pairs={{0,256},{32,288},{64,320},{96,352},{128,384},{160,416},{192,448},{... | collective-permute-start | bytes 393224 | tf_op jit(solution)/shard_map/ppermute | solution.py:81
  27.8 11.6 %collective-permute-start.1 = (bf16[2,128,512]{2,1,0:T(8,128)(2,1)S(1)}, bf16[2,128,512]{2,1,0:T(8,128)(2,1)S(1)}, u32[]{:S(2)}, u32[]{:S(2)}) collective-permute-start(bf16[2,128,512]{2,1,0:T(8,128)(2,1)S(1)} %maximum_select_fusion.2), channel_id=1, source_target_pairs={{0,32},{32,0},{64,96},{96,64},{128,160},{160,128},{192,224},{224,1... | collective-permute-start | bytes 786440 | tf_op jit(solution)/shard_map/ppermute | solution.py:81
  39.6 5.1 %collective-permute-done.1 = bf16[2,128,512]{2,1,0:T(8,128)(2,1)S(1)} collective-permute-done((bf16[2,128,512]{2,1,0:T(8,128)(2,1)S(1)}, bf16[2,128,512]{2,1,0:T(8,128)(2,1)S(1)}, u32[]{:S(2)}, u32[]{:S(2)}) %collective-permute-start.1) | collective-permute-done | bytes 262176 | tf_op jit(solution)/shard_map/ppermute | solution.py:81
  47.8 13.5 %collective-permute-done.2 = bf16[2,128,512]{2,1,0:T(8,128)(2,1)S(1)} collective-permute-done((bf16[2,128,512]{2,1,0:T(8,128)(2,1)S(1)}, bf16[2,128,512]{2,1,0:T(8,128)(2,1)S(1)}, u32[]{:S(2)}, u32[]{:S(2)}) %collective-permute-start.2) | collective-permute-done | bytes 262176 | tf_op jit(solution)/shard_map/ppermute | solution.py:91
  61.5 8.1 %collective-permute-start.3 = (bf16[1,128,512]{2,1,0:T(8,128)(2,1)S(1)}, bf16[1,128,512]{2,1,0:T(8,128)(2,1)S(1)}, u32[]{:S(2)}, u32[]{:S(2)}) collective-permute-start(bf16[1,128,512]{2,1,0:T(8,128)(2,1)S(1)} %select_bitcast_fusion.3), channel_id=1, source_target_pairs={{0,128},{32,160},{64,192},{96,224},{128,0},{160,32},{192,64},{224,... | collective-permute-start | bytes 393224 | tf_op jit(solution)/shard_map/ppermute | solution.py:91
  73.0 7.4 %collective-permute-done.3 = bf16[1,128,512]{2,1,0:T(8,128)(2,1)S(1)} collective-permute-done((bf16[1,128,512]{2,1,0:T(8,128)(2,1)S(1)}, bf16[1,128,512]{2,1,0:T(8,128)(2,1)S(1)}, u32[]{:S(2)}, u32[]{:S(2)}) %collective-permute-start.3) | collective-permute-done | bytes 131104 | tf_op jit(solution)/shard_map/ppermute | solution.py:91
  80.5 2.8 gather_fusion.2
  83.6 11.2 %collective-permute-start.4 = (bf16[1,128,512]{2,1,0:T(8,128)(2,1)S(1)}, bf16[1,128,512]{2,1,0:T(8,128)(2,1)S(1)}, u32[]{:S(2)}, u32[]{:S(2)}) collective-permute-start(bf16[1,128,512]{2,1,0:T(8,128)(2,1)S(1)} %bitcast.106), channel_id=1, source_target_pairs={{0,256},{32,288},{64,320},{96,352},{128,384},{160,416},{192,448},{... | collective-permute-start | bytes 393224 | tf_op jit(solution)/shard_map/ppermute | solution.py:81
  94.8 10.2 %collective-permute-done.4 = bf16[1,128,512]{2,1,0:T(8,128)(2,1)S(1)} collective-permute-done((bf16[1,128,512]{2,1,0:T(8,128)(2,1)S(1)}, bf16[1,128,512]{2,1,0:T(8,128)(2,1)S(1)}, u32[]{:S(2)}, u32[]{:S(2)}) %collective-permute-start.4) | collective-permute-done | bytes 131104 | tf_op jit(solution)/shard_map/ppermute | solution.py:81
  106.9 4.7 %gather_fusion.3 = bf16[24,128,512]{2,1,0:T(8,128)(2,1)} fusion(bf16[32,128,512]{2,1,0:T(8,128)(2,1)} %bitcast.104, s32[1024]{0:T(1024)S(1)} %get-tuple-element.21), kind=kCustom, calls=%fused_computation.5 | custom fusion | bytes 6291552 | tf_op jit(solution)/shard_map/jit(_take)/gather | solution.py:153
  112.9 4.2 %collective-permute-start.6 = (bf16[2,128,512]{2,1,0:T(8,128)(2,1)S(1)}, bf16[2,128,512]{2,1,0:T(8,128)(2,1)S(1)}, u32[]{:S(2)}, u32[]{:S(2)}) collective-permute-start(bf16[2,128,512]{2,1,0:T(8,128)(2,1)S(1)} %select_bitcast_fusion), channel_id=1, source_target_pairs={{0,64},{32,96},{64,0},{96,32},{128,192},{160,224},{192,128},{224,1... | collective-permute-start | bytes 786440 | tf_op jit(solution)/shard_map/ppermute | solution.py:91
  117.1 2.9 fusion.2
  120.0 7.8 %collective-permute-done.6 = bf16[2,128,512]{2,1,0:T(8,128)(2,1)S(1)} collective-permute-done((bf16[2,128,512]{2,1,0:T(8,128)(2,1)S(1)}, bf16[2,128,512]{2,1,0:T(8,128)(2,1)S(1)}, u32[]{:S(2)}, u32[]{:S(2)}) %collective-permute-start.6) | collective-permute-done | bytes 262176 | tf_op jit(solution)/shard_map/ppermute | solution.py:91
  127.9 9.9 %collective-permute-start.7 = (bf16[1,128,512]{2,1,0:T(8,128)(2,1)S(1)}, bf16[1,128,512]{2,1,0:T(8,128)(2,1)S(1)}, u32[]{:S(2)}, u32[]{:S(2)}) collective-permute-start(bf16[1,128,512]{2,1,0:T(8,128)(2,1)S(1)} %select_bitcast_fusion.2), channel_id=1, source_target_pairs={{0,128},{32,160},{64,192},{96,224},{128,0},{160,32},{192,64},{224,... | collective-permute-start | bytes 393224 | tf_op jit(solution)/shard_map/ppermute | solution.py:91
  138.4 9.5 %collective-permute-done.7 = bf16[1,128,512]{2,1,0:T(8,128)(2,1)S(1)} collective-permute-done((bf16[1,128,512]{2,1,0:T(8,128)(2,1)S(1)}, bf16[1,128,512]{2,1,0:T(8,128)(2,1)S(1)}, u32[]{:S(2)}, u32[]{:S(2)}) %collective-permute-start.7) | collective-permute-done | bytes 131104 | tf_op jit(solution)/shard_map/ppermute | solution.py:91
  156.9 10.7 %all-to-all-start = ((f32[32,32,512]{2,1,0:T(8,128)}), f32[32,32,512]{2,1,0:T(8,128)S(1)}, u32[]{:S(2)}, u32[]{:S(2)}) async-start(f32[32,32,512]{2,1,0:T(8,128)} %bitcast.97), calls=%async_computation | async-start | bytes 4194304 | tf_op jit(solution)/shard_map/all_to_all | solution.py:28
  168.9 26.5 %all-to-all-done = f32[32,32,512]{2,1,0:T(8,128)S(1)} async-done(((f32[32,32,512]{2,1,0:T(8,128)}), f32[32,32,512]{2,1,0:T(8,128)S(1)}, u32[]{:S(2)}, u32[]{:S(2)}) %all-to-all-start) | async-done | bytes 2097184 | tf_op jit(solution)/shard_map/all_to_all | solution.py:28
  197.5 3.3 %collective-permute-done.8 = f32[40,512]{1,0:T(8,128)S(1)} collective-permute-done((f32[40,512]{1,0:T(8,128)S(1)}, f32[40,512]{1,0:T(8,128)S(1)}, u32[]{:S(2)}, u32[]{:S(2)}) %collective-permute-start.8) | collective-permute-done | bytes 81952 | tf_op jit(solution)/shard_map/ppermute | solution.py:34
  202.7 4.8 %collective-permute-done.9 = f32[40,512]{1,0:T(8,128)S(1)} collective-permute-done((f32[40,512]{1,0:T(8,128)S(1)}, f32[40,512]{1,0:T(8,128)S(1)}, u32[]{:S(2)}, u32[]{:S(2)}) %collective-permute-start.9) | collective-permute-done | bytes 81952 | tf_op jit(solution)/shard_map/ppermute | solution.py:34
  207.5 4.6 %collective-permute-start.10 = (f32[40,512]{1,0:T(8,128)S(1)}, f32[40,512]{1,0:T(8,128)S(1)}, u32[]{:S(2)}, u32[]{:S(2)}) collective-permute-start(f32[40,512]{1,0:T(8,128)S(1)} %add.279), channel_id=1, source_target_pairs={{0,128},{32,160},{64,192},{96,224},{128,0},{160,32},{192,64},{224,... | collective-permute-start | bytes 245768 | tf_op jit(solution)/shard_map/ppermute | solution.py:34
  212.1 6.3 %collective-permute-done.10 = f32[40,512]{1,0:T(8,128)S(1)} collective-permute-done((f32[40,512]{1,0:T(8,128)S(1)}, f32[40,512]{1,0:T(8,128)S(1)}, u32[]{:S(2)}, u32[]{:S(2)}) %collective-permute-start.10) | collective-permute-done | bytes 81952 | tf_op jit(solution)/shard_map/ppermute | solution.py:34
  218.4 6.9 %collective-permute-start.11 = (f32[40,512]{1,0:T(8,128)S(1)}, f32[40,512]{1,0:T(8,128)S(1)}, u32[]{:S(2)}, u32[]{:S(2)}) collective-permute-start(f32[40,512]{1,0:T(8,128)S(1)} %add.280), channel_id=1, source_target_pairs={{0,256},{32,288},{64,320},{96,352},{128,384},{160,416},{192,448},{... | collective-permute-start | bytes 245768 | tf_op jit(solution)/shard_map/ppermute | solution.py:34
  225.4 9.3 %collective-permute-done.11 = f32[40,512]{1,0:T(8,128)S(1)} collective-permute-done((f32[40,512]{1,0:T(8,128)S(1)}, f32[40,512]{1,0:T(8,128)S(1)}, u32[]{:S(2)}, u32[]{:S(2)}) %collective-permute-start.11) | collective-permute-done | bytes 81952 | tf_op jit(solution)/shard_map/ppermute | solution.py:34
  234.7 8.9 %collective-permute-start.12 = (f32[40,512]{1,0:T(8,128)S(1)}, f32[40,512]{1,0:T(8,128)S(1)}, u32[]{:S(2)}, u32[]{:S(2)}) collective-permute-start(f32[40,512]{1,0:T(8,128)S(1)} %add.281), channel_id=1, source_target_pairs={{0,16},{1,5},{2,18},{3,7},{4,20},{5,1},{6,22},{7,3},{8,24},{9,13},... | collective-permute-start | bytes 245768 | tf_op jit(solution)/shard_map/ppermute | solution.py:42
  245.5 4.8 %collective-permute-start.13 = (f32[72,512]{1,0:T(8,128)S(1)}, f32[72,512]{1,0:T(8,128)S(1)}, u32[]{:S(2)}, u32[]{:S(2)}) collective-permute-start(f32[72,512]{1,0:T(8,128)S(1)} %pad_maximum_fusion.8), channel_id=1, source_target_pairs={{0,8},{1,3},{2,10},{3,1},{4,12},{5,7},{6,14},{7,5},{8,0},{9,11},{1... | collective-permute-start | bytes 442376 | tf_op jit(solution)/shard_map/ppermute | solution.py:42
  250.5 2.4 collective-permute-done.13
  252.9 4.8 %collective-permute-start.14 = (f32[136,512]{1,0:T(8,128)S(1)}, f32[136,512]{1,0:T(8,128)S(1)}, u32[]{:S(2)}, u32[]{:S(2)}) collective-permute-start(f32[136,512]{1,0:T(8,128)S(1)} %pad_maximum_fusion.5), channel_id=1, source_target_pairs={{0,4},{1,17},{2,6},{3,19},{4,0},{5,21},{6,2},{7,23},{8,12},{9,25},... | collective-permute-start | bytes 835592 | tf_op jit(solution)/shard_map/ppermute | solution.py:42
  257.8 3.9 %collective-permute-done.14 = f32[136,512]{1,0:T(8,128)S(1)} collective-permute-done((f32[136,512]{1,0:T(8,128)S(1)}, f32[136,512]{1,0:T(8,128)S(1)}, u32[]{:S(2)}, u32[]{:S(2)}) %collective-permute-start.14) | collective-permute-done | bytes 278560 | tf_op jit(solution)/shard_map/ppermute | solution.py:42
  261.8 5.0 %collective-permute-start.15 = (f32[264,512]{1,0:T(8,128)S(1)}, f32[264,512]{1,0:T(8,128)S(1)}, u32[]{:S(2)}, u32[]{:S(2)}) collective-permute-start(f32[264,512]{1,0:T(8,128)S(1)} %pad_maximum_fusion.4), channel_id=1, source_target_pairs={{0,2},{1,9},{2,0},{3,11},{4,6},{5,13},{6,4},{7,15},{8,10},{9,1},{1... | collective-permute-start | bytes 1622024 | tf_op jit(solution)/shard_map/ppermute | solution.py:42
  267.1 6.8 %collective-permute-done.15 = f32[264,512]{1,0:T(8,128)S(1)} collective-permute-done((f32[264,512]{1,0:T(8,128)S(1)}, f32[264,512]{1,0:T(8,128)S(1)}, u32[]{:S(2)}, u32[]{:S(2)}) %collective-permute-start.15) | collective-permute-done | bytes 540704 | tf_op jit(solution)/shard_map/ppermute | solution.py:42
  274.0 6.4 %collective-permute-start.16 = (f32[520,512]{1,0:T(8,128)S(1)}, f32[520,512]{1,0:T(8,128)}, u32[]{:S(2)}, u32[]{:S(2)}) collective-permute-start(f32[520,512]{1,0:T(8,128)S(1)} %pad_maximum_fusion.2), channel_id=1, source_target_pairs={{0,1},{1,0},{2,3},{3,2},{4,5},{5,4},{6,7},{7,6},{8,9},{9,8},{10,11... | collective-permute-start | bytes 3194888 | tf_op jit(solution)/shard_map/ppermute | solution.py:42
  285.5 2.3 gather_fusion.4
  (116 shorter events, 35.3 us)
Async XLA Ops:
  7.2 140.8 %copy-start = (bf16[512,512]{1,0:T(8,128)(2,1)S(1)}, bf16[512,512]{1,0:T(8,128)(2,1)}, u32[]{:S(2)}) copy-start(bf16[512,512]{1,0:T(8,128)(2,1)} %param.20) | copy-start | bytes 1572868
  7.2 19.4 %copy-start.1 = (s32[16]{0:T(128)S(1)}, s32[16]{0:T(128)}, u32[]{:S(2)}) copy-start(s32[16]{0:T(128)} %param.18) | copy-start | bytes 196
  7.2 32.3 %copy-start.9 = (s32[4]{0:T(128)S(1)}, s32[4]{0:T(128)}, u32[]{:S(2)}) copy-start(s32[4]{0:T(128)} %param.15) | copy-start | bytes 52
  7.2 73.2 %all-gather.2.cloned.1.call-start = ((), (), s32[]{:S(2)}) async-start(), calls=%async_computation.1 | async-start | bytes 4325376 | tf_op jit(solution)/shard_map/all_gather | solution.py:147
  8.9 18.9 %collective-permute-start = (bf16[1,128,512]{2,1,0:T(8,128)(2,1)S(1)}, bf16[1,128,512]{2,1,0:T(8,128)(2,1)S(1)}, u32[]{:S(2)}, u32[]{:S(2)}) collective-permute-start(bf16[1,128,512]{2,1,0:T(8,128)(2,1)S(1)} %slice_bitcast_fusion.6), channel_id=1, source_target_pairs={{0,256},{32,288},{64,320},{96,352},{128,384},{160,416},{192,448},{... | collective-permute-start | bytes 393224 | tf_op jit(solution)/shard_map/ppermute | solution.py:81
  27.8 16.9 %collective-permute-start.1 = (bf16[2,128,512]{2,1,0:T(8,128)(2,1)S(1)}, bf16[2,128,512]{2,1,0:T(8,128)(2,1)S(1)}, u32[]{:S(2)}, u32[]{:S(2)}) collective-permute-start(bf16[2,128,512]{2,1,0:T(8,128)(2,1)S(1)} %maximum_select_fusion.2), channel_id=1, source_target_pairs={{0,32},{32,0},{64,96},{96,64},{128,160},{160,128},{192,224},{224,1... | collective-permute-start | bytes 786440 | tf_op jit(solution)/shard_map/ppermute | solution.py:81
  45.4 2.2 copy-start.3
  45.6 24.0 %copy-start.7 = (s32[4,8]{1,0:T(4,128)S(1)}, s32[4,8]{1,0:T(4,128)}, u32[]{:S(2)}) copy-start(s32[4,8]{1,0:T(4,128)} %param.14) | copy-start | bytes 388
  45.6 15.8 %collective-permute-start.2 = (bf16[2,128,512]{2,1,0:T(8,128)(2,1)S(1)}, bf16[2,128,512]{2,1,0:T(8,128)(2,1)S(1)}, u32[]{:S(2)}, u32[]{:S(2)}) collective-permute-start(bf16[2,128,512]{2,1,0:T(8,128)(2,1)S(1)} %select_bitcast_fusion.1), channel_id=1, source_target_pairs={{0,64},{32,96},{64,0},{96,32},{128,192},{160,224},{192,128},{224,1... | collective-permute-start | bytes 786440 | tf_op jit(solution)/shard_map/ppermute | solution.py:91
  61.5 18.9 %collective-permute-start.3 = (bf16[1,128,512]{2,1,0:T(8,128)(2,1)S(1)}, bf16[1,128,512]{2,1,0:T(8,128)(2,1)S(1)}, u32[]{:S(2)}, u32[]{:S(2)}) collective-permute-start(bf16[1,128,512]{2,1,0:T(8,128)(2,1)S(1)} %select_bitcast_fusion.3), channel_id=1, source_target_pairs={{0,128},{32,160},{64,192},{96,224},{128,0},{160,32},{192,64},{224,... | collective-permute-start | bytes 393224 | tf_op jit(solution)/shard_map/ppermute | solution.py:91
  83.3 23.6 %copy-start.4 = (bf16[512,512]{1,0:T(8,128)(2,1)S(1)}, bf16[512,512]{1,0:T(8,128)(2,1)}, u32[]{:S(2)}) copy-start(bf16[512,512]{1,0:T(8,128)(2,1)} %param.12) | copy-start | bytes 1572868
  83.6 21.3 %collective-permute-start.4 = (bf16[1,128,512]{2,1,0:T(8,128)(2,1)S(1)}, bf16[1,128,512]{2,1,0:T(8,128)(2,1)S(1)}, u32[]{:S(2)}, u32[]{:S(2)}) collective-permute-start(bf16[1,128,512]{2,1,0:T(8,128)(2,1)S(1)} %bitcast.106), channel_id=1, source_target_pairs={{0,256},{32,288},{64,320},{96,352},{128,384},{160,416},{192,448},{... | collective-permute-start | bytes 393224 | tf_op jit(solution)/shard_map/ppermute | solution.py:81
  105.0 7.1 %collective-permute-start.5 = (bf16[2,128,512]{2,1,0:T(8,128)(2,1)S(1)}, bf16[2,128,512]{2,1,0:T(8,128)(2,1)S(1)}, u32[]{:S(2)}, u32[]{:S(2)}) collective-permute-start(bf16[2,128,512]{2,1,0:T(8,128)(2,1)S(1)} %maximum_select_fusion.3), channel_id=1, source_target_pairs={{0,32},{32,0},{64,96},{96,64},{128,160},{160,128},{192,224},{224,1... | collective-permute-start | bytes 786440 | tf_op jit(solution)/shard_map/ppermute | solution.py:81
  112.9 14.9 %collective-permute-start.6 = (bf16[2,128,512]{2,1,0:T(8,128)(2,1)S(1)}, bf16[2,128,512]{2,1,0:T(8,128)(2,1)S(1)}, u32[]{:S(2)}, u32[]{:S(2)}) collective-permute-start(bf16[2,128,512]{2,1,0:T(8,128)(2,1)S(1)} %select_bitcast_fusion), channel_id=1, source_target_pairs={{0,64},{32,96},{64,0},{96,32},{128,192},{160,224},{192,128},{224,1... | collective-permute-start | bytes 786440 | tf_op jit(solution)/shard_map/ppermute | solution.py:91
  120.0 17.8 %copy-start.5 = (bf16[512,512]{1,0:T(8,128)(2,1)S(1)}, bf16[512,512]{1,0:T(8,128)(2,1)}, u32[]{:S(2)}) copy-start(bf16[512,512]{1,0:T(8,128)(2,1)} %param.19) | copy-start | bytes 1572868
  127.9 20.1 %collective-permute-start.7 = (bf16[1,128,512]{2,1,0:T(8,128)(2,1)S(1)}, bf16[1,128,512]{2,1,0:T(8,128)(2,1)S(1)}, u32[]{:S(2)}, u32[]{:S(2)}) collective-permute-start(bf16[1,128,512]{2,1,0:T(8,128)(2,1)S(1)} %select_bitcast_fusion.2), channel_id=1, source_target_pairs={{0,128},{32,160},{64,192},{96,224},{128,0},{160,32},{192,64},{224,... | collective-permute-start | bytes 393224 | tf_op jit(solution)/shard_map/ppermute | solution.py:91
  148.7 1.1 copy-start.6
  156.9 38.5 %all-to-all-start = ((f32[32,32,512]{2,1,0:T(8,128)}), f32[32,32,512]{2,1,0:T(8,128)S(1)}, u32[]{:S(2)}, u32[]{:S(2)}) async-start(f32[32,32,512]{2,1,0:T(8,128)} %bitcast.97), calls=%async_computation | async-start | bytes 4194304 | tf_op jit(solution)/shard_map/all_to_all | solution.py:28
  195.6 5.2 %collective-permute-start.8 = (f32[40,512]{1,0:T(8,128)S(1)}, f32[40,512]{1,0:T(8,128)S(1)}, u32[]{:S(2)}, u32[]{:S(2)}) collective-permute-start(f32[40,512]{1,0:T(8,128)S(1)} %concatenate.64), channel_id=1, source_target_pairs={{0,32},{32,0},{64,96},{96,64},{128,160},{160,128},{192,224},{224,1... | collective-permute-start | bytes 245768 | tf_op jit(solution)/shard_map/ppermute | solution.py:34
  200.8 6.7 %collective-permute-start.9 = (f32[40,512]{1,0:T(8,128)S(1)}, f32[40,512]{1,0:T(8,128)S(1)}, u32[]{:S(2)}, u32[]{:S(2)}) collective-permute-start(f32[40,512]{1,0:T(8,128)S(1)} %pad_add_fusion), channel_id=1, source_target_pairs={{0,64},{32,96},{64,0},{96,32},{128,192},{160,224},{192,128},{224,1... | collective-permute-start | bytes 245768 | tf_op jit(solution)/shard_map/ppermute | solution.py:34
  207.5 10.9 %collective-permute-start.10 = (f32[40,512]{1,0:T(8,128)S(1)}, f32[40,512]{1,0:T(8,128)S(1)}, u32[]{:S(2)}, u32[]{:S(2)}) collective-permute-start(f32[40,512]{1,0:T(8,128)S(1)} %add.279), channel_id=1, source_target_pairs={{0,128},{32,160},{64,192},{96,224},{128,0},{160,32},{192,64},{224,... | collective-permute-start | bytes 245768 | tf_op jit(solution)/shard_map/ppermute | solution.py:34
  218.4 16.3 %collective-permute-start.11 = (f32[40,512]{1,0:T(8,128)S(1)}, f32[40,512]{1,0:T(8,128)S(1)}, u32[]{:S(2)}, u32[]{:S(2)}) collective-permute-start(f32[40,512]{1,0:T(8,128)S(1)} %add.280), channel_id=1, source_target_pairs={{0,256},{32,288},{64,320},{96,352},{128,384},{160,416},{192,448},{... | collective-permute-start | bytes 245768 | tf_op jit(solution)/shard_map/ppermute | solution.py:34
  234.7 10.7 %collective-permute-start.12 = (f32[40,512]{1,0:T(8,128)S(1)}, f32[40,512]{1,0:T(8,128)S(1)}, u32[]{:S(2)}, u32[]{:S(2)}) collective-permute-start(f32[40,512]{1,0:T(8,128)S(1)} %add.281), channel_id=1, source_target_pairs={{0,16},{1,5},{2,18},{3,7},{4,20},{5,1},{6,22},{7,3},{8,24},{9,13},... | collective-permute-start | bytes 245768 | tf_op jit(solution)/shard_map/ppermute | solution.py:42
  245.5 7.4 %collective-permute-start.13 = (f32[72,512]{1,0:T(8,128)S(1)}, f32[72,512]{1,0:T(8,128)S(1)}, u32[]{:S(2)}, u32[]{:S(2)}) collective-permute-start(f32[72,512]{1,0:T(8,128)S(1)} %pad_maximum_fusion.8), channel_id=1, source_target_pairs={{0,8},{1,3},{2,10},{3,1},{4,12},{5,7},{6,14},{7,5},{8,0},{9,11},{1... | collective-permute-start | bytes 442376 | tf_op jit(solution)/shard_map/ppermute | solution.py:42
  252.9 8.8 %collective-permute-start.14 = (f32[136,512]{1,0:T(8,128)S(1)}, f32[136,512]{1,0:T(8,128)S(1)}, u32[]{:S(2)}, u32[]{:S(2)}) collective-permute-start(f32[136,512]{1,0:T(8,128)S(1)} %pad_maximum_fusion.5), channel_id=1, source_target_pairs={{0,4},{1,17},{2,6},{3,19},{4,0},{5,21},{6,2},{7,23},{8,12},{9,25},... | collective-permute-start | bytes 835592 | tf_op jit(solution)/shard_map/ppermute | solution.py:42
  261.8 12.1 %collective-permute-start.15 = (f32[264,512]{1,0:T(8,128)S(1)}, f32[264,512]{1,0:T(8,128)S(1)}, u32[]{:S(2)}, u32[]{:S(2)}) collective-permute-start(f32[264,512]{1,0:T(8,128)S(1)} %pad_maximum_fusion.4), channel_id=1, source_target_pairs={{0,2},{1,9},{2,0},{3,11},{4,6},{5,13},{6,4},{7,15},{8,10},{9,1},{1... | collective-permute-start | bytes 1622024 | tf_op jit(solution)/shard_map/ppermute | solution.py:42
  273.9 6.5 %copy-start.8 = (s32[32]{0:T(128)S(1)}, s32[32]{0:T(128)}, u32[]{:S(2)}) copy-start(s32[32]{0:T(128)} %constant.294) | copy-start | bytes 388
  274.0 8.8 %collective-permute-start.16 = (f32[520,512]{1,0:T(8,128)S(1)}, f32[520,512]{1,0:T(8,128)}, u32[]{:S(2)}, u32[]{:S(2)}) collective-permute-start(f32[520,512]{1,0:T(8,128)S(1)} %pad_maximum_fusion.2), channel_id=1, source_target_pairs={{0,1},{1,0},{2,3},{3,2},{4,5},{5,4},{6,7},{7,6},{8,9},{9,8},{10,11... | collective-permute-start | bytes 3194888 | tf_op jit(solution)/shard_map/ppermute | solution.py:42
  284.1 1.3 copy-start.2
Sparse Core Ops, SparseCore 0:
  11.2 67.0 all-gather.1

commit v14 on v12

--- a/solution.py
+++ b/solution.py
@@ -118,6 +118,14 @@
     return hbar[0]
 
 
+def exact_dot(wide, narrow):
+    high = wide.astype(jnp.bfloat16)
+    low = (wide - high.astype(jnp.float32)).astype(jnp.bfloat16)
+    return jnp.dot(high, narrow, preferred_element_type=jnp.float32) + jnp.dot(
+        low, narrow, preferred_element_type=jnp.float32
+    )
+
+
 def embed(pre):
     return pre * lax.rsqrt(jnp.sum(pre * pre, axis=-1, keepdims=True) + 1e-06)
 
@@ -175,10 +183,10 @@
     grad_pos = -jax.nn.sigmoid(-s_pos) / nodes
     grad_neg = jax.nn.sigmoid(s_neg) / (NOISE * nodes)
     anchor = scale_factor * (
-        grad_pos[:, None] * partner + jnp.dot(grad_neg, noise_emb, precision=highest)
-    )
-    partner_grad = jnp.dot(pairing.T, scale_factor * grad_pos[:, None] * zeta, precision=highest)
-    dnoise = scale_factor * jnp.dot(grad_neg.T, zeta, precision=highest)
+        grad_pos[:, None] * partner + exact_dot(grad_neg, noise_emb.astype(jnp.bfloat16))
+    )
+    partner_grad = exact_dot((scale_factor * grad_pos[:, None] * zeta).T, pairing.astype(jnp.bfloat16)).T
+    dnoise = scale_factor * exact_dot(grad_neg.T, zeta_bf)
     dnoise = dnoise.astype(jnp.bfloat16).astype(jnp.float32)
     dzeta = jnp.concatenate([anchor + partner_grad, dnoise], axis=0)
     gpre = pull(dzeta)[0].astype(jnp.bfloat16)

time: 298 us -> 298 us (level)
  no operation moved by 1% of the time
where the time goes in v14:
time: 298 us; the launch traced here: 297 us
  waiting for transfers between devices  124 us (42%)
  starting transfers between devices  118 us (40%)
  between operations  21.4 us (7%)
  local copies, waits for them, and re-layouts  21 us (7%)
  matrix products  9.68 us (3%)
    ppermute x4, starting transfers between devices, route_forward(): got = lax.ppermute(held, 'row', xor_pairs(size, m))  41 us
    ppermute x4, waiting for transfers between devices, route_forward(): got = lax.ppermute(send, 'row', xor_pairs(size, m))  40.8 us
    ppermute x5, starting transfers between devices, tree_allreduce(): got = lax.ppermute(jnp.concatenate([buf, extra], axis=0), 'col', pairs)  30 us
    all_to_all x1, waiting for transfers between devices, tree_allreduce(): scattered = lax.all_to_all(chunks, 'col', 0, 0, tiled=False).sum(axis=0)  26.5 us
    ppermute x4, waiting for transfers between devices, tree_allreduce(): joined = joined + lax.ppermute(joined, axis, xor_pairs(size, mask))  23.4 us
    ppermute x4, starting transfers between devices, route_forward(): got = lax.ppermute(send, 'row', xor_pairs(size, m))  22.1 us
    ppermute x5, waiting for transfers between devices, tree_allreduce(): got = lax.ppermute(jnp.concatenate([buf, extra], axis=0), 'col', pairs)  16.4 us
    ppermute x4, waiting for transfers between devices, route_forward(): got = lax.ppermute(held, 'row', xor_pairs(size, m))  15.8 us
  transfers between devices with their start and end apart: 19, of which 17 were waited for; matrix products, arithmetic and copies ran while one was open for 5% of the time, Pallas kernels for 0%

profile of v14, /device:TPU:1, one launch (start us, length us, event | category | flops | bytes accessed | tf_op | source)
XLA Modules:
  0.0 297.0 jit_solution(12192966819859169217)
XLA Ops:
  8.9 16.3 %collective-permute-start = (bf16[1,128,512]{2,1,0:T(8,128)(2,1)S(1)}, bf16[1,128,512]{2,1,0:T(8,128)(2,1)S(1)}, u32[]{:S(2)}, u32[]{:S(2)}) collective-permute-start(bf16[1,128,512]{2,1,0:T(8,128)(2,1)S(1)} %slice_bitcast_fusion.6), channel_id=1, source_target_pairs={{0,256},{32,288},{64,320},{96,352},{128,384},{160,416},{192,448},{... | collective-permute-start | bytes 393224 | tf_op jit(solution)/shard_map/ppermute | solution.py:80
  27.8 11.6 %collective-permute-start.1 = (bf16[2,128,512]{2,1,0:T(8,128)(2,1)S(1)}, bf16[2,128,512]{2,1,0:T(8,128)(2,1)S(1)}, u32[]{:S(2)}, u32[]{:S(2)}) collective-permute-start(bf16[2,128,512]{2,1,0:T(8,128)(2,1)S(1)} %maximum_select_fusion.2), channel_id=1, source_target_pairs={{0,32},{32,0},{64,96},{96,64},{128,160},{160,128},{192,224},{224,1... | collective-permute-start | bytes 786440 | tf_op jit(solution)/shard_map/ppermute | solution.py:80
  39.6 5.1 %collective-permute-done.1 = bf16[2,128,512]{2,1,0:T(8,128)(2,1)S(1)} collective-permute-done((bf16[2,128,512]{2,1,0:T(8,128)(2,1)S(1)}, bf16[2,128,512]{2,1,0:T(8,128)(2,1)S(1)}, u32[]{:S(2)}, u32[]{:S(2)}) %collective-permute-start.1) | collective-permute-done | bytes 262176 | tf_op jit(solution)/shard_map/ppermute | solution.py:80
  45.6 2.1 collective-permute-start.2
  47.8 13.5 %collective-permute-done.2 = bf16[2,128,512]{2,1,0:T(8,128)(2,1)S(1)} collective-permute-done((bf16[2,128,512]{2,1,0:T(8,128)(2,1)S(1)}, bf16[2,128,512]{2,1,0:T(8,128)(2,1)S(1)}, u32[]{:S(2)}, u32[]{:S(2)}) %collective-permute-start.2) | collective-permute-done | bytes 262176 | tf_op jit(solution)/shard_map/ppermute | solution.py:90
  61.5 8.1 %collective-permute-start.3 = (bf16[1,128,512]{2,1,0:T(8,128)(2,1)S(1)}, bf16[1,128,512]{2,1,0:T(8,128)(2,1)S(1)}, u32[]{:S(2)}, u32[]{:S(2)}) collective-permute-start(bf16[1,128,512]{2,1,0:T(8,128)(2,1)S(1)} %select_bitcast_fusion.3), channel_id=1, source_target_pairs={{0,128},{32,160},{64,192},{96,224},{128,0},{160,32},{192,64},{224,... | collective-permute-start | bytes 393224 | tf_op jit(solution)/shard_map/ppermute | solution.py:90
  72.9 7.5 %collective-permute-done.3 = bf16[1,128,512]{2,1,0:T(8,128)(2,1)S(1)} collective-permute-done((bf16[1,128,512]{2,1,0:T(8,128)(2,1)S(1)}, bf16[1,128,512]{2,1,0:T(8,128)(2,1)S(1)}, u32[]{:S(2)}, u32[]{:S(2)}) %collective-permute-start.3) | collective-permute-done | bytes 131104 | tf_op jit(solution)/shard_map/ppermute | solution.py:90
  80.5 2.8 gather_fusion.2
  83.6 11.2 %collective-permute-start.4 = (bf16[1,128,512]{2,1,0:T(8,128)(2,1)S(1)}, bf16[1,128,512]{2,1,0:T(8,128)(2,1)S(1)}, u32[]{:S(2)}, u32[]{:S(2)}) collective-permute-start(bf16[1,128,512]{2,1,0:T(8,128)(2,1)S(1)} %bitcast.125), channel_id=1, source_target_pairs={{0,256},{32,288},{64,320},{96,352},{128,384},{160,416},{192,448},{... | collective-permute-start | bytes 393224 | tf_op jit(solution)/shard_map/ppermute | solution.py:80
  94.8 10.2 %collective-permute-done.4 = bf16[1,128,512]{2,1,0:T(8,128)(2,1)S(1)} collective-permute-done((bf16[1,128,512]{2,1,0:T(8,128)(2,1)S(1)}, bf16[1,128,512]{2,1,0:T(8,128)(2,1)S(1)}, u32[]{:S(2)}, u32[]{:S(2)}) %collective-permute-start.4) | collective-permute-done | bytes 131104 | tf_op jit(solution)/shard_map/ppermute | solution.py:80
  108.1 4.7 %gather_fusion.3 = bf16[24,128,512]{2,1,0:T(8,128)(2,1)} fusion(bf16[32,128,512]{2,1,0:T(8,128)(2,1)} %bitcast.123, s32[1024]{0:T(1024)S(1)} %get-tuple-element.22), kind=kCustom, calls=%fused_computation.5 | custom fusion | bytes 6291552 | tf_op jit(solution)/shard_map/jit(_take)/gather | solution.py:160
  113.6 3.5 %collective-permute-start.6 = (bf16[2,128,512]{2,1,0:T(8,128)(2,1)S(1)}, bf16[2,128,512]{2,1,0:T(8,128)(2,1)S(1)}, u32[]{:S(2)}, u32[]{:S(2)}) collective-permute-start(bf16[2,128,512]{2,1,0:T(8,128)(2,1)S(1)} %select_bitcast_fusion), channel_id=1, source_target_pairs={{0,64},{32,96},{64,0},{96,32},{128,192},{160,224},{192,128},{224,1... | collective-permute-start | bytes 786440 | tf_op jit(solution)/shard_map/ppermute | solution.py:90
  117.1 2.9 fusion.4
  120.0 9.0 %collective-permute-done.6 = bf16[2,128,512]{2,1,0:T(8,128)(2,1)S(1)} collective-permute-done((bf16[2,128,512]{2,1,0:T(8,128)(2,1)S(1)}, bf16[2,128,512]{2,1,0:T(8,128)(2,1)S(1)}, u32[]{:S(2)}, u32[]{:S(2)}) %collective-permute-start.6) | collective-permute-done | bytes 262176 | tf_op jit(solution)/shard_map/ppermute | solution.py:90
  129.2 8.4 %collective-permute-start.7 = (bf16[1,128,512]{2,1,0:T(8,128)(2,1)S(1)}, bf16[1,128,512]{2,1,0:T(8,128)(2,1)S(1)}, u32[]{:S(2)}, u32[]{:S(2)}) collective-permute-start(bf16[1,128,512]{2,1,0:T(8,128)(2,1)S(1)} %select_bitcast_fusion.2), channel_id=1, source_target_pairs={{0,128},{32,160},{64,192},{96,224},{128,0},{160,32},{192,64},{224,... | collective-permute-start | bytes 393224 | tf_op jit(solution)/shard_map/ppermute | solution.py:90
  138.2 10.7 %collective-permute-done.7 = bf16[1,128,512]{2,1,0:T(8,128)(2,1)S(1)} collective-permute-done((bf16[1,128,512]{2,1,0:T(8,128)(2,1)S(1)}, bf16[1,128,512]{2,1,0:T(8,128)(2,1)S(1)}, u32[]{:S(2)}, u32[]{:S(2)}) %collective-permute-start.7) | collective-permute-done | bytes 131104 | tf_op jit(solution)/shard_map/ppermute | solution.py:90
  158.7 9.5 %all-to-all-start = ((f32[32,32,512]{2,1,0:T(8,128)}), f32[32,32,512]{2,1,0:T(8,128)S(1)}, u32[]{:S(2)}, u32[]{:S(2)}) async-start(f32[32,32,512]{2,1,0:T(8,128)} %gather_fusion.4), calls=%async_computation | async-start | bytes 4194304 | tf_op jit(solution)/shard_map/all_to_all | solution.py:28
  169.6 26.5 %all-to-all-done = f32[32,32,512]{2,1,0:T(8,128)S(1)} async-done(((f32[32,32,512]{2,1,0:T(8,128)}), f32[32,32,512]{2,1,0:T(8,128)S(1)}, u32[]{:S(2)}, u32[]{:S(2)}) %all-to-all-start) | async-done | bytes 2097184 | tf_op jit(solution)/shard_map/all_to_all | solution.py:28
  198.2 3.3 %collective-permute-done.8 = f32[40,512]{1,0:T(8,128)S(1)} collective-permute-done((f32[40,512]{1,0:T(8,128)S(1)}, f32[40,512]{1,0:T(8,128)S(1)}, u32[]{:S(2)}, u32[]{:S(2)}) %collective-permute-start.8) | collective-permute-done | bytes 81952 | tf_op jit(solution)/shard_map/ppermute | solution.py:34
  203.4 4.8 %collective-permute-done.9 = f32[40,512]{1,0:T(8,128)S(1)} collective-permute-done((f32[40,512]{1,0:T(8,128)S(1)}, f32[40,512]{1,0:T(8,128)S(1)}, u32[]{:S(2)}, u32[]{:S(2)}) %collective-permute-start.9) | collective-permute-done | bytes 81952 | tf_op jit(solution)/shard_map/ppermute | solution.py:34
  208.2 4.7 %collective-permute-start.10 = (f32[40,512]{1,0:T(8,128)S(1)}, f32[40,512]{1,0:T(8,128)S(1)}, u32[]{:S(2)}, u32[]{:S(2)}) collective-permute-start(f32[40,512]{1,0:T(8,128)S(1)} %add.299), channel_id=1, source_target_pairs={{0,128},{32,160},{64,192},{96,224},{128,0},{160,32},{192,64},{224,... | collective-permute-start | bytes 245768 | tf_op jit(solution)/shard_map/ppermute | solution.py:34
  212.9 6.2 %collective-permute-done.10 = f32[40,512]{1,0:T(8,128)S(1)} collective-permute-done((f32[40,512]{1,0:T(8,128)S(1)}, f32[40,512]{1,0:T(8,128)S(1)}, u32[]{:S(2)}, u32[]{:S(2)}) %collective-permute-start.10) | collective-permute-done | bytes 81952 | tf_op jit(solution)/shard_map/ppermute | solution.py:34
  219.1 7.1 %collective-permute-start.11 = (f32[40,512]{1,0:T(8,128)S(1)}, f32[40,512]{1,0:T(8,128)S(1)}, u32[]{:S(2)}, u32[]{:S(2)}) collective-permute-start(f32[40,512]{1,0:T(8,128)S(1)} %add.300), channel_id=1, source_target_pairs={{0,256},{32,288},{64,320},{96,352},{128,384},{160,416},{192,448},{... | collective-permute-start | bytes 245768 | tf_op jit(solution)/shard_map/ppermute | solution.py:34
  226.3 9.3 %collective-permute-done.11 = f32[40,512]{1,0:T(8,128)S(1)} collective-permute-done((f32[40,512]{1,0:T(8,128)S(1)}, f32[40,512]{1,0:T(8,128)S(1)}, u32[]{:S(2)}, u32[]{:S(2)}) %collective-permute-start.11) | collective-permute-done | bytes 81952 | tf_op jit(solution)/shard_map/ppermute | solution.py:34
  235.6 8.9 %collective-permute-start.12 = (f32[40,512]{1,0:T(8,128)S(1)}, f32[40,512]{1,0:T(8,128)S(1)}, u32[]{:S(2)}, u32[]{:S(2)}) collective-permute-start(f32[40,512]{1,0:T(8,128)S(1)} %add.301), channel_id=1, source_target_pairs={{0,16},{1,5},{2,18},{3,7},{4,20},{5,1},{6,22},{7,3},{8,24},{9,13},... | collective-permute-start | bytes 245768 | tf_op jit(solution)/shard_map/ppermute | solution.py:42
  246.4 4.8 %collective-permute-start.13 = (f32[72,512]{1,0:T(8,128)S(1)}, f32[72,512]{1,0:T(8,128)S(1)}, u32[]{:S(2)}, u32[]{:S(2)}) collective-permute-start(f32[72,512]{1,0:T(8,128)S(1)} %pad_maximum_fusion.8), channel_id=1, source_target_pairs={{0,8},{1,3},{2,10},{3,1},{4,12},{5,7},{6,14},{7,5},{8,0},{9,11},{1... | collective-permute-start | bytes 442376 | tf_op jit(solution)/shard_map/ppermute | solution.py:42
  251.3 2.4 collective-permute-done.13
  253.8 4.8 %collective-permute-start.14 = (f32[136,512]{1,0:T(8,128)S(1)}, f32[136,512]{1,0:T(8,128)S(1)}, u32[]{:S(2)}, u32[]{:S(2)}) collective-permute-start(f32[136,512]{1,0:T(8,128)S(1)} %pad_maximum_fusion.5), channel_id=1, source_target_pairs={{0,4},{1,17},{2,6},{3,19},{4,0},{5,21},{6,2},{7,23},{8,12},{9,25},... | collective-permute-start | bytes 835592 | tf_op jit(solution)/shard_map/ppermute | solution.py:42
  258.7 3.9 %collective-permute-done.14 = f32[136,512]{1,0:T(8,128)S(1)} collective-permute-done((f32[136,512]{1,0:T(8,128)S(1)}, f32[136,512]{1,0:T(8,128)S(1)}, u32[]{:S(2)}, u32[]{:S(2)}) %collective-permute-start.14) | collective-permute-done | bytes 278560 | tf_op jit(solution)/shard_map/ppermute | solution.py:42
  262.6 5.0 %collective-permute-start.15 = (f32[264,512]{1,0:T(8,128)S(1)}, f32[264,512]{1,0:T(8,128)S(1)}, u32[]{:S(2)}, u32[]{:S(2)}) collective-permute-start(f32[264,512]{1,0:T(8,128)S(1)} %pad_maximum_fusion.4), channel_id=1, source_target_pairs={{0,2},{1,9},{2,0},{3,11},{4,6},{5,13},{6,4},{7,15},{8,10},{9,1},{1... | collective-permute-start | bytes 1622024 | tf_op jit(solution)/shard_map/ppermute | solution.py:42
  267.9 6.8 %collective-permute-done.15 = f32[264,512]{1,0:T(8,128)S(1)} collective-permute-done((f32[264,512]{1,0:T(8,128)S(1)}, f32[264,512]{1,0:T(8,128)S(1)}, u32[]{:S(2)}, u32[]{:S(2)}) %collective-permute-start.15) | collective-permute-done | bytes 540704 | tf_op jit(solution)/shard_map/ppermute | solution.py:42
  274.9 6.4 %collective-permute-start.16 = (f32[520,512]{1,0:T(8,128)S(1)}, f32[520,512]{1,0:T(8,128)}, u32[]{:S(2)}, u32[]{:S(2)}) collective-permute-start(f32[520,512]{1,0:T(8,128)S(1)} %pad_maximum_fusion.2), channel_id=1, source_target_pairs={{0,1},{1,0},{2,3},{3,2},{4,5},{5,4},{6,7},{7,6},{8,9},{9,8},{10,11... | collective-permute-start | bytes 3194888 | tf_op jit(solution)/shard_map/ppermute | solution.py:42
  (115 shorter events, 33.5 us)
Async XLA Ops:
  7.2 141.8 %copy-start = (bf16[512,512]{1,0:T(8,128)(2,1)S(1)}, bf16[512,512]{1,0:T(8,128)(2,1)}, u32[]{:S(2)}) copy-start(bf16[512,512]{1,0:T(8,128)(2,1)} %param.20) | copy-start | bytes 1572868
  7.2 19.4 %copy-start.1 = (s32[16]{0:T(128)S(1)}, s32[16]{0:T(128)}, u32[]{:S(2)}) copy-start(s32[16]{0:T(128)} %param.18) | copy-start | bytes 196
  7.2 32.3 %copy-start.7 = (s32[4]{0:T(128)S(1)}, s32[4]{0:T(128)}, u32[]{:S(2)}) copy-start(s32[4]{0:T(128)} %param.15) | copy-start | bytes 52
  7.2 73.2 %all-gather.2.cloned.1.call-start = ((), (), s32[]{:S(2)}) async-start(), calls=%async_computation.1 | async-start | bytes 4325376 | tf_op jit(solution)/shard_map/all_gather | solution.py:154
  8.9 18.9 %collective-permute-start = (bf16[1,128,512]{2,1,0:T(8,128)(2,1)S(1)}, bf16[1,128,512]{2,1,0:T(8,128)(2,1)S(1)}, u32[]{:S(2)}, u32[]{:S(2)}) collective-permute-start(bf16[1,128,512]{2,1,0:T(8,128)(2,1)S(1)} %slice_bitcast_fusion.6), channel_id=1, source_target_pairs={{0,256},{32,288},{64,320},{96,352},{128,384},{160,416},{192,448},{... | collective-permute-start | bytes 393224 | tf_op jit(solution)/shard_map/ppermute | solution.py:80
  27.8 16.9 %collective-permute-start.1 = (bf16[2,128,512]{2,1,0:T(8,128)(2,1)S(1)}, bf16[2,128,512]{2,1,0:T(8,128)(2,1)S(1)}, u32[]{:S(2)}, u32[]{:S(2)}) collective-permute-start(bf16[2,128,512]{2,1,0:T(8,128)(2,1)S(1)} %maximum_select_fusion.2), channel_id=1, source_target_pairs={{0,32},{32,0},{64,96},{96,64},{128,160},{160,128},{192,224},{224,1... | collective-permute-start | bytes 786440 | tf_op jit(solution)/shard_map/ppermute | solution.py:80
  45.4 2.2 copy-start.2
  45.6 24.0 %copy-start.5 = (s32[4,8]{1,0:T(4,128)S(1)}, s32[4,8]{1,0:T(4,128)}, u32[]{:S(2)}) copy-start(s32[4,8]{1,0:T(4,128)} %param.14) | copy-start | bytes 388
  45.6 15.8 %collective-permute-start.2 = (bf16[2,128,512]{2,1,0:T(8,128)(2,1)S(1)}, bf16[2,128,512]{2,1,0:T(8,128)(2,1)S(1)}, u32[]{:S(2)}, u32[]{:S(2)}) collective-permute-start(bf16[2,128,512]{2,1,0:T(8,128)(2,1)S(1)} %select_bitcast_fusion.1), channel_id=1, source_target_pairs={{0,64},{32,96},{64,0},{96,32},{128,192},{160,224},{192,128},{224,1... | collective-permute-start | bytes 786440 | tf_op jit(solution)/shard_map/ppermute | solution.py:90
  61.5 18.9 %collective-permute-start.3 = (bf16[1,128,512]{2,1,0:T(8,128)(2,1)S(1)}, bf16[1,128,512]{2,1,0:T(8,128)(2,1)S(1)}, u32[]{:S(2)}, u32[]{:S(2)}) collective-permute-start(bf16[1,128,512]{2,1,0:T(8,128)(2,1)S(1)} %select_bitcast_fusion.3), channel_id=1, source_target_pairs={{0,128},{32,160},{64,192},{96,224},{128,0},{160,32},{192,64},{224,... | collective-permute-start | bytes 393224 | tf_op jit(solution)/shard_map/ppermute | solution.py:90
  83.3 23.7 %copy-start.6 = (s32[32]{0:T(128)S(1)}, s32[32]{0:T(128)}, u32[]{:S(2)}) copy-start(s32[32]{0:T(128)} %constant.294) | copy-start | bytes 388
  83.6 21.3 %collective-permute-start.4 = (bf16[1,128,512]{2,1,0:T(8,128)(2,1)S(1)}, bf16[1,128,512]{2,1,0:T(8,128)(2,1)S(1)}, u32[]{:S(2)}, u32[]{:S(2)}) collective-permute-start(bf16[1,128,512]{2,1,0:T(8,128)(2,1)S(1)} %bitcast.125), channel_id=1, source_target_pairs={{0,256},{32,288},{64,320},{96,352},{128,384},{160,416},{192,448},{... | collective-permute-start | bytes 393224 | tf_op jit(solution)/shard_map/ppermute | solution.py:80
  105.0 7.8 %collective-permute-start.5 = (bf16[2,128,512]{2,1,0:T(8,128)(2,1)S(1)}, bf16[2,128,512]{2,1,0:T(8,128)(2,1)S(1)}, u32[]{:S(2)}, u32[]{:S(2)}) collective-permute-start(bf16[2,128,512]{2,1,0:T(8,128)(2,1)S(1)} %maximum_select_fusion.3), channel_id=1, source_target_pairs={{0,32},{32,0},{64,96},{96,64},{128,160},{160,128},{192,224},{224,1... | collective-permute-start | bytes 786440 | tf_op jit(solution)/shard_map/ppermute | solution.py:80
  113.6 15.4 %collective-permute-start.6 = (bf16[2,128,512]{2,1,0:T(8,128)(2,1)S(1)}, bf16[2,128,512]{2,1,0:T(8,128)(2,1)S(1)}, u32[]{:S(2)}, u32[]{:S(2)}) collective-permute-start(bf16[2,128,512]{2,1,0:T(8,128)(2,1)S(1)} %select_bitcast_fusion), channel_id=1, source_target_pairs={{0,64},{32,96},{64,0},{96,32},{128,192},{160,224},{192,128},{224,1... | collective-permute-start | bytes 786440 | tf_op jit(solution)/shard_map/ppermute | solution.py:90
  120.0 17.6 %copy-start.3 = (bf16[512,512]{1,0:T(8,128)(2,1)S(1)}, bf16[512,512]{1,0:T(8,128)(2,1)}, u32[]{:S(2)}) copy-start(bf16[512,512]{1,0:T(8,128)(2,1)} %param.19) | copy-start | bytes 1572868
  129.2 19.8 %collective-permute-start.7 = (bf16[1,128,512]{2,1,0:T(8,128)(2,1)S(1)}, bf16[1,128,512]{2,1,0:T(8,128)(2,1)S(1)}, u32[]{:S(2)}, u32[]{:S(2)}) collective-permute-start(bf16[1,128,512]{2,1,0:T(8,128)(2,1)S(1)} %select_bitcast_fusion.2), channel_id=1, source_target_pairs={{0,128},{32,160},{64,192},{96,224},{128,0},{160,32},{192,64},{224,... | collective-permute-start | bytes 393224 | tf_op jit(solution)/shard_map/ppermute | solution.py:90
  151.1 0.7 copy-start.4
  158.7 37.4 %all-to-all-start = ((f32[32,32,512]{2,1,0:T(8,128)}), f32[32,32,512]{2,1,0:T(8,128)S(1)}, u32[]{:S(2)}, u32[]{:S(2)}) async-start(f32[32,32,512]{2,1,0:T(8,128)} %gather_fusion.4), calls=%async_computation | async-start | bytes 4194304 | tf_op jit(solution)/shard_map/all_to_all | solution.py:28
  196.3 5.2 %collective-permute-start.8 = (f32[40,512]{1,0:T(8,128)S(1)}, f32[40,512]{1,0:T(8,128)S(1)}, u32[]{:S(2)}, u32[]{:S(2)}) collective-permute-start(f32[40,512]{1,0:T(8,128)S(1)} %concatenate.64), channel_id=1, source_target_pairs={{0,32},{32,0},{64,96},{96,64},{128,160},{160,128},{192,224},{224,1... | collective-permute-start | bytes 245768 | tf_op jit(solution)/shard_map/ppermute | solution.py:34
  201.5 6.7 %collective-permute-start.9 = (f32[40,512]{1,0:T(8,128)S(1)}, f32[40,512]{1,0:T(8,128)S(1)}, u32[]{:S(2)}, u32[]{:S(2)}) collective-permute-start(f32[40,512]{1,0:T(8,128)S(1)} %pad_add_fusion), channel_id=1, source_target_pairs={{0,64},{32,96},{64,0},{96,32},{128,192},{160,224},{192,128},{224,1... | collective-permute-start | bytes 245768 | tf_op jit(solution)/shard_map/ppermute | solution.py:34
  208.2 10.9 %collective-permute-start.10 = (f32[40,512]{1,0:T(8,128)S(1)}, f32[40,512]{1,0:T(8,128)S(1)}, u32[]{:S(2)}, u32[]{:S(2)}) collective-permute-start(f32[40,512]{1,0:T(8,128)S(1)} %add.299), channel_id=1, source_target_pairs={{0,128},{32,160},{64,192},{96,224},{128,0},{160,32},{192,64},{224,... | collective-permute-start | bytes 245768 | tf_op jit(solution)/shard_map/ppermute | solution.py:34
  219.1 16.4 %collective-permute-start.11 = (f32[40,512]{1,0:T(8,128)S(1)}, f32[40,512]{1,0:T(8,128)S(1)}, u32[]{:S(2)}, u32[]{:S(2)}) collective-permute-start(f32[40,512]{1,0:T(8,128)S(1)} %add.300), channel_id=1, source_target_pairs={{0,256},{32,288},{64,320},{96,352},{128,384},{160,416},{192,448},{... | collective-permute-start | bytes 245768 | tf_op jit(solution)/shard_map/ppermute | solution.py:34
  235.6 10.8 %collective-permute-start.12 = (f32[40,512]{1,0:T(8,128)S(1)}, f32[40,512]{1,0:T(8,128)S(1)}, u32[]{:S(2)}, u32[]{:S(2)}) collective-permute-start(f32[40,512]{1,0:T(8,128)S(1)} %add.301), channel_id=1, source_target_pairs={{0,16},{1,5},{2,18},{3,7},{4,20},{5,1},{6,22},{7,3},{8,24},{9,13},... | collective-permute-start | bytes 245768 | tf_op jit(solution)/shard_map/ppermute | solution.py:42
  246.4 7.4 %collective-permute-start.13 = (f32[72,512]{1,0:T(8,128)S(1)}, f32[72,512]{1,0:T(8,128)S(1)}, u32[]{:S(2)}, u32[]{:S(2)}) collective-permute-start(f32[72,512]{1,0:T(8,128)S(1)} %pad_maximum_fusion.8), channel_id=1, source_target_pairs={{0,8},{1,3},{2,10},{3,1},{4,12},{5,7},{6,14},{7,5},{8,0},{9,11},{1... | collective-permute-start | bytes 442376 | tf_op jit(solution)/shard_map/ppermute | solution.py:42
  253.8 8.8 %collective-permute-start.14 = (f32[136,512]{1,0:T(8,128)S(1)}, f32[136,512]{1,0:T(8,128)S(1)}, u32[]{:S(2)}, u32[]{:S(2)}) collective-permute-start(f32[136,512]{1,0:T(8,128)S(1)} %pad_maximum_fusion.5), channel_id=1, source_target_pairs={{0,4},{1,17},{2,6},{3,19},{4,0},{5,21},{6,2},{7,23},{8,12},{9,25},... | collective-permute-start | bytes 835592 | tf_op jit(solution)/shard_map/ppermute | solution.py:42
  262.6 12.1 %collective-permute-start.15 = (f32[264,512]{1,0:T(8,128)S(1)}, f32[264,512]{1,0:T(8,128)S(1)}, u32[]{:S(2)}, u32[]{:S(2)}) collective-permute-start(f32[264,512]{1,0:T(8,128)S(1)} %pad_maximum_fusion.4), channel_id=1, source_target_pairs={{0,2},{1,9},{2,0},{3,11},{4,6},{5,13},{6,4},{7,15},{8,10},{9,1},{1... | collective-permute-start | bytes 1622024 | tf_op jit(solution)/shard_map/ppermute | solution.py:42
  274.9 8.8 %collective-permute-start.16 = (f32[520,512]{1,0:T(8,128)S(1)}, f32[520,512]{1,0:T(8,128)}, u32[]{:S(2)}, u32[]{:S(2)}) collective-permute-start(f32[520,512]{1,0:T(8,128)S(1)} %pad_maximum_fusion.2), channel_id=1, source_target_pairs={{0,1},{1,0},{2,3},{3,2},{4,5},{5,4},{6,7},{7,6},{8,9},{9,8},{10,11... | collective-permute-start | bytes 3194888 | tf_op jit(solution)/shard_map/ppermute | solution.py:42
Sparse Core Ops, SparseCore 0:
  11.2 67.0 all-gather.1

commit v15 on v12

--- a/solution.py
+++ b/solution.py
@@ -34,18 +34,21 @@
         joined = joined + lax.ppermute(joined, axis, xor_pairs(size, mask))
     buf, extra = joined[:rows], joined[rows:]
     odd = me % 2 == 1
-    for even_mask, odd_mask in zip(*orders):
+    steps = list(zip(*orders))
+    for even_mask, odd_mask in steps:
         mask = jnp.where(odd, odd_mask, even_mask)
         bit = (me // mask) % 2
         held = buf.shape[0]
         pairs = [(i, i ^ (odd_mask if i % 2 else even_mask)) for i in range(ways)]
         got = lax.ppermute(jnp.concatenate([buf, extra], axis=0), "col", pairs)
         extra = extra + got[held:]
+        if (even_mask, odd_mask) == steps[-1]:
+            mine_first = bit == 0
+            return jnp.where(mine_first, buf, got[:held]), jnp.where(mine_first, got[:held], buf), extra
         out = jnp.zeros((2 * held,) + buf.shape[1:], buf.dtype)
         out = lax.dynamic_update_slice_in_dim(out, buf, bit * held, 0)
         out = lax.dynamic_update_slice_in_dim(out, got[:held], (1 - bit) * held, 0)
         buf = out
-    return buf, extra
 
 
 def route_plan(table):
@@ -185,9 +188,7 @@
     part_self = jnp.dot(all_feats.T, gpre, preferred_element_type=jnp.float32)
     neighbour_partial = jnp.dot(all_agg.T, gpre, preferred_element_type=jnp.float32)
     stacked = jnp.concatenate([part_self, neighbour_partial], axis=0)
-    total, loss_tile = tree_allreduce(stacked, jnp.broadcast_to(loss_part, (8, width)))
-    grad_self = total[:width]
-    neighbour_weight_gradient = total[width:]
+    grad_self, neighbour_weight_gradient, loss_tile = tree_allreduce(stacked, jnp.broadcast_to(loss_part, (8, width)))
     return (grad_self, neighbour_weight_gradient, loss_tile[0, 0])
 
 

time: 298 us -> 298 us (level)
  local copies, waits for them, and re-layouts: 20.6 us -> 17.5 us
where the time goes in v15:
time: 298 us; the launch traced here: 297 us
  waiting for transfers between devices  124 us (42%)
  starting transfers between devices  118 us (40%)
  between operations  21.4 us (7%)
  local copies, waits for them, and re-layouts  17.5 us (6%)
  matrix products  9.85 us (3%)
  other arithmetic  5.58 us (2%)
    ppermute x4, starting transfers between devices, route_forward(): got = lax.ppermute(held, 'row', xor_pairs(size, m))  41 us
    ppermute x4, waiting for transfers between devices, route_forward(): got = lax.ppermute(send, 'row', xor_pairs(size, m))  40.8 us
    ppermute x5, starting transfers between devices, tree_allreduce(): got = lax.ppermute(jnp.concatenate([buf, extra], axis=0), 'col', pairs)  30 us
    all_to_all x1, waiting for transfers between devices, tree_allreduce(): scattered = lax.all_to_all(chunks, 'col', 0, 0, tiled=False).sum(axis=0)  26.5 us
    ppermute x4, waiting for transfers between devices, tree_allreduce(): joined = joined + lax.ppermute(joined, axis, xor_pairs(size, mask))  23.4 us
    ppermute x4, starting transfers between devices, route_forward(): got = lax.ppermute(send, 'row', xor_pairs(size, m))  22.1 us
    ppermute x5, waiting for transfers between devices, tree_allreduce(): got = lax.ppermute(jnp.concatenate([buf, extra], axis=0), 'col', pairs)  16.7 us
    ppermute x4, waiting for transfers between devices, route_forward(): got = lax.ppermute(held, 'row', xor_pairs(size, m))  15.8 us
  transfers between devices with their start and end apart: 19, of which 17 were waited for; matrix products, arithmetic and copies ran while one was open for 5% of the time, Pallas kernels for 0%

profile of v15, /device:TPU:1, one launch (start us, length us, event | category | flops | bytes accessed | tf_op | source)
XLA Modules:
  0.0 296.8 jit_solution(13335960747956084594)
XLA Ops:
  8.9 16.3 %collective-permute-start = (bf16[1,128,512]{2,1,0:T(8,128)(2,1)S(1)}, bf16[1,128,512]{2,1,0:T(8,128)(2,1)S(1)}, u32[]{:S(2)}, u32[]{:S(2)}) collective-permute-start(bf16[1,128,512]{2,1,0:T(8,128)(2,1)S(1)} %slice_bitcast_fusion.6), channel_id=1, source_target_pairs={{0,256},{32,288},{64,320},{96,352},{128,384},{160,416},{192,448},{... | collective-permute-start | bytes 393224 | tf_op jit(solution)/shard_map/ppermute | solution.py:83
  27.8 11.6 %collective-permute-start.1 = (bf16[2,128,512]{2,1,0:T(8,128)(2,1)S(1)}, bf16[2,128,512]{2,1,0:T(8,128)(2,1)S(1)}, u32[]{:S(2)}, u32[]{:S(2)}) collective-permute-start(bf16[2,128,512]{2,1,0:T(8,128)(2,1)S(1)} %maximum_select_fusion.2), channel_id=1, source_target_pairs={{0,32},{32,0},{64,96},{96,64},{128,160},{160,128},{192,224},{224,1... | collective-permute-start | bytes 786440 | tf_op jit(solution)/shard_map/ppermute | solution.py:83
  39.6 5.1 %collective-permute-done.1 = bf16[2,128,512]{2,1,0:T(8,128)(2,1)S(1)} collective-permute-done((bf16[2,128,512]{2,1,0:T(8,128)(2,1)S(1)}, bf16[2,128,512]{2,1,0:T(8,128)(2,1)S(1)}, u32[]{:S(2)}, u32[]{:S(2)}) %collective-permute-start.1) | collective-permute-done | bytes 262176 | tf_op jit(solution)/shard_map/ppermute | solution.py:83
  47.8 13.5 %collective-permute-done.2 = bf16[2,128,512]{2,1,0:T(8,128)(2,1)S(1)} collective-permute-done((bf16[2,128,512]{2,1,0:T(8,128)(2,1)S(1)}, bf16[2,128,512]{2,1,0:T(8,128)(2,1)S(1)}, u32[]{:S(2)}, u32[]{:S(2)}) %collective-permute-start.2) | collective-permute-done | bytes 262176 | tf_op jit(solution)/shard_map/ppermute | solution.py:93
  61.5 8.1 %collective-permute-start.3 = (bf16[1,128,512]{2,1,0:T(8,128)(2,1)S(1)}, bf16[1,128,512]{2,1,0:T(8,128)(2,1)S(1)}, u32[]{:S(2)}, u32[]{:S(2)}) collective-permute-start(bf16[1,128,512]{2,1,0:T(8,128)(2,1)S(1)} %select_bitcast_fusion.3), channel_id=1, source_target_pairs={{0,128},{32,160},{64,192},{96,224},{128,0},{160,32},{192,64},{224,... | collective-permute-start | bytes 393224 | tf_op jit(solution)/shard_map/ppermute | solution.py:93
  72.9 7.5 %collective-permute-done.3 = bf16[1,128,512]{2,1,0:T(8,128)(2,1)S(1)} collective-permute-done((bf16[1,128,512]{2,1,0:T(8,128)(2,1)S(1)}, bf16[1,128,512]{2,1,0:T(8,128)(2,1)S(1)}, u32[]{:S(2)}, u32[]{:S(2)}) %collective-permute-start.3) | collective-permute-done | bytes 131104 | tf_op jit(solution)/shard_map/ppermute | solution.py:93
  80.5 2.8 gather_fusion.2
  83.6 11.2 %collective-permute-start.4 = (bf16[1,128,512]{2,1,0:T(8,128)(2,1)S(1)}, bf16[1,128,512]{2,1,0:T(8,128)(2,1)S(1)}, u32[]{:S(2)}, u32[]{:S(2)}) collective-permute-start(bf16[1,128,512]{2,1,0:T(8,128)(2,1)S(1)} %bitcast.102), channel_id=1, source_target_pairs={{0,256},{32,288},{64,320},{96,352},{128,384},{160,416},{192,448},{... | collective-permute-start | bytes 393224 | tf_op jit(solution)/shard_map/ppermute | solution.py:83
  94.8 10.2 %collective-permute-done.4 = bf16[1,128,512]{2,1,0:T(8,128)(2,1)S(1)} collective-permute-done((bf16[1,128,512]{2,1,0:T(8,128)(2,1)S(1)}, bf16[1,128,512]{2,1,0:T(8,128)(2,1)S(1)}, u32[]{:S(2)}, u32[]{:S(2)}) %collective-permute-start.4) | collective-permute-done | bytes 131104 | tf_op jit(solution)/shard_map/ppermute | solution.py:83
  108.1 4.7 %gather_fusion.3 = bf16[24,128,512]{2,1,0:T(8,128)(2,1)} fusion(bf16[32,128,512]{2,1,0:T(8,128)(2,1)} %bitcast.100, s32[1024]{0:T(1024)S(1)} %get-tuple-element.22), kind=kCustom, calls=%fused_computation.5 | custom fusion | bytes 6291552 | tf_op jit(solution)/shard_map/jit(_take)/gather | solution.py:155
  113.6 3.5 %collective-permute-start.6 = (bf16[2,128,512]{2,1,0:T(8,128)(2,1)S(1)}, bf16[2,128,512]{2,1,0:T(8,128)(2,1)S(1)}, u32[]{:S(2)}, u32[]{:S(2)}) collective-permute-start(bf16[2,128,512]{2,1,0:T(8,128)(2,1)S(1)} %select_bitcast_fusion), channel_id=1, source_target_pairs={{0,64},{32,96},{64,0},{96,32},{128,192},{160,224},{192,128},{224,1... | collective-permute-start | bytes 786440 | tf_op jit(solution)/shard_map/ppermute | solution.py:93
  117.1 2.9 fusion.2
  120.0 9.0 %collective-permute-done.6 = bf16[2,128,512]{2,1,0:T(8,128)(2,1)S(1)} collective-permute-done((bf16[2,128,512]{2,1,0:T(8,128)(2,1)S(1)}, bf16[2,128,512]{2,1,0:T(8,128)(2,1)S(1)}, u32[]{:S(2)}, u32[]{:S(2)}) %collective-permute-start.6) | collective-permute-done | bytes 262176 | tf_op jit(solution)/shard_map/ppermute | solution.py:93
  129.2 8.5 %collective-permute-start.7 = (bf16[1,128,512]{2,1,0:T(8,128)(2,1)S(1)}, bf16[1,128,512]{2,1,0:T(8,128)(2,1)S(1)}, u32[]{:S(2)}, u32[]{:S(2)}) collective-permute-start(bf16[1,128,512]{2,1,0:T(8,128)(2,1)S(1)} %select_bitcast_fusion.2), channel_id=1, source_target_pairs={{0,128},{32,160},{64,192},{96,224},{128,0},{160,32},{192,64},{224,... | collective-permute-start | bytes 393224 | tf_op jit(solution)/shard_map/ppermute | solution.py:93
  138.3 10.7 %collective-permute-done.7 = bf16[1,128,512]{2,1,0:T(8,128)(2,1)S(1)} collective-permute-done((bf16[1,128,512]{2,1,0:T(8,128)(2,1)S(1)}, bf16[1,128,512]{2,1,0:T(8,128)(2,1)S(1)}, u32[]{:S(2)}, u32[]{:S(2)}) %collective-permute-start.7) | collective-permute-done | bytes 131104 | tf_op jit(solution)/shard_map/ppermute | solution.py:93
  158.6 9.5 %all-to-all-start = ((f32[32,32,512]{2,1,0:T(8,128)}), f32[32,32,512]{2,1,0:T(8,128)S(1)}, u32[]{:S(2)}, u32[]{:S(2)}) async-start(f32[32,32,512]{2,1,0:T(8,128)} %gather_fusion.4), calls=%async_computation | async-start | bytes 4194304 | tf_op jit(solution)/shard_map/all_to_all | solution.py:28
  169.4 26.5 %all-to-all-done = f32[32,32,512]{2,1,0:T(8,128)S(1)} async-done(((f32[32,32,512]{2,1,0:T(8,128)}), f32[32,32,512]{2,1,0:T(8,128)S(1)}, u32[]{:S(2)}, u32[]{:S(2)}) %all-to-all-start) | async-done | bytes 2097184 | tf_op jit(solution)/shard_map/all_to_all | solution.py:28
  198.0 3.3 %collective-permute-done.8 = f32[40,512]{1,0:T(8,128)S(1)} collective-permute-done((f32[40,512]{1,0:T(8,128)S(1)}, f32[40,512]{1,0:T(8,128)S(1)}, u32[]{:S(2)}, u32[]{:S(2)}) %collective-permute-start.8) | collective-permute-done | bytes 81952 | tf_op jit(solution)/shard_map/ppermute | solution.py:34
  203.2 4.8 %collective-permute-done.9 = f32[40,512]{1,0:T(8,128)S(1)} collective-permute-done((f32[40,512]{1,0:T(8,128)S(1)}, f32[40,512]{1,0:T(8,128)S(1)}, u32[]{:S(2)}, u32[]{:S(2)}) %collective-permute-start.9) | collective-permute-done | bytes 81952 | tf_op jit(solution)/shard_map/ppermute | solution.py:34
  208.0 4.8 %collective-permute-start.10 = (f32[40,512]{1,0:T(8,128)S(1)}, f32[40,512]{1,0:T(8,128)S(1)}, u32[]{:S(2)}, u32[]{:S(2)}) collective-permute-start(f32[40,512]{1,0:T(8,128)S(1)} %add.276), channel_id=1, source_target_pairs={{0,128},{32,160},{64,192},{96,224},{128,0},{160,32},{192,64},{224,... | collective-permute-start | bytes 245768 | tf_op jit(solution)/shard_map/ppermute | solution.py:34
  212.8 6.2 %collective-permute-done.10 = f32[40,512]{1,0:T(8,128)S(1)} collective-permute-done((f32[40,512]{1,0:T(8,128)S(1)}, f32[40,512]{1,0:T(8,128)S(1)}, u32[]{:S(2)}, u32[]{:S(2)}) %collective-permute-start.10) | collective-permute-done | bytes 81952 | tf_op jit(solution)/shard_map/ppermute | solution.py:34
  218.9 7.1 %collective-permute-start.11 = (f32[40,512]{1,0:T(8,128)S(1)}, f32[40,512]{1,0:T(8,128)S(1)}, u32[]{:S(2)}, u32[]{:S(2)}) collective-permute-start(f32[40,512]{1,0:T(8,128)S(1)} %add.277), channel_id=1, source_target_pairs={{0,256},{32,288},{64,320},{96,352},{128,384},{160,416},{192,448},{... | collective-permute-start | bytes 245768 | tf_op jit(solution)/shard_map/ppermute | solution.py:34
  226.1 9.3 %collective-permute-done.11 = f32[40,512]{1,0:T(8,128)S(1)} collective-permute-done((f32[40,512]{1,0:T(8,128)S(1)}, f32[40,512]{1,0:T(8,128)S(1)}, u32[]{:S(2)}, u32[]{:S(2)}) %collective-permute-start.11) | collective-permute-done | bytes 81952 | tf_op jit(solution)/shard_map/ppermute | solution.py:34
  235.4 8.9 %collective-permute-start.12 = (f32[40,512]{1,0:T(8,128)S(1)}, f32[40,512]{1,0:T(8,128)S(1)}, u32[]{:S(2)}, u32[]{:S(2)}) collective-permute-start(f32[40,512]{1,0:T(8,128)S(1)} %add.278), channel_id=1, source_target_pairs={{0,16},{1,5},{2,18},{3,7},{4,20},{5,1},{6,22},{7,3},{8,24},{9,13},... | collective-permute-start | bytes 245768 | tf_op jit(solution)/shard_map/ppermute | solution.py:43
  246.2 4.8 %collective-permute-start.13 = (f32[72,512]{1,0:T(8,128)S(1)}, f32[72,512]{1,0:T(8,128)S(1)}, u32[]{:S(2)}, u32[]{:S(2)}) collective-permute-start(f32[72,512]{1,0:T(8,128)S(1)} %pad_maximum_fusion.8), channel_id=1, source_target_pairs={{0,8},{1,3},{2,10},{3,1},{4,12},{5,7},{6,14},{7,5},{8,0},{9,11},{1... | collective-permute-start | bytes 442376 | tf_op jit(solution)/shard_map/ppermute | solution.py:43
  251.2 2.4 collective-permute-done.13
  253.6 4.8 %collective-permute-start.14 = (f32[136,512]{1,0:T(8,128)S(1)}, f32[136,512]{1,0:T(8,128)S(1)}, u32[]{:S(2)}, u32[]{:S(2)}) collective-permute-start(f32[136,512]{1,0:T(8,128)S(1)} %pad_maximum_fusion.5), channel_id=1, source_target_pairs={{0,4},{1,17},{2,6},{3,19},{4,0},{5,21},{6,2},{7,23},{8,12},{9,25},... | collective-permute-start | bytes 835592 | tf_op jit(solution)/shard_map/ppermute | solution.py:43
  258.5 3.9 %collective-permute-done.14 = f32[136,512]{1,0:T(8,128)S(1)} collective-permute-done((f32[136,512]{1,0:T(8,128)S(1)}, f32[136,512]{1,0:T(8,128)S(1)}, u32[]{:S(2)}, u32[]{:S(2)}) %collective-permute-start.14) | collective-permute-done | bytes 278560 | tf_op jit(solution)/shard_map/ppermute | solution.py:43
  262.5 5.0 %collective-permute-start.15 = (f32[264,512]{1,0:T(8,128)S(1)}, f32[264,512]{1,0:T(8,128)S(1)}, u32[]{:S(2)}, u32[]{:S(2)}) collective-permute-start(f32[264,512]{1,0:T(8,128)S(1)} %pad_maximum_fusion.4), channel_id=1, source_target_pairs={{0,2},{1,9},{2,0},{3,11},{4,6},{5,13},{6,4},{7,15},{8,10},{9,1},{1... | collective-permute-start | bytes 1622024 | tf_op jit(solution)/shard_map/ppermute | solution.py:43
  267.8 6.8 %collective-permute-done.15 = f32[264,512]{1,0:T(8,128)S(1)} collective-permute-done((f32[264,512]{1,0:T(8,128)S(1)}, f32[264,512]{1,0:T(8,128)S(1)}, u32[]{:S(2)}, u32[]{:S(2)}) %collective-permute-start.15) | collective-permute-done | bytes 540704 | tf_op jit(solution)/shard_map/ppermute | solution.py:43
  274.7 6.4 %collective-permute-start.16 = (f32[520,512]{1,0:T(8,128)S(1)}, f32[520,512]{1,0:T(8,128)}, u32[]{:S(2)}, u32[]{:S(2)}) collective-permute-start(f32[520,512]{1,0:T(8,128)S(1)} %pad_maximum_fusion.2), channel_id=1, source_target_pairs={{0,1},{1,0},{2,3},{3,2},{4,5},{5,4},{6,7},{7,6},{8,9},{9,8},{10,11... | collective-permute-start | bytes 3194888 | tf_op jit(solution)/shard_map/ppermute | solution.py:43
  286.0 2.8 slice_select_fusion
  (109 shorter events, 32.5 us)
Async XLA Ops:
  7.2 141.9 %copy-start = (bf16[512,512]{1,0:T(8,128)(2,1)S(1)}, bf16[512,512]{1,0:T(8,128)(2,1)}, u32[]{:S(2)}) copy-start(bf16[512,512]{1,0:T(8,128)(2,1)} %param.20) | copy-start | bytes 1572868
  7.2 19.4 %copy-start.1 = (s32[16]{0:T(128)S(1)}, s32[16]{0:T(128)}, u32[]{:S(2)}) copy-start(s32[16]{0:T(128)} %param.18) | copy-start | bytes 196
  7.2 32.3 %copy-start.7 = (s32[4]{0:T(128)S(1)}, s32[4]{0:T(128)}, u32[]{:S(2)}) copy-start(s32[4]{0:T(128)} %param.15) | copy-start | bytes 52
  7.2 73.2 %all-gather.2.cloned.1.call-start = ((), (), s32[]{:S(2)}) async-start(), calls=%async_computation.1 | async-start | bytes 4325376 | tf_op jit(solution)/shard_map/all_gather | solution.py:149
  8.9 18.9 %collective-permute-start = (bf16[1,128,512]{2,1,0:T(8,128)(2,1)S(1)}, bf16[1,128,512]{2,1,0:T(8,128)(2,1)S(1)}, u32[]{:S(2)}, u32[]{:S(2)}) collective-permute-start(bf16[1,128,512]{2,1,0:T(8,128)(2,1)S(1)} %slice_bitcast_fusion.6), channel_id=1, source_target_pairs={{0,256},{32,288},{64,320},{96,352},{128,384},{160,416},{192,448},{... | collective-permute-start | bytes 393224 | tf_op jit(solution)/shard_map/ppermute | solution.py:83
  27.8 16.9 %collective-permute-start.1 = (bf16[2,128,512]{2,1,0:T(8,128)(2,1)S(1)}, bf16[2,128,512]{2,1,0:T(8,128)(2,1)S(1)}, u32[]{:S(2)}, u32[]{:S(2)}) collective-permute-start(bf16[2,128,512]{2,1,0:T(8,128)(2,1)S(1)} %maximum_select_fusion.2), channel_id=1, source_target_pairs={{0,32},{32,0},{64,96},{96,64},{128,160},{160,128},{192,224},{224,1... | collective-permute-start | bytes 786440 | tf_op jit(solution)/shard_map/ppermute | solution.py:83
  45.4 2.2 copy-start.2
  45.6 24.0 %copy-start.5 = (s32[4,8]{1,0:T(4,128)S(1)}, s32[4,8]{1,0:T(4,128)}, u32[]{:S(2)}) copy-start(s32[4,8]{1,0:T(4,128)} %param.14) | copy-start | bytes 388
  45.6 15.8 %collective-permute-start.2 = (bf16[2,128,512]{2,1,0:T(8,128)(2,1)S(1)}, bf16[2,128,512]{2,1,0:T(8,128)(2,1)S(1)}, u32[]{:S(2)}, u32[]{:S(2)}) collective-permute-start(bf16[2,128,512]{2,1,0:T(8,128)(2,1)S(1)} %select_bitcast_fusion.1), channel_id=1, source_target_pairs={{0,64},{32,96},{64,0},{96,32},{128,192},{160,224},{192,128},{224,1... | collective-permute-start | bytes 786440 | tf_op jit(solution)/shard_map/ppermute | solution.py:93
  61.5 18.9 %collective-permute-start.3 = (bf16[1,128,512]{2,1,0:T(8,128)(2,1)S(1)}, bf16[1,128,512]{2,1,0:T(8,128)(2,1)S(1)}, u32[]{:S(2)}, u32[]{:S(2)}) collective-permute-start(bf16[1,128,512]{2,1,0:T(8,128)(2,1)S(1)} %select_bitcast_fusion.3), channel_id=1, source_target_pairs={{0,128},{32,160},{64,192},{96,224},{128,0},{160,32},{192,64},{224,... | collective-permute-start | bytes 393224 | tf_op jit(solution)/shard_map/ppermute | solution.py:93
  83.3 23.7 %copy-start.6 = (s32[32]{0:T(128)S(1)}, s32[32]{0:T(128)}, u32[]{:S(2)}) copy-start(s32[32]{0:T(128)} %constant.291) | copy-start | bytes 388
  83.6 21.3 %collective-permute-start.4 = (bf16[1,128,512]{2,1,0:T(8,128)(2,1)S(1)}, bf16[1,128,512]{2,1,0:T(8,128)(2,1)S(1)}, u32[]{:S(2)}, u32[]{:S(2)}) collective-permute-start(bf16[1,128,512]{2,1,0:T(8,128)(2,1)S(1)} %bitcast.102), channel_id=1, source_target_pairs={{0,256},{32,288},{64,320},{96,352},{128,384},{160,416},{192,448},{... | collective-permute-start | bytes 393224 | tf_op jit(solution)/shard_map/ppermute | solution.py:83
  105.0 7.8 %collective-permute-start.5 = (bf16[2,128,512]{2,1,0:T(8,128)(2,1)S(1)}, bf16[2,128,512]{2,1,0:T(8,128)(2,1)S(1)}, u32[]{:S(2)}, u32[]{:S(2)}) collective-permute-start(bf16[2,128,512]{2,1,0:T(8,128)(2,1)S(1)} %maximum_select_fusion.3), channel_id=1, source_target_pairs={{0,32},{32,0},{64,96},{96,64},{128,160},{160,128},{192,224},{224,1... | collective-permute-start | bytes 786440 | tf_op jit(solution)/shard_map/ppermute | solution.py:83
  113.6 15.4 %collective-permute-start.6 = (bf16[2,128,512]{2,1,0:T(8,128)(2,1)S(1)}, bf16[2,128,512]{2,1,0:T(8,128)(2,1)S(1)}, u32[]{:S(2)}, u32[]{:S(2)}) collective-permute-start(bf16[2,128,512]{2,1,0:T(8,128)(2,1)S(1)} %select_bitcast_fusion), channel_id=1, source_target_pairs={{0,64},{32,96},{64,0},{96,32},{128,192},{160,224},{192,128},{224,1... | collective-permute-start | bytes 786440 | tf_op jit(solution)/shard_map/ppermute | solution.py:93
  120.0 17.7 %copy-start.3 = (bf16[512,512]{1,0:T(8,128)(2,1)S(1)}, bf16[512,512]{1,0:T(8,128)(2,1)}, u32[]{:S(2)}) copy-start(bf16[512,512]{1,0:T(8,128)(2,1)} %param.19) | copy-start | bytes 1572868
  129.2 19.9 %collective-permute-start.7 = (bf16[1,128,512]{2,1,0:T(8,128)(2,1)S(1)}, bf16[1,128,512]{2,1,0:T(8,128)(2,1)S(1)}, u32[]{:S(2)}, u32[]{:S(2)}) collective-permute-start(bf16[1,128,512]{2,1,0:T(8,128)(2,1)S(1)} %select_bitcast_fusion.2), channel_id=1, source_target_pairs={{0,128},{32,160},{64,192},{96,224},{128,0},{160,32},{192,64},{224,... | collective-permute-start | bytes 393224 | tf_op jit(solution)/shard_map/ppermute | solution.py:93
  149.7 1.1 copy-start.4
  158.6 37.3 %all-to-all-start = ((f32[32,32,512]{2,1,0:T(8,128)}), f32[32,32,512]{2,1,0:T(8,128)S(1)}, u32[]{:S(2)}, u32[]{:S(2)}) async-start(f32[32,32,512]{2,1,0:T(8,128)} %gather_fusion.4), calls=%async_computation | async-start | bytes 4194304 | tf_op jit(solution)/shard_map/all_to_all | solution.py:28
  196.1 5.2 %collective-permute-start.8 = (f32[40,512]{1,0:T(8,128)S(1)}, f32[40,512]{1,0:T(8,128)S(1)}, u32[]{:S(2)}, u32[]{:S(2)}) collective-permute-start(f32[40,512]{1,0:T(8,128)S(1)} %concatenate.64), channel_id=1, source_target_pairs={{0,32},{32,0},{64,96},{96,64},{128,160},{160,128},{192,224},{224,1... | collective-permute-start | bytes 245768 | tf_op jit(solution)/shard_map/ppermute | solution.py:34
  201.3 6.7 %collective-permute-start.9 = (f32[40,512]{1,0:T(8,128)S(1)}, f32[40,512]{1,0:T(8,128)S(1)}, u32[]{:S(2)}, u32[]{:S(2)}) collective-permute-start(f32[40,512]{1,0:T(8,128)S(1)} %pad_add_fusion), channel_id=1, source_target_pairs={{0,64},{32,96},{64,0},{96,32},{128,192},{160,224},{192,128},{224,1... | collective-permute-start | bytes 245768 | tf_op jit(solution)/shard_map/ppermute | solution.py:34
  208.0 10.9 %collective-permute-start.10 = (f32[40,512]{1,0:T(8,128)S(1)}, f32[40,512]{1,0:T(8,128)S(1)}, u32[]{:S(2)}, u32[]{:S(2)}) collective-permute-start(f32[40,512]{1,0:T(8,128)S(1)} %add.276), channel_id=1, source_target_pairs={{0,128},{32,160},{64,192},{96,224},{128,0},{160,32},{192,64},{224,... | collective-permute-start | bytes 245768 | tf_op jit(solution)/shard_map/ppermute | solution.py:34
  218.9 16.4 %collective-permute-start.11 = (f32[40,512]{1,0:T(8,128)S(1)}, f32[40,512]{1,0:T(8,128)S(1)}, u32[]{:S(2)}, u32[]{:S(2)}) collective-permute-start(f32[40,512]{1,0:T(8,128)S(1)} %add.277), channel_id=1, source_target_pairs={{0,256},{32,288},{64,320},{96,352},{128,384},{160,416},{192,448},{... | collective-permute-start | bytes 245768 | tf_op jit(solution)/shard_map/ppermute | solution.py:34
  235.4 10.8 %collective-permute-start.12 = (f32[40,512]{1,0:T(8,128)S(1)}, f32[40,512]{1,0:T(8,128)S(1)}, u32[]{:S(2)}, u32[]{:S(2)}) collective-permute-start(f32[40,512]{1,0:T(8,128)S(1)} %add.278), channel_id=1, source_target_pairs={{0,16},{1,5},{2,18},{3,7},{4,20},{5,1},{6,22},{7,3},{8,24},{9,13},... | collective-permute-start | bytes 245768 | tf_op jit(solution)/shard_map/ppermute | solution.py:43
  246.2 7.4 %collective-permute-start.13 = (f32[72,512]{1,0:T(8,128)S(1)}, f32[72,512]{1,0:T(8,128)S(1)}, u32[]{:S(2)}, u32[]{:S(2)}) collective-permute-start(f32[72,512]{1,0:T(8,128)S(1)} %pad_maximum_fusion.8), channel_id=1, source_target_pairs={{0,8},{1,3},{2,10},{3,1},{4,12},{5,7},{6,14},{7,5},{8,0},{9,11},{1... | collective-permute-start | bytes 442376 | tf_op jit(solution)/shard_map/ppermute | solution.py:43
  253.6 8.8 %collective-permute-start.14 = (f32[136,512]{1,0:T(8,128)S(1)}, f32[136,512]{1,0:T(8,128)S(1)}, u32[]{:S(2)}, u32[]{:S(2)}) collective-permute-start(f32[136,512]{1,0:T(8,128)S(1)} %pad_maximum_fusion.5), channel_id=1, source_target_pairs={{0,4},{1,17},{2,6},{3,19},{4,0},{5,21},{6,2},{7,23},{8,12},{9,25},... | collective-permute-start | bytes 835592 | tf_op jit(solution)/shard_map/ppermute | solution.py:43
  262.5 12.1 %collective-permute-start.15 = (f32[264,512]{1,0:T(8,128)S(1)}, f32[264,512]{1,0:T(8,128)S(1)}, u32[]{:S(2)}, u32[]{:S(2)}) collective-permute-start(f32[264,512]{1,0:T(8,128)S(1)} %pad_maximum_fusion.4), channel_id=1, source_target_pairs={{0,2},{1,9},{2,0},{3,11},{4,6},{5,13},{6,4},{7,15},{8,10},{9,1},{1... | collective-permute-start | bytes 1622024 | tf_op jit(solution)/shard_map/ppermute | solution.py:43
  274.7 8.8 %collective-permute-start.16 = (f32[520,512]{1,0:T(8,128)S(1)}, f32[520,512]{1,0:T(8,128)}, u32[]{:S(2)}, u32[]{:S(2)}) collective-permute-start(f32[520,512]{1,0:T(8,128)S(1)} %pad_maximum_fusion.2), channel_id=1, source_target_pairs={{0,1},{1,0},{2,3},{3,2},{4,5},{5,4},{6,7},{7,6},{8,9},{9,8},{10,11... | collective-permute-start | bytes 3194888 | tf_op jit(solution)/shard_map/ppermute | solution.py:43
Sparse Core Ops, SparseCore 0:
  11.2 67.0 all-gather.1
